TPU v7x, 256 devices: a whole 4x4x8 slice. The times are simulated.
256 devices in a mesh: gx: 64 (over y_hi, x, z), gy: 4 (over y_lo, core).
Axes of the slice: x: 4, y: 4 (y_hi: 2, y_lo: 2; y = y_hi * 2 + y_lo), z: 8, core: 2. Of those that a mesh axis runs over, the one named last changes fastest.
Arguments:
- base_flow: float32 [3, 1536, 32, 1024], P(None, 'gx', None, 'gy'), may hold values from -6 to 6
- adjoint: float32 [3, 1536, 32, 1024], P(None, 'gx', None, 'gy'), may hold values from -6 to 6
- first_op: bfloat16 [1024, 1024], replicated, may hold values from -2 to 2
- second_op: bfloat16 [1024, 1024], replicated, may hold values from -9 to 5
Outputs:
- new_adjoint: float32 [3, 1536, 32, 1024], P(None, 'gx', None, 'gy')
All inputs are finite; a program needn't handle non-finite values.
Results may differ from a plain program's by a relative error of at most 0.0025.
Values may be sent and summed in bfloat16 or wider, within the bound.
No kernel may reach another device: no remote copies, remote signals or barrier semaphores. Data moves between devices by JAX's collectives and lax.ppermute only.
A program may use at most 128 MiB of HBM per device.

v0:
```python
import jax
import jax.numpy as jnp
from jax import lax
from jax.sharding import PartitionSpec as P

C_FIRST = (0.8, -0.2, 4.0 / 105.0, -1.0 / 280.0)
C_SECOND = (1.6, -0.2, 8.0 / 315.0, -1.0 / 560.0)
C_CENTER = -205.0 / 72.0
VISCOSITY = 0.1
STEP_WEIGHT = 0.5


def padded(cells, sides, width):
    for axis, dim in sides:
        count = lax.axis_size(axis)
        head = lax.slice_in_dim(cells, 0, width, axis=dim)
        tail = lax.slice_in_dim(cells, cells.shape[dim] - width, cells.shape[dim], axis=dim)
        cells = jnp.concatenate(
            [
                lax.ppermute(tail, axis, [(i, (i + 1) % count) for i in range(count)]),
                cells,
                lax.ppermute(head, axis, [((i + 1) % count, i) for i in range(count)]),
            ],
            axis=dim,
        )
    return cells


def first_streamwise(extended, cells):
    result = C_FIRST[0] * (extended[:, 5 : 5 + cells] - extended[:, 3 : 3 + cells])
    for offset in range(2, 5):
        result = result + C_FIRST[offset - 1] * (
            extended[:, 4 + offset : 4 + offset + cells]
            - extended[:, 4 - offset : 4 - offset + cells]
        )
    return result


def second_streamwise(extended, cells):
    result = C_CENTER * extended[:, 4 : 4 + cells]
    for offset in range(1, 5):
        result = result + C_SECOND[offset - 1] * (
            extended[:, 4 + offset : 4 + offset + cells]
            + extended[:, 4 - offset : 4 - offset + cells]
        )
    return result


def first_periodic(field, direction):
    result = C_FIRST[0] * (jnp.roll(field, -1, direction) - jnp.roll(field, 1, direction))
    for offset in range(2, 5):
        result = result + C_FIRST[offset - 1] * (
            jnp.roll(field, -offset, direction) - jnp.roll(field, offset, direction)
        )
    return result


def second_periodic(field, direction):
    result = C_CENTER * field
    for offset in range(1, 5):
        result = result + C_SECOND[offset - 1] * (
            jnp.roll(field, -offset, direction) + jnp.roll(field, offset, direction)
        )
    return result


def wall_combine(normal_vel, slope_adj, curvature, adjoint_low, slope_base):
    coupling = jnp.sum(adjoint_low * slope_base, axis=0)
    first_part = normal_vel * slope_adj[0] + VISCOSITY * curvature[0]
    middle_part = normal_vel * slope_adj[1] + VISCOSITY * curvature[1] - coupling
    last_part = normal_vel * slope_adj[2] + VISCOSITY * curvature[2]
    return jnp.stack((first_part, middle_part, last_part), 0)


def body(base_flow, adjoint, first_op, second_op):
    cells = base_flow.shape[1]
    spanwise = base_flow.shape[2]
    local_rows = base_flow.shape[3]
    groups = lax.axis_size("gy")
    total_rows = local_rows * groups
    extended_base = padded(base_flow, (("gx", 1),), 4)
    extended_adj = padded(adjoint, (("gx", 1),), 4)
    base_low = lax.optimization_barrier(base_flow.astype(jnp.bfloat16))
    adjoint_low = lax.optimization_barrier(adjoint.astype(jnp.bfloat16))
    base_blocks = base_low.reshape(3, cells, spanwise, 1, local_rows)
    adjoint_blocks = adjoint_low.reshape(3, cells, spanwise, 1, local_rows)
    first_blocks = first_op.reshape(total_rows, groups, local_rows)
    second_blocks = second_op.reshape(total_rows, groups, local_rows)

    def to_blocks(field):
        return field.reshape(field.shape[0], field.shape[1], field.shape[2], groups, local_rows)

    base_lines = lax.all_to_all(base_blocks, "gy", split_axis=2, concat_axis=3, tiled=True)
    adjoint_lines = lax.all_to_all(adjoint_blocks, "gy", split_axis=2, concat_axis=3, tiled=True)
    slope_base = jnp.einsum(
        "fxzpk,ipk->fxzi", base_lines, first_blocks, preferred_element_type=jnp.float32
    )
    slope_adj = jnp.einsum(
        "fxzpk,ipk->fxzi", adjoint_lines, first_blocks, preferred_element_type=jnp.float32
    )
    curves = jnp.einsum(
        "fxzpk,ipk->fxzi", adjoint_lines, second_blocks, preferred_element_type=jnp.float32
    )
    returned = (
        lax.all_to_all(to_blocks(slope_base), "gy", split_axis=3, concat_axis=2, tiled=True),
        lax.all_to_all(to_blocks(slope_adj), "gy", split_axis=3, concat_axis=2, tiled=True),
        lax.all_to_all(to_blocks(curves), "gy", split_axis=3, concat_axis=2, tiled=True),
    )
    dx_base = first_streamwise(extended_base, cells)
    dz_base = first_periodic(base_flow, 2)
    dx_adj = first_streamwise(extended_adj, cells)
    dxx_adj = second_streamwise(extended_adj, cells)
    dz_adj = first_periodic(adjoint, 2)
    dzz_adj = second_periodic(adjoint, 2)
    carried = (
        base_flow[0][None] * dx_adj + base_flow[2][None] * dz_adj + VISCOSITY * (dxx_adj + dzz_adj)
    )
    first_coupling = jnp.sum(adjoint * dx_base, axis=0)
    last_coupling = jnp.sum(adjoint * dz_base, axis=0)
    tendency = jnp.stack((carried[0] - first_coupling, carried[1], carried[2] - last_coupling), 0)
    field_shape = (3, cells, spanwise, local_rows)
    slope_base = returned[0].reshape(field_shape)
    slope_adj = returned[1].reshape(field_shape)
    curves = returned[2].reshape(field_shape)
    wall_part = wall_combine(
        base_low[1].astype(jnp.float32),
        slope_adj,
        curves,
        adjoint_low.astype(jnp.float32),
        slope_base,
    )
    updated = adjoint + STEP_WEIGHT * (tendency + wall_part)
    wall_index = lax.axis_index("gy") * local_rows + jnp.arange(local_rows, dtype=jnp.int32)
    interior = (wall_index > 0) & (wall_index < total_rows - 1)
    return jnp.where(interior, updated, jnp.float32(0.0))


def solution(mesh):
    return jax.shard_map(
        body,
        mesh=mesh,
        in_specs=(P(None, "gx", None, "gy"), P(None, "gx", None, "gy"), P(), P()),
        out_specs=P(None, "gx", None, "gy"),
        check_vma=False,
    )
```

profile of v0, /device:TPU:1, one launch (start us, length us, event | category | flops | bytes accessed | tf_op | source)
XLA Modules:
  0.0 195.5 jit_solution(18336623169807040037)
XLA Ops:
  0.0 4.7 %constant_dynamic-update-slice_fusion.3 = (f32[3,28,32,256]{3,1,2,0:T(8,128)}, f32[3,24,32,256]{3,1,2,0:T(8,128)S(1)}) fusion(f32[3,24,32,256]{3,2,1,0:T(8,128)} %param.4), kind=kLoop, calls=%fused_computation.102 | loop fusion | bytes 7077888
  4.7 1.1 fusion.60
  5.8 11.2 %collective-permute-start.2 = (f32[3,4,32,256]{3,1,2,0:T(4,128)}, f32[3,4,32,256]{3,1,2,0:T(4,128)}, u32[]{:S(2)}, u32[]{:S(2)}) collective-permute-start(f32[3,4,32,256]{3,1,2,0:T(4,128)} %get-tuple-element.16), channel_id=1, source_target_pairs={{4,0},{8,4},{12,8},{16,12},{20,16},{24,20},{28,24},{32,28},{36,32}... | collective-permute-start | bytes 1179656 | tf_op jit(solution)/shard_map/ppermute | solution.py:22
  17.0 2.3 %copy.219 = bf16[3,24,32,256]{3,1,0,2:T(8,128)(2,1)} copy(f32[3,24,32,256]{3,2,1,0:T(8,128)S(1)} %copy-done.1) | data formatting | bytes 3538944 | tf_op args[1]
  19.3 5.2 %all-to-all-start = ((bf16[3,24,32,1,256]{4,1,0,3,2:T(8,128)(2,1)}), bf16[3,24,32,1,256]{4,1,0,3,2:T(8,128)(2,1)}, u32[]{:S(2)}, u32[]{:S(2)}) async-start(bf16[3,24,32,1,256]{4,1,0,3,2:T(8,128)(2,1)} %bitcast.4), calls=%async_computation | async-start | bytes 2359296 | tf_op jit(solution)/shard_map/all_to_all | solution.py:94
  24.5 0.4 fusion.68
  24.9 0.4 fusion.66
  25.3 0.3 fusion.64
  25.6 0.4 fusion.62
  26.0 0.0 copy-start.2
  26.2 1.5 copy-done.2
  27.7 4.3 %fusion.24 = f32[24,32,256]{2,0,1:T(8,128)} fusion(f32[3,24,1,256]{3,1,2,0:T(8,128)S(1)} %get-tuple-element.33, f32[3,24,31,256]{3,1,2,0:T(8,128)S(1)} %get-tuple-element.35, f32[3,24,31,256]{3,1,2,0:T(8,128)S(1)} %get-tuple-element.34, f32[3,24,1,256]{3,1,2,0:T(8,128)S(1)} %get-tuple-element.32, f32[3,24,2,256]{3,1,2,0:T(8,128)S(1)} %get-tuple-element.29, ...), kind=kLoop, calls=%fused_computation.47 | loop fusion | flops 12189696 | bytes 22020096 | tf_op jit(solution)/shard_map/reduce_sum | solution.py:119
  32.0 0.1 slice_bitcast_fusion.4
  32.1 1.3 copy.220
  33.4 1.3 copy.94
  34.7 1.3 copy.99
  36.1 2.9 %copy.142 = bf16[1024,1024]{0,1:T(8,128)(2,1)S(1)} copy(bf16[1024,1024]{1,0:T(8,128)(2,1)} %param.6) | data formatting | bytes 4194304 | tf_op args[2]
  38.9 2.6 %copy.143 = bf16[1024,256,4]{1,0,2:T(8,128)(2,1)} copy(bf16[1024,256,4]{0,1,2:T(8,128)(2,1)S(1)} %bitcast.82) | data formatting | bytes 4194304 | tf_op jit(solution)/shard_map/fxzpk,ipk->fxzi/dot_general | solution.py:98
  41.5 3.9 %copy.148 = bf16[1024,1024]{0,1:T(8,128)(2,1)} copy(bf16[1024,1024]{1,0:T(8,128)(2,1)} %param.7) | data formatting | bytes 4194304 | tf_op args[3]
  45.5 4.1 %copy.149 = bf16[1024,256,4]{1,0,2:T(8,128)(2,1)} copy(bf16[1024,256,4]{0,1,2:T(8,128)(2,1)} %bitcast.83) | data formatting | bytes 4194304 | tf_op jit(solution)/shard_map/fxzpk,ipk->fxzi/dot_general | solution.py:101
  49.6 1.1 copy.156
  50.7 2.8 %constant_dynamic-update-slice_fusion.1 = f32[3,28,32,256]{3,1,2,0:T(8,128)} fusion(f32[3,24,32,256]{3,2,1,0:T(8,128)S(1)} %copy-done.3), kind=kLoop, calls=%fused_computation.100 | loop fusion | bytes 4718592
  53.4 1.9 constant_dynamic-update-slice_fusion.2
  55.3 4.5 %all-to-all-start.3 = ((bf16[3,24,32,1,256]{4,1,0,3,2:T(8,128)(2,1)}), bf16[3,24,32,1,256]{4,1,0,3,2:T(8,128)(2,1)}, u32[]{:S(2)}, u32[]{:S(2)}) async-start(bf16[3,24,32,1,256]{4,1,0,3,2:T(8,128)(2,1)} %copy.156), calls=%async_computation.3 | async-start | bytes 2359296 | tf_op jit(solution)/shard_map/all_to_all | solution.py:93
  59.8 0.0 collective-permute-done.3
  59.8 13.2 %fusion.6 = (f32[24,32,256]{2,0,1:T(8,128)}, f32[3,24,32,256]{3,1,2,0:T(8,128)S(1)}) fusion(f32[3,24,32,256]{3,1,2,0:T(8,128)} %copy-done, f32[3,4,32,256]{3,1,2,0:T(4,128)} %collective-permute-done.3, f32[3,28,32,256]{3,1,2,0:T(8,128)} %constant_dynamic-update-slice_fusion.2, f32[3,24,32,256]{3,2,1,0:T(8,128)} %param.5), kind=kLoop, calls=%fused_computation.18 | loop fusion | flops 9830400 | bytes 17694720 | tf_op jit(solution)/shard_map/reduce_sum | solution.py:118
  73.0 4.1 %fusion.38 = f32[3,24,8,4,256]{4,2,1,0,3:T(8,128)} fusion(bf16[4,256,256,4,1,1]{2,1,0,3,5,4:T(8,128)(2,1)S(1)} %bitcast.85, bf16[3,24,32,1,256]{4,1,0,3,2:T(8,128)(2,1)} %all-to-all-done), kind=kOutput, calls=%fused_computation.70 | convolution fusion | flops 1207959552 | bytes 5636096 | tf_op jit(solution)/shard_map/fxzpk,ipk->fxzi/dot_general | solution.py:98
  77.1 0.0 all-to-all-done.3
  77.1 4.7 %all-to-all-start.1 = ((f32[3,24,8,4,256]{4,2,1,0,3:T(8,128)}), f32[3,24,8,4,256]{4,2,1,0,3:T(8,128)}, u32[]{:S(2)}, u32[]{:S(2)}) async-start(f32[3,24,8,4,256]{4,2,1,0,3:T(8,128)} %fusion.38), calls=%async_computation.1 | async-start | bytes 4718592 | tf_op jit(solution)/shard_map/all_to_all | solution.py:106
  81.8 1.0 fusion.69
  82.9 7.5 %collective-permute-start = (f32[3,4,32,256]{3,1,2,0:T(4,128)}, f32[3,4,32,256]{3,1,2,0:T(4,128)}, u32[]{:S(2)}, u32[]{:S(2)}) collective-permute-start(f32[3,4,32,256]{3,1,2,0:T(4,128)} %get-tuple-element.38), channel_id=1, source_target_pairs={{4,0},{8,4},{12,8},{16,12},{20,16},{24,20},{28,24},{32,28},{36,32}... | collective-permute-start | bytes 1179656 | tf_op jit(solution)/shard_map/ppermute | solution.py:22
  90.3 0.8 fusion.75
  91.2 0.9 fusion.77
  92.0 2.4 %fusion.76 = (f32[3,24,28,256]{3,1,2,0:T(8,128)}, f32[3,24,28,256]{3,1,2,0:T(8,128)}) fusion(f32[3,24,32,256]{3,1,2,0:T(8,128)S(1)} %get-tuple-element.15), kind=kLoop, calls=%fused_computation.121 | loop fusion | bytes 8257536 | tf_op jit(solution)/shard_map/jit(_roll_static)/slice | solution.py:53
  94.4 2.4 %fusion.74 = (f32[3,24,29,256]{3,1,2,0:T(8,128)}, f32[3,24,29,256]{3,1,2,0:T(8,128)}) fusion(f32[3,24,32,256]{3,1,2,0:T(8,128)S(1)} %get-tuple-element.15), kind=kLoop, calls=%fused_computation.119 | loop fusion | bytes 8552448 | tf_op jit(solution)/shard_map/jit(_roll_static)/slice | solution.py:53
  96.8 4.1 %fusion.44 = f32[3,24,8,4,256]{4,2,1,0,3:T(8,128)} fusion(bf16[4,256,256,4,1,1]{2,1,0,3,5,4:T(8,128)(2,1)S(1)} %bitcast.87, bf16[3,24,32,1,256]{4,1,0,3,2:T(8,128)(2,1)} %all-to-all-done), kind=kOutput, calls=%fused_computation.72 | convolution fusion | flops 1207959552 | bytes 5636096 | tf_op jit(solution)/shard_map/fxzpk,ipk->fxzi/dot_general | solution.py:101
  100.9 8.5 %all-to-all-done.1 = f32[3,24,8,4,256]{4,2,1,0,3:T(8,128)} async-done(((f32[3,24,8,4,256]{4,2,1,0,3:T(8,128)}), f32[3,24,8,4,256]{4,2,1,0,3:T(8,128)}, u32[]{:S(2)}, u32[]{:S(2)}) %all-to-all-start.1) | async-done | bytes 2359328 | tf_op jit(solution)/shard_map/all_to_all | solution.py:106
  109.5 5.4 %all-to-all-start.2 = ((f32[3,24,8,4,256]{4,2,1,0,3:T(8,128)}), f32[3,24,8,4,256]{4,2,1,0,3:T(8,128)}, u32[]{:S(2)}, u32[]{:S(2)}) async-start(f32[3,24,8,4,256]{4,2,1,0,3:T(8,128)} %fusion.44), calls=%async_computation.2 | async-start | bytes 4718592 | tf_op jit(solution)/shard_map/all_to_all | solution.py:107
  114.9 0.7 fusion.73
  115.6 2.5 %fusion.70 = (f32[3,24,31,256]{3,1,2,0:T(8,128)}, f32[3,24,31,256]{3,1,2,0:T(8,128)}) fusion(f32[3,24,32,256]{3,1,2,0:T(8,128)S(1)} %get-tuple-element.15), kind=kLoop, calls=%fused_computation.115 | loop fusion | bytes 9142272 | tf_op jit(solution)/shard_map/jit(_roll_static)/slice | solution.py:50
  118.1 0.7 fusion.71
  118.7 0.0 collective-permute-start.1
  118.7 2.5 %fusion.72 = (f32[3,24,30,256]{3,1,2,0:T(8,128)}, f32[3,24,30,256]{3,1,2,0:T(8,128)}) fusion(f32[3,24,32,256]{3,1,2,0:T(8,128)S(1)} %get-tuple-element.15), kind=kLoop, calls=%fused_computation.117 | loop fusion | bytes 8847360 | tf_op jit(solution)/shard_map/jit(_roll_static)/slice | solution.py:53
  121.2 0.0 collective-permute-done
  121.2 1.9 constant_dynamic-update-slice_fusion
  123.1 4.2 %fusion.41 = f32[3,24,8,4,256]{4,2,1,0,3:T(8,128)} fusion(bf16[4,256,256,4,1,1]{2,1,0,3,5,4:T(8,128)(2,1)S(1)} %bitcast.86, bf16[3,24,32,1,256]{4,1,0,3,2:T(8,128)(2,1)} %all-to-all-done.3), kind=kOutput, calls=%fused_computation.71 | convolution fusion | flops 1207959552 | bytes 5636096 | tf_op jit(solution)/shard_map/fxzpk,ipk->fxzi/dot_general | solution.py:95
  127.3 23.7 %all-to-all-done.2 = f32[3,24,8,4,256]{4,2,1,0,3:T(8,128)} async-done(((f32[3,24,8,4,256]{4,2,1,0,3:T(8,128)}), f32[3,24,8,4,256]{4,2,1,0,3:T(8,128)}, u32[]{:S(2)}, u32[]{:S(2)}) %all-to-all-start.2) | async-done | bytes 2359328 | tf_op jit(solution)/shard_map/all_to_all | solution.py:107
  150.9 5.4 %all-to-all-start.4 = ((f32[3,24,8,4,256]{4,2,1,0,3:T(8,128)}), f32[3,24,8,4,256]{4,2,1,0,3:T(8,128)}, u32[]{:S(2)}, u32[]{:S(2)}) async-start(f32[3,24,8,4,256]{4,2,1,0,3:T(8,128)} %fusion.41), calls=%async_computation.4 | async-start | bytes 4718592 | tf_op jit(solution)/shard_map/all_to_all | solution.py:105
  156.4 0.0 collective-permute-done.1
  156.4 14.2 %multiply_add_fusion = f32[3,24,32,256]{3,1,2,0:T(8,128)S(1)} fusion(f32[3,24,32,256]{3,1,2,0:T(8,128)S(1)} %get-tuple-element.15, f32[3,24,28,256]{3,1,2,0:T(8,128)} %get-tuple-element.53, f32[3,24,4,256]{3,1,2,0:T(8,128)} %get-tuple-element.55, f32[3,24,4,256]{3,1,2,0:T(8,128)} %get-tuple-element.54, f32[3,24,28,256]{3,1,2,0:T(8,128)} %get-tuple-element.52, ...), kind=kLoop, calls=%fused_computation.63 | loop fusion | flops 38338560 | bytes 34996224 | tf_op jit(solution)/shard_map/add | solution.py:116
  170.6 0.3 slice_subtract_fusion.1
  170.9 1.9 copy.224
  172.9 1.9 copy.223
  174.8 1.5 slice_bitcast_fusion.2
  176.3 1.5 fusion.59
  177.8 6.2 %all-to-all-done.4 = f32[3,24,8,4,256]{4,2,1,0,3:T(8,128)} async-done(((f32[3,24,8,4,256]{4,2,1,0,3:T(8,128)}), f32[3,24,8,4,256]{4,2,1,0,3:T(8,128)}, u32[]{:S(2)}, u32[]{:S(2)}) %all-to-all-start.4) | async-done | bytes 2359328 | tf_op jit(solution)/shard_map/all_to_all | solution.py:105
  184.0 2.5 %copy.160 = f32[3,24,4,8,1,256]{5,1,0,3,2,4:T(8,128)S(1)} copy(f32[3,24,4,8,1,256]{5,3,1,0,2,4:T(8,128)} %bitcast.40) | data formatting | bytes 4718592 | tf_op jit(solution)/shard_map/all_to_all | solution.py:105
  186.5 0.0 copy-start.11
  186.5 2.0 %fusion.31 = f32[24,32,256]{2,0,1:T(8,128)S(1)} fusion(f32[3,24,4,8,1,256]{5,1,0,3,2,4:T(8,128)S(1)} %copy.160, bf16[3,24,32,256]{3,1,0,2:T(8,128)(2,1)} %copy.219), kind=kLoop, calls=%fused_computation.59 | loop fusion | flops 1572864 | bytes 4325376 | tf_op jit(solution)/shard_map/reduce_sum | solution.py:68
  188.5 0.1 copy-done.11
  188.6 0.2 copy-done.12
  188.9 2.7 %fusion.53 = (f32[1,24,32,256]{3,1,2,0:T(8,128)S(1)}, f32[1,24,32,256]{3,1,2,0:T(8,128)S(1)}, f32[1,24,32,256]{3,1,2,0:T(8,128)S(1)}) fusion(f32[1,24,32,256]{3,2,1,0:T(8,128)S(1)} %copy-done.11, f32[1,24,32,256]{3,2,1,0:T(8,128)S(1)} %copy-done.8, bf16[3,24,32,256]{3,1,2,0:T(8,128)(2,1)S(1)} %copy.220, f32[1,24,32,256]{3,2,1,0:T(8,128)S(1)} %copy-done.12, ...), kind=kLoop, calls=%fused_computation.82 | loop fusion | flops 1572864 | bytes 8257536 | tf_op jit(solution)/shard_map/add | solution.py:69
  191.5 1.8 fusion.30
  193.3 2.1 %copy.164 = f32[3,24,32,256]{3,2,1,0:T(8,128)} copy(f32[3,24,32,256]{3,1,2,0:T(8,128)S(1)} %fusion.30) | data formatting | bytes 4718592 | tf_op jit(solution)/shard_map/jit(_where)/select_n | solution.py:135
  (37 shorter events, 0.2 us)
Async XLA Ops:
  0.0 17.0 %copy-start.1 = (f32[3,24,32,256]{3,2,1,0:T(8,128)S(1)}, f32[3,24,32,256]{3,2,1,0:T(8,128)}, u32[]{:S(2)}) copy-start(f32[3,24,32,256]{3,2,1,0:T(8,128)} %param.5) | copy-start | bytes 7077892
  4.7 21.5 %copy-start = (f32[3,24,32,256]{3,1,2,0:T(8,128)}, f32[3,24,32,256]{3,1,2,0:T(8,128)S(1)}, u32[]{:S(2)}) copy-start(f32[3,24,32,256]{3,1,2,0:T(8,128)S(1)} %get-tuple-element.19) | copy-start | bytes 7077892
  5.8 47.6 %collective-permute-start.2 = (f32[3,4,32,256]{3,1,2,0:T(4,128)}, f32[3,4,32,256]{3,1,2,0:T(4,128)}, u32[]{:S(2)}, u32[]{:S(2)}) collective-permute-start(f32[3,4,32,256]{3,1,2,0:T(4,128)} %get-tuple-element.16), channel_id=1, source_target_pairs={{4,0},{8,4},{12,8},{16,12},{20,16},{24,20},{28,24},{32,28},{36,32}... | collective-permute-start | bytes 1179656 | tf_op jit(solution)/shard_map/ppermute | solution.py:22
  17.0 42.8 %collective-permute-start.3 = (f32[3,4,32,256]{3,1,2,0:T(4,128)}, f32[3,4,32,256]{3,1,2,0:T(4,128)}, u32[]{:S(2)}, u32[]{:S(2)}) collective-permute-start(f32[3,4,32,256]{3,1,2,0:T(4,128)} %get-tuple-element.17), channel_id=1, source_target_pairs={{0,4},{4,8},{8,12},{12,16},{16,20},{20,24},{24,28},{28,32},{32,36}... | collective-permute-start | bytes 1179656 | tf_op jit(solution)/shard_map/ppermute | solution.py:20
  19.3 36.0 %all-to-all-start = ((bf16[3,24,32,1,256]{4,1,0,3,2:T(8,128)(2,1)}), bf16[3,24,32,1,256]{4,1,0,3,2:T(8,128)(2,1)}, u32[]{:S(2)}, u32[]{:S(2)}) async-start(bf16[3,24,32,1,256]{4,1,0,3,2:T(8,128)(2,1)} %bitcast.4), calls=%async_computation | async-start | bytes 2359296 | tf_op jit(solution)/shard_map/all_to_all | solution.py:94
  26.0 1.7 copy-start.2
  27.7 4.3 %copy-start.5 = (f32[3,24,32,256]{3,2,1,0:T(8,128)S(1)}, f32[3,24,32,256]{3,2,1,0:T(8,128)}, u32[]{:S(2)}) copy-start(f32[3,24,32,256]{3,2,1,0:T(8,128)} %param.4) | copy-start | bytes 7077892
  45.5 5.2 %copy-start.3 = (f32[3,24,32,256]{3,2,1,0:T(8,128)S(1)}, f32[3,24,32,256]{3,2,1,0:T(8,128)}, u32[]{:S(2)}) copy-start(f32[3,24,32,256]{3,2,1,0:T(8,128)} %param.5) | copy-start | bytes 7077892
  55.3 21.8 %all-to-all-start.3 = ((bf16[3,24,32,1,256]{4,1,0,3,2:T(8,128)(2,1)}), bf16[3,24,32,1,256]{4,1,0,3,2:T(8,128)(2,1)}, u32[]{:S(2)}, u32[]{:S(2)}) async-start(bf16[3,24,32,1,256]{4,1,0,3,2:T(8,128)(2,1)} %copy.156), calls=%async_computation.3 | async-start | bytes 2359296 | tf_op jit(solution)/shard_map/all_to_all | solution.py:93
  59.8 13.2 %copy-start.14 = (bf16[1024,256,4]{1,0,2:T(8,128)(2,1)S(1)}, bf16[1024,256,4]{1,0,2:T(8,128)(2,1)}, u32[]{:S(2)}) copy-start(bf16[1024,256,4]{1,0,2:T(8,128)(2,1)} %copy.143) | copy-start | bytes 6291460
  77.1 32.3 %all-to-all-start.1 = ((f32[3,24,8,4,256]{4,2,1,0,3:T(8,128)}), f32[3,24,8,4,256]{4,2,1,0,3:T(8,128)}, u32[]{:S(2)}, u32[]{:S(2)}) async-start(f32[3,24,8,4,256]{4,2,1,0,3:T(8,128)} %fusion.38), calls=%async_computation.1 | async-start | bytes 4718592 | tf_op jit(solution)/shard_map/all_to_all | solution.py:106
  82.9 38.4 %collective-permute-start = (f32[3,4,32,256]{3,1,2,0:T(4,128)}, f32[3,4,32,256]{3,1,2,0:T(4,128)}, u32[]{:S(2)}, u32[]{:S(2)}) collective-permute-start(f32[3,4,32,256]{3,1,2,0:T(4,128)} %get-tuple-element.38), channel_id=1, source_target_pairs={{4,0},{8,4},{12,8},{16,12},{20,16},{24,20},{28,24},{32,28},{36,32}... | collective-permute-start | bytes 1179656 | tf_op jit(solution)/shard_map/ppermute | solution.py:22
  94.4 2.4 %copy-start.16 = (bf16[1024,256,4]{1,0,2:T(8,128)(2,1)S(1)}, bf16[1024,256,4]{1,0,2:T(8,128)(2,1)}, u32[]{:S(2)}) copy-start(bf16[1024,256,4]{1,0,2:T(8,128)(2,1)} %copy.149) | copy-start | bytes 6291460
  109.5 41.5 %all-to-all-start.2 = ((f32[3,24,8,4,256]{4,2,1,0,3:T(8,128)}), f32[3,24,8,4,256]{4,2,1,0,3:T(8,128)}, u32[]{:S(2)}, u32[]{:S(2)}) async-start(f32[3,24,8,4,256]{4,2,1,0,3:T(8,128)} %fusion.44), calls=%async_computation.2 | async-start | bytes 4718592 | tf_op jit(solution)/shard_map/all_to_all | solution.py:107
  118.7 4.4 %copy-start.15 = (bf16[1024,256,4]{1,0,2:T(8,128)(2,1)S(1)}, bf16[1024,256,4]{1,0,2:T(8,128)(2,1)}, u32[]{:S(2)}) copy-start(bf16[1024,256,4]{1,0,2:T(8,128)(2,1)} %copy.143) | copy-start | bytes 6291460
  118.7 37.6 %collective-permute-start.1 = (f32[3,4,32,256]{3,1,2,0:T(4,128)}, f32[3,4,32,256]{3,1,2,0:T(4,128)}, u32[]{:S(2)}, u32[]{:S(2)}) collective-permute-start(f32[3,4,32,256]{3,1,2,0:T(4,128)} %get-tuple-element.39), channel_id=1, source_target_pairs={{0,4},{4,8},{8,12},{12,16},{16,20},{20,24},{24,28},{28,32},{32,36}... | collective-permute-start | bytes 1179656 | tf_op jit(solution)/shard_map/ppermute | solution.py:20
  150.9 33.0 %all-to-all-start.4 = ((f32[3,24,8,4,256]{4,2,1,0,3:T(8,128)}), f32[3,24,8,4,256]{4,2,1,0,3:T(8,128)}, u32[]{:S(2)}, u32[]{:S(2)}) async-start(f32[3,24,8,4,256]{4,2,1,0,3:T(8,128)} %fusion.41), calls=%async_computation.4 | async-start | bytes 4718592 | tf_op jit(solution)/shard_map/all_to_all | solution.py:105
  156.4 14.3 %copy-start.6 = (f32[24,32,256]{2,0,1:T(8,128)S(1)}, f32[24,32,256]{2,0,1:T(8,128)}, u32[]{:S(2)}) copy-start(f32[24,32,256]{2,0,1:T(8,128)} %fusion.24) | copy-start | bytes 2359300
  156.4 14.3 %copy-start.7 = (f32[24,32,256]{2,0,1:T(8,128)S(1)}, f32[24,32,256]{2,0,1:T(8,128)}, u32[]{:S(2)}) copy-start(f32[24,32,256]{2,0,1:T(8,128)} %get-tuple-element.14) | copy-start | bytes 2359300
  184.0 4.5 %copy-start.13 = (f32[1,24,32,256]{3,2,1,0:T(8,128)S(1)}, f32[1,24,32,256]{3,2,1,0:T(8,128)}, u32[]{:S(2)}) copy-start(f32[1,24,32,256]{3,2,1,0:T(8,128)} %get-tuple-element.10) | copy-start | bytes 2359300
  186.4 2.1 %copy-start.8 = (f32[1,24,32,256]{3,2,1,0:T(8,128)S(1)}, f32[1,24,32,256]{3,2,1,0:T(8,128)}, u32[]{:S(2)}) copy-start(f32[1,24,32,256]{3,2,1,0:T(8,128)} %get-tuple-element.5) | copy-start | bytes 2359300
  186.4 2.1 %copy-start.9 = (f32[1,24,32,256]{3,2,1,0:T(8,128)S(1)}, f32[1,24,32,256]{3,2,1,0:T(8,128)}, u32[]{:S(2)}) copy-start(f32[1,24,32,256]{3,2,1,0:T(8,128)} %get-tuple-element.6) | copy-start | bytes 2359300
  186.5 2.1 %copy-start.10 = (f32[1,24,32,256]{3,2,1,0:T(8,128)S(1)}, f32[1,24,32,256]{3,2,1,0:T(8,128)}, u32[]{:S(2)}) copy-start(f32[1,24,32,256]{3,2,1,0:T(8,128)} %get-tuple-element.7) | copy-start | bytes 2359300
  186.5 2.2 %copy-start.11 = (f32[1,24,32,256]{3,2,1,0:T(8,128)S(1)}, f32[1,24,32,256]{3,2,1,0:T(8,128)}, u32[]{:S(2)}) copy-start(f32[1,24,32,256]{3,2,1,0:T(8,128)} %get-tuple-element.8) | copy-start | bytes 2359300
  186.5 2.4 %copy-start.12 = (f32[1,24,32,256]{3,2,1,0:T(8,128)S(1)}, f32[1,24,32,256]{3,2,1,0:T(8,128)}, u32[]{:S(2)}) copy-start(f32[1,24,32,256]{3,2,1,0:T(8,128)} %get-tuple-element.9) | copy-start | bytes 2359300
  188.9 2.7 %copy-start.4 = (f32[3,24,32,256]{3,2,1,0:T(8,128)S(1)}, f32[3,24,32,256]{3,2,1,0:T(8,128)}, u32[]{:S(2)}) copy-start(f32[3,24,32,256]{3,2,1,0:T(8,128)} %param.5) | copy-start | bytes 7077892
where the time goes:
time: 196 us; the launch traced here: 195 us
  local copies, waits for them, and re-layouts  60.5 us (31%)
  starting transfers between devices  43.9 us (22%)
  other arithmetic  39.9 us (20%)
  waiting for transfers between devices  38.4 us (20%)
  matrix products  12.4 us (6%)
    all_to_all x1, waiting for transfers between devices, body(): lax.all_to_all(to_blocks(curves), 'gy', split_axis=3, concat_axis=2, tile...  23.7 us
    unnamed x40, local copies, waits for them, and re-layouts  19.7 us
    ppermute x2, starting transfers between devices, padded(): lax.ppermute(head, axis, [((i + 1) % count, i) for i in range(count)])  18.7 us
    add x1, other arithmetic, body(): base_flow[0][None] * dx_adj + base_flow[2][None] * dz_adj  14.2 us
    reduce_sum x1, other arithmetic, body(): first_coupling = jnp.sum(adjoint * dx_base, axis=0)  13.2 us
    slice x6, local copies, waits for them, and re-layouts, first_periodic(): jnp.roll(field, -offset, direction) - jnp.roll(field, offset, direction)  9.69 us
    all_to_all x1, waiting for transfers between devices, body(): lax.all_to_all(to_blocks(slope_adj), 'gy', split_axis=3, concat_axis=2, t...  8.55 us
    all_to_all x1, waiting for transfers between devices, body(): lax.all_to_all(to_blocks(slope_base), 'gy', split_axis=3, concat_axis=2,...  6.21 us
  transfers between devices with their start and end apart: 9, of which 3 were waited for; matrix products, arithmetic and copies ran while one was open for 48% of the time, Pallas kernels for 0%

commit v1 on v0

v1 whole, which is shorter than its diff:
```python
import jax
import jax.numpy as jnp
from jax import lax
from jax.sharding import PartitionSpec as P

C_FIRST = (0.8, -0.2, 4.0 / 105.0, -1.0 / 280.0)
C_SECOND = (1.6, -0.2, 8.0 / 315.0, -1.0 / 560.0)
C_CENTER = -205.0 / 72.0
VISCOSITY = 0.1
STEP_WEIGHT = 0.5
HALO = 4


def ring_shift(value, axis, forward):
    count = lax.axis_size(axis)
    if forward:
        pairs = [(i, (i + 1) % count) for i in range(count)]
    else:
        pairs = [((i + 1) % count, i) for i in range(count)]
    return lax.ppermute(value, axis, pairs)


def first_streamwise(extended, cells):
    result = C_FIRST[0] * (extended[:, HALO + 1 : HALO + 1 + cells] - extended[:, HALO - 1 : HALO - 1 + cells])
    for offset in range(2, 5):
        result = result + C_FIRST[offset - 1] * (
            extended[:, HALO + offset : HALO + offset + cells]
            - extended[:, HALO - offset : HALO - offset + cells]
        )
    return result


def second_streamwise(extended, cells):
    result = C_CENTER * extended[:, HALO : HALO + cells]
    for offset in range(1, 5):
        result = result + C_SECOND[offset - 1] * (
            extended[:, HALO + offset : HALO + offset + cells]
            + extended[:, HALO - offset : HALO - offset + cells]
        )
    return result


def first_periodic(field, direction):
    result = C_FIRST[0] * (jnp.roll(field, -1, direction) - jnp.roll(field, 1, direction))
    for offset in range(2, 5):
        result = result + C_FIRST[offset - 1] * (
            jnp.roll(field, -offset, direction) - jnp.roll(field, offset, direction)
        )
    return result


def second_periodic(field, direction):
    result = C_CENTER * field
    for offset in range(1, 5):
        result = result + C_SECOND[offset - 1] * (
            jnp.roll(field, -offset, direction) + jnp.roll(field, offset, direction)
        )
    return result


def body(base_flow, adjoint, first_op, second_op):
    comps, cells, spanwise, local_rows = base_flow.shape
    groups = lax.axis_size("gy")
    total_rows = local_rows * groups
    part = spanwise // groups

    tails = ring_shift(jnp.stack((base_flow[:, cells - HALO :], adjoint[:, cells - HALO :]), 0), "gx", True)
    heads = ring_shift(jnp.stack((base_flow[:, :HALO], adjoint[:, :HALO]), 0), "gx", False)

    base_low = lax.optimization_barrier(base_flow.astype(jnp.bfloat16))
    adjoint_low = lax.optimization_barrier(adjoint.astype(jnp.bfloat16))
    low = jnp.concatenate((base_low, adjoint_low), 0).reshape(2 * comps, cells, spanwise, 1, local_rows)
    lines = lax.all_to_all(low, "gy", split_axis=2, concat_axis=3, tiled=True)
    lines = lines.reshape(2 * comps, cells, part, total_rows)
    base_lines = lines[:comps]
    adj_lines = lines[comps:]
    slope_base = jnp.einsum("fxzk,ik->fxzi", base_lines, first_op, preferred_element_type=jnp.float32)
    slope_adj = jnp.einsum("fxzk,ik->fxzi", adj_lines, first_op, preferred_element_type=jnp.float32)
    curves = jnp.einsum("fxzk,ik->fxzi", adj_lines, second_op, preferred_element_type=jnp.float32)
    normal_vel = base_lines[1].astype(jnp.float32)
    coupling = jnp.sum(adj_lines.astype(jnp.float32) * slope_base, axis=0)
    wall_part = normal_vel[None] * slope_adj + VISCOSITY * curves
    wall_part = wall_part.at[1].add(-coupling)
    wall_part = wall_part.reshape(comps, cells, part, groups, local_rows)
    wall_part = lax.all_to_all(wall_part, "gy", split_axis=3, concat_axis=2, tiled=True)
    wall_part = wall_part.reshape(comps, cells, spanwise, local_rows)

    extended_base = jnp.concatenate((tails[0], base_flow, heads[0]), axis=1)
    extended_adj = jnp.concatenate((tails[1], adjoint, heads[1]), axis=1)
    dx_base = first_streamwise(extended_base, cells)
    dz_base = first_periodic(base_flow, 2)
    dx_adj = first_streamwise(extended_adj, cells)
    dxx_adj = second_streamwise(extended_adj, cells)
    dz_adj = first_periodic(adjoint, 2)
    dzz_adj = second_periodic(adjoint, 2)
    carried = (
        base_flow[0][None] * dx_adj + base_flow[2][None] * dz_adj + VISCOSITY * (dxx_adj + dzz_adj)
    )
    first_coupling = jnp.sum(adjoint * dx_base, axis=0)
    last_coupling = jnp.sum(adjoint * dz_base, axis=0)
    tendency = jnp.stack((carried[0] - first_coupling, carried[1], carried[2] - last_coupling), 0)
    updated = adjoint + STEP_WEIGHT * (tendency + wall_part)
    wall_index = lax.axis_index("gy") * local_rows + jnp.arange(local_rows, dtype=jnp.int32)
    interior = (wall_index > 0) & (wall_index < total_rows - 1)
    return jnp.where(interior, updated, jnp.float32(0.0))


def solution(mesh):
    return jax.shard_map(
        body,
        mesh=mesh,
        in_specs=(P(None, "gx", None, "gy"), P(None, "gx", None, "gy"), P(), P()),
        out_specs=P(None, "gx", None, "gy"),
        check_vma=False,
    )
```

time: 196 us -> 113 us (0.58)
  waiting for transfers between devices: 38.4 us -> 14.1 us
  local copies, waits for them, and re-layouts: 60.5 us -> 37.1 us
  starting transfers between devices: 43.9 us -> 21.6 us
  matrix products: 12.4 us -> 4.32 us
  other arithmetic: 39.9 us -> 35 us
    all_to_all x5 -> x2, waiting for transfers between devices: 38.4 us -> 14.1 us  [the longest x1 9.27 us: body(): lax.all_to_all(wall_part, 'gy', split_axis=3, concat_axis=2, tiled=True)]
    unnamed x40 -> x20, local copies, waits for them, and re-layouts: 19.7 us -> 3.8 us
    all_to_all x5 -> x2, starting transfers between devices: 25.2 us -> 10.3 us  [the longest x1 5.42 us: body(): lines = lax.all_to_all(low, 'gy', split_axis=2, concat_axis=3, tiled=True)]
    reduce_sum x1, other arithmetic: 13.2 us -> 3.56 us  [body(): first_coupling = jnp.sum(adjoint * dx_base, axis=0)]
    dot_general x3, matrix products: 12.4 us -> 4.32 us  [the longest x1 1.45 us: body(): jnp.einsum('fxzk,ik->fxzi', adj_lines, first_op, preferred_element_type=j...]
    ppermute x4 -> x2, starting transfers between devices: 18.7 us -> 11.2 us  [ring_shift(): return lax.ppermute(value, axis, pairs)]
    dot_general x2 -> x0, local copies, waits for them, and re-layouts: 6.69 us -> none  [the longest x1 4.11 us: body(): jnp.einsum('fxzpk,ipk->fxzi', adjoint_lines, second_blocks, preferred_ele...]
    slice x6, local copies, waits for them, and re-layouts: 9.69 us -> 13.5 us  [first_periodic(): jnp.roll(field, -offset, direction) - jnp.roll(field, offset, direction)]
  transfers between devices with their start and end apart: 9 -> 4, of which waited for: 3 -> 2; matrix products, arithmetic and copies ran while one was open for 48% -> 52% of each run, Pallas kernels for 0% -> 0%
where the time goes in v1:
time: 113 us; the launch traced here: 112 us
  local copies, waits for them, and re-layouts  37.1 us (33%)
  other arithmetic  35 us (31%)
  starting transfers between devices  21.6 us (19%)
  waiting for transfers between devices  14.1 us (12%)
  matrix products  4.32 us (4%)
    add x1, other arithmetic, body(): base_flow[0][None] * dx_adj + base_flow[2][None] * dz_adj  16.8 us
    slice x6, local copies, waits for them, and re-layouts, first_periodic(): jnp.roll(field, -offset, direction) - jnp.roll(field, offset, direction)  13.5 us
    ppermute x2, starting transfers between devices, ring_shift(): return lax.ppermute(value, axis, pairs)  11.2 us
    all_to_all x1, waiting for transfers between devices, body(): lax.all_to_all(wall_part, 'gy', split_axis=3, concat_axis=2, tiled=True)  9.27 us
    slice x2, local copies, waits for them, and re-layouts, first_periodic(): jnp.roll(field, -1, direction) - jnp.roll(field, 1, direction)  6.24 us
    all_to_all x1, starting transfers between devices, body(): lines = lax.all_to_all(low, 'gy', split_axis=2, concat_axis=3, tiled=True)  5.42 us
    select_n x1, other arithmetic, body(): return jnp.where(interior, updated, jnp.float32(0.0))  5.39 us
    all_to_all x1, starting transfers between devices, body(): lax.all_to_all(wall_part, 'gy', split_axis=3, concat_axis=2, tiled=True)  4.91 us
  transfers between devices with their start and end apart: 4, of which 2 were waited for; matrix products, arithmetic and copies ran while one was open for 52% of the time, Pallas kernels for 0%

profile of v1, /device:TPU:1, one launch (start us, length us, event | category | flops | bytes accessed | tf_op | source)
XLA Modules:
  0.0 112.3 jit_solution(949035114485395903)
XLA Ops:
  0.0 0.0 copy-start
  0.0 1.6 %slice_bitcast_fusion.6 = (f32[1,3,4,32,256]{4,3,2,1,0:T(8,128)S(1)}, f32[1,3,4,32,256]{4,3,2,1,0:T(8,128)S(1)}, f32[1,3,4,32,256]{4,3,2,1,0:T(8,128)S(1)}, f32[1,3,4,32,256]{4,3,2,1,0:T(8,128)S(1)}) fusion(f32[3,24,32,256]{3,2,1,0:T(8,128)} %param.7, f32[3,24,32,256]{3,2,1,0:T(8,128)} %param.6), kind=kLoop, calls=%fused_computation.103 | loop fusion | bytes 3145728 | tf_op jit(solution)/shard_map/stack | solution.py:67
  1.6 0.0 copy-start.4
  1.6 0.9 pad_maximum_fusion.12
  2.6 11.2 %collective-permute-start = (f32[2,3,4,32,256]{4,3,2,1,0:T(8,128)}, f32[2,3,4,32,256]{4,3,2,1,0:T(8,128)}, u32[]{:S(2)}, u32[]{:S(2)}) collective-permute-start(f32[2,3,4,32,256]{4,3,2,1,0:T(8,128)} %pad_maximum_fusion.12), channel_id=1, source_target_pairs={{4,0},{8,4},{12,8},{16,12},{20,16},{24,20},{28,24},{32,28},{36,32}... | collective-permute-start | bytes 2359304 | tf_op jit(solution)/shard_map/ppermute | solution.py:20
  13.8 0.0 copy-start.1
  13.8 1.0 pad_maximum_fusion.13
  14.8 0.0 collective-permute-start.1
  14.8 0.0 copy-done.4
  14.8 1.3 %copy.21 = bf16[3,24,32,256]{3,1,0,2:T(8,128)(2,1)S(1)} copy(f32[3,24,32,256]{3,2,1,0:T(8,128)S(1)} %copy-done.4) | data formatting | bytes 3538944 | tf_op args[0]
  16.1 0.0 copy-done.1
  16.1 1.3 %copy.20 = bf16[3,24,32,256]{3,1,0,2:T(8,128)(2,1)S(1)} copy(f32[3,24,32,256]{3,2,1,0:T(8,128)S(1)} %copy-done.1) | data formatting | bytes 3538944 | tf_op args[1]
  17.4 1.6 %maximum_bitcast_fusion = bf16[6,24,32,1,256]{4,1,0,3,2:T(8,128)(2,1)} fusion(bf16[3,24,32,256]{3,1,0,2:T(8,128)(2,1)S(1)} %copy.20, bf16[3,24,32,256]{3,1,0,2:T(8,128)(2,1)S(1)} %copy.21), kind=kLoop, calls=%fused_computation.78 | loop fusion | flops 1179648 | bytes 4718592 | tf_op jit(solution)/shard_map/reshape | solution.py:72
  19.0 5.4 %all-to-all-start = ((bf16[6,24,32,1,256]{4,1,0,3,2:T(8,128)(2,1)}), bf16[6,24,32,1,256]{4,1,0,3,2:T(8,128)(2,1)}, u32[]{:S(2)}, u32[]{:S(2)}) async-start(bf16[6,24,32,1,256]{4,1,0,3,2:T(8,128)(2,1)} %maximum_bitcast_fusion), calls=%async_computation | async-start | bytes 4718592 | tf_op jit(solution)/shard_map/all_to_all | solution.py:73
  24.4 0.0 copy-start.2
  24.4 5.5 %fusion.57 = (f32[3,24,31,256]{3,2,1,0:T(8,128)}, f32[3,24,31,256]{3,2,1,0:T(8,128)}) fusion(f32[3,24,32,256]{3,2,1,0:T(8,128)} %param.7), kind=kLoop, calls=%fused_computation.117 | loop fusion | bytes 9142272 | tf_op jit(solution)/shard_map/jit(_roll_static)/slice | solution.py:44
  29.9 0.0 copy-done.2
  29.9 2.7 %fusion.59 = (f32[3,24,30,256]{3,2,1,0:T(8,128)}, f32[3,24,30,256]{3,2,1,0:T(8,128)}) fusion(f32[3,24,32,256]{3,2,1,0:T(8,128)S(1)} %copy-done.2), kind=kLoop, calls=%fused_computation.119 | loop fusion | bytes 8847360 | tf_op jit(solution)/shard_map/jit(_roll_static)/slice | solution.py:47
  32.6 0.0 copy-start.5
  32.6 2.6 %fusion.61 = (f32[3,24,29,256]{3,2,1,0:T(8,128)}, f32[3,24,29,256]{3,2,1,0:T(8,128)}) fusion(f32[3,24,32,256]{3,2,1,0:T(8,128)S(1)} %copy-done.2), kind=kLoop, calls=%fused_computation.121 | loop fusion | bytes 8552448 | tf_op jit(solution)/shard_map/jit(_roll_static)/slice | solution.py:47
  35.2 0.0 copy-done.5
  35.2 1.3 %slice_bitcast_fusion.1 = (f32[24,32,256]{2,1,0:T(8,128)}, f32[24,32,256]{2,1,0:T(8,128)}) fusion(f32[3,24,32,256]{3,2,1,0:T(8,128)S(1)} %copy-done.5), kind=kLoop, calls=%fused_computation.98 | loop fusion | bytes 3145728 | tf_op jit(solution)/shard_map/mul | solution.py:97
  36.5 0.9 fusion.62
  37.5 0.9 fusion.64
  38.4 0.6 fusion.50
  39.0 0.6 fusion.52
  39.7 0.6 fusion.54
  40.3 0.6 fusion.56
  41.0 0.1 fusion.49
  41.1 0.1 fusion.51
  41.2 0.1 fusion.53
  41.3 0.1 fusion.55
  41.4 3.8 %fusion.30 = f32[24,32,256]{2,1,0:T(8,128)S(1)} fusion(f32[3,24,32,256]{3,2,1,0:T(8,128)S(1)} %copy-done.2, f32[3,24,1,256]{3,2,1,0:T(1,128)S(1)} %get-tuple-element.35, f32[3,24,31,256]{3,2,1,0:T(8,128)S(1)} %get-tuple-element.37, f32[3,24,31,256]{3,2,1,0:T(8,128)S(1)} %get-tuple-element.36, f32[3,24,1,256]{3,2,1,0:T(1,128)S(1)} %get-tuple-element.34, ...), kind=kLoop, calls=%fused_computation.67 | loop fusion | flops 12189696 | bytes 22020096 | tf_op jit(solution)/shard_map/reduce_sum | solution.py:100
  45.3 0.8 fusion.60
  46.0 0.7 fusion.58
  46.8 0.0 copy-start.6
  46.8 5.6 %fusion.63 = (f32[3,24,28,256]{3,2,1,0:T(8,128)}, f32[3,24,28,256]{3,2,1,0:T(8,128)}) fusion(f32[3,24,32,256]{3,2,1,0:T(8,128)} %param.7), kind=kLoop, calls=%fused_computation.123 | loop fusion | bytes 8257536 | tf_op jit(solution)/shard_map/jit(_roll_static)/slice | solution.py:47
  52.4 0.0 copy-start.3
  52.4 0.0 collective-permute-done
  52.4 1.3 %slice_bitcast_fusion.3 = (f32[3,4,32,256]{3,2,1,0:T(8,128)S(1)}, f32[3,4,32,256]{3,2,1,0:T(8,128)S(1)}) fusion(f32[2,3,4,32,256]{4,3,2,1,0:T(8,128)} %collective-permute-done), kind=kLoop, calls=%fused_computation.100 | loop fusion | bytes 1572864 | tf_op jit(solution)/shard_map/squeeze | solution.py:88
  53.7 0.0 collective-permute-done.1
  53.7 1.9 %slice_bitcast_fusion.2 = (f32[3,4,32,256]{3,2,1,0:T(8,128)S(1)}, f32[3,4,32,256]{3,2,1,0:T(8,128)}) fusion(f32[2,3,4,32,256]{4,3,2,1,0:T(8,128)} %collective-permute-done.1), kind=kLoop, calls=%fused_computation.99 | loop fusion | bytes 1572864 | tf_op jit(solution)/shard_map/squeeze | solution.py:88
  55.7 0.0 copy-done.6
  55.7 0.0 copy-done.3
  55.7 3.6 %fusion.6 = f32[24,32,256]{2,1,0:T(8,128)} fusion(f32[3,24,32,256]{3,2,1,0:T(8,128)S(1)} %copy-done.3, f32[3,24,32,256]{3,2,1,0:T(8,128)S(1)} %copy-done.6, f32[3,4,32,256]{3,2,1,0:T(8,128)S(1)} %get-tuple-element.62, f32[3,4,32,256]{3,2,1,0:T(8,128)S(1)} %get-tuple-element.60), kind=kLoop, calls=%fused_computation.30 | loop fusion | flops 12189696 | bytes 6291456 | tf_op jit(solution)/shard_map/reduce_sum | solution.py:99
  59.2 4.8 %all-to-all-done = bf16[6,24,32,1,256]{4,1,0,3,2:T(8,128)(2,1)} async-done(((bf16[6,24,32,1,256]{4,1,0,3,2:T(8,128)(2,1)}), bf16[6,24,32,1,256]{4,1,0,3,2:T(8,128)(2,1)}, u32[]{:S(2)}, u32[]{:S(2)}) %all-to-all-start) | async-done | bytes 2359328 | tf_op jit(solution)/shard_map/all_to_all | solution.py:73
  64.0 2.5 %copy.22 = bf16[6,24,4,8,1,256]{5,3,2,1,0,4:T(8,128)(2,1)S(1)} copy(bf16[6,24,4,8,1,256]{5,1,0,3,2,4:T(8,128)(2,1)} %bitcast.13) | data formatting | bytes 4718592 | tf_op jit(solution)/shard_map/all_to_all | solution.py:73
  66.6 0.0 copy-start.8
  66.6 0.2 fusion.48
  66.8 0.1 convert.1
  66.9 1.3 %copy-done.8 = bf16[1024,1024]{1,0:T(8,128)(2,1)S(1)} copy-done((bf16[1024,1024]{1,0:T(8,128)(2,1)S(1)}, bf16[1024,1024]{1,0:T(8,128)(2,1)}, u32[]{:S(2)}) %copy-start.8) | copy-done | bytes 2097176
  68.2 1.4 %fusion.37 = f32[3,24,8,1024]{3,2,1,0:T(8,128)S(1)} fusion(bf16[3,24,8,1024]{3,2,1,0:T(8,128)(2,1)S(1)} %bitcast.65, bf16[1024,1024]{1,0:T(8,128)(2,1)S(1)} %copy-done.8), kind=kOutput, calls=%fused_computation.85 | convolution fusion | flops 1207959552 | bytes 5636096 | tf_op jit(solution)/shard_map/fxzk,ik->fxzi/dot_general | solution.py:79
  69.6 0.0 copy-done
  69.6 1.4 %multiply_reduce_fusion = f32[24,8,1024]{2,1,0:T(8,128)S(1)} fusion(bf16[3,24,8,1024]{3,2,1,0:T(8,128)(2,1)S(1)} %bitcast.66, bf16[3,24,8,1024]{3,2,1,0:T(8,128)(2,1)S(1)} %bitcast.69, bf16[1024,1024]{1,0:T(8,128)(2,1)S(1)} %copy-done), kind=kOutput, calls=%fused_computation.82 | convolution fusion | flops 1209532416 | bytes 5242880 | tf_op jit(solution)/shard_map/fxzk,ik->fxzi/dot_general | solution.py:77
  71.1 1.5 %multiply_add_fusion = f32[3,24,8,1024]{3,2,1,0:T(8,128)S(1)} fusion(f32[3,24,8,1024]{3,2,1,0:T(8,128)S(1)} %fusion.37, bf16[3,24,8,1024]{3,2,1,0:T(8,128)(2,1)S(1)} %bitcast.67, bf16[1024,1024]{1,0:T(8,128)(2,1)S(1)} %copy-done, f32[24,8,1024]{2,1,0:T(8,128)S(1)} %convert.1), kind=kOutput, calls=%fused_computation.83 | convolution fusion | flops 1209729024 | bytes 8781824 | tf_op jit(solution)/shard_map/fxzk,ik->fxzi/dot_general | solution.py:78
  72.5 0.2 fusion.47
  72.8 1.6 %copy.12 = f32[3,24,8,4,256]{4,2,1,0,3:T(8,128)} copy(f32[3,24,8,4,256]{4,2,3,1,0:T(8,128)S(1)} %bitcast.62) | data formatting | bytes 4718592 | tf_op jit(solution)/shard_map/reshape | solution.py:84
  74.4 4.9 %all-to-all-start.1 = ((f32[3,24,8,4,256]{4,2,1,0,3:T(8,128)}), f32[3,24,8,4,256]{4,2,1,0,3:T(8,128)}, u32[]{:S(2)}, u32[]{:S(2)}) async-start(f32[3,24,8,4,256]{4,2,1,0,3:T(8,128)} %copy.12), calls=%async_computation.1 | async-start | bytes 4718592 | tf_op jit(solution)/shard_map/all_to_all | solution.py:85
  79.3 0.0 copy-start.7
  79.3 16.8 %multiply_add_fusion.1 = f32[3,24,32,256]{3,2,1,0:T(8,128)S(1)} fusion(f32[3,24,32,256]{3,2,1,0:T(8,128)} %param.7, f32[3,24,28,256]{3,2,1,0:T(8,128)} %get-tuple-element.57, f32[3,24,4,256]{3,2,1,0:T(4,128)} %get-tuple-element.59, f32[3,24,4,256]{3,2,1,0:T(4,128)} %get-tuple-element.58, f32[3,24,28,256]{3,2,1,0:T(8,128)} %get-tuple-element.56, ...), kind=kLoop, calls=%fused_computation.84 | loop fusion | flops 40697856 | bytes 25952256 | tf_op jit(solution)/shard_map/add | solution.py:97
  96.1 0.0 copy-done.7
  96.1 1.5 %slice_subtract_fusion.1 = (f32[1,24,32,256]{3,2,1,0:T(8,128)}, f32[1,24,32,256]{3,2,1,0:T(8,128)}, f32[1,24,32,256]{3,2,1,0:T(8,128)}) fusion(f32[3,24,32,256]{3,2,1,0:T(8,128)S(1)} %multiply_add_fusion.1, f32[24,32,256]{2,1,0:T(8,128)S(1)} %copy-done.7, f32[24,32,256]{2,1,0:T(8,128)S(1)} %fusion.30), kind=kLoop, calls=%fused_computation.94 | loop fusion | flops 393216 | bytes 6291456 | tf_op jit(solution)/shard_map/sub | solution.py:101
  97.7 9.3 %all-to-all-done.1 = f32[3,24,8,4,256]{4,2,1,0,3:T(8,128)} async-done(((f32[3,24,8,4,256]{4,2,1,0,3:T(8,128)}), f32[3,24,8,4,256]{4,2,1,0,3:T(8,128)}, u32[]{:S(2)}, u32[]{:S(2)}) %all-to-all-start.1) | async-done | bytes 2359328 | tf_op jit(solution)/shard_map/all_to_all | solution.py:85
  106.9 5.4 %fusion.36 = f32[3,24,32,256]{3,2,1,0:T(8,128)} fusion(f32[3,24,32,256]{3,2,1,0:T(8,128)} %param.7, f32[1,24,32,256]{3,2,1,0:T(8,128)} %get-tuple-element.20, f32[1,24,32,256]{3,2,1,0:T(8,128)} %get-tuple-element.21, f32[1,24,32,256]{3,2,1,0:T(8,128)} %get-tuple-element.19, f32[3,24,8,4,256]{4,2,1,0,3:T(8,128)} %all-to-all-done.1, ...), kind=kLoop, calls=%fused_computation.77 | loop fusion | flops 3538944 | bytes 9437440 | tf_op jit(solution)/shard_map/jit(_where)/select_n | solution.py:105
  (2 shorter events, 0.0 us)
Async XLA Ops:
  0.0 69.6 %copy-start = (bf16[1024,1024]{1,0:T(8,128)(2,1)S(1)}, bf16[1024,1024]{1,0:T(8,128)(2,1)}, u32[]{:S(2)}) copy-start(bf16[1024,1024]{1,0:T(8,128)(2,1)} %param.8) | copy-start | bytes 6291460
  1.6 13.2 %copy-start.4 = (f32[3,24,32,256]{3,2,1,0:T(8,128)S(1)}, f32[3,24,32,256]{3,2,1,0:T(8,128)}, u32[]{:S(2)}) copy-start(f32[3,24,32,256]{3,2,1,0:T(8,128)} %param.6) | copy-start | bytes 7077892
  2.6 49.8 %collective-permute-start = (f32[2,3,4,32,256]{4,3,2,1,0:T(8,128)}, f32[2,3,4,32,256]{4,3,2,1,0:T(8,128)}, u32[]{:S(2)}, u32[]{:S(2)}) collective-permute-start(f32[2,3,4,32,256]{4,3,2,1,0:T(8,128)} %pad_maximum_fusion.12), channel_id=1, source_target_pairs={{4,0},{8,4},{12,8},{16,12},{20,16},{24,20},{28,24},{32,28},{36,32}... | collective-permute-start | bytes 2359304 | tf_op jit(solution)/shard_map/ppermute | solution.py:20
  13.8 2.3 %copy-start.1 = (f32[3,24,32,256]{3,2,1,0:T(8,128)S(1)}, f32[3,24,32,256]{3,2,1,0:T(8,128)}, u32[]{:S(2)}) copy-start(f32[3,24,32,256]{3,2,1,0:T(8,128)} %param.7) | copy-start | bytes 7077892
  14.8 38.9 %collective-permute-start.1 = (f32[2,3,4,32,256]{4,3,2,1,0:T(8,128)}, f32[2,3,4,32,256]{4,3,2,1,0:T(8,128)}, u32[]{:S(2)}, u32[]{:S(2)}) collective-permute-start(f32[2,3,4,32,256]{4,3,2,1,0:T(8,128)} %pad_maximum_fusion.13), channel_id=1, source_target_pairs={{0,4},{4,8},{8,12},{12,16},{16,20},{20,24},{24,28},{28,32},{32,36}... | collective-permute-start | bytes 2359304 | tf_op jit(solution)/shard_map/ppermute | solution.py:20
  19.0 45.1 %all-to-all-start = ((bf16[6,24,32,1,256]{4,1,0,3,2:T(8,128)(2,1)}), bf16[6,24,32,1,256]{4,1,0,3,2:T(8,128)(2,1)}, u32[]{:S(2)}, u32[]{:S(2)}) async-start(bf16[6,24,32,1,256]{4,1,0,3,2:T(8,128)(2,1)} %maximum_bitcast_fusion), calls=%async_computation | async-start | bytes 4718592 | tf_op jit(solution)/shard_map/all_to_all | solution.py:73
  24.4 5.5 %copy-start.2 = (f32[3,24,32,256]{3,2,1,0:T(8,128)S(1)}, f32[3,24,32,256]{3,2,1,0:T(8,128)}, u32[]{:S(2)}) copy-start(f32[3,24,32,256]{3,2,1,0:T(8,128)} %param.7) | copy-start | bytes 7077892
  32.6 2.6 %copy-start.5 = (f32[3,24,32,256]{3,2,1,0:T(8,128)S(1)}, f32[3,24,32,256]{3,2,1,0:T(8,128)}, u32[]{:S(2)}) copy-start(f32[3,24,32,256]{3,2,1,0:T(8,128)} %param.6) | copy-start | bytes 7077892
  46.8 8.9 %copy-start.6 = (f32[3,24,32,256]{3,2,1,0:T(8,128)S(1)}, f32[3,24,32,256]{3,2,1,0:T(8,128)}, u32[]{:S(2)}) copy-start(f32[3,24,32,256]{3,2,1,0:T(8,128)} %param.6) | copy-start | bytes 7077892
  52.4 3.3 %copy-start.3 = (f32[3,24,32,256]{3,2,1,0:T(8,128)S(1)}, f32[3,24,32,256]{3,2,1,0:T(8,128)}, u32[]{:S(2)}) copy-start(f32[3,24,32,256]{3,2,1,0:T(8,128)} %param.7) | copy-start | bytes 7077892
  66.6 1.6 %copy-start.8 = (bf16[1024,1024]{1,0:T(8,128)(2,1)S(1)}, bf16[1024,1024]{1,0:T(8,128)(2,1)}, u32[]{:S(2)}) copy-start(bf16[1024,1024]{1,0:T(8,128)(2,1)} %param.9) | copy-start | bytes 6291460
  74.4 32.5 %all-to-all-start.1 = ((f32[3,24,8,4,256]{4,2,1,0,3:T(8,128)}), f32[3,24,8,4,256]{4,2,1,0,3:T(8,128)}, u32[]{:S(2)}, u32[]{:S(2)}) async-start(f32[3,24,8,4,256]{4,2,1,0,3:T(8,128)} %copy.12), calls=%async_computation.1 | async-start | bytes 4718592 | tf_op jit(solution)/shard_map/all_to_all | solution.py:85
  79.3 16.8 %copy-start.7 = (f32[24,32,256]{2,1,0:T(8,128)S(1)}, f32[24,32,256]{2,1,0:T(8,128)}, u32[]{:S(2)}) copy-start(f32[24,32,256]{2,1,0:T(8,128)} %fusion.6) | copy-start | bytes 2359300

commit v2 on v1

--- a/solution.py
+++ b/solution.py
@@ -81,9 +81,9 @@
     coupling = jnp.sum(adj_lines.astype(jnp.float32) * slope_base, axis=0)
     wall_part = normal_vel[None] * slope_adj + VISCOSITY * curves
     wall_part = wall_part.at[1].add(-coupling)
-    wall_part = wall_part.reshape(comps, cells, part, groups, local_rows)
+    wall_part = wall_part.astype(jnp.bfloat16).reshape(comps, cells, part, groups, local_rows)
     wall_part = lax.all_to_all(wall_part, "gy", split_axis=3, concat_axis=2, tiled=True)
-    wall_part = wall_part.reshape(comps, cells, spanwise, local_rows)
+    wall_part = wall_part.reshape(comps, cells, spanwise, local_rows).astype(jnp.float32)
 
     extended_base = jnp.concatenate((tails[0], base_flow, heads[0]), axis=1)
     extended_adj = jnp.concatenate((tails[1], adjoint, heads[1]), axis=1)

time: 113 us -> 99.3 us (0.88)
  waiting for transfers between devices: 14.1 us -> 3.45 us
  local copies, waits for them, and re-layouts: 37.1 us -> 34.7 us
  starting transfers between devices: 21.6 us -> 20.4 us
    reduce_sum x1, other arithmetic: 3.56 us -> 9.84 us  [body(): first_coupling = jnp.sum(adjoint * dx_base, axis=0)]
    all_to_all x1, waiting for transfers between devices: 9.27 us -> 3.44 us  [body(): lax.all_to_all(wall_part, 'gy', split_axis=3, concat_axis=2, tiled=True)]
    add x1, other arithmetic: 16.8 us -> 11.1 us  [body(): base_flow[0][None] * dx_adj + base_flow[2][None] * dz_adj]
    all_to_all x1, waiting for transfers between devices: 4.82 us -> 0.01 us  [body(): lines = lax.all_to_all(low, 'gy', split_axis=2, concat_axis=3, tiled=True)]
    slice x6, local copies, waits for them, and re-layouts: 13.5 us -> 10.5 us  [first_periodic(): jnp.roll(field, -offset, direction) - jnp.roll(field, offset, direction)]
    squeeze x2, local copies, waits for them, and re-layouts: 3.26 us -> 4.64 us  [body(): extended_base = jnp.concatenate((tails[0], base_flow, heads[0]), axis=1)]
    all_to_all x1, starting transfers between devices: 4.91 us -> 3.73 us  [body(): lax.all_to_all(wall_part, 'gy', split_axis=3, concat_axis=2, tiled=True)]
    unnamed x20 -> x30, local copies, waits for them, and re-layouts: 3.8 us -> 3.82 us
  transfers between devices with their start and end apart: 4 -> 4, of which waited for: 2 -> 1; matrix products, arithmetic and copies ran while one was open for 52% -> 58% of each run, Pallas kernels for 0% -> 0%
where the time goes in v2:
time: 99.3 us; the launch traced here: 98.9 us
  other arithmetic  35.8 us (36%)
  local copies, waits for them, and re-layouts  34.7 us (35%)
  starting transfers between devices  20.4 us (21%)
  matrix products  4.32 us (4%)
  waiting for transfers between devices  3.45 us (3%)
    ppermute x2, starting transfers between devices, ring_shift(): return lax.ppermute(value, axis, pairs)  11.2 us
    add x1, other arithmetic, body(): base_flow[0][None] * dx_adj + base_flow[2][None] * dz_adj  11.1 us
    slice x6, local copies, waits for them, and re-layouts, first_periodic(): jnp.roll(field, -offset, direction) - jnp.roll(field, offset, direction)  10.5 us
    reduce_sum x1, other arithmetic, body(): first_coupling = jnp.sum(adjoint * dx_base, axis=0)  9.84 us
    slice x2, local copies, waits for them, and re-layouts, first_periodic(): jnp.roll(field, -1, direction) - jnp.roll(field, 1, direction)  6.23 us
    all_to_all x1, starting transfers between devices, body(): lines = lax.all_to_all(low, 'gy', split_axis=2, concat_axis=3, tiled=True)  5.4 us
    reduce_sum x1, other arithmetic, body(): last_coupling = jnp.sum(adjoint * dz_base, axis=0)  4.73 us
    squeeze x2, local copies, waits for them, and re-layouts, body(): extended_base = jnp.concatenate((tails[0], base_flow, heads[0]), axis=1)  4.64 us
  transfers between devices with their start and end apart: 4, of which 1 were waited for; matrix products, arithmetic and copies ran while one was open for 58% of the time, Pallas kernels for 0%

profile of v2, /device:TPU:1, one launch (start us, length us, event | category | flops | bytes accessed | tf_op | source)
XLA Modules:
  0.0 98.9 jit_solution(3645262524697566129)
XLA Ops:
  0.0 0.0 copy-start
  0.0 1.6 %slice_bitcast_fusion.6 = (f32[1,3,4,32,256]{4,3,2,1,0:T(8,128)S(1)}, f32[1,3,4,32,256]{4,3,2,1,0:T(8,128)S(1)}, f32[1,3,4,32,256]{4,3,2,1,0:T(8,128)S(1)}, f32[1,3,4,32,256]{4,3,2,1,0:T(8,128)S(1)}) fusion(f32[3,24,32,256]{3,2,1,0:T(8,128)} %param.7, f32[3,24,32,256]{3,2,1,0:T(8,128)} %param.6), kind=kLoop, calls=%fused_computation.103 | loop fusion | bytes 3145728 | tf_op jit(solution)/shard_map/stack | solution.py:67
  1.6 0.0 copy-start.4
  1.6 1.0 pad_maximum_fusion.12
  2.6 11.2 %collective-permute-start = (f32[2,3,4,32,256]{4,3,2,1,0:T(8,128)}, f32[2,3,4,32,256]{4,3,2,1,0:T(8,128)}, u32[]{:S(2)}, u32[]{:S(2)}) collective-permute-start(f32[2,3,4,32,256]{4,3,2,1,0:T(8,128)} %pad_maximum_fusion.12), channel_id=1, source_target_pairs={{4,0},{8,4},{12,8},{16,12},{20,16},{24,20},{28,24},{32,28},{36,32}... | collective-permute-start | bytes 2359304 | tf_op jit(solution)/shard_map/ppermute | solution.py:20
  13.8 0.9 pad_maximum_fusion.13
  14.8 0.0 collective-permute-start.1
  14.8 0.0 copy-done.4
  14.8 1.3 %copy.21 = bf16[3,24,32,256]{3,1,0,2:T(8,128)(2,1)S(1)} copy(f32[3,24,32,256]{3,2,1,0:T(8,128)S(1)} %copy-done.4) | data formatting | bytes 3538944 | tf_op args[0]
  16.0 0.0 copy-done.1
  16.0 1.3 %copy.20 = bf16[3,24,32,256]{3,1,0,2:T(8,128)(2,1)S(1)} copy(f32[3,24,32,256]{3,2,1,0:T(8,128)S(1)} %copy-done.1) | data formatting | bytes 3538944 | tf_op args[1]
  17.3 1.6 %maximum_bitcast_fusion = bf16[6,24,32,1,256]{4,1,0,3,2:T(8,128)(2,1)} fusion(bf16[3,24,32,256]{3,1,0,2:T(8,128)(2,1)S(1)} %copy.20, bf16[3,24,32,256]{3,1,0,2:T(8,128)(2,1)S(1)} %copy.21), kind=kLoop, calls=%fused_computation.78 | loop fusion | flops 1179648 | bytes 4718592 | tf_op jit(solution)/shard_map/reshape | solution.py:72
  18.9 5.4 %all-to-all-start = ((bf16[6,24,32,1,256]{4,1,0,3,2:T(8,128)(2,1)}), bf16[6,24,32,1,256]{4,1,0,3,2:T(8,128)(2,1)}, u32[]{:S(2)}, u32[]{:S(2)}) async-start(bf16[6,24,32,1,256]{4,1,0,3,2:T(8,128)(2,1)} %maximum_bitcast_fusion), calls=%async_computation | async-start | bytes 4718592 | tf_op jit(solution)/shard_map/all_to_all | solution.py:73
  24.4 5.5 %fusion.57 = (f32[3,24,31,256]{3,2,1,0:T(8,128)}, f32[3,24,31,256]{3,2,1,0:T(8,128)}) fusion(f32[3,24,32,256]{3,2,1,0:T(8,128)} %param.7), kind=kLoop, calls=%fused_computation.117 | loop fusion | bytes 9142272 | tf_op jit(solution)/shard_map/jit(_roll_static)/slice | solution.py:44
  29.9 0.0 copy-done.2
  29.9 2.7 %fusion.59 = (f32[3,24,30,256]{3,2,1,0:T(8,128)}, f32[3,24,30,256]{3,2,1,0:T(8,128)}) fusion(f32[3,24,32,256]{3,2,1,0:T(8,128)S(1)} %copy-done.2), kind=kLoop, calls=%fused_computation.119 | loop fusion | bytes 8847360 | tf_op jit(solution)/shard_map/jit(_roll_static)/slice | solution.py:47
  32.5 2.6 %fusion.61 = (f32[3,24,29,256]{3,2,1,0:T(8,128)}, f32[3,24,29,256]{3,2,1,0:T(8,128)}) fusion(f32[3,24,32,256]{3,2,1,0:T(8,128)S(1)} %copy-done.2), kind=kLoop, calls=%fused_computation.121 | loop fusion | bytes 8552448 | tf_op jit(solution)/shard_map/jit(_roll_static)/slice | solution.py:47
  35.2 0.0 copy-done.5
  35.2 1.0 %slice_bitcast_fusion.1 = (f32[24,32,256]{2,1,0:T(8,128)S(1)}, f32[24,32,256]{2,1,0:T(8,128)}) fusion(f32[3,24,32,256]{3,2,1,0:T(8,128)S(1)} %copy-done.5), kind=kLoop, calls=%fused_computation.98 | loop fusion | bytes 3145728 | tf_op jit(solution)/shard_map/mul | solution.py:97
  36.2 0.1 fusion.62
  36.3 0.9 fusion.64
  37.2 0.6 fusion.50
  37.9 0.6 fusion.52
  38.5 0.6 fusion.54
  39.1 0.6 fusion.56
  39.8 0.1 fusion.49
  39.9 0.1 fusion.51
  40.0 0.1 fusion.53
  40.1 0.1 fusion.55
  40.2 4.7 %fusion.30 = f32[24,32,256]{2,1,0:T(8,128)} fusion(f32[3,24,32,256]{3,2,1,0:T(8,128)S(1)} %copy-done.2, f32[3,24,1,256]{3,2,1,0:T(1,128)S(1)} %get-tuple-element.35, f32[3,24,31,256]{3,2,1,0:T(8,128)S(1)} %get-tuple-element.37, f32[3,24,31,256]{3,2,1,0:T(8,128)S(1)} %get-tuple-element.36, f32[3,24,1,256]{3,2,1,0:T(1,128)S(1)} %get-tuple-element.34, ...), kind=kLoop, calls=%fused_computation.67 | loop fusion | flops 12189696 | bytes 22020096 | tf_op jit(solution)/shard_map/reduce_sum | solution.py:100
  44.9 0.8 fusion.60
  45.8 0.7 fusion.58
  46.5 0.0 copy-start.9
  46.5 0.0 copy-start.10
  46.5 3.4 %fusion.63 = (f32[3,24,28,256]{3,2,1,0:T(8,128)S(1)}, f32[3,24,28,256]{3,2,1,0:T(8,128)S(1)}) fusion(f32[3,24,32,256]{3,2,1,0:T(8,128)} %param.7), kind=kLoop, calls=%fused_computation.123 | loop fusion | bytes 8257536 | tf_op jit(solution)/shard_map/jit(_roll_static)/slice | solution.py:47
  49.9 0.0 copy-start.3
  49.9 0.0 copy-start.12
  50.0 0.0 collective-permute-done
  50.0 2.7 %slice_bitcast_fusion.3 = (f32[3,4,32,256]{3,2,1,0:T(8,128)}, f32[3,4,32,256]{3,2,1,0:T(8,128)S(1)}) fusion(f32[2,3,4,32,256]{4,3,2,1,0:T(8,128)} %collective-permute-done), kind=kLoop, calls=%fused_computation.100 | loop fusion | bytes 1572864 | tf_op jit(solution)/shard_map/squeeze | solution.py:88
  52.7 0.0 collective-permute-done.1
  52.7 1.9 %slice_bitcast_fusion.2 = (f32[3,4,32,256]{3,2,1,0:T(8,128)}, f32[3,4,32,256]{3,2,1,0:T(8,128)S(1)}) fusion(f32[2,3,4,32,256]{4,3,2,1,0:T(8,128)} %collective-permute-done.1), kind=kLoop, calls=%fused_computation.99 | loop fusion | bytes 1572864 | tf_op jit(solution)/shard_map/squeeze | solution.py:88
  54.6 0.0 copy-done.7
  54.6 0.0 copy-done.8
  54.6 0.0 copy-done.10
  54.6 0.0 copy-done.3
  54.6 0.0 copy-done.12
  54.6 11.1 %multiply_add_fusion.1 = f32[3,24,32,256]{3,2,1,0:T(8,128)} fusion(f32[3,24,32,256]{3,2,1,0:T(8,128)S(1)} %copy-done.3, f32[3,24,28,256]{3,2,1,0:T(8,128)S(1)} %get-tuple-element.57, f32[3,24,4,256]{3,2,1,0:T(4,128)} %get-tuple-element.59, f32[3,24,4,256]{3,2,1,0:T(4,128)} %get-tuple-element.58, f32[3,24,28,256]{3,2,1,0:T(8,128)S(1)} %get-tuple-element.56, ...), kind=kLoop, calls=%fused_computation.84 | loop fusion | flops 40697856 | bytes 25952256 | tf_op jit(solution)/shard_map/add | solution.py:97
  65.7 0.0 all-to-all-done
  65.7 2.5 %copy.22 = bf16[6,24,4,8,1,256]{5,3,2,1,0,4:T(8,128)(2,1)S(1)} copy(bf16[6,24,4,8,1,256]{5,1,0,3,2,4:T(8,128)(2,1)} %bitcast.13) | data formatting | bytes 4718592 | tf_op jit(solution)/shard_map/all_to_all | solution.py:73
  68.3 0.0 copy-start.13
  68.3 0.2 fusion.48
  68.5 0.1 convert.4
  68.6 1.3 %copy-done.13 = bf16[1024,1024]{1,0:T(8,128)(2,1)S(1)} copy-done((bf16[1024,1024]{1,0:T(8,128)(2,1)S(1)}, bf16[1024,1024]{1,0:T(8,128)(2,1)}, u32[]{:S(2)}) %copy-start.13) | copy-done | bytes 2097176
  69.9 1.4 %fusion.37 = f32[3,24,8,1024]{3,2,1,0:T(8,128)S(1)} fusion(bf16[3,24,8,1024]{3,2,1,0:T(8,128)(2,1)S(1)} %bitcast.65, bf16[1024,1024]{1,0:T(8,128)(2,1)S(1)} %copy-done.13), kind=kOutput, calls=%fused_computation.85 | convolution fusion | flops 1207959552 | bytes 5636096 | tf_op jit(solution)/shard_map/fxzk,ik->fxzi/dot_general | solution.py:79
  71.3 1.5 %multiply_reduce_fusion = f32[24,8,1024]{2,1,0:T(8,128)S(1)} fusion(bf16[3,24,8,1024]{3,2,1,0:T(8,128)(2,1)S(1)} %bitcast.66, bf16[3,24,8,1024]{3,2,1,0:T(8,128)(2,1)S(1)} %bitcast.70, bf16[1024,1024]{1,0:T(8,128)(2,1)S(1)} %copy-done), kind=kOutput, calls=%fused_computation.82 | convolution fusion | flops 1209532416 | bytes 5242880 | tf_op jit(solution)/shard_map/fxzk,ik->fxzi/dot_general | solution.py:77
  72.7 1.5 %multiply_add_fusion = f32[3,24,8,1024]{3,2,1,0:T(8,128)S(1)} fusion(f32[3,24,8,1024]{3,2,1,0:T(8,128)S(1)} %fusion.37, bf16[3,24,8,1024]{3,2,1,0:T(8,128)(2,1)S(1)} %bitcast.67, bf16[1024,1024]{1,0:T(8,128)(2,1)S(1)} %copy-done, f32[24,8,1024]{2,1,0:T(8,128)S(1)} %convert.4), kind=kOutput, calls=%fused_computation.83 | convolution fusion | flops 1209729024 | bytes 8781824 | tf_op jit(solution)/shard_map/fxzk,ik->fxzi/dot_general | solution.py:78
  74.2 0.2 fusion.47
  74.5 0.2 convert_element_type.39
  74.6 1.1 %copy.12 = bf16[3,24,8,4,256]{4,2,1,0,3:T(8,128)(2,1)} copy(bf16[3,24,8,4,256]{4,2,3,1,0:T(8,128)(2,1)S(1)} %bitcast.68) | data formatting | bytes 2359296 | tf_op jit(solution)/shard_map/reshape | solution.py:84
  75.8 3.7 %all-to-all-start.1 = ((bf16[3,24,8,4,256]{4,2,1,0,3:T(8,128)(2,1)}), bf16[3,24,8,4,256]{4,2,1,0,3:T(8,128)(2,1)S(1)}, u32[]{:S(2)}, u32[]{:S(2)}) async-start(bf16[3,24,8,4,256]{4,2,1,0,3:T(8,128)(2,1)} %copy.12), calls=%async_computation.1 | async-start | bytes 2359296 | tf_op jit(solution)/shard_map/all_to_all | solution.py:85
  79.5 9.8 %fusion.6 = f32[24,32,256]{2,1,0:T(8,128)S(1)} fusion(f32[3,24,32,256]{3,2,1,0:T(8,128)} %param.7, f32[3,24,32,256]{3,2,1,0:T(8,128)} %param.6, f32[3,4,32,256]{3,2,1,0:T(8,128)} %get-tuple-element.62, f32[3,4,32,256]{3,2,1,0:T(8,128)} %get-tuple-element.60), kind=kLoop, calls=%fused_computation.30 | loop fusion | flops 12189696 | bytes 6291456 | tf_op jit(solution)/shard_map/reduce_sum | solution.py:99
  89.4 1.6 %slice_subtract_fusion.1 = (f32[1,24,32,256]{3,2,1,0:T(8,128)}, f32[1,24,32,256]{3,2,1,0:T(8,128)}, f32[1,24,32,256]{3,2,1,0:T(8,128)}) fusion(f32[3,24,32,256]{3,2,1,0:T(8,128)S(1)} %copy-done.6, f32[24,32,256]{2,1,0:T(8,128)S(1)} %fusion.6, f32[24,32,256]{2,1,0:T(8,128)S(1)} %copy-done.11), kind=kLoop, calls=%fused_computation.94 | loop fusion | flops 393216 | bytes 6291456 | tf_op jit(solution)/shard_map/sub | solution.py:101
  90.9 3.4 %all-to-all-done.1 = bf16[3,24,8,4,256]{4,2,1,0,3:T(8,128)(2,1)S(1)} async-done(((bf16[3,24,8,4,256]{4,2,1,0,3:T(8,128)(2,1)}), bf16[3,24,8,4,256]{4,2,1,0,3:T(8,128)(2,1)S(1)}, u32[]{:S(2)}, u32[]{:S(2)}) %all-to-all-start.1) | async-done | bytes 1179680 | tf_op jit(solution)/shard_map/all_to_all | solution.py:85
  94.4 4.6 %fusion.36 = f32[3,24,32,256]{3,2,1,0:T(8,128)} fusion(f32[3,24,32,256]{3,2,1,0:T(8,128)} %param.7, f32[1,24,32,256]{3,2,1,0:T(8,128)} %get-tuple-element.20, f32[1,24,32,256]{3,2,1,0:T(8,128)} %get-tuple-element.21, f32[1,24,32,256]{3,2,1,0:T(8,128)} %get-tuple-element.19, bf16[3,24,8,4,256]{4,2,1,0,3:T(8,128)(2,1)S(1)} %all-to-all-done.1, ...), kind=kLoop, calls=%fused_computation.77 | loop fusion | flops 4128768 | bytes 8257792 | tf_op jit(solution)/shard_map/jit(_where)/select_n | solution.py:105
  (13 shorter events, 0.1 us)
Async XLA Ops:
  0.0 71.3 %copy-start = (bf16[1024,1024]{1,0:T(8,128)(2,1)S(1)}, bf16[1024,1024]{1,0:T(8,128)(2,1)}, u32[]{:S(2)}) copy-start(bf16[1024,1024]{1,0:T(8,128)(2,1)} %param.8) | copy-start | bytes 6291460
  1.6 13.1 %copy-start.4 = (f32[3,24,32,256]{3,2,1,0:T(8,128)S(1)}, f32[3,24,32,256]{3,2,1,0:T(8,128)}, u32[]{:S(2)}) copy-start(f32[3,24,32,256]{3,2,1,0:T(8,128)} %param.6) | copy-start | bytes 7077892
  2.6 47.4 %collective-permute-start = (f32[2,3,4,32,256]{4,3,2,1,0:T(8,128)}, f32[2,3,4,32,256]{4,3,2,1,0:T(8,128)}, u32[]{:S(2)}, u32[]{:S(2)}) collective-permute-start(f32[2,3,4,32,256]{4,3,2,1,0:T(8,128)} %pad_maximum_fusion.12), channel_id=1, source_target_pairs={{4,0},{8,4},{12,8},{16,12},{20,16},{24,20},{28,24},{32,28},{36,32}... | collective-permute-start | bytes 2359304 | tf_op jit(solution)/shard_map/ppermute | solution.py:20
  13.8 2.2 %copy-start.1 = (f32[3,24,32,256]{3,2,1,0:T(8,128)S(1)}, f32[3,24,32,256]{3,2,1,0:T(8,128)}, u32[]{:S(2)}) copy-start(f32[3,24,32,256]{3,2,1,0:T(8,128)} %param.7) | copy-start | bytes 7077892
  14.8 37.9 %collective-permute-start.1 = (f32[2,3,4,32,256]{4,3,2,1,0:T(8,128)}, f32[2,3,4,32,256]{4,3,2,1,0:T(8,128)}, u32[]{:S(2)}, u32[]{:S(2)}) collective-permute-start(f32[2,3,4,32,256]{4,3,2,1,0:T(8,128)} %pad_maximum_fusion.13), channel_id=1, source_target_pairs={{0,4},{4,8},{8,12},{12,16},{16,20},{20,24},{24,28},{28,32},{32,36}... | collective-permute-start | bytes 2359304 | tf_op jit(solution)/shard_map/ppermute | solution.py:20
  18.9 46.8 %all-to-all-start = ((bf16[6,24,32,1,256]{4,1,0,3,2:T(8,128)(2,1)}), bf16[6,24,32,1,256]{4,1,0,3,2:T(8,128)(2,1)}, u32[]{:S(2)}, u32[]{:S(2)}) async-start(bf16[6,24,32,1,256]{4,1,0,3,2:T(8,128)(2,1)} %maximum_bitcast_fusion), calls=%async_computation | async-start | bytes 4718592 | tf_op jit(solution)/shard_map/all_to_all | solution.py:73
  24.4 5.5 %copy-start.2 = (f32[3,24,32,256]{3,2,1,0:T(8,128)S(1)}, f32[3,24,32,256]{3,2,1,0:T(8,128)}, u32[]{:S(2)}) copy-start(f32[3,24,32,256]{3,2,1,0:T(8,128)} %param.7) | copy-start | bytes 7077892
  32.5 2.7 %copy-start.5 = (f32[3,24,32,256]{3,2,1,0:T(8,128)S(1)}, f32[3,24,32,256]{3,2,1,0:T(8,128)}, u32[]{:S(2)}) copy-start(f32[3,24,32,256]{3,2,1,0:T(8,128)} %param.6) | copy-start | bytes 7077892
  46.5 8.1 %copy-start.7 = (f32[3,24,31,256]{3,2,1,0:T(8,128)S(1)}, f32[3,24,31,256]{3,2,1,0:T(8,128)}, u32[]{:S(2)}) copy-start(f32[3,24,31,256]{3,2,1,0:T(8,128)} %get-tuple-element.44) | copy-start | bytes 6856708
  46.5 8.1 %copy-start.8 = (f32[3,24,31,256]{3,2,1,0:T(8,128)S(1)}, f32[3,24,31,256]{3,2,1,0:T(8,128)}, u32[]{:S(2)}) copy-start(f32[3,24,31,256]{3,2,1,0:T(8,128)} %get-tuple-element.45) | copy-start | bytes 6856708
  46.5 8.1 %copy-start.9 = (f32[3,24,30,256]{3,2,1,0:T(8,128)S(1)}, f32[3,24,30,256]{3,2,1,0:T(8,128)}, u32[]{:S(2)}) copy-start(f32[3,24,30,256]{3,2,1,0:T(8,128)} %get-tuple-element.48) | copy-start | bytes 6635524
  46.5 8.1 %copy-start.10 = (f32[3,24,30,256]{3,2,1,0:T(8,128)S(1)}, f32[3,24,30,256]{3,2,1,0:T(8,128)}, u32[]{:S(2)}) copy-start(f32[3,24,30,256]{3,2,1,0:T(8,128)} %get-tuple-element.49) | copy-start | bytes 6635524
  49.9 4.7 %copy-start.3 = (f32[3,24,32,256]{3,2,1,0:T(8,128)S(1)}, f32[3,24,32,256]{3,2,1,0:T(8,128)}, u32[]{:S(2)}) copy-start(f32[3,24,32,256]{3,2,1,0:T(8,128)} %param.7) | copy-start | bytes 7077892
  49.9 4.7 %copy-start.12 = (f32[24,32,256]{2,1,0:T(8,128)S(1)}, f32[24,32,256]{2,1,0:T(8,128)}, u32[]{:S(2)}) copy-start(f32[24,32,256]{2,1,0:T(8,128)} %get-tuple-element.39) | copy-start | bytes 2359300
  68.3 1.6 %copy-start.13 = (bf16[1024,1024]{1,0:T(8,128)(2,1)S(1)}, bf16[1024,1024]{1,0:T(8,128)(2,1)}, u32[]{:S(2)}) copy-start(bf16[1024,1024]{1,0:T(8,128)(2,1)} %param.9) | copy-start | bytes 6291460
  75.8 18.6 %all-to-all-start.1 = ((bf16[3,24,8,4,256]{4,2,1,0,3:T(8,128)(2,1)}), bf16[3,24,8,4,256]{4,2,1,0,3:T(8,128)(2,1)S(1)}, u32[]{:S(2)}, u32[]{:S(2)}) async-start(bf16[3,24,8,4,256]{4,2,1,0,3:T(8,128)(2,1)} %copy.12), calls=%async_computation.1 | async-start | bytes 2359296 | tf_op jit(solution)/shard_map/all_to_all | solution.py:85
  79.5 9.9 %copy-start.6 = (f32[3,24,32,256]{3,2,1,0:T(8,128)S(1)}, f32[3,24,32,256]{3,2,1,0:T(8,128)}, u32[]{:S(2)}) copy-start(f32[3,24,32,256]{3,2,1,0:T(8,128)} %multiply_add_fusion.1) | copy-start | bytes 7077892
  79.5 9.9 %copy-start.11 = (f32[24,32,256]{2,1,0:T(8,128)S(1)}, f32[24,32,256]{2,1,0:T(8,128)}, u32[]{:S(2)}) copy-start(f32[24,32,256]{2,1,0:T(8,128)} %fusion.30) | copy-start | bytes 2359300

commit v3 on v2

v3 whole, which is shorter than its diff:
```python
import jax
import jax.numpy as jnp
from jax import lax
from jax.experimental import pallas as pl
from jax.experimental.pallas import tpu as pltpu
from jax.sharding import PartitionSpec as P

C_FIRST = (0.8, -0.2, 4.0 / 105.0, -1.0 / 280.0)
C_SECOND = (1.6, -0.2, 8.0 / 315.0, -1.0 / 560.0)
C_CENTER = -205.0 / 72.0
VISCOSITY = 0.1
STEP_WEIGHT = 0.5
HALO = 4
LANES = 128


def ring_shift(value, axis, forward):
    count = lax.axis_size(axis)
    if forward:
        pairs = [(i, (i + 1) % count) for i in range(count)]
    else:
        pairs = [((i + 1) % count, i) for i in range(count)]
    return lax.ppermute(value, axis, pairs)


def stencil_kernel(base_ref, adj_ref, tail_ref, head_ref, out_ref, ext_ref):
    comps, cells, span, lanes = base_ref.shape
    ext_ref[0, :, HALO : HALO + cells] = base_ref[...]
    ext_ref[1, :, HALO : HALO + cells] = adj_ref[...]
    ext_ref[:, :, :HALO] = tail_ref[...]
    ext_ref[:, :, HALO + cells :] = head_ref[...]

    def zshift(v, k):
        return pltpu.roll(v, (span - k) % span, 0)

    def derivs(field, c, xi, second):
        center = ext_ref[field, c, xi]
        plus = [ext_ref[field, c, xi + k] for k in range(1, 5)]
        minus = [ext_ref[field, c, xi - k] for k in range(1, 5)]
        zp = [zshift(center, k) for k in range(1, 5)]
        zm = [zshift(center, span - k) for k in range(1, 5)]
        dx = C_FIRST[0] * (plus[0] - minus[0])
        dz = C_FIRST[0] * (zp[0] - zm[0])
        for k in range(1, 4):
            dx = dx + C_FIRST[k] * (plus[k] - minus[k])
            dz = dz + C_FIRST[k] * (zp[k] - zm[k])
        if not second:
            return center, dx, dz, None, None
        dxx = C_CENTER * center
        dzz = C_CENTER * center
        for k in range(4):
            dxx = dxx + C_SECOND[k] * (plus[k] + minus[k])
            dzz = dzz + C_SECOND[k] * (zp[k] + zm[k])
        return center, dx, dz, dxx, dzz

    def step(x, carry):
        xi = x + HALO
        base = [derivs(0, j, xi, False) for j in range(comps)]
        adj = [derivs(1, c, xi, True) for c in range(comps)]
        first_coupling = adj[0][0] * base[0][1] + adj[1][0] * base[1][1] + adj[2][0] * base[2][1]
        last_coupling = adj[0][0] * base[0][2] + adj[1][0] * base[1][2] + adj[2][0] * base[2][2]
        for c in range(comps):
            center, dx, dz, dxx, dzz = adj[c]
            tendency = base[0][0] * dx + base[2][0] * dz + VISCOSITY * (dxx + dzz)
            if c == 0:
                tendency = tendency - first_coupling
            elif c == comps - 1:
                tendency = tendency - last_coupling
            out_ref[c, x] = center + STEP_WEIGHT * tendency
        return carry

    lax.fori_loop(0, cells, step, 0)


def stencil_update(base_flow, adjoint, tails, heads):
    comps, cells, span, rows = base_flow.shape
    lanes = LANES if rows % LANES == 0 else rows
    field_spec = pl.BlockSpec((comps, cells, span, lanes), lambda j: (0, 0, 0, j))
    halo_spec = pl.BlockSpec((2, comps, HALO, span, lanes), lambda j: (0, 0, 0, 0, j))
    return pl.pallas_call(
        stencil_kernel,
        grid=(rows // lanes,),
        in_specs=[field_spec, field_spec, halo_spec, halo_spec],
        out_specs=field_spec,
        out_shape=jax.ShapeDtypeStruct(base_flow.shape, jnp.float32),
        scratch_shapes=[pltpu.VMEM((2, comps, cells + 2 * HALO, span, lanes), jnp.float32)],
    )(base_flow, adjoint, tails, heads)


def body(base_flow, adjoint, first_op, second_op):
    comps, cells, spanwise, local_rows = base_flow.shape
    groups = lax.axis_size("gy")
    total_rows = local_rows * groups
    part = spanwise // groups

    tails = ring_shift(jnp.stack((base_flow[:, cells - HALO :], adjoint[:, cells - HALO :]), 0), "gx", True)
    heads = ring_shift(jnp.stack((base_flow[:, :HALO], adjoint[:, :HALO]), 0), "gx", False)

    base_low = lax.optimization_barrier(base_flow.astype(jnp.bfloat16))
    adjoint_low = lax.optimization_barrier(adjoint.astype(jnp.bfloat16))
    low = jnp.concatenate((base_low, adjoint_low), 0).reshape(2 * comps, cells, spanwise, 1, local_rows)
    lines = lax.all_to_all(low, "gy", split_axis=2, concat_axis=3, tiled=True)
    lines = lines.reshape(2 * comps, cells, part, total_rows)
    base_lines = lines[:comps]
    adj_lines = lines[comps:]
    slope_base = jnp.einsum("fxzk,ik->fxzi", base_lines, first_op, preferred_element_type=jnp.float32)
    slope_adj = jnp.einsum("fxzk,ik->fxzi", adj_lines, first_op, preferred_element_type=jnp.float32)
    curves = jnp.einsum("fxzk,ik->fxzi", adj_lines, second_op, preferred_element_type=jnp.float32)
    normal_vel = base_lines[1].astype(jnp.float32)
    coupling = jnp.sum(adj_lines.astype(jnp.float32) * slope_base, axis=0)
    wall_part = normal_vel[None] * slope_adj + VISCOSITY * curves
    wall_part = wall_part.at[1].add(-coupling)
    wall_part = wall_part.astype(jnp.bfloat16).reshape(comps, cells, part, groups, local_rows)
    wall_part = lax.all_to_all(wall_part, "gy", split_axis=3, concat_axis=2, tiled=True)
    wall_part = wall_part.reshape(comps, cells, spanwise, local_rows).astype(jnp.float32)

    partial = stencil_update(base_flow, adjoint, tails, heads)
    updated = partial + STEP_WEIGHT * wall_part
    wall_index = lax.axis_index("gy") * local_rows + jnp.arange(local_rows, dtype=jnp.int32)
    interior = (wall_index > 0) & (wall_index < total_rows - 1)
    return jnp.where(interior, updated, jnp.float32(0.0))


def solution(mesh):
    return jax.shard_map(
        body,
        mesh=mesh,
        in_specs=(P(None, "gx", None, "gy"), P(None, "gx", None, "gy"), P(), P()),
        out_specs=P(None, "gx", None, "gy"),
        check_vma=False,
    )
```

time: 99.3 us -> 119 us (1.20)
  waiting for transfers between devices: 3.45 us -> 59.3 us
  other arithmetic: 35.8 us -> 8.74 us
  local copies, waits for them, and re-layouts: 34.7 us -> 11.9 us
  Pallas kernels: 0 us -> 13.2 us
    ppermute x2, waiting for transfers between devices: 0.01 us -> 43.7 us  [ring_shift(): return lax.ppermute(value, axis, pairs)]
    slice x16 -> x0, local copies, waits for them, and re-layouts: 19.7 us -> none  [the longest x6 10.5 us: first_periodic(): jnp.roll(field, -offset, direction) - jnp.roll(field, offset, direction)]
    all_to_all x1, waiting for transfers between devices: 0.01 us -> 15.6 us  [body(): lines = lax.all_to_all(low, 'gy', split_axis=2, concat_axis=3, tiled=True)]
    reduce_sum x2 -> x0, other arithmetic: 14.6 us -> none  [the longest x1 9.84 us: body(): first_coupling = jnp.sum(adjoint * dx_base, axis=0)]
    pallas_call x0 -> x1, Pallas kernels: none -> 13.2 us  [stencil_update(): pl.pallas_call(stencil_kernel, grid=(rows // lanes,), in_specs=[field_spe...]
    add x1 -> x0, other arithmetic: 11.1 us -> none  [body(): base_flow[0][None] * dx_adj + base_flow[2][None] * dz_adj]
    squeeze x2 -> x0, local copies, waits for them, and re-layouts: 4.64 us -> none  [body(): extended_base = jnp.concatenate((tails[0], base_flow, heads[0]), axis=1)]
    all_to_all x1, waiting for transfers between devices: 3.44 us -> 0.01 us  [body(): lax.all_to_all(wall_part, 'gy', split_axis=3, concat_axis=2, tiled=True)]
  transfers between devices with their start and end apart: 4 -> 4, of which waited for: 1 -> 2; matrix products, arithmetic and copies ran while one was open for 58% -> 12% of each run, Pallas kernels for 0% -> 11%
where the time goes in v3:
time: 119 us; the launch traced here: 118 us
  waiting for transfers between devices  59.3 us (50%)
  starting transfers between devices  20.8 us (17%)
  Pallas kernels  13.2 us (11%)
  local copies, waits for them, and re-layouts  11.9 us (10%)
  other arithmetic  8.74 us (7%)
  matrix products  4.32 us (4%)
    ppermute x2, waiting for transfers between devices, ring_shift(): return lax.ppermute(value, axis, pairs)  43.7 us
    all_to_all x1, waiting for transfers between devices, body(): lines = lax.all_to_all(low, 'gy', split_axis=2, concat_axis=3, tiled=True)  15.6 us
    pallas_call x1, Pallas kernels, stencil_update(): pl.pallas_call(stencil_kernel, grid=(rows // lanes,), in_specs=[field_spe...  13.2 us
    ppermute x2, starting transfers between devices, ring_shift(): return lax.ppermute(value, axis, pairs)  8.7 us
    all_to_all x1, starting transfers between devices, body(): lines = lax.all_to_all(low, 'gy', split_axis=2, concat_axis=3, tiled=True)  7.66 us
    unnamed x8, local copies, waits for them, and re-layouts  5.6 us
    all_to_all x1, starting transfers between devices, body(): lax.all_to_all(wall_part, 'gy', split_axis=3, concat_axis=2, tiled=True)  4.46 us
    select_n x1, other arithmetic, body(): return jnp.where(interior, updated, jnp.float32(0.0))  3.63 us
  transfers between devices with their start and end apart: 4, of which 2 were waited for; matrix products, arithmetic and copies ran while one was open for 12% of the time, Pallas kernels for 11%

profile of v3, /device:TPU:1, one launch (start us, length us, event | category | flops | bytes accessed | tf_op | source)
XLA Modules:
  0.0 118.4 jit_solution(16259393363531956539)
XLA Ops:
  0.0 0.0 copy-start
  0.0 0.0 copy-start.1
  0.0 3.1 %copy.17 = bf16[3,24,32,256]{3,1,0,2:T(8,128)(2,1)S(1)} copy(f32[3,24,32,256]{3,2,1,0:T(8,128)} %base_ref.1) | data formatting | bytes 3538944 | tf_op args[0]
  3.1 0.0 copy-done.1
  3.1 1.3 %copy.16 = bf16[3,24,32,256]{3,1,0,2:T(8,128)(2,1)S(1)} copy(f32[3,24,32,256]{3,2,1,0:T(8,128)S(1)} %copy-done.1) | data formatting | bytes 3538944 | tf_op args[1]
  4.4 1.6 %maximum_bitcast_fusion = bf16[6,24,32,1,256]{4,1,0,3,2:T(8,128)(2,1)} fusion(bf16[3,24,32,256]{3,1,0,2:T(8,128)(2,1)S(1)} %copy.16, bf16[3,24,32,256]{3,1,0,2:T(8,128)(2,1)S(1)} %copy.17), kind=kLoop, calls=%fused_computation | loop fusion | flops 1179648 | bytes 4718592 | tf_op jit(solution)/shard_map/reshape | solution.py:101
  6.0 7.7 %all-to-all-start = ((bf16[6,24,32,1,256]{4,1,0,3,2:T(8,128)(2,1)}), bf16[6,24,32,1,256]{4,1,0,3,2:T(8,128)(2,1)}, u32[]{:S(2)}, u32[]{:S(2)}) async-start(bf16[6,24,32,1,256]{4,1,0,3,2:T(8,128)(2,1)} %maximum_bitcast_fusion), calls=%async_computation | async-start | bytes 4718592 | tf_op jit(solution)/shard_map/all_to_all | solution.py:102
  13.6 2.4 %slice_bitcast_fusion = (f32[1,3,4,32,256]{4,3,2,1,0:T(8,128)S(1)}, f32[1,3,4,32,256]{4,3,2,1,0:T(8,128)}, f32[1,3,4,32,256]{4,3,2,1,0:T(8,128)}, f32[1,3,4,32,256]{4,3,2,1,0:T(8,128)S(1)}) fusion(f32[3,24,32,256]{3,2,1,0:T(8,128)} %adj_ref.1, f32[3,24,32,256]{3,2,1,0:T(8,128)} %base_ref.1), kind=kLoop, calls=%fused_computation.19 | loop fusion | bytes 3145728 | tf_op jit(solution)/shard_map/stack | solution.py:97
  16.0 0.9 pad_maximum_fusion.1
  17.0 8.7 %collective-permute-start.1 = (f32[2,3,4,32,256]{4,3,2,1,0:T(8,128)}, f32[2,3,4,32,256]{4,3,2,1,0:T(8,128)}, u32[]{:S(2)}, u32[]{:S(2)}) collective-permute-start(f32[2,3,4,32,256]{4,3,2,1,0:T(8,128)} %pad_maximum_fusion.1), channel_id=1, source_target_pairs={{4,0},{8,4},{12,8},{16,12},{20,16},{24,20},{28,24},{32,28},{36,32}... | collective-permute-start | bytes 2359304 | tf_op jit(solution)/shard_map/ppermute | solution.py:23
  25.7 15.6 %all-to-all-done = bf16[6,24,32,1,256]{4,1,0,3,2:T(8,128)(2,1)} async-done(((bf16[6,24,32,1,256]{4,1,0,3,2:T(8,128)(2,1)}), bf16[6,24,32,1,256]{4,1,0,3,2:T(8,128)(2,1)}, u32[]{:S(2)}, u32[]{:S(2)}) %all-to-all-start) | async-done | bytes 2359328 | tf_op jit(solution)/shard_map/all_to_all | solution.py:102
  41.2 2.5 %copy.18 = bf16[6,24,4,8,1,256]{5,3,2,1,0,4:T(8,128)(2,1)S(1)} copy(bf16[6,24,4,8,1,256]{5,1,0,3,2,4:T(8,128)(2,1)} %bitcast.5) | data formatting | bytes 4718592 | tf_op jit(solution)/shard_map/all_to_all | solution.py:102
  43.8 0.0 copy-start.2
  43.8 0.2 fusion.12
  44.0 0.1 convert.1
  44.1 1.3 %copy-done.2 = bf16[1024,1024]{1,0:T(8,128)(2,1)S(1)} copy-done((bf16[1024,1024]{1,0:T(8,128)(2,1)S(1)}, bf16[1024,1024]{1,0:T(8,128)(2,1)}, u32[]{:S(2)}) %copy-start.2) | copy-done | bytes 2097176
  45.4 1.4 %fusion.1 = f32[3,24,8,1024]{3,2,1,0:T(8,128)S(1)} fusion(bf16[3,24,8,1024]{3,2,1,0:T(8,128)(2,1)S(1)} %bitcast.51, bf16[1024,1024]{1,0:T(8,128)(2,1)S(1)} %copy-done.2), kind=kOutput, calls=%fused_computation.9 | convolution fusion | flops 1207959552 | bytes 5636096 | tf_op jit(solution)/shard_map/fxzk,ik->fxzi/dot_general | solution.py:108
  46.8 0.0 copy-done
  46.8 1.5 %multiply_reduce_fusion = f32[24,8,1024]{2,1,0:T(8,128)S(1)} fusion(bf16[3,24,8,1024]{3,2,1,0:T(8,128)(2,1)S(1)} %bitcast.52, bf16[3,24,8,1024]{3,2,1,0:T(8,128)(2,1)S(1)} %bitcast.56, bf16[1024,1024]{1,0:T(8,128)(2,1)S(1)} %copy-done), kind=kOutput, calls=%fused_computation.7 | convolution fusion | flops 1209532416 | bytes 5242880 | tf_op jit(solution)/shard_map/fxzk,ik->fxzi/dot_general | solution.py:106
  48.3 1.5 %multiply_add_fusion = f32[3,24,8,1024]{3,2,1,0:T(8,128)S(1)} fusion(f32[3,24,8,1024]{3,2,1,0:T(8,128)S(1)} %fusion.1, bf16[3,24,8,1024]{3,2,1,0:T(8,128)(2,1)S(1)} %bitcast.53, bf16[1024,1024]{1,0:T(8,128)(2,1)S(1)} %copy-done, f32[24,8,1024]{2,1,0:T(8,128)S(1)} %convert.1), kind=kOutput, calls=%fused_computation.8 | convolution fusion | flops 1209729024 | bytes 8781824 | tf_op jit(solution)/shard_map/fxzk,ik->fxzi/dot_general | solution.py:107
  49.7 0.2 fusion.11
  50.0 0.2 convert_element_type.33
  50.1 1.1 copy.8
  51.3 4.5 %all-to-all-start.1 = ((bf16[3,24,8,4,256]{4,2,1,0,3:T(8,128)(2,1)}), bf16[3,24,8,4,256]{4,2,1,0,3:T(8,128)(2,1)S(1)}, u32[]{:S(2)}, u32[]{:S(2)}) async-start(bf16[3,24,8,4,256]{4,2,1,0,3:T(8,128)(2,1)} %copy.8), calls=%async_computation.1 | async-start | bytes 2359296 | tf_op jit(solution)/shard_map/all_to_all | solution.py:114
  55.8 2.1 %pad_maximum_fusion = f32[2,3,4,32,256]{4,3,2,1,0:T(8,128)} fusion(f32[1,3,4,32,256]{4,3,2,1,0:T(8,128)} %get-tuple-element.22, f32[1,3,4,32,256]{4,3,2,1,0:T(8,128)} %get-tuple-element.23), kind=kLoop, calls=%fused_computation.17 | loop fusion | flops 196608 | bytes 1572864 | tf_op jit(solution)/shard_map/stack | solution.py:96
  57.8 0.0 collective-permute-start
  57.8 0.0 collective-permute-done.1.head_ref
  57.9 43.7 %collective-permute-done.tail_ref = f32[2,3,4,32,256]{4,3,2,1,0:T(8,128)} collective-permute-done((f32[2,3,4,32,256]{4,3,2,1,0:T(8,128)}, f32[2,3,4,32,256]{4,3,2,1,0:T(8,128)}, u32[]{:S(2)}, u32[]{:S(2)}) %collective-permute-start) | collective-permute-done | bytes 786464 | tf_op jit(solution)/shard_map/ppermute | solution.py:23
  101.6 13.2 %shard_map.46 = f32[3,24,32,256]{3,2,1,0:T(8,128)} custom-call(f32[3,24,32,256]{3,2,1,0:T(8,128)} %base_ref.1, f32[3,24,32,256]{3,2,1,0:T(8,128)} %adj_ref.1, f32[2,3,4,32,256]{4,3,2,1,0:T(8,128)} %collective-permute-done.tail_ref, f32[2,3,4,32,256]{4,3,2,1,0:T(8,128)} %collective-permute-done.1.head_ref), custom_call_target="tpu_custom_call" | custom-call | tf_op jit(solution)/shard_map/pallas_call | solution.py:80
  114.8 0.0 all-to-all-done.1
  114.8 3.6 %fusion = f32[3,24,32,256]{3,2,1,0:T(8,128)} fusion(f32[3,24,32,256]{3,2,1,0:T(8,128)} %shard_map.46, pred[256]{0:T(512)(128)(4,1)S(1)} %compare_and_fusion, bf16[3,24,8,4,256]{4,2,1,0,3:T(8,128)(2,1)S(1)} %all-to-all-done.1), kind=kLoop, calls=%fused_computation.2 | loop fusion | flops 2359296 | bytes 5898496 | tf_op jit(solution)/shard_map/jit(_where)/select_n | solution.py:121
  (2 shorter events, 0.0 us)
Async XLA Ops:
  0.0 46.8 %copy-start = (bf16[1024,1024]{1,0:T(8,128)(2,1)S(1)}, bf16[1024,1024]{1,0:T(8,128)(2,1)}, u32[]{:S(2)}) copy-start(bf16[1024,1024]{1,0:T(8,128)(2,1)} %param.8) | copy-start | bytes 6291460
  0.0 3.1 %copy-start.1 = (f32[3,24,32,256]{3,2,1,0:T(8,128)S(1)}, f32[3,24,32,256]{3,2,1,0:T(8,128)}, u32[]{:S(2)}) copy-start(f32[3,24,32,256]{3,2,1,0:T(8,128)} %adj_ref.1) | copy-start | bytes 7077892
  6.0 35.3 %all-to-all-start = ((bf16[6,24,32,1,256]{4,1,0,3,2:T(8,128)(2,1)}), bf16[6,24,32,1,256]{4,1,0,3,2:T(8,128)(2,1)}, u32[]{:S(2)}, u32[]{:S(2)}) async-start(bf16[6,24,32,1,256]{4,1,0,3,2:T(8,128)(2,1)} %maximum_bitcast_fusion), calls=%async_computation | async-start | bytes 4718592 | tf_op jit(solution)/shard_map/all_to_all | solution.py:102
  17.0 40.9 %collective-permute-start.1 = (f32[2,3,4,32,256]{4,3,2,1,0:T(8,128)}, f32[2,3,4,32,256]{4,3,2,1,0:T(8,128)}, u32[]{:S(2)}, u32[]{:S(2)}) collective-permute-start(f32[2,3,4,32,256]{4,3,2,1,0:T(8,128)} %pad_maximum_fusion.1), channel_id=1, source_target_pairs={{4,0},{8,4},{12,8},{16,12},{20,16},{24,20},{28,24},{32,28},{36,32}... | collective-permute-start | bytes 2359304 | tf_op jit(solution)/shard_map/ppermute | solution.py:23
  43.8 1.6 %copy-start.2 = (bf16[1024,1024]{1,0:T(8,128)(2,1)S(1)}, bf16[1024,1024]{1,0:T(8,128)(2,1)}, u32[]{:S(2)}) copy-start(bf16[1024,1024]{1,0:T(8,128)(2,1)} %param.9) | copy-start | bytes 6291460
  51.3 63.5 %all-to-all-start.1 = ((bf16[3,24,8,4,256]{4,2,1,0,3:T(8,128)(2,1)}), bf16[3,24,8,4,256]{4,2,1,0,3:T(8,128)(2,1)S(1)}, u32[]{:S(2)}, u32[]{:S(2)}) async-start(bf16[3,24,8,4,256]{4,2,1,0,3:T(8,128)(2,1)} %copy.8), calls=%async_computation.1 | async-start | bytes 2359296 | tf_op jit(solution)/shard_map/all_to_all | solution.py:114
  57.8 43.7 %collective-permute-start = (f32[2,3,4,32,256]{4,3,2,1,0:T(8,128)}, f32[2,3,4,32,256]{4,3,2,1,0:T(8,128)}, u32[]{:S(2)}, u32[]{:S(2)}) collective-permute-start(f32[2,3,4,32,256]{4,3,2,1,0:T(8,128)} %pad_maximum_fusion), channel_id=1, source_target_pairs={{0,4},{4,8},{8,12},{12,16},{16,20},{20,24},{24,28},{28,32},{32,36}... | collective-permute-start | bytes 2359304 | tf_op jit(solution)/shard_map/ppermute | solution.py:23

commit v4 on v3

--- a/solution.py
+++ b/solution.py
@@ -23,7 +23,8 @@
     return lax.ppermute(value, axis, pairs)
 
 
-def stencil_kernel(base_ref, adj_ref, tail_ref, head_ref, out_ref, ext_ref):
+def stencil_kernel(base_ref, adj_ref, tail_ref, head_ref, *rest):
+    out_ref, ext_ref = rest[-2:]
     comps, cells, span, lanes = base_ref.shape
     ext_ref[0, :, HALO : HALO + cells] = base_ref[...]
     ext_ref[1, :, HALO : HALO + cells] = adj_ref[...]
@@ -72,19 +73,26 @@
     lax.fori_loop(0, cells, step, 0)
 
 
-def stencil_update(base_flow, adjoint, tails, heads):
+def stencil_update(base_flow, adjoint, tails, heads, block, previous=None):
     comps, cells, span, rows = base_flow.shape
-    lanes = LANES if rows % LANES == 0 else rows
-    field_spec = pl.BlockSpec((comps, cells, span, lanes), lambda j: (0, 0, 0, j))
-    halo_spec = pl.BlockSpec((2, comps, HALO, span, lanes), lambda j: (0, 0, 0, 0, j))
+    field_spec = pl.BlockSpec((comps, cells, span, LANES), lambda j: (0, 0, 0, block))
+    halo_spec = pl.BlockSpec((2, comps, HALO, span, LANES), lambda j: (0, 0, 0, 0, block))
+    in_specs = [field_spec, field_spec, halo_spec, halo_spec]
+    operands = [base_flow, adjoint, tails, heads]
+    aliases = {}
+    if previous is not None:
+        in_specs.append(pl.BlockSpec(memory_space=pl.ANY))
+        operands.append(previous)
+        aliases = {4: 0}
     return pl.pallas_call(
         stencil_kernel,
-        grid=(rows // lanes,),
-        in_specs=[field_spec, field_spec, halo_spec, halo_spec],
+        grid=(1,),
+        in_specs=in_specs,
         out_specs=field_spec,
         out_shape=jax.ShapeDtypeStruct(base_flow.shape, jnp.float32),
-        scratch_shapes=[pltpu.VMEM((2, comps, cells + 2 * HALO, span, lanes), jnp.float32)],
-    )(base_flow, adjoint, tails, heads)
+        scratch_shapes=[pltpu.VMEM((2, comps, cells + 2 * HALO, span, LANES), jnp.float32)],
+        input_output_aliases=aliases,
+    )(*operands)
 
 
 def body(base_flow, adjoint, first_op, second_op):
@@ -100,6 +108,8 @@
     adjoint_low = lax.optimization_barrier(adjoint.astype(jnp.bfloat16))
     low = jnp.concatenate((base_low, adjoint_low), 0).reshape(2 * comps, cells, spanwise, 1, local_rows)
     lines = lax.all_to_all(low, "gy", split_axis=2, concat_axis=3, tiled=True)
+    partial = stencil_update(base_flow, adjoint, tails, heads, 0)
+    lines, partial = lax.optimization_barrier((lines, partial))
     lines = lines.reshape(2 * comps, cells, part, total_rows)
     base_lines = lines[:comps]
     adj_lines = lines[comps:]
@@ -111,10 +121,12 @@
     wall_part = normal_vel[None] * slope_adj + VISCOSITY * curves
     wall_part = wall_part.at[1].add(-coupling)
     wall_part = wall_part.astype(jnp.bfloat16).reshape(comps, cells, part, groups, local_rows)
+    wall_part, partial = lax.optimization_barrier((wall_part, partial))
     wall_part = lax.all_to_all(wall_part, "gy", split_axis=3, concat_axis=2, tiled=True)
     wall_part = wall_part.reshape(comps, cells, spanwise, local_rows).astype(jnp.float32)
 
-    partial = stencil_update(base_flow, adjoint, tails, heads)
+    for block in range(1, local_rows // LANES):
+        partial = stencil_update(base_flow, adjoint, tails, heads, block, partial)
     updated = partial + STEP_WEIGHT * wall_part
     wall_index = lax.axis_index("gy") * local_rows + jnp.arange(local_rows, dtype=jnp.int32)
     interior = (wall_index > 0) & (wall_index < total_rows - 1)

time: 119 us -> 91.5 us (0.77)
  waiting for transfers between devices: 59.3 us -> 32 us
  other arithmetic: 8.74 us -> 5.85 us
  Pallas kernels: 13.2 us -> 15.9 us
    ppermute x2, waiting for transfers between devices: 43.7 us -> 17.7 us  [ring_shift(): return lax.ppermute(value, axis, pairs)]
    all_to_all x1, waiting for transfers between devices: 15.6 us -> 7.42 us  [body(): lines = lax.all_to_all(low, 'gy', split_axis=2, concat_axis=3, tiled=True)]
    all_to_all x1, waiting for transfers between devices: 0.01 us -> 6.9 us  [body(): lax.all_to_all(wall_part, 'gy', split_axis=3, concat_axis=2, tiled=True)]
    pallas_call x1 -> x2, Pallas kernels: 13.2 us -> 15.9 us  [stencil_update(): pl.pallas_call(stencil_kernel, grid=(1,), in_specs=in_specs, out_specs=fi...]
    another operation x1, other arithmetic: 2.07 us -> 0.05 us  [body(): jnp.stack((base_flow[:, cells - HALO:], adjoint[:, cells - HALO:]), 0)]
    unnamed x8 -> x10, local copies, waits for them, and re-layouts: 5.6 us -> 6.55 us
  transfers between devices with their start and end apart: 4 -> 4, of which waited for: 2 -> 3; matrix products, arithmetic and copies ran while one was open for 12% -> 2% of each run, Pallas kernels for 11% -> 17%
where the time goes in v4:
time: 91.5 us; the launch traced here: 91.1 us
  waiting for transfers between devices  32 us (35%)
  starting transfers between devices  21 us (23%)
  Pallas kernels  15.9 us (17%)
  local copies, waits for them, and re-layouts  11.9 us (13%)
  other arithmetic  5.85 us (6%)
  matrix products  4.32 us (5%)
    ppermute x2, waiting for transfers between devices, ring_shift(): return lax.ppermute(value, axis, pairs)  17.7 us
    pallas_call x2, Pallas kernels, stencil_update(): pl.pallas_call(stencil_kernel, grid=(1,), in_specs=in_specs, out_specs=fi...  15.9 us
    ppermute x2, starting transfers between devices, ring_shift(): return lax.ppermute(value, axis, pairs)  8.85 us
    all_to_all x1, starting transfers between devices, body(): lines = lax.all_to_all(low, 'gy', split_axis=2, concat_axis=3, tiled=True)  7.65 us
    all_to_all x1, waiting for transfers between devices, body(): lines = lax.all_to_all(low, 'gy', split_axis=2, concat_axis=3, tiled=True)  7.42 us
    all_to_all x1, waiting for transfers between devices, body(): lax.all_to_all(wall_part, 'gy', split_axis=3, concat_axis=2, tiled=True)  6.9 us
    unnamed x10, local copies, waits for them, and re-layouts  6.55 us
    all_to_all x1, starting transfers between devices, body(): lax.all_to_all(wall_part, 'gy', split_axis=3, concat_axis=2, tiled=True)  4.47 us
  transfers between devices with their start and end apart: 4, of which 3 were waited for; matrix products, arithmetic and copies ran while one was open for 2% of the time, Pallas kernels for 17%

profile of v4, /device:TPU:1, one launch (start us, length us, event | category | flops | bytes accessed | tf_op | source)
XLA Modules:
  0.0 91.1 jit_solution(15590597654113810677)
XLA Ops:
  0.0 0.0 copy-start
  0.0 0.0 copy-start.1
  0.0 3.1 %copy.18 = bf16[3,24,32,256]{3,1,0,2:T(8,128)(2,1)S(1)} copy(f32[3,24,32,256]{3,2,1,0:T(8,128)} %base_ref.3) | data formatting | bytes 3538944 | tf_op args[0]
  3.1 0.0 copy-done.1
  3.1 1.3 %copy.17 = bf16[3,24,32,256]{3,1,0,2:T(8,128)(2,1)S(1)} copy(f32[3,24,32,256]{3,2,1,0:T(8,128)S(1)} %copy-done.1) | data formatting | bytes 3538944 | tf_op args[1]
  4.4 1.6 %maximum_bitcast_fusion = bf16[6,24,32,1,256]{4,1,0,3,2:T(8,128)(2,1)} fusion(bf16[3,24,32,256]{3,1,0,2:T(8,128)(2,1)S(1)} %copy.17, bf16[3,24,32,256]{3,1,0,2:T(8,128)(2,1)S(1)} %copy.18), kind=kLoop, calls=%fused_computation | loop fusion | flops 1179648 | bytes 4718592 | tf_op jit(solution)/shard_map/reshape | solution.py:109
  6.0 7.7 %all-to-all-start = ((bf16[6,24,32,1,256]{4,1,0,3,2:T(8,128)(2,1)}), bf16[6,24,32,1,256]{4,1,0,3,2:T(8,128)(2,1)}, u32[]{:S(2)}, u32[]{:S(2)}) async-start(bf16[6,24,32,1,256]{4,1,0,3,2:T(8,128)(2,1)} %maximum_bitcast_fusion), calls=%async_computation | async-start | bytes 4718592 | tf_op jit(solution)/shard_map/all_to_all | solution.py:110
  13.6 1.5 %slice_bitcast_fusion = (f32[1,3,4,32,256]{4,3,2,1,0:T(8,128)S(1)}, f32[1,3,4,32,256]{4,3,2,1,0:T(8,128)S(1)}, f32[1,3,4,32,256]{4,3,2,1,0:T(8,128)S(1)}, f32[1,3,4,32,256]{4,3,2,1,0:T(8,128)S(1)}) fusion(f32[3,24,32,256]{3,2,1,0:T(8,128)} %adj_ref.3, f32[3,24,32,256]{3,2,1,0:T(8,128)} %base_ref.3), kind=kLoop, calls=%fused_computation.19 | loop fusion | bytes 3145728 | tf_op jit(solution)/shard_map/stack | solution.py:105
  15.1 0.1 pad_maximum_fusion
  15.2 0.1 collective-permute-start
  15.2 0.1 pad_maximum_fusion.1
  15.3 8.8 %collective-permute-start.1 = (f32[2,3,4,32,256]{4,3,2,1,0:T(8,128)S(1)}, f32[2,3,4,32,256]{4,3,2,1,0:T(8,128)}, u32[]{:S(2)}, u32[]{:S(2)}) collective-permute-start(f32[2,3,4,32,256]{4,3,2,1,0:T(8,128)S(1)} %pad_maximum_fusion.1), channel_id=1, source_target_pairs={{4,0},{8,4},{12,8},{16,12},{20,16},{24,20},{28,24},{32,28},{36,32}... | collective-permute-start | bytes 2359304 | tf_op jit(solution)/shard_map/ppermute | solution.py:23
  24.1 17.7 %collective-permute-done.tail_ref = f32[2,3,4,32,256]{4,3,2,1,0:T(8,128)S(1)} collective-permute-done((f32[2,3,4,32,256]{4,3,2,1,0:T(8,128)S(1)}, f32[2,3,4,32,256]{4,3,2,1,0:T(8,128)S(1)}, u32[]{:S(2)}, u32[]{:S(2)}) %collective-permute-start) | collective-permute-done | bytes 786464 | tf_op jit(solution)/shard_map/ppermute | solution.py:23
  41.8 0.0 copy-start.2
  41.8 0.0 collective-permute-done.1.head_ref
  41.8 0.9 %copy-done.2 = f32[2,3,4,32,256]{4,3,2,1,0:T(8,128)} copy-done((f32[2,3,4,32,256]{4,3,2,1,0:T(8,128)}, f32[2,3,4,32,256]{4,3,2,1,0:T(8,128)S(1)}, u32[]{:S(2)}) %copy-start.2) | copy-done | bytes 786456
  42.7 8.0 %shard_map.46.rest_0_ = f32[3,24,32,256]{3,2,1,0:T(8,128)} custom-call(f32[3,24,32,256]{3,2,1,0:T(8,128)} %base_ref.3, f32[3,24,32,256]{3,2,1,0:T(8,128)} %adj_ref.3, f32[2,3,4,32,256]{4,3,2,1,0:T(8,128)} %copy-done.2, f32[2,3,4,32,256]{4,3,2,1,0:T(8,128)} %collective-permute-done.1.head_ref), custom_call_target="tpu_custom_call" | custom-call | tf_op jit(solution)/shard_map/pallas_call | solution.py:87
  50.7 7.4 %all-to-all-done = bf16[6,24,32,1,256]{4,1,0,3,2:T(8,128)(2,1)} async-done(((bf16[6,24,32,1,256]{4,1,0,3,2:T(8,128)(2,1)}), bf16[6,24,32,1,256]{4,1,0,3,2:T(8,128)(2,1)}, u32[]{:S(2)}, u32[]{:S(2)}) %all-to-all-start) | async-done | bytes 2359328 | tf_op jit(solution)/shard_map/all_to_all | solution.py:110
  58.1 2.5 %copy.19 = bf16[6,24,4,8,1,256]{5,3,2,1,0,4:T(8,128)(2,1)S(1)} copy(bf16[6,24,4,8,1,256]{5,1,0,3,2,4:T(8,128)(2,1)} %bitcast.5) | data formatting | bytes 4718592 | tf_op jit(solution)/shard_map/all_to_all | solution.py:110
  60.7 0.0 copy-start.3
  60.7 0.2 fusion.12
  60.9 0.1 convert.1
  61.0 1.3 %copy-done.3 = bf16[1024,1024]{1,0:T(8,128)(2,1)S(1)} copy-done((bf16[1024,1024]{1,0:T(8,128)(2,1)S(1)}, bf16[1024,1024]{1,0:T(8,128)(2,1)}, u32[]{:S(2)}) %copy-start.3) | copy-done | bytes 2097176
  62.3 1.4 %fusion.1 = f32[3,24,8,1024]{3,2,1,0:T(8,128)S(1)} fusion(bf16[3,24,8,1024]{3,2,1,0:T(8,128)(2,1)S(1)} %bitcast.53, bf16[1024,1024]{1,0:T(8,128)(2,1)S(1)} %copy-done.3), kind=kOutput, calls=%fused_computation.9 | convolution fusion | flops 1207959552 | bytes 5636096 | tf_op jit(solution)/shard_map/fxzk,ik->fxzi/dot_general | solution.py:118
  63.7 0.0 copy-done
  63.7 1.4 %multiply_reduce_fusion = f32[24,8,1024]{2,1,0:T(8,128)S(1)} fusion(bf16[3,24,8,1024]{3,2,1,0:T(8,128)(2,1)S(1)} %bitcast.54, bf16[3,24,8,1024]{3,2,1,0:T(8,128)(2,1)S(1)} %bitcast.58, bf16[1024,1024]{1,0:T(8,128)(2,1)S(1)} %copy-done), kind=kOutput, calls=%fused_computation.7 | convolution fusion | flops 1209532416 | bytes 5242880 | tf_op jit(solution)/shard_map/fxzk,ik->fxzi/dot_general | solution.py:116
  65.1 1.5 %multiply_add_fusion = f32[3,24,8,1024]{3,2,1,0:T(8,128)S(1)} fusion(f32[3,24,8,1024]{3,2,1,0:T(8,128)S(1)} %fusion.1, bf16[3,24,8,1024]{3,2,1,0:T(8,128)(2,1)S(1)} %bitcast.55, bf16[1024,1024]{1,0:T(8,128)(2,1)S(1)} %copy-done, f32[24,8,1024]{2,1,0:T(8,128)S(1)} %convert.1), kind=kOutput, calls=%fused_computation.8 | convolution fusion | flops 1209729024 | bytes 8781824 | tf_op jit(solution)/shard_map/fxzk,ik->fxzi/dot_general | solution.py:117
  66.6 0.2 fusion.11
  66.9 0.2 convert_element_type.33
  67.0 1.1 %copy.9 = bf16[3,24,8,4,256]{4,2,1,0,3:T(8,128)(2,1)} copy(bf16[3,24,8,4,256]{4,2,3,1,0:T(8,128)(2,1)S(1)} %bitcast.56) | data formatting | bytes 2359296 | tf_op jit(solution)/shard_map/optimization_barrier | solution.py:124
  68.2 4.5 %all-to-all-start.1 = ((bf16[3,24,8,4,256]{4,2,1,0,3:T(8,128)(2,1)}), bf16[3,24,8,4,256]{4,2,1,0,3:T(8,128)(2,1)S(1)}, u32[]{:S(2)}, u32[]{:S(2)}) async-start(bf16[3,24,8,4,256]{4,2,1,0,3:T(8,128)(2,1)} %copy.9), calls=%async_computation.1 | async-start | bytes 2359296 | tf_op jit(solution)/shard_map/all_to_all | solution.py:125
  72.7 8.0 %shard_map.47 = f32[3,24,32,256]{3,2,1,0:T(8,128)} custom-call(f32[3,24,32,256]{3,2,1,0:T(8,128)} %base_ref.3, f32[3,24,32,256]{3,2,1,0:T(8,128)} %adj_ref.3, f32[2,3,4,32,256]{4,3,2,1,0:T(8,128)} %copy-done.2, f32[2,3,4,32,256]{4,3,2,1,0:T(8,128)} %collective-permute-done.1.head_ref, ...), custom_call_target="tpu_custom_call", output_to_operand_aliasing={{}: (4, {})} | custom-call | tf_op jit(solution)/shard_map/pallas_call | solution.py:87
  80.6 6.9 %all-to-all-done.1 = bf16[3,24,8,4,256]{4,2,1,0,3:T(8,128)(2,1)S(1)} async-done(((bf16[3,24,8,4,256]{4,2,1,0,3:T(8,128)(2,1)}), bf16[3,24,8,4,256]{4,2,1,0,3:T(8,128)(2,1)S(1)}, u32[]{:S(2)}, u32[]{:S(2)}) %all-to-all-start.1) | async-done | bytes 1179680 | tf_op jit(solution)/shard_map/all_to_all | solution.py:125
  87.5 3.6 %fusion = f32[3,24,32,256]{3,2,1,0:T(8,128)} fusion(f32[3,24,32,256]{3,2,1,0:T(8,128)} %shard_map.47, pred[256]{0:T(512)(128)(4,1)S(1)} %compare_and_fusion, bf16[3,24,8,4,256]{4,2,1,0,3:T(8,128)(2,1)S(1)} %all-to-all-done.1), kind=kLoop, calls=%fused_computation.2 | loop fusion | flops 2359296 | bytes 5898496 | tf_op jit(solution)/shard_map/jit(_where)/select_n | solution.py:133
  (2 shorter events, 0.0 us)
Async XLA Ops:
  0.0 63.7 %copy-start = (bf16[1024,1024]{1,0:T(8,128)(2,1)S(1)}, bf16[1024,1024]{1,0:T(8,128)(2,1)}, u32[]{:S(2)}) copy-start(bf16[1024,1024]{1,0:T(8,128)(2,1)} %param.8) | copy-start | bytes 6291460
  0.0 3.1 %copy-start.1 = (f32[3,24,32,256]{3,2,1,0:T(8,128)S(1)}, f32[3,24,32,256]{3,2,1,0:T(8,128)}, u32[]{:S(2)}) copy-start(f32[3,24,32,256]{3,2,1,0:T(8,128)} %adj_ref.3) | copy-start | bytes 7077892
  6.0 52.1 %all-to-all-start = ((bf16[6,24,32,1,256]{4,1,0,3,2:T(8,128)(2,1)}), bf16[6,24,32,1,256]{4,1,0,3,2:T(8,128)(2,1)}, u32[]{:S(2)}, u32[]{:S(2)}) async-start(bf16[6,24,32,1,256]{4,1,0,3,2:T(8,128)(2,1)} %maximum_bitcast_fusion), calls=%async_computation | async-start | bytes 4718592 | tf_op jit(solution)/shard_map/all_to_all | solution.py:110
  15.2 26.6 %collective-permute-start = (f32[2,3,4,32,256]{4,3,2,1,0:T(8,128)S(1)}, f32[2,3,4,32,256]{4,3,2,1,0:T(8,128)S(1)}, u32[]{:S(2)}, u32[]{:S(2)}) collective-permute-start(f32[2,3,4,32,256]{4,3,2,1,0:T(8,128)S(1)} %pad_maximum_fusion), channel_id=1, source_target_pairs={{0,4},{4,8},{8,12},{12,16},{16,20},{20,24},{24,28},{28,32},{32,36}... | collective-permute-start | bytes 2359304 | tf_op jit(solution)/shard_map/ppermute | solution.py:23
  15.3 26.5 %collective-permute-start.1 = (f32[2,3,4,32,256]{4,3,2,1,0:T(8,128)S(1)}, f32[2,3,4,32,256]{4,3,2,1,0:T(8,128)}, u32[]{:S(2)}, u32[]{:S(2)}) collective-permute-start(f32[2,3,4,32,256]{4,3,2,1,0:T(8,128)S(1)} %pad_maximum_fusion.1), channel_id=1, source_target_pairs={{4,0},{8,4},{12,8},{16,12},{20,16},{24,20},{28,24},{32,28},{36,32}... | collective-permute-start | bytes 2359304 | tf_op jit(solution)/shard_map/ppermute | solution.py:23
  41.8 0.9 %copy-start.2 = (f32[2,3,4,32,256]{4,3,2,1,0:T(8,128)}, f32[2,3,4,32,256]{4,3,2,1,0:T(8,128)S(1)}, u32[]{:S(2)}) copy-start(f32[2,3,4,32,256]{4,3,2,1,0:T(8,128)S(1)} %collective-permute-done.tail_ref) | copy-start | bytes 2359300
  60.7 1.6 %copy-start.3 = (bf16[1024,1024]{1,0:T(8,128)(2,1)S(1)}, bf16[1024,1024]{1,0:T(8,128)(2,1)}, u32[]{:S(2)}) copy-start(bf16[1024,1024]{1,0:T(8,128)(2,1)} %param.9) | copy-start | bytes 6291460
  68.2 19.3 %all-to-all-start.1 = ((bf16[3,24,8,4,256]{4,2,1,0,3:T(8,128)(2,1)}), bf16[3,24,8,4,256]{4,2,1,0,3:T(8,128)(2,1)S(1)}, u32[]{:S(2)}, u32[]{:S(2)}) async-start(bf16[3,24,8,4,256]{4,2,1,0,3:T(8,128)(2,1)} %copy.9), calls=%async_computation.1 | async-start | bytes 2359296 | tf_op jit(solution)/shard_map/all_to_all | solution.py:125

commit v5 on v3

v5 whole, which is shorter than its diff:
```python
import jax
import jax.numpy as jnp
from jax import lax
from jax.experimental import pallas as pl
from jax.experimental.pallas import tpu as pltpu
from jax.sharding import PartitionSpec as P

C_FIRST = (0.8, -0.2, 4.0 / 105.0, -1.0 / 280.0)
C_SECOND = (1.6, -0.2, 8.0 / 315.0, -1.0 / 560.0)
C_CENTER = -205.0 / 72.0
VISCOSITY = 0.1
STEP_WEIGHT = 0.5
HALO = 4
LANES = 128


def ring_shift(value, axis, forward):
    count = lax.axis_size(axis)
    if forward:
        pairs = [(i, (i + 1) % count) for i in range(count)]
    else:
        pairs = [((i + 1) % count, i) for i in range(count)]
    return lax.ppermute(value, axis, pairs)


def cell_update(load, x, write):
    span = load(0, 0, x).shape[0]

    def zshift(v, k):
        return pltpu.roll(v, (span - k) % span, 0)

    def derivs(field, c, second):
        center = load(field, c, x)
        plus = [load(field, c, x + k) for k in range(1, 5)]
        minus = [load(field, c, x - k) for k in range(1, 5)]
        zp = [zshift(center, k) for k in range(1, 5)]
        zm = [zshift(center, span - k) for k in range(1, 5)]
        dx = C_FIRST[0] * (plus[0] - minus[0])
        dz = C_FIRST[0] * (zp[0] - zm[0])
        for k in range(1, 4):
            dx = dx + C_FIRST[k] * (plus[k] - minus[k])
            dz = dz + C_FIRST[k] * (zp[k] - zm[k])
        if not second:
            return center, dx, dz, None, None
        dxx = C_CENTER * center
        dzz = C_CENTER * center
        for k in range(4):
            dxx = dxx + C_SECOND[k] * (plus[k] + minus[k])
            dzz = dzz + C_SECOND[k] * (zp[k] + zm[k])
        return center, dx, dz, dxx, dzz

    base = [derivs(0, j, False) for j in range(3)]
    adj = [derivs(1, c, True) for c in range(3)]
    first_coupling = adj[0][0] * base[0][1] + adj[1][0] * base[1][1] + adj[2][0] * base[2][1]
    last_coupling = adj[0][0] * base[0][2] + adj[1][0] * base[1][2] + adj[2][0] * base[2][2]
    for c in range(3):
        center, dx, dz, dxx, dzz = adj[c]
        tendency = base[0][0] * dx + base[2][0] * dz + VISCOSITY * (dxx + dzz)
        if c == 0:
            tendency = tendency - first_coupling
        elif c == 2:
            tendency = tendency - last_coupling
        write(c, center + STEP_WEIGHT * tendency)


def interior_kernel(base_ref, adj_ref, out_ref):
    first = (pl.program_id(1) + 1) * HALO

    def load(field, c, x):
        return (base_ref if field == 0 else adj_ref)[c, x]

    def step(i, carry):
        def write(c, value):
            out_ref[c, i] = value

        cell_update(load, first + i, write)
        return carry

    lax.fori_loop(0, HALO, step, 0)


def interior_update(base_flow, adjoint):
    comps, cells, span, rows = base_flow.shape
    field_spec = pl.BlockSpec((comps, cells, span, LANES), lambda j, b: (0, 0, 0, j))
    out_spec = pl.BlockSpec((comps, HALO, span, LANES), lambda j, b: (0, b + 1, 0, j))
    return pl.pallas_call(
        interior_kernel,
        grid=(rows // LANES, cells // HALO - 2),
        in_specs=[field_spec, field_spec],
        out_specs=out_spec,
        out_shape=jax.ShapeDtypeStruct(base_flow.shape, jnp.float32),
    )(base_flow, adjoint)


def boundary_kernel(base_ref, adj_ref, tail_ref, head_ref, prev_ref, out_ref, ext_ref):
    comps, cells, span, rows = base_ref.shape
    side = pl.program_id(0)

    @pl.when(side == 0)
    def _():
        ext_ref[0, :, HALO : HALO + cells] = base_ref[...]
        ext_ref[1, :, HALO : HALO + cells] = adj_ref[...]
        ext_ref[:, :, :HALO] = tail_ref[...]
        ext_ref[:, :, HALO + cells :] = head_ref[...]

    first = side * (cells - HALO)
    for lane in range(rows // LANES):
        lanes = pl.ds(lane * LANES, LANES)

        def load(field, c, x, lanes=lanes):
            return ext_ref[field, c, x + HALO, :, lanes]

        def step(i, carry, lanes=lanes, load=load):
            def write(c, value):
                out_ref[c, i, :, lanes] = value

            cell_update(load, first + i, write)
            return carry

        lax.fori_loop(0, HALO, step, 0)


def boundary_update(base_flow, adjoint, tails, heads, previous):
    comps, cells, span, rows = base_flow.shape
    full_spec = pl.BlockSpec((comps, cells, span, rows), lambda s: (0, 0, 0, 0))
    halo_spec = pl.BlockSpec((2, comps, HALO, span, rows), lambda s: (0, 0, 0, 0, 0))
    out_spec = pl.BlockSpec((comps, HALO, span, rows), lambda s: (0, s * (cells // HALO - 1), 0, 0))
    return pl.pallas_call(
        boundary_kernel,
        grid=(2,),
        in_specs=[full_spec, full_spec, halo_spec, halo_spec, pl.BlockSpec(memory_space=pl.ANY)],
        out_specs=out_spec,
        out_shape=jax.ShapeDtypeStruct(base_flow.shape, jnp.float32),
        scratch_shapes=[pltpu.VMEM((2, comps, cells + 2 * HALO, span, rows), jnp.float32)],
        input_output_aliases={4: 0},
    )(base_flow, adjoint, tails, heads, previous)


def body(base_flow, adjoint, first_op, second_op):
    comps, cells, spanwise, local_rows = base_flow.shape
    groups = lax.axis_size("gy")
    total_rows = local_rows * groups
    part = spanwise // groups

    base_low = lax.optimization_barrier(base_flow.astype(jnp.bfloat16))
    adjoint_low = lax.optimization_barrier(adjoint.astype(jnp.bfloat16))
    low = jnp.concatenate((base_low, adjoint_low), 0).reshape(2 * comps, cells, spanwise, 1, local_rows)
    lines = lax.all_to_all(low, "gy", split_axis=2, concat_axis=3, tiled=True)
    partial = interior_update(base_flow, adjoint)
    tail_cells = jnp.stack((base_flow[:, cells - HALO :], adjoint[:, cells - HALO :]), 0)
    head_cells = jnp.stack((base_flow[:, :HALO], adjoint[:, :HALO]), 0)
    lines, partial, tail_cells, head_cells = lax.optimization_barrier((lines, partial, tail_cells, head_cells))
    tails = ring_shift(tail_cells, "gx", True)
    heads = ring_shift(head_cells, "gx", False)
    lines = lines.reshape(2 * comps, cells, part, total_rows)
    base_lines = lines[:comps]
    adj_lines = lines[comps:]
    slope_base = jnp.einsum("fxzk,ik->fxzi", base_lines, first_op, preferred_element_type=jnp.float32)
    slope_adj = jnp.einsum("fxzk,ik->fxzi", adj_lines, first_op, preferred_element_type=jnp.float32)
    curves = jnp.einsum("fxzk,ik->fxzi", adj_lines, second_op, preferred_element_type=jnp.float32)
    normal_vel = base_lines[1].astype(jnp.float32)
    coupling = jnp.sum(adj_lines.astype(jnp.float32) * slope_base, axis=0)
    wall_part = normal_vel[None] * slope_adj + VISCOSITY * curves
    wall_part = wall_part.at[1].add(-coupling)
    wall_part = wall_part.astype(jnp.bfloat16).reshape(comps, cells, part, groups, local_rows)
    wall_part, partial = lax.optimization_barrier((wall_part, partial))
    wall_part = lax.all_to_all(wall_part, "gy", split_axis=3, concat_axis=2, tiled=True)
    wall_part = wall_part.reshape(comps, cells, spanwise, local_rows).astype(jnp.float32)

    partial = boundary_update(base_flow, adjoint, tails, heads, partial)
    updated = partial + STEP_WEIGHT * wall_part
    wall_index = lax.axis_index("gy") * local_rows + jnp.arange(local_rows, dtype=jnp.int32)
    interior = (wall_index > 0) & (wall_index < total_rows - 1)
    return jnp.where(interior, updated, jnp.float32(0.0))


def solution(mesh):
    return jax.shard_map(
        body,
        mesh=mesh,
        in_specs=(P(None, "gx", None, "gy"), P(None, "gx", None, "gy"), P(), P()),
        out_specs=P(None, "gx", None, "gy"),
        check_vma=False,
    )
```

time: 119 us -> 93.9 us (0.79)
  waiting for transfers between devices: 59.3 us -> 32.1 us
  Pallas kernels: 13.2 us -> 17.2 us
  other arithmetic: 8.74 us -> 7.02 us
    ppermute x2, waiting for transfers between devices: 43.7 us -> 18.1 us  [ring_shift(): return lax.ppermute(value, axis, pairs)]
    pallas_call x1 -> x2, Pallas kernels: 13.2 us -> 17.2 us  [the longest x1 9.97 us: interior_update(): pl.pallas_call(interior_kernel, grid=(rows // LANES, cells // HALO - 2),...]
    all_to_all x1, waiting for transfers between devices: 15.6 us -> 14 us  [body(): lines = lax.all_to_all(low, 'gy', split_axis=2, concat_axis=3, tiled=True)]
    another operation x1 -> x2, local copies, waits for them, and re-layouts: 2.41 us -> 2.34 us  [body(): head_cells = jnp.stack((base_flow[:, :HALO], adjoint[:, :HALO]), 0)]
  transfers between devices with their start and end apart: 4 -> 4, of which waited for: 2 -> 2; matrix products, arithmetic and copies ran while one was open for 12% -> 4% of each run, Pallas kernels for 11% -> 18%
where the time goes in v5:
time: 93.9 us; the launch traced here: 93.5 us
  waiting for transfers between devices  32.1 us (34%)
  starting transfers between devices  20.8 us (22%)
  Pallas kernels  17.2 us (18%)
  local copies, waits for them, and re-layouts  11.9 us (13%)
  other arithmetic  7.02 us (7%)
  matrix products  4.31 us (5%)
    ppermute x2, waiting for transfers between devices, ring_shift(): return lax.ppermute(value, axis, pairs)  18.1 us
    all_to_all x1, waiting for transfers between devices, body(): lines = lax.all_to_all(low, 'gy', split_axis=2, concat_axis=3, tiled=True)  14 us
    pallas_call x1, Pallas kernels, interior_update(): pl.pallas_call(interior_kernel, grid=(rows // LANES, cells // HALO - 2),...  9.97 us
    ppermute x2, starting transfers between devices, ring_shift(): return lax.ppermute(value, axis, pairs)  8.7 us
    all_to_all x1, starting transfers between devices, body(): lines = lax.all_to_all(low, 'gy', split_axis=2, concat_axis=3, tiled=True)  7.65 us
    pallas_call x1, Pallas kernels, boundary_update(): pl.pallas_call(boundary_kernel, grid=(2,), in_specs=[full_spec, full_spec...  7.25 us
    unnamed x8, local copies, waits for them, and re-layouts  5.63 us
    all_to_all x1, starting transfers between devices, body(): lax.all_to_all(wall_part, 'gy', split_axis=3, concat_axis=2, tiled=True)  4.47 us
  transfers between devices with their start and end apart: 4, of which 2 were waited for; matrix products, arithmetic and copies ran while one was open for 4% of the time, Pallas kernels for 18%

profile of v5, /device:TPU:1, one launch (start us, length us, event | category | flops | bytes accessed | tf_op | source)
XLA Modules:
  0.0 93.5 jit_solution(7005387011680669420)
XLA Ops:
  0.0 0.0 copy-start
  0.0 0.0 copy-start.1
  0.0 3.1 %copy.18 = bf16[3,24,32,256]{3,1,0,2:T(8,128)(2,1)S(1)} copy(f32[3,24,32,256]{3,2,1,0:T(8,128)} %base_ref.3) | data formatting | bytes 3538944 | tf_op args[0]
  3.1 0.0 copy-done.1
  3.1 1.3 %copy.17 = bf16[3,24,32,256]{3,1,0,2:T(8,128)(2,1)S(1)} copy(f32[3,24,32,256]{3,2,1,0:T(8,128)S(1)} %copy-done.1) | data formatting | bytes 3538944 | tf_op args[1]
  4.4 1.6 %maximum_bitcast_fusion = bf16[6,24,32,1,256]{4,1,0,3,2:T(8,128)(2,1)} fusion(bf16[3,24,32,256]{3,1,0,2:T(8,128)(2,1)S(1)} %copy.17, bf16[3,24,32,256]{3,1,0,2:T(8,128)(2,1)S(1)} %copy.18), kind=kLoop, calls=%fused_computation | loop fusion | flops 1179648 | bytes 4718592 | tf_op jit(solution)/shard_map/reshape | solution.py:147
  6.0 7.6 %all-to-all-start = ((bf16[6,24,32,1,256]{4,1,0,3,2:T(8,128)(2,1)}), bf16[6,24,32,1,256]{4,1,0,3,2:T(8,128)(2,1)}, u32[]{:S(2)}, u32[]{:S(2)}) async-start(bf16[6,24,32,1,256]{4,1,0,3,2:T(8,128)(2,1)} %maximum_bitcast_fusion), calls=%async_computation | async-start | bytes 4718592 | tf_op jit(solution)/shard_map/all_to_all | solution.py:148
  13.6 10.0 %shard_map.46.prev_ref = f32[3,24,32,256]{3,2,1,0:T(8,128)} custom-call(f32[3,24,32,256]{3,2,1,0:T(8,128)} %base_ref.3, f32[3,24,32,256]{3,2,1,0:T(8,128)} %adj_ref.3), custom_call_target="tpu_custom_call" | custom-call | tf_op jit(solution)/shard_map/pallas_call | solution.py:86
  23.6 1.2 %slice_bitcast_fusion.1 = (f32[1,3,4,32,256]{4,3,2,1,0:T(8,128)S(1)}, f32[1,3,4,32,256]{4,3,2,1,0:T(8,128)S(1)}) fusion(f32[3,24,32,256]{3,2,1,0:T(8,128)} %base_ref.3), kind=kLoop, calls=%fused_computation.20 | loop fusion | bytes 1572864 | tf_op jit(solution)/shard_map/stack | solution.py:151
  24.8 1.2 %slice_bitcast_fusion = (f32[1,3,4,32,256]{4,3,2,1,0:T(8,128)S(1)}, f32[1,3,4,32,256]{4,3,2,1,0:T(8,128)S(1)}) fusion(f32[3,24,32,256]{3,2,1,0:T(8,128)} %adj_ref.3), kind=kLoop, calls=%fused_computation.19 | loop fusion | bytes 1572864 | tf_op jit(solution)/shard_map/stack | solution.py:151
  26.0 1.3 %pad_maximum_fusion = (f32[2,3,4,32,256]{4,3,2,1,0:T(8,128)}, f32[2,3,4,32,256]{4,3,2,1,0:T(8,128)}) fusion(f32[1,3,4,32,256]{4,3,2,1,0:T(8,128)S(1)} %get-tuple-element.34, f32[1,3,4,32,256]{4,3,2,1,0:T(8,128)S(1)} %get-tuple-element.32, f32[1,3,4,32,256]{4,3,2,1,0:T(8,128)S(1)} %get-tuple-element.33, f32[1,3,4,32,256]{4,3,2,1,0:T(8,128)S(1)} %get-tuple-element.31), kind=kLoop, calls=%fused_computation.17 | loop fusion | flops 393216 | bytes 3145728 | tf_op jit(solution)/shard_map/stack | solution.py:150
  27.2 14.0 %all-to-all-done = bf16[6,24,32,1,256]{4,1,0,3,2:T(8,128)(2,1)} async-done(((bf16[6,24,32,1,256]{4,1,0,3,2:T(8,128)(2,1)}), bf16[6,24,32,1,256]{4,1,0,3,2:T(8,128)(2,1)}, u32[]{:S(2)}, u32[]{:S(2)}) %all-to-all-start) | async-done | bytes 2359328 | tf_op jit(solution)/shard_map/all_to_all | solution.py:148
  41.2 2.5 %copy.19 = bf16[6,24,4,8,1,256]{5,3,2,1,0,4:T(8,128)(2,1)S(1)} copy(bf16[6,24,4,8,1,256]{5,1,0,3,2,4:T(8,128)(2,1)} %bitcast.1) | data formatting | bytes 4718592 | tf_op jit(solution)/shard_map/all_to_all | solution.py:148
  43.8 0.0 copy-start.2
  43.8 0.2 fusion.12
  44.0 0.1 convert.1
  44.1 1.3 %copy-done.2 = bf16[1024,1024]{1,0:T(8,128)(2,1)S(1)} copy-done((bf16[1024,1024]{1,0:T(8,128)(2,1)S(1)}, bf16[1024,1024]{1,0:T(8,128)(2,1)}, u32[]{:S(2)}) %copy-start.2) | copy-done | bytes 2097176
  45.4 1.4 %fusion.1 = f32[3,24,8,1024]{3,2,1,0:T(8,128)S(1)} fusion(bf16[3,24,8,1024]{3,2,1,0:T(8,128)(2,1)S(1)} %bitcast.53, bf16[1024,1024]{1,0:T(8,128)(2,1)S(1)} %copy-done.2), kind=kOutput, calls=%fused_computation.9 | convolution fusion | flops 1207959552 | bytes 5636096 | tf_op jit(solution)/shard_map/fxzk,ik->fxzi/dot_general | solution.py:160
  46.8 0.0 copy-done
  46.8 1.4 %multiply_reduce_fusion = f32[24,8,1024]{2,1,0:T(8,128)S(1)} fusion(bf16[3,24,8,1024]{3,2,1,0:T(8,128)(2,1)S(1)} %bitcast.54, bf16[3,24,8,1024]{3,2,1,0:T(8,128)(2,1)S(1)} %bitcast.58, bf16[1024,1024]{1,0:T(8,128)(2,1)S(1)} %copy-done), kind=kOutput, calls=%fused_computation.7 | convolution fusion | flops 1209532416 | bytes 5242880 | tf_op jit(solution)/shard_map/fxzk,ik->fxzi/dot_general | solution.py:158
  48.3 1.5 %multiply_add_fusion = f32[3,24,8,1024]{3,2,1,0:T(8,128)S(1)} fusion(f32[3,24,8,1024]{3,2,1,0:T(8,128)S(1)} %fusion.1, bf16[3,24,8,1024]{3,2,1,0:T(8,128)(2,1)S(1)} %bitcast.55, bf16[1024,1024]{1,0:T(8,128)(2,1)S(1)} %copy-done, f32[24,8,1024]{2,1,0:T(8,128)S(1)} %convert.1), kind=kOutput, calls=%fused_computation.8 | convolution fusion | flops 1209729024 | bytes 8781824 | tf_op jit(solution)/shard_map/fxzk,ik->fxzi/dot_general | solution.py:159
  49.7 0.2 fusion.11
  50.0 0.2 convert_element_type.33
  50.2 1.1 %copy.9 = bf16[3,24,8,4,256]{4,2,1,0,3:T(8,128)(2,1)} copy(bf16[3,24,8,4,256]{4,2,3,1,0:T(8,128)(2,1)S(1)} %bitcast.56) | data formatting | bytes 2359296 | tf_op jit(solution)/shard_map/optimization_barrier | solution.py:166
  51.3 4.5 %all-to-all-start.1 = ((bf16[3,24,8,4,256]{4,2,1,0,3:T(8,128)(2,1)}), bf16[3,24,8,4,256]{4,2,1,0,3:T(8,128)(2,1)S(1)}, u32[]{:S(2)}, u32[]{:S(2)}) async-start(bf16[3,24,8,4,256]{4,2,1,0,3:T(8,128)(2,1)} %copy.9), calls=%async_computation.1 | async-start | bytes 2359296 | tf_op jit(solution)/shard_map/all_to_all | solution.py:167
  55.8 0.0 collective-permute-start
  55.8 8.7 %collective-permute-start.1 = (f32[2,3,4,32,256]{4,3,2,1,0:T(8,128)}, f32[2,3,4,32,256]{4,3,2,1,0:T(8,128)}, u32[]{:S(2)}, u32[]{:S(2)}) collective-permute-start(f32[2,3,4,32,256]{4,3,2,1,0:T(8,128)} %get-tuple-element.24), channel_id=1, source_target_pairs={{4,0},{8,4},{12,8},{16,12},{20,16},{24,20},{28,24},{32,28},{36,32}... | collective-permute-start | bytes 2359304 | tf_op jit(solution)/shard_map/ppermute | solution.py:23
  64.5 18.1 %collective-permute-done.tail_ref = f32[2,3,4,32,256]{4,3,2,1,0:T(8,128)} collective-permute-done((f32[2,3,4,32,256]{4,3,2,1,0:T(8,128)}, f32[2,3,4,32,256]{4,3,2,1,0:T(8,128)}, u32[]{:S(2)}, u32[]{:S(2)}) %collective-permute-start) | collective-permute-done | bytes 786464 | tf_op jit(solution)/shard_map/ppermute | solution.py:23
  82.6 0.0 collective-permute-done.1.head_ref
  82.6 7.3 %shard_map.47 = f32[3,24,32,256]{3,2,1,0:T(8,128)} custom-call(f32[3,24,32,256]{3,2,1,0:T(8,128)} %base_ref.3, f32[3,24,32,256]{3,2,1,0:T(8,128)} %adj_ref.3, f32[2,3,4,32,256]{4,3,2,1,0:T(8,128)} %collective-permute-done.tail_ref, f32[2,3,4,32,256]{4,3,2,1,0:T(8,128)} %collective-permute-done.1.head_ref, ...), custom_call_target="tpu_custom_call", output_to_operand_aliasing={{}: (4, {})} | custom-call | tf_op jit(solution)/shard_map/pallas_call | solution.py:128
  89.8 0.0 all-to-all-done.1
  89.8 3.6 %fusion = f32[3,24,32,256]{3,2,1,0:T(8,128)} fusion(f32[3,24,32,256]{3,2,1,0:T(8,128)} %shard_map.47, pred[256]{0:T(512)(128)(4,1)S(1)} %compare_and_fusion, bf16[3,24,8,4,256]{4,2,1,0,3:T(8,128)(2,1)S(1)} %all-to-all-done.1), kind=kLoop, calls=%fused_computation.2 | loop fusion | flops 2359296 | bytes 5898496 | tf_op jit(solution)/shard_map/jit(_where)/select_n | solution.py:174
  (2 shorter events, 0.0 us)
Async XLA Ops:
  0.0 46.8 %copy-start = (bf16[1024,1024]{1,0:T(8,128)(2,1)S(1)}, bf16[1024,1024]{1,0:T(8,128)(2,1)}, u32[]{:S(2)}) copy-start(bf16[1024,1024]{1,0:T(8,128)(2,1)} %param.8) | copy-start | bytes 6291460
  0.0 3.1 %copy-start.1 = (f32[3,24,32,256]{3,2,1,0:T(8,128)S(1)}, f32[3,24,32,256]{3,2,1,0:T(8,128)}, u32[]{:S(2)}) copy-start(f32[3,24,32,256]{3,2,1,0:T(8,128)} %adj_ref.3) | copy-start | bytes 7077892
  6.0 35.3 %all-to-all-start = ((bf16[6,24,32,1,256]{4,1,0,3,2:T(8,128)(2,1)}), bf16[6,24,32,1,256]{4,1,0,3,2:T(8,128)(2,1)}, u32[]{:S(2)}, u32[]{:S(2)}) async-start(bf16[6,24,32,1,256]{4,1,0,3,2:T(8,128)(2,1)} %maximum_bitcast_fusion), calls=%async_computation | async-start | bytes 4718592 | tf_op jit(solution)/shard_map/all_to_all | solution.py:148
  43.8 1.6 %copy-start.2 = (bf16[1024,1024]{1,0:T(8,128)(2,1)S(1)}, bf16[1024,1024]{1,0:T(8,128)(2,1)}, u32[]{:S(2)}) copy-start(bf16[1024,1024]{1,0:T(8,128)(2,1)} %param.9) | copy-start | bytes 6291460
  51.3 38.5 %all-to-all-start.1 = ((bf16[3,24,8,4,256]{4,2,1,0,3:T(8,128)(2,1)}), bf16[3,24,8,4,256]{4,2,1,0,3:T(8,128)(2,1)S(1)}, u32[]{:S(2)}, u32[]{:S(2)}) async-start(bf16[3,24,8,4,256]{4,2,1,0,3:T(8,128)(2,1)} %copy.9), calls=%async_computation.1 | async-start | bytes 2359296 | tf_op jit(solution)/shard_map/all_to_all | solution.py:167
  55.8 26.8 %collective-permute-start = (f32[2,3,4,32,256]{4,3,2,1,0:T(8,128)}, f32[2,3,4,32,256]{4,3,2,1,0:T(8,128)}, u32[]{:S(2)}, u32[]{:S(2)}) collective-permute-start(f32[2,3,4,32,256]{4,3,2,1,0:T(8,128)} %get-tuple-element.23), channel_id=1, source_target_pairs={{0,4},{4,8},{8,12},{12,16},{16,20},{20,24},{24,28},{28,32},{32,36}... | collective-permute-start | bytes 2359304 | tf_op jit(solution)/shard_map/ppermute | solution.py:23
  55.8 26.8 %collective-permute-start.1 = (f32[2,3,4,32,256]{4,3,2,1,0:T(8,128)}, f32[2,3,4,32,256]{4,3,2,1,0:T(8,128)}, u32[]{:S(2)}, u32[]{:S(2)}) collective-permute-start(f32[2,3,4,32,256]{4,3,2,1,0:T(8,128)} %get-tuple-element.24), channel_id=1, source_target_pairs={{4,0},{8,4},{12,8},{16,12},{20,16},{24,20},{28,24},{32,28},{36,32}... | collective-permute-start | bytes 2359304 | tf_op jit(solution)/shard_map/ppermute | solution.py:23

commit v6 on v5

--- a/solution.py
+++ b/solution.py
@@ -142,30 +142,36 @@
     total_rows = local_rows * groups
     part = spanwise // groups
 
-    base_low = lax.optimization_barrier(base_flow.astype(jnp.bfloat16))
-    adjoint_low = lax.optimization_barrier(adjoint.astype(jnp.bfloat16))
-    low = jnp.concatenate((base_low, adjoint_low), 0).reshape(2 * comps, cells, spanwise, 1, local_rows)
-    lines = lax.all_to_all(low, "gy", split_axis=2, concat_axis=3, tiled=True)
+    base_low = base_flow.astype(jnp.bfloat16)
+    adjoint_low = adjoint.astype(jnp.bfloat16)
+    span_cells = cells // groups
+    low = jnp.concatenate((base_low, adjoint_low), 0).reshape(2 * comps, groups, span_cells, spanwise, local_rows)
+    low = jnp.transpose(low, (1, 0, 2, 3, 4))
+    lines = lax.all_to_all(low, "gy", split_axis=0, concat_axis=0, tiled=True)
     partial = interior_update(base_flow, adjoint)
     tail_cells = jnp.stack((base_flow[:, cells - HALO :], adjoint[:, cells - HALO :]), 0)
     head_cells = jnp.stack((base_flow[:, :HALO], adjoint[:, :HALO]), 0)
     lines, partial, tail_cells, head_cells = lax.optimization_barrier((lines, partial, tail_cells, head_cells))
     tails = ring_shift(tail_cells, "gx", True)
     heads = ring_shift(head_cells, "gx", False)
-    lines = lines.reshape(2 * comps, cells, part, total_rows)
-    base_lines = lines[:comps]
-    adj_lines = lines[comps:]
-    slope_base = jnp.einsum("fxzk,ik->fxzi", base_lines, first_op, preferred_element_type=jnp.float32)
-    slope_adj = jnp.einsum("fxzk,ik->fxzi", adj_lines, first_op, preferred_element_type=jnp.float32)
-    curves = jnp.einsum("fxzk,ik->fxzi", adj_lines, second_op, preferred_element_type=jnp.float32)
-    normal_vel = base_lines[1].astype(jnp.float32)
-    coupling = jnp.sum(adj_lines.astype(jnp.float32) * slope_base, axis=0)
+    first_blocks = first_op.reshape(total_rows, groups, local_rows)
+    second_blocks = second_op.reshape(total_rows, groups, local_rows)
+    base_lines = lines[:, :comps]
+    adj_lines = lines[:, comps:]
+    slope_base = jnp.einsum("qfxzr,iqr->fxzi", base_lines, first_blocks, preferred_element_type=jnp.float32)
+    slope_adj = jnp.einsum("qfxzr,iqr->fxzi", adj_lines, first_blocks, preferred_element_type=jnp.float32)
+    curves = jnp.einsum("qfxzr,iqr->fxzi", adj_lines, second_blocks, preferred_element_type=jnp.float32)
+    def to_lines(value):
+        return jnp.transpose(value, (1, 2, 3, 0, 4)).reshape(value.shape[1], span_cells, spanwise, total_rows)
+    normal_vel = to_lines(base_lines[:, 1:2])[0].astype(jnp.float32)
+    coupling = jnp.sum(to_lines(adj_lines).astype(jnp.float32) * slope_base, axis=0)
     wall_part = normal_vel[None] * slope_adj + VISCOSITY * curves
     wall_part = wall_part.at[1].add(-coupling)
-    wall_part = wall_part.astype(jnp.bfloat16).reshape(comps, cells, part, groups, local_rows)
+    wall_part = wall_part.astype(jnp.bfloat16).reshape(comps, span_cells, spanwise, groups, local_rows)
+    wall_part = jnp.transpose(wall_part, (3, 0, 1, 2, 4))
     wall_part, partial = lax.optimization_barrier((wall_part, partial))
-    wall_part = lax.all_to_all(wall_part, "gy", split_axis=3, concat_axis=2, tiled=True)
-    wall_part = wall_part.reshape(comps, cells, spanwise, local_rows).astype(jnp.float32)
+    wall_part = lax.all_to_all(wall_part, "gy", split_axis=0, concat_axis=0, tiled=True)
+    wall_part = jnp.transpose(wall_part, (1, 0, 2, 3, 4)).reshape(comps, cells, spanwise, local_rows).astype(jnp.float32)
 
     partial = boundary_update(base_flow, adjoint, tails, heads, partial)
     updated = partial + STEP_WEIGHT * wall_part

time: 93.9 us -> 97.6 us (1.039)
  local copies, waits for them, and re-layouts: 11.9 us -> 23 us
  waiting for transfers between devices: 32.1 us -> 22.6 us
  matrix products: 4.31 us -> 5.88 us
  other arithmetic: 7.02 us -> 8.08 us
    reshape x0 -> x3, local copies, waits for them, and re-layouts: none -> 10.2 us  [the longest x1 4.53 us: body(): second_blocks = second_op.reshape(total_rows, groups, local_rows)]
    all_to_all x2, waiting for transfers between devices: 14 us -> 4.86 us  [the longest x1 4.86 us: body(): lines = lax.all_to_all(low, 'gy', split_axis=0, concat_axis=0, tiled=True)]
    convert_element_type x0 -> x3, local copies, waits for them, and re-layouts: none -> 5.11 us  [the longest x2 3.02 us: body(): normal_vel = to_lines(base_lines[:, 1:2])[0].astype(jnp.float32)]
    all_to_all x1 -> x0, local copies, waits for them, and re-layouts: 2.53 us -> none  [body(): lines = lax.all_to_all(low, 'gy', split_axis=2, concat_axis=3, tiled=True)]
    unnamed x8 -> x16, local copies, waits for them, and re-layouts: 5.63 us -> 3.38 us
    convert_element_type x1 -> x3, other arithmetic: 0.07 us -> 2.22 us  [the longest x1 1.99 us: body(): base_low = base_flow.astype(jnp.bfloat16)]
    unnamed x0 -> x1, other arithmetic: none -> 1.73 us
    select_n x1, other arithmetic: 3.63 us -> 1.91 us  [body(): return jnp.where(interior, updated, jnp.float32(0.0))]
  transfers between devices with their start and end apart: 4 -> 4, of which waited for: 2 -> 2; matrix products, arithmetic and copies ran while one was open for 4% -> 13% of each run, Pallas kernels for 18% -> 18%
where the time goes in v6:
time: 97.6 us; the launch traced here: 97 us
  local copies, waits for them, and re-layouts  23 us (24%)
  waiting for transfers between devices  22.6 us (23%)
  starting transfers between devices  20 us (20%)
  Pallas kernels  17.2 us (18%)
  other arithmetic  8.08 us (8%)
  matrix products  5.88 us (6%)
    ppermute x2, waiting for transfers between devices, ring_shift(): return lax.ppermute(value, axis, pairs)  17.7 us
    pallas_call x1, Pallas kernels, interior_update(): pl.pallas_call(interior_kernel, grid=(rows // LANES, cells // HALO - 2),...  9.97 us
    ppermute x2, starting transfers between devices, ring_shift(): return lax.ppermute(value, axis, pairs)  8.77 us
    pallas_call x1, Pallas kernels, boundary_update(): pl.pallas_call(boundary_kernel, grid=(2,), in_specs=[full_spec, full_spec...  7.25 us
    all_to_all x1, starting transfers between devices, body(): lines = lax.all_to_all(low, 'gy', split_axis=0, concat_axis=0, tiled=True)  6.8 us
    all_to_all x1, waiting for transfers between devices, body(): lines = lax.all_to_all(low, 'gy', split_axis=0, concat_axis=0, tiled=True)  4.86 us
    reshape x1, local copies, waits for them, and re-layouts, body(): second_blocks = second_op.reshape(total_rows, groups, local_rows)  4.53 us
    reshape x1, local copies, waits for them, and re-layouts, body(): first_blocks = first_op.reshape(total_rows, groups, local_rows)  4.51 us
  transfers between devices with their start and end apart: 4, of which 2 were waited for; matrix products, arithmetic and copies ran while one was open for 13% of the time, Pallas kernels for 18%

profile of v6, /device:TPU:1, one launch (start us, length us, event | category | flops | bytes accessed | tf_op | source)
XLA Modules:
  0.0 97.0 jit_solution(11337446128389675814)
XLA Ops:
  0.0 0.0 copy-start
  0.0 2.0 %convert_element_type.36 = bf16[3,24,32,256]{3,2,1,0:T(8,128)(2,1)S(1)} convert(f32[3,24,32,256]{3,2,1,0:T(8,128)} %base_ref.3) | non-fusion elementwise | flops 589824 | bytes 3538944 | tf_op jit(solution)/shard_map/convert_element_type | solution.py:145
  2.0 0.4 copy-done
  2.4 0.2 convert_element_type.37
  2.6 0.2 pad_maximum_fusion
  2.8 1.7 %copy.17 = bf16[4,6,6,32,256]{4,3,2,1,0:T(8,128)(2,1)} copy(bf16[4,6,6,32,256]{4,3,2,0,1:T(8,128)(2,1)S(1)} %bitcast.70) | data formatting | bytes 4718592 | tf_op jit(solution)/shard_map/transpose | solution.py:149
  4.5 6.8 %all-to-all-start = ((bf16[4,6,6,32,256]{4,3,2,1,0:T(8,128)(2,1)}), bf16[4,6,6,32,256]{4,3,2,1,0:T(8,128)(2,1)S(1)}, u32[]{:S(2)}, u32[]{:S(2)}) async-start(bf16[4,6,6,32,256]{4,3,2,1,0:T(8,128)(2,1)} %copy.17), calls=%async_computation | async-start | bytes 4718592 | tf_op jit(solution)/shard_map/all_to_all | solution.py:150
  11.3 10.0 %shard_map.46.prev_ref = f32[3,24,32,256]{3,2,1,0:T(8,128)} custom-call(f32[3,24,32,256]{3,2,1,0:T(8,128)} %base_ref.3, f32[3,24,32,256]{3,2,1,0:T(8,128)} %adj_ref.3), custom_call_target="tpu_custom_call" | custom-call | tf_op jit(solution)/shard_map/pallas_call | solution.py:86
  21.3 4.5 %reshape.69 = bf16[1024,4,256]{2,1,0:T(4,128)(2,1)} reshape(bf16[1024,1024]{1,0:T(8,128)(2,1)} %param.9) | data formatting | bytes 4194304 | tf_op jit(solution)/shard_map/reshape | solution.py:158
  25.8 4.5 %reshape.68 = bf16[1024,4,256]{2,1,0:T(4,128)(2,1)} reshape(bf16[1024,1024]{1,0:T(8,128)(2,1)} %param.8) | data formatting | bytes 4194304 | tf_op jit(solution)/shard_map/reshape | solution.py:157
  30.3 1.2 %slice_bitcast_fusion.1 = (f32[1,3,4,32,256]{4,3,2,1,0:T(8,128)S(1)}, f32[1,3,4,32,256]{4,3,2,1,0:T(8,128)S(1)}) fusion(f32[3,24,32,256]{3,2,1,0:T(8,128)} %base_ref.3), kind=kLoop, calls=%fused_computation.25 | loop fusion | bytes 1572864 | tf_op jit(solution)/shard_map/stack | solution.py:153
  31.5 1.2 %slice_bitcast_fusion = (f32[1,3,4,32,256]{4,3,2,1,0:T(8,128)S(1)}, f32[1,3,4,32,256]{4,3,2,1,0:T(8,128)S(1)}) fusion(f32[3,24,32,256]{3,2,1,0:T(8,128)} %adj_ref.3), kind=kLoop, calls=%fused_computation.24 | loop fusion | bytes 1572864 | tf_op jit(solution)/shard_map/stack | solution.py:153
  32.6 1.3 %pad_maximum_fusion.1 = (f32[2,3,4,32,256]{4,3,2,1,0:T(8,128)}, f32[2,3,4,32,256]{4,3,2,1,0:T(8,128)}) fusion(f32[1,3,4,32,256]{4,3,2,1,0:T(8,128)S(1)} %get-tuple-element.32, f32[1,3,4,32,256]{4,3,2,1,0:T(8,128)S(1)} %get-tuple-element.30, f32[1,3,4,32,256]{4,3,2,1,0:T(8,128)S(1)} %get-tuple-element.31, f32[1,3,4,32,256]{4,3,2,1,0:T(8,128)S(1)} %get-tuple-element.29), kind=kLoop, calls=%fused_computation.21 | loop fusion | flops 393216 | bytes 3145728 | tf_op jit(solution)/shard_map/stack | solution.py:152
  33.9 4.9 %all-to-all-done = bf16[4,6,6,32,256]{4,3,2,1,0:T(8,128)(2,1)S(1)} async-done(((bf16[4,6,6,32,256]{4,3,2,1,0:T(8,128)(2,1)}), bf16[4,6,6,32,256]{4,3,2,1,0:T(8,128)(2,1)S(1)}, u32[]{:S(2)}, u32[]{:S(2)}) %all-to-all-start) | async-done | bytes 2359328 | tf_op jit(solution)/shard_map/all_to_all | solution.py:150
  38.8 0.0 copy-start.4
  38.8 0.1 convert_bitcast_fusion.1
  38.9 1.7 %convert_bitcast_fusion = f32[3,6,4,4,8,256]{5,4,3,2,1,0:T(8,128)} fusion(bf16[4,6,6,32,256]{4,3,2,1,0:T(8,128)(2,1)S(1)} %all-to-all-done), kind=kLoop, calls=%fused_computation.6 | loop fusion | flops 589824 | bytes 3538944
  40.6 0.4 copy-done.4
  40.9 2.8 %fusion.2 = f32[3,6,32,1024,1]{3,2,1,0,4:T(8,128)} fusion(bf16[4,6,6,32,256]{4,3,2,1,0:T(8,128)(2,1)S(1)} %all-to-all-done, bf16[1024,4,256,1,1]{2,1,0,4,3:T(4,128)(2,1)S(1)} %bitcast.75), kind=kOutput, calls=%fused_computation.9 | convolution fusion | flops 1207959552 | bytes 6815744 | tf_op jit(solution)/shard_map/qfxzr,iqr->fxzi/dot_general | solution.py:163
  43.8 1.5 %copy.18 = f32[1,6,32,4,256]{4,3,2,1,0:T(4,128)} copy(f32[1,6,32,4,256]{4,2,1,0,3:T(8,128)S(1)} %convert_bitcast_fusion.1) | data formatting | bytes 1572864 | tf_op jit(solution)/shard_map/convert_element_type | solution.py:166
  45.3 1.5 %reshape.71 = f32[6,32,1024]{2,1,0:T(8,128)S(1)} reshape(f32[1,6,32,4,256]{4,3,2,1,0:T(4,128)} %copy.18) | data formatting | bytes 1572864 | tf_op jit(solution)/shard_map/convert_element_type | solution.py:166
  46.8 0.0 copy-start.2
  46.8 2.1 %copy.40 = f32[3,6,4,4,8,256]{5,4,2,3,1,0:T(8,128)S(1)} copy(f32[3,6,4,4,8,256]{5,4,3,2,1,0:T(8,128)} %convert_bitcast_fusion) | data formatting | bytes 4718592 | tf_op jit(solution)/shard_map/convert_element_type | solution.py:167
  48.9 0.2 copy-done.2
  49.1 0.0 copy-start.3
  49.1 1.5 %fusion = f32[6,32,1024]{2,1,0:T(8,128)S(1)} fusion(f32[3,6,32,1024]{3,2,1,0:T(8,128)S(1)} %bitcast.74, bf16[4,6,6,32,256]{4,3,2,1,0:T(8,128)(2,1)S(1)} %all-to-all-done, bf16[1024,4,256,1,1]{2,1,0,4,3:T(4,128)(2,1)S(1)} %bitcast.71), kind=kOutput, calls=%fused_computation.1 | convolution fusion | flops 1208942592 | bytes 7602176 | tf_op jit(solution)/shard_map/qfxzr,iqr->fxzi/dot_general | solution.py:161
  50.6 0.2 copy-done.3
  50.8 1.6 %fusion.1 = f32[3,6,32,1024]{3,2,1,0:T(8,128)S(1)} fusion(f32[3,6,32,1024,1]{3,2,1,0,4:T(8,128)S(1)} %copy-done.3, bf16[4,6,6,32,256]{4,3,2,1,0:T(8,128)(2,1)S(1)} %all-to-all-done, bf16[1024,4,256,1,1]{2,1,0,4,3:T(4,128)(2,1)S(1)} %bitcast.72, f32[6,32,1024]{2,1,0:T(8,128)S(1)} %reshape.71), kind=kOutput, calls=%fused_computation.3 | convolution fusion | flops 1209729024 | bytes 9961472 | tf_op jit(solution)/shard_map/qfxzr,iqr->fxzi/dot_general | solution.py:162
  52.3 0.2 fusion.15
  52.6 0.2 convert_element_type.44
  52.8 0.0 copy-start.6
  52.8 0.0 copy-start.5
  52.8 1.2 %copy.60 = bf16[3,6,4,4,8,256]{5,4,2,1,0,3:T(8,128)(2,1)} copy(bf16[3,6,4,4,8,256]{5,4,3,2,1,0:T(8,128)(2,1)S(1)} %bitcast.73) | data formatting | bytes 2359296 | tf_op jit(solution)/shard_map/reshape | solution.py:170
  53.9 4.5 %all-to-all-start.1 = ((bf16[4,3,6,32,256]{4,3,2,1,0:T(8,128)(2,1)}), bf16[4,3,6,32,256]{4,3,2,1,0:T(8,128)(2,1)S(1)}, u32[]{:S(2)}, u32[]{:S(2)}) async-start(bf16[4,3,6,32,256]{4,3,2,1,0:T(8,128)(2,1)} %bitcast.68), calls=%async_computation.1 | async-start | bytes 2359296 | tf_op jit(solution)/shard_map/all_to_all | solution.py:173
  58.4 0.0 copy-done.6
  58.4 0.0 collective-permute-start
  58.4 0.0 copy-done.5
  58.4 8.8 %collective-permute-start.1 = (f32[2,3,4,32,256]{4,3,2,1,0:T(8,128)S(1)}, f32[2,3,4,32,256]{4,3,2,1,0:T(8,128)}, u32[]{:S(2)}, u32[]{:S(2)}) collective-permute-start(f32[2,3,4,32,256]{4,3,2,1,0:T(8,128)S(1)} %copy-done.5), channel_id=1, source_target_pairs={{4,0},{8,4},{12,8},{16,12},{20,16},{24,20},{28,24},{32,28},{36,32}... | collective-permute-start | bytes 2359304 | tf_op jit(solution)/shard_map/ppermute | solution.py:23
  67.2 17.7 %collective-permute-done.tail_ref = f32[2,3,4,32,256]{4,3,2,1,0:T(8,128)S(1)} collective-permute-done((f32[2,3,4,32,256]{4,3,2,1,0:T(8,128)S(1)}, f32[2,3,4,32,256]{4,3,2,1,0:T(8,128)S(1)}, u32[]{:S(2)}, u32[]{:S(2)}) %collective-permute-start) | collective-permute-done | bytes 786464 | tf_op jit(solution)/shard_map/ppermute | solution.py:23
  84.9 0.0 copy-start.7
  84.9 0.0 collective-permute-done.1.head_ref
  84.9 0.9 copy-done.7
  85.8 7.3 %shard_map.47 = f32[3,24,32,256]{3,2,1,0:T(8,128)} custom-call(f32[3,24,32,256]{3,2,1,0:T(8,128)} %base_ref.3, f32[3,24,32,256]{3,2,1,0:T(8,128)} %adj_ref.3, f32[2,3,4,32,256]{4,3,2,1,0:T(8,128)} %copy-done.7, f32[2,3,4,32,256]{4,3,2,1,0:T(8,128)} %collective-permute-done.1.head_ref, ...), custom_call_target="tpu_custom_call", output_to_operand_aliasing={{}: (4, {})} | custom-call | tf_op jit(solution)/shard_map/pallas_call | solution.py:128
  93.1 0.0 all-to-all-done.1
  93.1 0.3 multiply_bitcast_fusion
  93.4 0.0 copy-start.1
  93.4 0.3 copy.26
  93.7 1.4 %copy-done.1 = f32[3,24,32,256]{3,2,1,0:T(8,128)S(1)} copy-done((f32[3,24,32,256]{3,2,1,0:T(8,128)S(1)}, f32[3,24,32,256]{3,2,1,0:T(8,128)}, u32[]{:S(2)}) %copy-start.1) | copy-done | bytes 2359320
  95.1 1.9 %add_select_fusion = f32[3,24,32,256]{3,2,1,0:T(8,128)} fusion(f32[3,24,32,256]{3,2,1,0:T(8,128)S(1)} %copy-done.1, f32[3,24,32,256]{3,2,1,0:T(8,128)S(1)} %bitcast.69, pred[256]{0:T(512)(128)(4,1)S(1)} %compare_and_fusion), kind=kLoop, calls=%fused_computation.7 | loop fusion | flops 1179648 | bytes 7078144 | tf_op jit(solution)/shard_map/jit(_where)/select_n | solution.py:180
  (1 shorter events, 0.0 us)
Async XLA Ops:
  0.0 2.4 %copy-start = (f32[3,24,32,256]{3,2,1,0:T(8,128)S(1)}, f32[3,24,32,256]{3,2,1,0:T(8,128)}, u32[]{:S(2)}) copy-start(f32[3,24,32,256]{3,2,1,0:T(8,128)} %adj_ref.3) | copy-start | bytes 7077892
  4.5 34.3 %all-to-all-start = ((bf16[4,6,6,32,256]{4,3,2,1,0:T(8,128)(2,1)}), bf16[4,6,6,32,256]{4,3,2,1,0:T(8,128)(2,1)S(1)}, u32[]{:S(2)}, u32[]{:S(2)}) async-start(bf16[4,6,6,32,256]{4,3,2,1,0:T(8,128)(2,1)} %copy.17), calls=%async_computation | async-start | bytes 4718592 | tf_op jit(solution)/shard_map/all_to_all | solution.py:150
  38.8 2.2 %copy-start.4 = (bf16[1024,4,256]{2,1,0:T(4,128)(2,1)S(1)}, bf16[1024,4,256]{2,1,0:T(4,128)(2,1)}, u32[]{:S(2)}) copy-start(bf16[1024,4,256]{2,1,0:T(4,128)(2,1)} %reshape.69) | copy-start | bytes 6291460
  46.8 2.3 %copy-start.2 = (bf16[1024,4,256]{2,1,0:T(4,128)(2,1)S(1)}, bf16[1024,4,256]{2,1,0:T(4,128)(2,1)}, u32[]{:S(2)}) copy-start(bf16[1024,4,256]{2,1,0:T(4,128)(2,1)} %reshape.68) | copy-start | bytes 6291460
  49.1 1.7 %copy-start.3 = (f32[3,6,32,1024,1]{3,2,1,0,4:T(8,128)S(1)}, f32[3,6,32,1024,1]{3,2,1,0,4:T(8,128)}, u32[]{:S(2)}) copy-start(f32[3,6,32,1024,1]{3,2,1,0,4:T(8,128)} %fusion.2) | copy-start | bytes 7077892
  52.8 5.7 %copy-start.6 = (f32[2,3,4,32,256]{4,3,2,1,0:T(8,128)S(1)}, f32[2,3,4,32,256]{4,3,2,1,0:T(8,128)}, u32[]{:S(2)}) copy-start(f32[2,3,4,32,256]{4,3,2,1,0:T(8,128)} %get-tuple-element.23) | copy-start | bytes 2359300
  52.8 5.7 %copy-start.5 = (f32[2,3,4,32,256]{4,3,2,1,0:T(8,128)S(1)}, f32[2,3,4,32,256]{4,3,2,1,0:T(8,128)}, u32[]{:S(2)}) copy-start(f32[2,3,4,32,256]{4,3,2,1,0:T(8,128)} %get-tuple-element.24) | copy-start | bytes 2359300
  53.9 39.1 %all-to-all-start.1 = ((bf16[4,3,6,32,256]{4,3,2,1,0:T(8,128)(2,1)}), bf16[4,3,6,32,256]{4,3,2,1,0:T(8,128)(2,1)S(1)}, u32[]{:S(2)}, u32[]{:S(2)}) async-start(bf16[4,3,6,32,256]{4,3,2,1,0:T(8,128)(2,1)} %bitcast.68), calls=%async_computation.1 | async-start | bytes 2359296 | tf_op jit(solution)/shard_map/all_to_all | solution.py:173
  58.4 26.5 %collective-permute-start = (f32[2,3,4,32,256]{4,3,2,1,0:T(8,128)S(1)}, f32[2,3,4,32,256]{4,3,2,1,0:T(8,128)S(1)}, u32[]{:S(2)}, u32[]{:S(2)}) collective-permute-start(f32[2,3,4,32,256]{4,3,2,1,0:T(8,128)S(1)} %copy-done.6), channel_id=1, source_target_pairs={{0,4},{4,8},{8,12},{12,16},{16,20},{20,24},{24,28},{28,32},{32,36}... | collective-permute-start | bytes 2359304 | tf_op jit(solution)/shard_map/ppermute | solution.py:23
  58.4 26.5 %collective-permute-start.1 = (f32[2,3,4,32,256]{4,3,2,1,0:T(8,128)S(1)}, f32[2,3,4,32,256]{4,3,2,1,0:T(8,128)}, u32[]{:S(2)}, u32[]{:S(2)}) collective-permute-start(f32[2,3,4,32,256]{4,3,2,1,0:T(8,128)S(1)} %copy-done.5), channel_id=1, source_target_pairs={{4,0},{8,4},{12,8},{16,12},{20,16},{24,20},{28,24},{32,28},{36,32}... | collective-permute-start | bytes 2359304 | tf_op jit(solution)/shard_map/ppermute | solution.py:23
  84.9 0.9 copy-start.7
  93.4 1.7 %copy-start.1 = (f32[3,24,32,256]{3,2,1,0:T(8,128)S(1)}, f32[3,24,32,256]{3,2,1,0:T(8,128)}, u32[]{:S(2)}) copy-start(f32[3,24,32,256]{3,2,1,0:T(8,128)} %shard_map.47) | copy-start | bytes 7077892

commit v7 on v5

--- a/solution.py
+++ b/solution.py
@@ -1,3 +1,5 @@
+import functools
+
 import jax
 import jax.numpy as jnp
 from jax import lax
@@ -14,12 +16,13 @@
 LANES = 128
 
 
-def ring_shift(value, axis, forward):
+def ring_shift(value, axis, forward, far, want_far):
     count = lax.axis_size(axis)
+    links = [i for i in range(count) if far[i] == want_far]
     if forward:
-        pairs = [(i, (i + 1) % count) for i in range(count)]
+        pairs = [(i, (i + 1) % count) for i in links]
     else:
-        pairs = [((i + 1) % count, i) for i in range(count)]
+        pairs = [((i + 1) % count, i) for i in links]
     return lax.ppermute(value, axis, pairs)
 
 
@@ -92,7 +95,7 @@
     )(base_flow, adjoint)
 
 
-def boundary_kernel(base_ref, adj_ref, tail_ref, head_ref, prev_ref, out_ref, ext_ref):
+def boundary_kernel(base_ref, adj_ref, tail_ref, head_ref, far_tail_ref, far_head_ref, prev_ref, out_ref, ext_ref):
     comps, cells, span, rows = base_ref.shape
     side = pl.program_id(0)
 
@@ -100,8 +103,8 @@
     def _():
         ext_ref[0, :, HALO : HALO + cells] = base_ref[...]
         ext_ref[1, :, HALO : HALO + cells] = adj_ref[...]
-        ext_ref[:, :, :HALO] = tail_ref[...]
-        ext_ref[:, :, HALO + cells :] = head_ref[...]
+        ext_ref[:, :, :HALO] = tail_ref[...] + far_tail_ref[...]
+        ext_ref[:, :, HALO + cells :] = head_ref[...] + far_head_ref[...]
 
     first = side * (cells - HALO)
     for lane in range(rows // LANES):
@@ -120,7 +123,7 @@
         lax.fori_loop(0, HALO, step, 0)
 
 
-def boundary_update(base_flow, adjoint, tails, heads, previous):
+def boundary_update(base_flow, adjoint, tails, heads, far_tails, far_heads, previous):
     comps, cells, span, rows = base_flow.shape
     full_spec = pl.BlockSpec((comps, cells, span, rows), lambda s: (0, 0, 0, 0))
     halo_spec = pl.BlockSpec((2, comps, HALO, span, rows), lambda s: (0, 0, 0, 0, 0))
@@ -128,15 +131,15 @@
     return pl.pallas_call(
         boundary_kernel,
         grid=(2,),
-        in_specs=[full_spec, full_spec, halo_spec, halo_spec, pl.BlockSpec(memory_space=pl.ANY)],
+        in_specs=[full_spec, full_spec, halo_spec, halo_spec, halo_spec, halo_spec, pl.BlockSpec(memory_space=pl.ANY)],
         out_specs=out_spec,
         out_shape=jax.ShapeDtypeStruct(base_flow.shape, jnp.float32),
         scratch_shapes=[pltpu.VMEM((2, comps, cells + 2 * HALO, span, rows), jnp.float32)],
-        input_output_aliases={4: 0},
-    )(base_flow, adjoint, tails, heads, previous)
+        input_output_aliases={6: 0},
+    )(base_flow, adjoint, tails, heads, far_tails, far_heads, previous)
 
 
-def body(base_flow, adjoint, first_op, second_op):
+def body(base_flow, adjoint, first_op, second_op, far=()):
     comps, cells, spanwise, local_rows = base_flow.shape
     groups = lax.axis_size("gy")
     total_rows = local_rows * groups
@@ -146,12 +149,16 @@
     adjoint_low = lax.optimization_barrier(adjoint.astype(jnp.bfloat16))
     low = jnp.concatenate((base_low, adjoint_low), 0).reshape(2 * comps, cells, spanwise, 1, local_rows)
     lines = lax.all_to_all(low, "gy", split_axis=2, concat_axis=3, tiled=True)
-    partial = interior_update(base_flow, adjoint)
     tail_cells = jnp.stack((base_flow[:, cells - HALO :], adjoint[:, cells - HALO :]), 0)
     head_cells = jnp.stack((base_flow[:, :HALO], adjoint[:, :HALO]), 0)
-    lines, partial, tail_cells, head_cells = lax.optimization_barrier((lines, partial, tail_cells, head_cells))
-    tails = ring_shift(tail_cells, "gx", True)
-    heads = ring_shift(head_cells, "gx", False)
+    tails = ring_shift(tail_cells, "gx", True, far, False)
+    heads = ring_shift(head_cells, "gx", False, far, False)
+    partial = interior_update(base_flow, adjoint)
+    lines, partial, tails, heads, tail_cells, head_cells = lax.optimization_barrier(
+        (lines, partial, tails, heads, tail_cells, head_cells)
+    )
+    far_tails = ring_shift(tail_cells, "gx", True, far, True)
+    far_heads = ring_shift(head_cells, "gx", False, far, True)
     lines = lines.reshape(2 * comps, cells, part, total_rows)
     base_lines = lines[:comps]
     adj_lines = lines[comps:]
@@ -167,16 +174,24 @@
     wall_part = lax.all_to_all(wall_part, "gy", split_axis=3, concat_axis=2, tiled=True)
     wall_part = wall_part.reshape(comps, cells, spanwise, local_rows).astype(jnp.float32)
 
-    partial = boundary_update(base_flow, adjoint, tails, heads, partial)
+    partial = boundary_update(base_flow, adjoint, tails, heads, far_tails, far_heads, partial)
     updated = partial + STEP_WEIGHT * wall_part
     wall_index = lax.axis_index("gy") * local_rows + jnp.arange(local_rows, dtype=jnp.int32)
     interior = (wall_index > 0) & (wall_index < total_rows - 1)
     return jnp.where(interior, updated, jnp.float32(0.0))
 
 
+def far_links(mesh):
+    devices = mesh.devices
+    count = devices.shape[0]
+    return tuple(
+        bool(devices[i, 0].coords[1] != devices[(i + 1) % count, 0].coords[1]) for i in range(count)
+    )
+
+
 def solution(mesh):
     return jax.shard_map(
-        body,
+        functools.partial(body, far=far_links(mesh)),
         mesh=mesh,
         in_specs=(P(None, "gx", None, "gy"), P(None, "gx", None, "gy"), P(), P()),
         out_specs=P(None, "gx", None, "gy"),

time: 93.9 us -> 97.9 us (1.043)
  starting transfers between devices: 20.8 us -> 28.9 us
  waiting for transfers between devices: 32.1 us -> 27.3 us
    ppermute x2 -> x4, starting transfers between devices: 8.7 us -> 16.8 us  [ring_shift(): return lax.ppermute(value, axis, pairs)]
    all_to_all x1, waiting for transfers between devices: 14 us -> 11.1 us  [body(): lines = lax.all_to_all(low, 'gy', split_axis=2, concat_axis=3, tiled=True)]
    ppermute x2 -> x4, waiting for transfers between devices: 18.1 us -> 16.3 us  [ring_shift(): return lax.ppermute(value, axis, pairs)]
    another operation x2 -> x1, local copies, waits for them, and re-layouts: 2.34 us -> 1.46 us  [body(): head_cells = jnp.stack((base_flow[:, :HALO], adjoint[:, :HALO]), 0)]
    unnamed x8 -> x10, local copies, waits for them, and re-layouts: 5.63 us -> 5.89 us
  transfers between devices with their start and end apart: 4 -> 6, of which waited for: 2 -> 3; matrix products, arithmetic and copies ran while one was open for 4% -> 6% of each run, Pallas kernels for 18% -> 18%
where the time goes in v7:
time: 97.9 us; the launch traced here: 97.4 us
  starting transfers between devices  28.9 us (30%)
  waiting for transfers between devices  27.3 us (28%)
  Pallas kernels  17.8 us (18%)
  local copies, waits for them, and re-layouts  11.2 us (11%)
  other arithmetic  7.65 us (8%)
  matrix products  4.32 us (4%)
    ppermute x4, starting transfers between devices, ring_shift(): return lax.ppermute(value, axis, pairs)  16.8 us
    ppermute x4, waiting for transfers between devices, ring_shift(): return lax.ppermute(value, axis, pairs)  16.3 us
    all_to_all x1, waiting for transfers between devices, body(): lines = lax.all_to_all(low, 'gy', split_axis=2, concat_axis=3, tiled=True)  11.1 us
    pallas_call x1, Pallas kernels, interior_update(): pl.pallas_call(interior_kernel, grid=(rows // LANES, cells // HALO - 2),...  10 us
    pallas_call x1, Pallas kernels, boundary_update(): pl.pallas_call(boundary_kernel, grid=(2,), in_specs=[full_spec, full_spec...  7.76 us
    all_to_all x1, starting transfers between devices, body(): lines = lax.all_to_all(low, 'gy', split_axis=2, concat_axis=3, tiled=True)  7.64 us
    unnamed x10, local copies, waits for them, and re-layouts  5.89 us
    all_to_all x1, starting transfers between devices, body(): lax.all_to_all(wall_part, 'gy', split_axis=3, concat_axis=2, tiled=True)  4.46 us
  transfers between devices with their start and end apart: 6, of which 3 were waited for; matrix products, arithmetic and copies ran while one was open for 6% of the time, Pallas kernels for 18%

profile of v7, /device:TPU:1, one launch (start us, length us, event | category | flops | bytes accessed | tf_op | source)
XLA Modules:
  0.0 97.4 jit_solution(5770057009815386522)
XLA Ops:
  0.0 0.0 copy-start
  0.0 0.0 copy-start.1
  0.0 3.1 %copy.18 = bf16[3,24,32,256]{3,1,0,2:T(8,128)(2,1)S(1)} copy(f32[3,24,32,256]{3,2,1,0:T(8,128)} %base_ref.3) | data formatting | bytes 3538944 | tf_op args[0]
  3.1 0.0 copy-done.1
  3.1 1.3 %copy.17 = bf16[3,24,32,256]{3,1,0,2:T(8,128)(2,1)S(1)} copy(f32[3,24,32,256]{3,2,1,0:T(8,128)S(1)} %copy-done.1) | data formatting | bytes 3538944 | tf_op args[1]
  4.4 1.6 %maximum_bitcast_fusion = bf16[6,24,32,1,256]{4,1,0,3,2:T(8,128)(2,1)} fusion(bf16[3,24,32,256]{3,1,0,2:T(8,128)(2,1)S(1)} %copy.17, bf16[3,24,32,256]{3,1,0,2:T(8,128)(2,1)S(1)} %copy.18), kind=kLoop, calls=%fused_computation | loop fusion | flops 1179648 | bytes 4718592 | tf_op jit(solution)/shard_map/reshape | solution.py:150
  6.0 7.6 %all-to-all-start = ((bf16[6,24,32,1,256]{4,1,0,3,2:T(8,128)(2,1)}), bf16[6,24,32,1,256]{4,1,0,3,2:T(8,128)(2,1)}, u32[]{:S(2)}, u32[]{:S(2)}) async-start(bf16[6,24,32,1,256]{4,1,0,3,2:T(8,128)(2,1)} %maximum_bitcast_fusion), calls=%async_computation | async-start | bytes 4718592 | tf_op jit(solution)/shard_map/all_to_all | solution.py:151
  13.6 1.5 %slice_bitcast_fusion = (f32[1,3,4,32,256]{4,3,2,1,0:T(8,128)S(1)}, f32[1,3,4,32,256]{4,3,2,1,0:T(8,128)S(1)}, f32[1,3,4,32,256]{4,3,2,1,0:T(8,128)S(1)}, f32[1,3,4,32,256]{4,3,2,1,0:T(8,128)S(1)}) fusion(f32[3,24,32,256]{3,2,1,0:T(8,128)} %adj_ref.3, f32[3,24,32,256]{3,2,1,0:T(8,128)} %base_ref.3), kind=kLoop, calls=%fused_computation.19 | loop fusion | bytes 3145728 | tf_op jit(solution)/shard_map/stack | solution.py:153
  15.1 1.0 pad_maximum_fusion
  16.0 1.9 %collective-permute-start = (f32[2,3,4,32,256]{4,3,2,1,0:T(8,128)}, f32[2,3,4,32,256]{4,3,2,1,0:T(8,128)S(1)}, u32[]{:S(2)}, u32[]{:S(2)}) collective-permute-start(f32[2,3,4,32,256]{4,3,2,1,0:T(8,128)} %pad_maximum_fusion), channel_id=1, source_target_pairs={{0,4},{4,8},{8,12},{12,16},{16,20},{20,24},{24,28},{28,32},{32,36}... | collective-permute-start | bytes 2359304 | tf_op jit(solution)/shard_map/ppermute | solution.py:26
  17.9 0.9 pad_maximum_fusion.1
  18.9 1.3 %collective-permute-start.1 = (f32[2,3,4,32,256]{4,3,2,1,0:T(8,128)}, f32[2,3,4,32,256]{4,3,2,1,0:T(8,128)}, u32[]{:S(2)}, u32[]{:S(2)}) collective-permute-start(f32[2,3,4,32,256]{4,3,2,1,0:T(8,128)} %pad_maximum_fusion.1), channel_id=1, source_target_pairs={{4,0},{8,4},{12,8},{16,12},{20,16},{24,20},{28,24},{32,28},{36,32}... | collective-permute-start | bytes 2359304 | tf_op jit(solution)/shard_map/ppermute | solution.py:26
  20.2 10.0 %shard_map.46.prev_ref = f32[3,24,32,256]{3,2,1,0:T(8,128)} custom-call(f32[3,24,32,256]{3,2,1,0:T(8,128)} %base_ref.3, f32[3,24,32,256]{3,2,1,0:T(8,128)} %adj_ref.3), custom_call_target="tpu_custom_call" | custom-call | tf_op jit(solution)/shard_map/pallas_call | solution.py:89
  30.2 11.1 %all-to-all-done = bf16[6,24,32,1,256]{4,1,0,3,2:T(8,128)(2,1)} async-done(((bf16[6,24,32,1,256]{4,1,0,3,2:T(8,128)(2,1)}), bf16[6,24,32,1,256]{4,1,0,3,2:T(8,128)(2,1)}, u32[]{:S(2)}, u32[]{:S(2)}) %all-to-all-start) | async-done | bytes 2359328 | tf_op jit(solution)/shard_map/all_to_all | solution.py:151
  41.2 2.5 %copy.19 = bf16[6,24,4,8,1,256]{5,3,2,1,0,4:T(8,128)(2,1)S(1)} copy(bf16[6,24,4,8,1,256]{5,1,0,3,2,4:T(8,128)(2,1)} %bitcast.1) | data formatting | bytes 4718592 | tf_op jit(solution)/shard_map/all_to_all | solution.py:151
  43.8 0.0 collective-permute-done.tail_ref
  43.8 0.0 copy-start.2
  43.8 0.0 collective-permute-done.1.head_ref
  43.8 0.0 copy-start.3
  43.8 0.2 fusion.12
  44.0 0.7 copy-done.2
  44.7 0.1 convert.1
  44.8 0.9 copy-done.3
  45.7 1.4 %fusion.1 = f32[3,24,8,1024]{3,2,1,0:T(8,128)S(1)} fusion(bf16[3,24,8,1024]{3,2,1,0:T(8,128)(2,1)S(1)} %bitcast.53, bf16[1024,1024]{1,0:T(8,128)(2,1)S(1)} %copy-done.3), kind=kOutput, calls=%fused_computation.9 | convolution fusion | flops 1207959552 | bytes 5636096 | tf_op jit(solution)/shard_map/fxzk,ik->fxzi/dot_general | solution.py:167
  47.1 0.0 copy-done
  47.1 1.5 %multiply_reduce_fusion = f32[24,8,1024]{2,1,0:T(8,128)S(1)} fusion(bf16[3,24,8,1024]{3,2,1,0:T(8,128)(2,1)S(1)} %bitcast.54, bf16[3,24,8,1024]{3,2,1,0:T(8,128)(2,1)S(1)} %bitcast.58, bf16[1024,1024]{1,0:T(8,128)(2,1)S(1)} %copy-done), kind=kOutput, calls=%fused_computation.7 | convolution fusion | flops 1209532416 | bytes 5242880 | tf_op jit(solution)/shard_map/fxzk,ik->fxzi/dot_general | solution.py:165
  48.6 1.5 %multiply_add_fusion = f32[3,24,8,1024]{3,2,1,0:T(8,128)S(1)} fusion(f32[3,24,8,1024]{3,2,1,0:T(8,128)S(1)} %fusion.1, bf16[3,24,8,1024]{3,2,1,0:T(8,128)(2,1)S(1)} %bitcast.55, bf16[1024,1024]{1,0:T(8,128)(2,1)S(1)} %copy-done, f32[24,8,1024]{2,1,0:T(8,128)S(1)} %convert.1), kind=kOutput, calls=%fused_computation.8 | convolution fusion | flops 1209729024 | bytes 8781824 | tf_op jit(solution)/shard_map/fxzk,ik->fxzi/dot_general | solution.py:166
  50.0 0.2 fusion.11
  50.3 0.2 convert_element_type.33
  50.4 1.1 %copy.9 = bf16[3,24,8,4,256]{4,2,1,0,3:T(8,128)(2,1)} copy(bf16[3,24,8,4,256]{4,2,3,1,0:T(8,128)(2,1)S(1)} %bitcast.56) | data formatting | bytes 2359296 | tf_op jit(solution)/shard_map/optimization_barrier | solution.py:173
  51.6 4.5 %all-to-all-start.1 = ((bf16[3,24,8,4,256]{4,2,1,0,3:T(8,128)(2,1)}), bf16[3,24,8,4,256]{4,2,1,0,3:T(8,128)(2,1)S(1)}, u32[]{:S(2)}, u32[]{:S(2)}) async-start(bf16[3,24,8,4,256]{4,2,1,0,3:T(8,128)(2,1)} %copy.9), calls=%async_computation.1 | async-start | bytes 2359296 | tf_op jit(solution)/shard_map/all_to_all | solution.py:174
  56.0 1.3 %collective-permute-start.2 = (f32[2,3,4,32,256]{4,3,2,1,0:T(8,128)}, f32[2,3,4,32,256]{4,3,2,1,0:T(8,128)}, u32[]{:S(2)}, u32[]{:S(2)}) collective-permute-start(f32[2,3,4,32,256]{4,3,2,1,0:T(8,128)} %pad_maximum_fusion), channel_id=1, source_target_pairs={{124,128},{252,0},{125,129},{253,1},{126,130},{254,2},{127,131},{2... | collective-permute-start | bytes 2359304 | tf_op jit(solution)/shard_map/ppermute | solution.py:26
  57.3 12.4 %collective-permute-start.3 = (f32[2,3,4,32,256]{4,3,2,1,0:T(8,128)}, f32[2,3,4,32,256]{4,3,2,1,0:T(8,128)}, u32[]{:S(2)}, u32[]{:S(2)}) collective-permute-start(f32[2,3,4,32,256]{4,3,2,1,0:T(8,128)} %pad_maximum_fusion.1), channel_id=1, source_target_pairs={{128,124},{0,252},{129,125},{1,253},{130,126},{2,254},{131,127},{3... | collective-permute-start | bytes 2359304 | tf_op jit(solution)/shard_map/ppermute | solution.py:26
  69.7 14.5 %collective-permute-done.2.far_tail_ref = f32[2,3,4,32,256]{4,3,2,1,0:T(8,128)} collective-permute-done((f32[2,3,4,32,256]{4,3,2,1,0:T(8,128)}, f32[2,3,4,32,256]{4,3,2,1,0:T(8,128)}, u32[]{:S(2)}, u32[]{:S(2)}) %collective-permute-start.2) | collective-permute-done | bytes 786464 | tf_op jit(solution)/shard_map/ppermute | solution.py:26
  84.2 1.8 %collective-permute-done.3.far_head_ref = f32[2,3,4,32,256]{4,3,2,1,0:T(8,128)} collective-permute-done((f32[2,3,4,32,256]{4,3,2,1,0:T(8,128)}, f32[2,3,4,32,256]{4,3,2,1,0:T(8,128)}, u32[]{:S(2)}, u32[]{:S(2)}) %collective-permute-start.3) | collective-permute-done | bytes 786464 | tf_op jit(solution)/shard_map/ppermute | solution.py:26
  86.0 7.8 %shard_map.47 = f32[3,24,32,256]{3,2,1,0:T(8,128)} custom-call(f32[3,24,32,256]{3,2,1,0:T(8,128)} %base_ref.3, f32[3,24,32,256]{3,2,1,0:T(8,128)} %adj_ref.3, f32[2,3,4,32,256]{4,3,2,1,0:T(8,128)} %copy-done.2, f32[2,3,4,32,256]{4,3,2,1,0:T(8,128)} %collective-permute-done.1.head_ref, ...), custom_call_target="tpu_custom_call", output_to_operand_aliasing={{}: (6, {})} | custom-call | tf_op jit(solution)/shard_map/pallas_call | solution.py:131
  93.7 0.0 all-to-all-done.1
  93.7 3.6 %fusion = f32[3,24,32,256]{3,2,1,0:T(8,128)} fusion(f32[3,24,32,256]{3,2,1,0:T(8,128)} %shard_map.47, pred[256]{0:T(512)(128)(4,1)S(1)} %compare_and_fusion, bf16[3,24,8,4,256]{4,2,1,0,3:T(8,128)(2,1)S(1)} %all-to-all-done.1), kind=kLoop, calls=%fused_computation.2 | loop fusion | flops 2359296 | bytes 5898496 | tf_op jit(solution)/shard_map/jit(_where)/select_n | solution.py:181
  (2 shorter events, 0.0 us)
Async XLA Ops:
  0.0 47.1 %copy-start = (bf16[1024,1024]{1,0:T(8,128)(2,1)S(1)}, bf16[1024,1024]{1,0:T(8,128)(2,1)}, u32[]{:S(2)}) copy-start(bf16[1024,1024]{1,0:T(8,128)(2,1)} %param.8) | copy-start | bytes 6291460
  0.0 3.1 %copy-start.1 = (f32[3,24,32,256]{3,2,1,0:T(8,128)S(1)}, f32[3,24,32,256]{3,2,1,0:T(8,128)}, u32[]{:S(2)}) copy-start(f32[3,24,32,256]{3,2,1,0:T(8,128)} %adj_ref.3) | copy-start | bytes 7077892
  6.0 35.3 %all-to-all-start = ((bf16[6,24,32,1,256]{4,1,0,3,2:T(8,128)(2,1)}), bf16[6,24,32,1,256]{4,1,0,3,2:T(8,128)(2,1)}, u32[]{:S(2)}, u32[]{:S(2)}) async-start(bf16[6,24,32,1,256]{4,1,0,3,2:T(8,128)(2,1)} %maximum_bitcast_fusion), calls=%async_computation | async-start | bytes 4718592 | tf_op jit(solution)/shard_map/all_to_all | solution.py:151
  16.0 27.7 %collective-permute-start = (f32[2,3,4,32,256]{4,3,2,1,0:T(8,128)}, f32[2,3,4,32,256]{4,3,2,1,0:T(8,128)S(1)}, u32[]{:S(2)}, u32[]{:S(2)}) collective-permute-start(f32[2,3,4,32,256]{4,3,2,1,0:T(8,128)} %pad_maximum_fusion), channel_id=1, source_target_pairs={{0,4},{4,8},{8,12},{12,16},{16,20},{20,24},{24,28},{28,32},{32,36}... | collective-permute-start | bytes 2359304 | tf_op jit(solution)/shard_map/ppermute | solution.py:26
  18.9 24.9 %collective-permute-start.1 = (f32[2,3,4,32,256]{4,3,2,1,0:T(8,128)}, f32[2,3,4,32,256]{4,3,2,1,0:T(8,128)}, u32[]{:S(2)}, u32[]{:S(2)}) collective-permute-start(f32[2,3,4,32,256]{4,3,2,1,0:T(8,128)} %pad_maximum_fusion.1), channel_id=1, source_target_pairs={{4,0},{8,4},{12,8},{16,12},{20,16},{24,20},{28,24},{32,28},{36,32}... | collective-permute-start | bytes 2359304 | tf_op jit(solution)/shard_map/ppermute | solution.py:26
  43.8 0.9 copy-start.2
  43.8 1.9 %copy-start.3 = (bf16[1024,1024]{1,0:T(8,128)(2,1)S(1)}, bf16[1024,1024]{1,0:T(8,128)(2,1)}, u32[]{:S(2)}) copy-start(bf16[1024,1024]{1,0:T(8,128)(2,1)} %param.9) | copy-start | bytes 6291460
  51.6 42.1 %all-to-all-start.1 = ((bf16[3,24,8,4,256]{4,2,1,0,3:T(8,128)(2,1)}), bf16[3,24,8,4,256]{4,2,1,0,3:T(8,128)(2,1)S(1)}, u32[]{:S(2)}, u32[]{:S(2)}) async-start(bf16[3,24,8,4,256]{4,2,1,0,3:T(8,128)(2,1)} %copy.9), calls=%async_computation.1 | async-start | bytes 2359296 | tf_op jit(solution)/shard_map/all_to_all | solution.py:174
  56.0 28.1 %collective-permute-start.2 = (f32[2,3,4,32,256]{4,3,2,1,0:T(8,128)}, f32[2,3,4,32,256]{4,3,2,1,0:T(8,128)}, u32[]{:S(2)}, u32[]{:S(2)}) collective-permute-start(f32[2,3,4,32,256]{4,3,2,1,0:T(8,128)} %pad_maximum_fusion), channel_id=1, source_target_pairs={{124,128},{252,0},{125,129},{253,1},{126,130},{254,2},{127,131},{2... | collective-permute-start | bytes 2359304 | tf_op jit(solution)/shard_map/ppermute | solution.py:26
  57.3 28.6 %collective-permute-start.3 = (f32[2,3,4,32,256]{4,3,2,1,0:T(8,128)}, f32[2,3,4,32,256]{4,3,2,1,0:T(8,128)}, u32[]{:S(2)}, u32[]{:S(2)}) collective-permute-start(f32[2,3,4,32,256]{4,3,2,1,0:T(8,128)} %pad_maximum_fusion.1), channel_id=1, source_target_pairs={{128,124},{0,252},{129,125},{1,253},{130,126},{2,254},{131,127},{3... | collective-permute-start | bytes 2359304 | tf_op jit(solution)/shard_map/ppermute | solution.py:26

commit v8 on v7

--- a/solution.py
+++ b/solution.py
@@ -157,8 +157,7 @@
     lines, partial, tails, heads, tail_cells, head_cells = lax.optimization_barrier(
         (lines, partial, tails, heads, tail_cells, head_cells)
     )
-    far_tails = ring_shift(tail_cells, "gx", True, far, True)
-    far_heads = ring_shift(head_cells, "gx", False, far, True)
+    far_tails, far_heads = far_exchange(tail_cells, head_cells, far)
     lines = lines.reshape(2 * comps, cells, part, total_rows)
     base_lines = lines[:comps]
     adj_lines = lines[comps:]
@@ -181,6 +180,31 @@
     return jnp.where(interior, updated, jnp.float32(0.0))
 
 
+def far_exchange(tail_cells, head_cells, far):
+    count = lax.axis_size("gx")
+    links = [i for i in range(count) if far[i]]
+    tail_senders = set(links)
+    head_senders = {(i + 1) % count for i in links}
+    if not links:
+        return jnp.zeros_like(tail_cells), jnp.zeros_like(head_cells)
+    if tail_senders & head_senders:
+        return (
+            ring_shift(tail_cells, "gx", True, far, True),
+            ring_shift(head_cells, "gx", False, far, True),
+        )
+    pairs = [(i, (i + 1) % count) for i in links] + [((i + 1) % count, i) for i in links]
+    position = lax.axis_index("gx")
+    sends_tail = jnp.zeros((), jnp.bool_)
+    for i in links:
+        sends_tail = sends_tail | (position == i)
+    received = lax.ppermute(jnp.where(sends_tail, tail_cells, head_cells), "gx", pairs)
+    zero = jnp.zeros_like(received)
+    gets_tail = jnp.zeros((), jnp.bool_)
+    for i in links:
+        gets_tail = gets_tail | (position == (i + 1) % count)
+    return jnp.where(gets_tail, received, zero), jnp.where(sends_tail, received, zero)
+
+
 def far_links(mesh):
     devices = mesh.devices
     count = devices.shape[0]

time: 97.9 us -> 88.6 us (0.905)
  waiting for transfers between devices: 27.3 us -> 18.9 us
  other arithmetic: 7.65 us -> 11.5 us
  starting transfers between devices: 28.9 us -> 25.8 us
  local copies, waits for them, and re-layouts: 11.2 us -> 9.7 us
    ppermute x4 -> x2, waiting for transfers between devices: 16.3 us -> 0.01 us  [ring_shift(): return lax.ppermute(value, axis, pairs)]
    ppermute x4 -> x2, starting transfers between devices: 16.8 us -> 4.03 us  [ring_shift(): return lax.ppermute(value, axis, pairs)]
    ppermute x0 -> x1, starting transfers between devices: none -> 9.33 us  [far_exchange(): lax.ppermute(jnp.where(sends_tail, tail_cells, head_cells), 'gx', pairs)]
    ppermute x0 -> x1, waiting for transfers between devices: none -> 6.54 us  [far_exchange(): lax.ppermute(jnp.where(sends_tail, tail_cells, head_cells), 'gx', pairs)]
    select_n x0 -> x2, other arithmetic: none -> 4.78 us  [the longest x1 2.49 us: far_exchange(): jnp.where(sends_tail, received, zero)]
    unnamed x10 -> x8, local copies, waits for them, and re-layouts: 5.89 us -> 4.35 us
    all_to_all x1, waiting for transfers between devices: 0.01 us -> 1.25 us  [body(): lax.all_to_all(wall_part, 'gy', split_axis=3, concat_axis=2, tiled=True)]
  transfers between devices with their start and end apart: 6 -> 5, of which waited for: 3 -> 3; matrix products, arithmetic and copies ran while one was open for 6% -> 15% of each run, Pallas kernels for 18% -> 20%
where the time goes in v8:
time: 88.6 us; the launch traced here: 88.1 us
  starting transfers between devices  25.8 us (29%)
  waiting for transfers between devices  18.9 us (21%)
  Pallas kernels  17.8 us (20%)
  other arithmetic  11.5 us (13%)
  local copies, waits for them, and re-layouts  9.7 us (11%)
  matrix products  4.33 us (5%)
    all_to_all x1, waiting for transfers between devices, body(): lines = lax.all_to_all(low, 'gy', split_axis=2, concat_axis=3, tiled=True)  11.1 us
    pallas_call x1, Pallas kernels, interior_update(): pl.pallas_call(interior_kernel, grid=(rows // LANES, cells // HALO - 2),...  10 us
    ppermute x1, starting transfers between devices, far_exchange(): lax.ppermute(jnp.where(sends_tail, tail_cells, head_cells), 'gx', pairs)  9.33 us
    pallas_call x1, Pallas kernels, boundary_update(): pl.pallas_call(boundary_kernel, grid=(2,), in_specs=[full_spec, full_spec...  7.76 us
    all_to_all x1, starting transfers between devices, body(): lines = lax.all_to_all(low, 'gy', split_axis=2, concat_axis=3, tiled=True)  7.65 us
    ppermute x1, waiting for transfers between devices, far_exchange(): lax.ppermute(jnp.where(sends_tail, tail_cells, head_cells), 'gx', pairs)  6.54 us
    all_to_all x1, starting transfers between devices, body(): lax.all_to_all(wall_part, 'gy', split_axis=3, concat_axis=2, tiled=True)  4.74 us
    unnamed x8, local copies, waits for them, and re-layouts  4.35 us
  transfers between devices with their start and end apart: 5, of which 3 were waited for; matrix products, arithmetic and copies ran while one was open for 15% of the time, Pallas kernels for 20%

profile of v8, /device:TPU:1, one launch (start us, length us, event | category | flops | bytes accessed | tf_op | source)
XLA Modules:
  0.0 88.1 jit_solution(12522771730444204360)
XLA Ops:
  0.0 0.0 copy-start
  0.0 0.0 copy-start.1
  0.0 3.1 %copy.18 = bf16[3,24,32,256]{3,1,0,2:T(8,128)(2,1)S(1)} copy(f32[3,24,32,256]{3,2,1,0:T(8,128)} %base_ref.3) | data formatting | bytes 3538944 | tf_op args[0]
  3.1 0.0 copy-done.1
  3.1 1.3 %copy.17 = bf16[3,24,32,256]{3,1,0,2:T(8,128)(2,1)S(1)} copy(f32[3,24,32,256]{3,2,1,0:T(8,128)S(1)} %copy-done.1) | data formatting | bytes 3538944 | tf_op args[1]
  4.4 1.6 %maximum_bitcast_fusion = bf16[6,24,32,1,256]{4,1,0,3,2:T(8,128)(2,1)} fusion(bf16[3,24,32,256]{3,1,0,2:T(8,128)(2,1)S(1)} %copy.17, bf16[3,24,32,256]{3,1,0,2:T(8,128)(2,1)S(1)} %copy.18), kind=kLoop, calls=%fused_computation | loop fusion | flops 1179648 | bytes 4718592 | tf_op jit(solution)/shard_map/reshape | solution.py:150
  6.0 7.6 %all-to-all-start = ((bf16[6,24,32,1,256]{4,1,0,3,2:T(8,128)(2,1)}), bf16[6,24,32,1,256]{4,1,0,3,2:T(8,128)(2,1)}, u32[]{:S(2)}, u32[]{:S(2)}) async-start(bf16[6,24,32,1,256]{4,1,0,3,2:T(8,128)(2,1)} %maximum_bitcast_fusion), calls=%async_computation | async-start | bytes 4718592 | tf_op jit(solution)/shard_map/all_to_all | solution.py:151
  13.6 1.5 %slice_bitcast_fusion = (f32[1,3,4,32,256]{4,3,2,1,0:T(8,128)S(1)}, f32[1,3,4,32,256]{4,3,2,1,0:T(8,128)S(1)}, f32[1,3,4,32,256]{4,3,2,1,0:T(8,128)S(1)}, f32[1,3,4,32,256]{4,3,2,1,0:T(8,128)S(1)}) fusion(f32[3,24,32,256]{3,2,1,0:T(8,128)} %adj_ref.3, f32[3,24,32,256]{3,2,1,0:T(8,128)} %base_ref.3), kind=kLoop, calls=%fused_computation.21 | loop fusion | bytes 3145728 | tf_op jit(solution)/shard_map/stack | solution.py:153
  15.1 0.1 pad_maximum_fusion
  15.2 2.8 %collective-permute-start = (f32[2,3,4,32,256]{4,3,2,1,0:T(8,128)S(1)}, f32[2,3,4,32,256]{4,3,2,1,0:T(8,128)}, u32[]{:S(2)}, u32[]{:S(2)}) collective-permute-start(f32[2,3,4,32,256]{4,3,2,1,0:T(8,128)S(1)} %pad_maximum_fusion), channel_id=1, source_target_pairs={{0,4},{4,8},{8,12},{12,16},{16,20},{20,24},{24,28},{28,32},{32,36}... | collective-permute-start | bytes 2359304 | tf_op jit(solution)/shard_map/ppermute | solution.py:26
  17.9 1.0 %pad_maximum_fusion.1 = f32[2,3,4,32,256]{4,3,2,1,0:T(8,128)} fusion(f32[1,3,4,32,256]{4,3,2,1,0:T(8,128)S(1)} %get-tuple-element.37, f32[1,3,4,32,256]{4,3,2,1,0:T(8,128)S(1)} %get-tuple-element.42), kind=kLoop, calls=%fused_computation.18 | loop fusion | flops 196608 | bytes 1572864 | tf_op jit(solution)/shard_map/stack | solution.py:153
  18.9 1.3 %collective-permute-start.1 = (f32[2,3,4,32,256]{4,3,2,1,0:T(8,128)}, f32[2,3,4,32,256]{4,3,2,1,0:T(8,128)}, u32[]{:S(2)}, u32[]{:S(2)}) collective-permute-start(f32[2,3,4,32,256]{4,3,2,1,0:T(8,128)} %pad_maximum_fusion.1), channel_id=1, source_target_pairs={{4,0},{8,4},{12,8},{16,12},{20,16},{24,20},{28,24},{32,28},{36,32}... | collective-permute-start | bytes 2359304 | tf_op jit(solution)/shard_map/ppermute | solution.py:26
  20.2 10.0 %shard_map.46.prev_ref = f32[3,24,32,256]{3,2,1,0:T(8,128)} custom-call(f32[3,24,32,256]{3,2,1,0:T(8,128)} %base_ref.3, f32[3,24,32,256]{3,2,1,0:T(8,128)} %adj_ref.3), custom_call_target="tpu_custom_call" | custom-call | tf_op jit(solution)/shard_map/pallas_call | solution.py:89
  30.2 11.1 %all-to-all-done = bf16[6,24,32,1,256]{4,1,0,3,2:T(8,128)(2,1)} async-done(((bf16[6,24,32,1,256]{4,1,0,3,2:T(8,128)(2,1)}), bf16[6,24,32,1,256]{4,1,0,3,2:T(8,128)(2,1)}, u32[]{:S(2)}, u32[]{:S(2)}) %all-to-all-start) | async-done | bytes 2359328 | tf_op jit(solution)/shard_map/all_to_all | solution.py:151
  41.2 2.5 %copy.19 = bf16[6,24,4,8,1,256]{5,3,2,1,0,4:T(8,128)(2,1)S(1)} copy(bf16[6,24,4,8,1,256]{5,1,0,3,2,4:T(8,128)(2,1)} %bitcast.1) | data formatting | bytes 4718592 | tf_op jit(solution)/shard_map/all_to_all | solution.py:151
  43.8 0.0 collective-permute-done.tail_ref
  43.8 0.0 collective-permute-done.1.head_ref
  43.8 0.2 fusion.12
  44.0 0.0 copy-start.2
  44.0 0.1 convert.1
  44.1 2.3 %broadcast_select_fusion.2 = f32[2,3,4,32,256]{4,3,2,1,0:T(8,128)} fusion(f32[2,3,4,32,256]{4,3,2,1,0:T(8,128)S(1)} %pad_maximum_fusion, f32[2,3,4,32,256]{4,3,2,1,0:T(8,128)} %pad_maximum_fusion.1, pred[]{:T(512)S(6)} %or.7), kind=kLoop, calls=%fused_computation.25 | loop fusion | flops 196608 | bytes 2359297 | tf_op jit(solution)/shard_map/jit(_where)/select_n | solution.py:200
  46.4 9.3 %collective-permute-start.2 = (f32[2,3,4,32,256]{4,3,2,1,0:T(8,128)}, f32[2,3,4,32,256]{4,3,2,1,0:T(8,128)}, u32[]{:S(2)}, u32[]{:S(2)}) collective-permute-start(f32[2,3,4,32,256]{4,3,2,1,0:T(8,128)} %broadcast_select_fusion.2), channel_id=1, source_target_pairs={{124,128},{252,0},{128,124},{0,252},{125,129},{253,1},{129,125},{1... | collective-permute-start | bytes 2359304 | tf_op jit(solution)/shard_map/ppermute | solution.py:200
  55.8 0.0 copy-done.2
  55.8 1.4 %fusion.1 = f32[3,24,8,1024]{3,2,1,0:T(8,128)S(1)} fusion(bf16[3,24,8,1024]{3,2,1,0:T(8,128)(2,1)S(1)} %bitcast.53, bf16[1024,1024]{1,0:T(8,128)(2,1)S(1)} %copy-done.2), kind=kOutput, calls=%fused_computation.9 | convolution fusion | flops 1207959552 | bytes 5636096 | tf_op jit(solution)/shard_map/fxzk,ik->fxzi/dot_general | solution.py:166
  57.2 0.0 copy-done
  57.2 1.5 %multiply_reduce_fusion = f32[24,8,1024]{2,1,0:T(8,128)S(1)} fusion(bf16[3,24,8,1024]{3,2,1,0:T(8,128)(2,1)S(1)} %bitcast.54, bf16[3,24,8,1024]{3,2,1,0:T(8,128)(2,1)S(1)} %bitcast.58, bf16[1024,1024]{1,0:T(8,128)(2,1)S(1)} %copy-done), kind=kOutput, calls=%fused_computation.7 | convolution fusion | flops 1209532416 | bytes 5242880 | tf_op jit(solution)/shard_map/fxzk,ik->fxzi/dot_general | solution.py:164
  58.7 1.5 %multiply_add_fusion = f32[3,24,8,1024]{3,2,1,0:T(8,128)S(1)} fusion(f32[3,24,8,1024]{3,2,1,0:T(8,128)S(1)} %fusion.1, bf16[3,24,8,1024]{3,2,1,0:T(8,128)(2,1)S(1)} %bitcast.55, bf16[1024,1024]{1,0:T(8,128)(2,1)S(1)} %copy-done, f32[24,8,1024]{2,1,0:T(8,128)S(1)} %convert.1), kind=kOutput, calls=%fused_computation.8 | convolution fusion | flops 1209729024 | bytes 8781824 | tf_op jit(solution)/shard_map/fxzk,ik->fxzi/dot_general | solution.py:165
  60.1 0.2 fusion.11
  60.4 0.2 convert_element_type.33
  60.6 1.1 %copy.9 = bf16[3,24,8,4,256]{4,2,1,0,3:T(8,128)(2,1)} copy(bf16[3,24,8,4,256]{4,2,3,1,0:T(8,128)(2,1)S(1)} %bitcast.56) | data formatting | bytes 2359296 | tf_op jit(solution)/shard_map/optimization_barrier | solution.py:172
  61.7 4.7 %all-to-all-start.1 = ((bf16[3,24,8,4,256]{4,2,1,0,3:T(8,128)(2,1)}), bf16[3,24,8,4,256]{4,2,1,0,3:T(8,128)(2,1)S(1)}, u32[]{:S(2)}, u32[]{:S(2)}) async-start(bf16[3,24,8,4,256]{4,2,1,0,3:T(8,128)(2,1)} %copy.9), calls=%async_computation.1 | async-start | bytes 2359296 | tf_op jit(solution)/shard_map/all_to_all | solution.py:173
  66.4 6.5 %collective-permute-done.2 = f32[2,3,4,32,256]{4,3,2,1,0:T(8,128)} collective-permute-done((f32[2,3,4,32,256]{4,3,2,1,0:T(8,128)}, f32[2,3,4,32,256]{4,3,2,1,0:T(8,128)}, u32[]{:S(2)}, u32[]{:S(2)}) %collective-permute-start.2) | collective-permute-done | bytes 786464 | tf_op jit(solution)/shard_map/ppermute | solution.py:200
  73.0 2.5 %broadcast_select_fusion = (f32[2,3,4,32,256]{4,3,2,1,0:T(8,128)}, f32[2,3,4,32,256]{4,3,2,1,0:T(8,128)}) fusion(f32[2,3,4,32,256]{4,3,2,1,0:T(8,128)} %collective-permute-done.2, pred[]{:T(512)S(6)} %or.7, pred[]{:T(512)S(6)} %or.6), kind=kLoop, calls=%fused_computation.19 | loop fusion | flops 393216 | bytes 2359298 | tf_op jit(solution)/shard_map/jit(_where)/select_n | solution.py:205
  75.5 7.8 %shard_map.47 = f32[3,24,32,256]{3,2,1,0:T(8,128)} custom-call(f32[3,24,32,256]{3,2,1,0:T(8,128)} %base_ref.3, f32[3,24,32,256]{3,2,1,0:T(8,128)} %adj_ref.3, f32[2,3,4,32,256]{4,3,2,1,0:T(8,128)} %collective-permute-done.tail_ref, f32[2,3,4,32,256]{4,3,2,1,0:T(8,128)} %collective-permute-done.1.head_ref, ...), custom_call_target="tpu_custom_call", output_to_operand_aliasing={{}: (6, {})} | custom-call | tf_op jit(solution)/shard_map/pallas_call | solution.py:131
  83.2 1.2 %all-to-all-done.1 = bf16[3,24,8,4,256]{4,2,1,0,3:T(8,128)(2,1)S(1)} async-done(((bf16[3,24,8,4,256]{4,2,1,0,3:T(8,128)(2,1)}), bf16[3,24,8,4,256]{4,2,1,0,3:T(8,128)(2,1)S(1)}, u32[]{:S(2)}, u32[]{:S(2)}) %all-to-all-start.1) | async-done | bytes 1179680 | tf_op jit(solution)/shard_map/all_to_all | solution.py:173
  84.5 3.6 %fusion = f32[3,24,32,256]{3,2,1,0:T(8,128)} fusion(f32[3,24,32,256]{3,2,1,0:T(8,128)} %shard_map.47, pred[256]{0:T(512)(128)(4,1)S(1)} %compare_and_fusion, bf16[3,24,8,4,256]{4,2,1,0,3:T(8,128)(2,1)S(1)} %all-to-all-done.1), kind=kLoop, calls=%fused_computation.2 | loop fusion | flops 2359296 | bytes 5898496 | tf_op jit(solution)/shard_map/jit(_where)/select_n | solution.py:180
  (2 shorter events, 0.0 us)
Async XLA Ops:
  0.0 57.2 %copy-start = (bf16[1024,1024]{1,0:T(8,128)(2,1)S(1)}, bf16[1024,1024]{1,0:T(8,128)(2,1)}, u32[]{:S(2)}) copy-start(bf16[1024,1024]{1,0:T(8,128)(2,1)} %param.8) | copy-start | bytes 6291460
  0.0 3.1 %copy-start.1 = (f32[3,24,32,256]{3,2,1,0:T(8,128)S(1)}, f32[3,24,32,256]{3,2,1,0:T(8,128)}, u32[]{:S(2)}) copy-start(f32[3,24,32,256]{3,2,1,0:T(8,128)} %adj_ref.3) | copy-start | bytes 7077892
  6.0 35.3 %all-to-all-start = ((bf16[6,24,32,1,256]{4,1,0,3,2:T(8,128)(2,1)}), bf16[6,24,32,1,256]{4,1,0,3,2:T(8,128)(2,1)}, u32[]{:S(2)}, u32[]{:S(2)}) async-start(bf16[6,24,32,1,256]{4,1,0,3,2:T(8,128)(2,1)} %maximum_bitcast_fusion), calls=%async_computation | async-start | bytes 4718592 | tf_op jit(solution)/shard_map/all_to_all | solution.py:151
  15.2 28.6 %collective-permute-start = (f32[2,3,4,32,256]{4,3,2,1,0:T(8,128)S(1)}, f32[2,3,4,32,256]{4,3,2,1,0:T(8,128)}, u32[]{:S(2)}, u32[]{:S(2)}) collective-permute-start(f32[2,3,4,32,256]{4,3,2,1,0:T(8,128)S(1)} %pad_maximum_fusion), channel_id=1, source_target_pairs={{0,4},{4,8},{8,12},{12,16},{16,20},{20,24},{24,28},{28,32},{32,36}... | collective-permute-start | bytes 2359304 | tf_op jit(solution)/shard_map/ppermute | solution.py:26
  18.9 24.9 %collective-permute-start.1 = (f32[2,3,4,32,256]{4,3,2,1,0:T(8,128)}, f32[2,3,4,32,256]{4,3,2,1,0:T(8,128)}, u32[]{:S(2)}, u32[]{:S(2)}) collective-permute-start(f32[2,3,4,32,256]{4,3,2,1,0:T(8,128)} %pad_maximum_fusion.1), channel_id=1, source_target_pairs={{4,0},{8,4},{12,8},{16,12},{20,16},{24,20},{28,24},{32,28},{36,32}... | collective-permute-start | bytes 2359304 | tf_op jit(solution)/shard_map/ppermute | solution.py:26
  44.0 11.7 %copy-start.2 = (bf16[1024,1024]{1,0:T(8,128)(2,1)S(1)}, bf16[1024,1024]{1,0:T(8,128)(2,1)}, u32[]{:S(2)}) copy-start(bf16[1024,1024]{1,0:T(8,128)(2,1)} %param.9) | copy-start | bytes 6291460
  46.4 26.6 %collective-permute-start.2 = (f32[2,3,4,32,256]{4,3,2,1,0:T(8,128)}, f32[2,3,4,32,256]{4,3,2,1,0:T(8,128)}, u32[]{:S(2)}, u32[]{:S(2)}) collective-permute-start(f32[2,3,4,32,256]{4,3,2,1,0:T(8,128)} %broadcast_select_fusion.2), channel_id=1, source_target_pairs={{124,128},{252,0},{128,124},{0,252},{125,129},{253,1},{129,125},{1... | collective-permute-start | bytes 2359304 | tf_op jit(solution)/shard_map/ppermute | solution.py:200
  61.7 22.8 %all-to-all-start.1 = ((bf16[3,24,8,4,256]{4,2,1,0,3:T(8,128)(2,1)}), bf16[3,24,8,4,256]{4,2,1,0,3:T(8,128)(2,1)S(1)}, u32[]{:S(2)}, u32[]{:S(2)}) async-start(bf16[3,24,8,4,256]{4,2,1,0,3:T(8,128)(2,1)} %copy.9), calls=%async_computation.1 | async-start | bytes 2359296 | tf_op jit(solution)/shard_map/all_to_all | solution.py:173

commit v9 on v7

--- a/solution.py
+++ b/solution.py
@@ -95,7 +95,7 @@
     )(base_flow, adjoint)
 
 
-def boundary_kernel(base_ref, adj_ref, tail_ref, head_ref, far_tail_ref, far_head_ref, prev_ref, out_ref, ext_ref):
+def boundary_kernel(flag_ref, base_ref, adj_ref, tail_ref, head_ref, far_ref, prev_ref, out_ref, ext_ref):
     comps, cells, span, rows = base_ref.shape
     side = pl.program_id(0)
 
@@ -103,8 +103,16 @@
     def _():
         ext_ref[0, :, HALO : HALO + cells] = base_ref[...]
         ext_ref[1, :, HALO : HALO + cells] = adj_ref[...]
-        ext_ref[:, :, :HALO] = tail_ref[...] + far_tail_ref[...]
-        ext_ref[:, :, HALO + cells :] = head_ref[...] + far_head_ref[...]
+        ext_ref[:, :, :HALO] = tail_ref[...]
+        ext_ref[:, :, HALO + cells :] = head_ref[...]
+
+        @pl.when(flag_ref[0] == 1)
+        def _():
+            ext_ref[:, :, :HALO] = far_ref[...]
+
+        @pl.when(flag_ref[1] == 1)
+        def _():
+            ext_ref[:, :, HALO + cells :] = far_ref[...]
 
     first = side * (cells - HALO)
     for lane in range(rows // LANES):
@@ -123,7 +131,7 @@
         lax.fori_loop(0, HALO, step, 0)
 
 
-def boundary_update(base_flow, adjoint, tails, heads, far_tails, far_heads, previous):
+def boundary_update(base_flow, adjoint, tails, heads, far_cells, far_flags, previous):
     comps, cells, span, rows = base_flow.shape
     full_spec = pl.BlockSpec((comps, cells, span, rows), lambda s: (0, 0, 0, 0))
     halo_spec = pl.BlockSpec((2, comps, HALO, span, rows), lambda s: (0, 0, 0, 0, 0))
@@ -131,12 +139,20 @@
     return pl.pallas_call(
         boundary_kernel,
         grid=(2,),
-        in_specs=[full_spec, full_spec, halo_spec, halo_spec, halo_spec, halo_spec, pl.BlockSpec(memory_space=pl.ANY)],
+        in_specs=[
+            pl.BlockSpec(memory_space=pltpu.SMEM),
+            full_spec,
+            full_spec,
+            halo_spec,
+            halo_spec,
+            halo_spec,
+            pl.BlockSpec(memory_space=pl.ANY),
+        ],
         out_specs=out_spec,
         out_shape=jax.ShapeDtypeStruct(base_flow.shape, jnp.float32),
         scratch_shapes=[pltpu.VMEM((2, comps, cells + 2 * HALO, span, rows), jnp.float32)],
         input_output_aliases={6: 0},
-    )(base_flow, adjoint, tails, heads, far_tails, far_heads, previous)
+    )(far_flags, base_flow, adjoint, tails, heads, far_cells, previous)
 
 
 def body(base_flow, adjoint, first_op, second_op, far=()):
@@ -157,8 +173,7 @@
     lines, partial, tails, heads, tail_cells, head_cells = lax.optimization_barrier(
         (lines, partial, tails, heads, tail_cells, head_cells)
     )
-    far_tails = ring_shift(tail_cells, "gx", True, far, True)
-    far_heads = ring_shift(head_cells, "gx", False, far, True)
+    far_cells, far_flags = far_exchange(tail_cells, head_cells, far)
     lines = lines.reshape(2 * comps, cells, part, total_rows)
     base_lines = lines[:comps]
     adj_lines = lines[comps:]
@@ -174,11 +189,29 @@
     wall_part = lax.all_to_all(wall_part, "gy", split_axis=3, concat_axis=2, tiled=True)
     wall_part = wall_part.reshape(comps, cells, spanwise, local_rows).astype(jnp.float32)
 
-    partial = boundary_update(base_flow, adjoint, tails, heads, far_tails, far_heads, partial)
+    partial = boundary_update(base_flow, adjoint, tails, heads, far_cells, far_flags, partial)
     updated = partial + STEP_WEIGHT * wall_part
     wall_index = lax.axis_index("gy") * local_rows + jnp.arange(local_rows, dtype=jnp.int32)
     interior = (wall_index > 0) & (wall_index < total_rows - 1)
     return jnp.where(interior, updated, jnp.float32(0.0))
+
+
+def far_exchange(tail_cells, head_cells, far):
+    count = lax.axis_size("gx")
+    links = [i for i in range(count) if far[i]]
+    tail_senders = {i for i in links}
+    head_senders = {(i + 1) % count for i in links}
+    assert links and not (tail_senders & head_senders)
+    pairs = [(i, (i + 1) % count) for i in links] + [((i + 1) % count, i) for i in links]
+    position = lax.axis_index("gx")
+    sends_tail = jnp.zeros((), jnp.bool_)
+    gets_tail = jnp.zeros((), jnp.bool_)
+    for i in links:
+        sends_tail = sends_tail | (position == i)
+        gets_tail = gets_tail | (position == (i + 1) % count)
+    received = lax.ppermute(jnp.where(sends_tail, tail_cells, head_cells), "gx", pairs)
+    flags = jnp.stack((gets_tail, sends_tail)).astype(jnp.int32)
+    return received, flags
 
 
 def far_links(mesh):

time: 97.9 us -> 98.5 us (level)
  starting transfers between devices: 28.9 us -> 26.7 us
  other arithmetic: 7.65 us -> 9.53 us
  waiting for transfers between devices: 27.3 us -> 28.6 us
    ppermute x0 -> x1, waiting for transfers between devices: none -> 17.5 us  [far_exchange(): lax.ppermute(jnp.where(sends_tail, tail_cells, head_cells), 'gx', pairs)]
    ppermute x4 -> x2, waiting for transfers between devices: 16.3 us -> 0.01 us  [ring_shift(): return lax.ppermute(value, axis, pairs)]
    ppermute x4 -> x2, starting transfers between devices: 16.8 us -> 4.03 us  [ring_shift(): return lax.ppermute(value, axis, pairs)]
    ppermute x0 -> x1, starting transfers between devices: none -> 10.6 us  [far_exchange(): lax.ppermute(jnp.where(sends_tail, tail_cells, head_cells), 'gx', pairs)]
    select_n x0 -> x1, other arithmetic: none -> 2.16 us  [far_exchange(): jnp.where(sends_tail, tail_cells, head_cells)]
  transfers between devices with their start and end apart: 6 -> 5, of which waited for: 3 -> 2; matrix products, arithmetic and copies ran while one was open for 6% -> 8% of each run, Pallas kernels for 18% -> 18%
where the time goes in v9:
time: 98.5 us; the launch traced here: 97.9 us
  waiting for transfers between devices  28.6 us (29%)
  starting transfers between devices  26.7 us (27%)
  Pallas kernels  17.6 us (18%)
  local copies, waits for them, and re-layouts  11 us (11%)
  other arithmetic  9.53 us (10%)
  matrix products  4.32 us (4%)
    ppermute x1, waiting for transfers between devices, far_exchange(): lax.ppermute(jnp.where(sends_tail, tail_cells, head_cells), 'gx', pairs)  17.5 us
    all_to_all x1, waiting for transfers between devices, body(): lines = lax.all_to_all(low, 'gy', split_axis=2, concat_axis=3, tiled=True)  11.1 us
    ppermute x1, starting transfers between devices, far_exchange(): lax.ppermute(jnp.where(sends_tail, tail_cells, head_cells), 'gx', pairs)  10.6 us
    pallas_call x1, Pallas kernels, interior_update(): pl.pallas_call(interior_kernel, grid=(rows // LANES, cells // HALO - 2),...  10 us
    all_to_all x1, starting transfers between devices, body(): lines = lax.all_to_all(low, 'gy', split_axis=2, concat_axis=3, tiled=True)  7.65 us
    pallas_call x1, Pallas kernels, boundary_update(): pl.pallas_call(boundary_kernel, grid=(2,), in_specs=[pl.BlockSpec(memory_...  7.55 us
    unnamed x10, local copies, waits for them, and re-layouts  5.64 us
    all_to_all x1, starting transfers between devices, body(): lax.all_to_all(wall_part, 'gy', split_axis=3, concat_axis=2, tiled=True)  4.47 us
  transfers between devices with their start and end apart: 5, of which 2 were waited for; matrix products, arithmetic and copies ran while one was open for 8% of the time, Pallas kernels for 18%

profile of v9, /device:TPU:1, one launch (start us, length us, event | category | flops | bytes accessed | tf_op | source)
XLA Modules:
  0.0 97.9 jit_solution(3257876624612700405)
XLA Ops:
  0.0 0.0 copy-start
  0.0 0.0 copy-start.1
  0.0 3.1 %copy.18 = bf16[3,24,32,256]{3,1,0,2:T(8,128)(2,1)S(1)} copy(f32[3,24,32,256]{3,2,1,0:T(8,128)} %base_ref.3) | data formatting | bytes 3538944 | tf_op args[0]
  3.1 0.0 copy-done.1
  3.1 1.3 %copy.17 = bf16[3,24,32,256]{3,1,0,2:T(8,128)(2,1)S(1)} copy(f32[3,24,32,256]{3,2,1,0:T(8,128)S(1)} %copy-done.1) | data formatting | bytes 3538944 | tf_op args[1]
  4.4 1.6 %maximum_bitcast_fusion = bf16[6,24,32,1,256]{4,1,0,3,2:T(8,128)(2,1)} fusion(bf16[3,24,32,256]{3,1,0,2:T(8,128)(2,1)S(1)} %copy.17, bf16[3,24,32,256]{3,1,0,2:T(8,128)(2,1)S(1)} %copy.18), kind=kLoop, calls=%fused_computation | loop fusion | flops 1179648 | bytes 4718592 | tf_op jit(solution)/shard_map/reshape | solution.py:166
  6.0 7.6 %all-to-all-start = ((bf16[6,24,32,1,256]{4,1,0,3,2:T(8,128)(2,1)}), bf16[6,24,32,1,256]{4,1,0,3,2:T(8,128)(2,1)}, u32[]{:S(2)}, u32[]{:S(2)}) async-start(bf16[6,24,32,1,256]{4,1,0,3,2:T(8,128)(2,1)} %maximum_bitcast_fusion), calls=%async_computation | async-start | bytes 4718592 | tf_op jit(solution)/shard_map/all_to_all | solution.py:167
  13.6 1.5 %slice_bitcast_fusion = (f32[1,3,4,32,256]{4,3,2,1,0:T(8,128)S(1)}, f32[1,3,4,32,256]{4,3,2,1,0:T(8,128)S(1)}, f32[1,3,4,32,256]{4,3,2,1,0:T(8,128)S(1)}, f32[1,3,4,32,256]{4,3,2,1,0:T(8,128)S(1)}) fusion(f32[3,24,32,256]{3,2,1,0:T(8,128)} %adj_ref.3, f32[3,24,32,256]{3,2,1,0:T(8,128)} %base_ref.3), kind=kLoop, calls=%fused_computation.19 | loop fusion | bytes 3145728 | tf_op jit(solution)/shard_map/stack | solution.py:169
  15.1 0.1 pad_maximum_fusion
  15.2 0.0 copy-start.2
  15.2 2.8 %collective-permute-start = (f32[2,3,4,32,256]{4,3,2,1,0:T(8,128)S(1)}, f32[2,3,4,32,256]{4,3,2,1,0:T(8,128)}, u32[]{:S(2)}, u32[]{:S(2)}) collective-permute-start(f32[2,3,4,32,256]{4,3,2,1,0:T(8,128)S(1)} %pad_maximum_fusion), channel_id=1, source_target_pairs={{0,4},{4,8},{8,12},{12,16},{16,20},{20,24},{24,28},{28,32},{32,36}... | collective-permute-start | bytes 2359304 | tf_op jit(solution)/shard_map/ppermute | solution.py:26
  17.9 1.0 pad_maximum_fusion.1
  18.9 1.3 %collective-permute-start.1 = (f32[2,3,4,32,256]{4,3,2,1,0:T(8,128)}, f32[2,3,4,32,256]{4,3,2,1,0:T(8,128)}, u32[]{:S(2)}, u32[]{:S(2)}) collective-permute-start(f32[2,3,4,32,256]{4,3,2,1,0:T(8,128)} %pad_maximum_fusion.1), channel_id=1, source_target_pairs={{4,0},{8,4},{12,8},{16,12},{20,16},{24,20},{28,24},{32,28},{36,32}... | collective-permute-start | bytes 2359304 | tf_op jit(solution)/shard_map/ppermute | solution.py:26
  20.2 10.0 %shard_map.46.prev_ref = f32[3,24,32,256]{3,2,1,0:T(8,128)} custom-call(f32[3,24,32,256]{3,2,1,0:T(8,128)} %base_ref.3, f32[3,24,32,256]{3,2,1,0:T(8,128)} %adj_ref.3), custom_call_target="tpu_custom_call" | custom-call | tf_op jit(solution)/shard_map/pallas_call | solution.py:89
  30.2 0.0 copy-done.2
  30.2 11.1 %all-to-all-done = bf16[6,24,32,1,256]{4,1,0,3,2:T(8,128)(2,1)} async-done(((bf16[6,24,32,1,256]{4,1,0,3,2:T(8,128)(2,1)}), bf16[6,24,32,1,256]{4,1,0,3,2:T(8,128)(2,1)}, u32[]{:S(2)}, u32[]{:S(2)}) %all-to-all-start) | async-done | bytes 2359328 | tf_op jit(solution)/shard_map/all_to_all | solution.py:167
  41.2 2.5 %copy.19 = bf16[6,24,4,8,1,256]{5,3,2,1,0,4:T(8,128)(2,1)S(1)} copy(bf16[6,24,4,8,1,256]{5,1,0,3,2,4:T(8,128)(2,1)} %bitcast.3) | data formatting | bytes 4718592 | tf_op jit(solution)/shard_map/all_to_all | solution.py:167
  43.8 0.0 collective-permute-done.tail_ref
  43.8 0.0 collective-permute-done.1.head_ref
  43.8 0.0 copy-start.3
  43.8 0.2 fusion.12
  44.0 0.1 convert.1
  44.1 1.3 %copy-done.3 = bf16[1024,1024]{1,0:T(8,128)(2,1)S(1)} copy-done((bf16[1024,1024]{1,0:T(8,128)(2,1)S(1)}, bf16[1024,1024]{1,0:T(8,128)(2,1)}, u32[]{:S(2)}) %copy-start.3) | copy-done | bytes 2097176
  45.4 1.4 %fusion.1 = f32[3,24,8,1024]{3,2,1,0:T(8,128)S(1)} fusion(bf16[3,24,8,1024]{3,2,1,0:T(8,128)(2,1)S(1)} %bitcast.55, bf16[1024,1024]{1,0:T(8,128)(2,1)S(1)} %copy-done.3), kind=kOutput, calls=%fused_computation.9 | convolution fusion | flops 1207959552 | bytes 5636096 | tf_op jit(solution)/shard_map/fxzk,ik->fxzi/dot_general | solution.py:182
  46.8 0.0 copy-done
  46.9 1.4 %multiply_reduce_fusion = f32[24,8,1024]{2,1,0:T(8,128)S(1)} fusion(bf16[3,24,8,1024]{3,2,1,0:T(8,128)(2,1)S(1)} %bitcast.56, bf16[3,24,8,1024]{3,2,1,0:T(8,128)(2,1)S(1)} %bitcast.60, bf16[1024,1024]{1,0:T(8,128)(2,1)S(1)} %copy-done), kind=kOutput, calls=%fused_computation.7 | convolution fusion | flops 1209532416 | bytes 5242880 | tf_op jit(solution)/shard_map/fxzk,ik->fxzi/dot_general | solution.py:180
  48.3 1.5 %multiply_add_fusion = f32[3,24,8,1024]{3,2,1,0:T(8,128)S(1)} fusion(f32[3,24,8,1024]{3,2,1,0:T(8,128)S(1)} %fusion.1, bf16[3,24,8,1024]{3,2,1,0:T(8,128)(2,1)S(1)} %bitcast.57, bf16[1024,1024]{1,0:T(8,128)(2,1)S(1)} %copy-done, f32[24,8,1024]{2,1,0:T(8,128)S(1)} %convert.1), kind=kOutput, calls=%fused_computation.8 | convolution fusion | flops 1209729024 | bytes 8781824 | tf_op jit(solution)/shard_map/fxzk,ik->fxzi/dot_general | solution.py:181
  49.8 0.2 fusion.11
  50.0 0.2 convert_element_type.37
  50.2 1.1 %copy.9 = bf16[3,24,8,4,256]{4,2,1,0,3:T(8,128)(2,1)} copy(bf16[3,24,8,4,256]{4,2,3,1,0:T(8,128)(2,1)S(1)} %bitcast.58) | data formatting | bytes 2359296 | tf_op jit(solution)/shard_map/optimization_barrier | solution.py:188
  51.3 4.5 %all-to-all-start.1 = ((bf16[3,24,8,4,256]{4,2,1,0,3:T(8,128)(2,1)}), bf16[3,24,8,4,256]{4,2,1,0,3:T(8,128)(2,1)S(1)}, u32[]{:S(2)}, u32[]{:S(2)}) async-start(bf16[3,24,8,4,256]{4,2,1,0,3:T(8,128)(2,1)} %copy.9), calls=%async_computation.1 | async-start | bytes 2359296 | tf_op jit(solution)/shard_map/all_to_all | solution.py:189
  55.8 2.2 %broadcast_select_fusion = f32[2,3,4,32,256]{4,3,2,1,0:T(8,128)} fusion(f32[2,3,4,32,256]{4,3,2,1,0:T(8,128)} %copy-done.2, f32[2,3,4,32,256]{4,3,2,1,0:T(8,128)} %pad_maximum_fusion.1, pred[]{:T(512)} %or.7), kind=kLoop, calls=%fused_computation.23 | loop fusion | flops 196608 | bytes 2359297 | tf_op jit(solution)/shard_map/jit(_where)/select_n | solution.py:212
  58.0 10.6 %collective-permute-start.2 = (f32[2,3,4,32,256]{4,3,2,1,0:T(8,128)}, f32[2,3,4,32,256]{4,3,2,1,0:T(8,128)}, u32[]{:S(2)}, u32[]{:S(2)}) collective-permute-start(f32[2,3,4,32,256]{4,3,2,1,0:T(8,128)} %broadcast_select_fusion), channel_id=1, source_target_pairs={{124,128},{252,0},{128,124},{0,252},{125,129},{253,1},{129,125},{1... | collective-permute-start | bytes 2359304 | tf_op jit(solution)/shard_map/ppermute | solution.py:212
  68.6 0.6 add_convert_fusion.flag_ref
  69.2 17.5 %collective-permute-done.2.far_ref = f32[2,3,4,32,256]{4,3,2,1,0:T(8,128)} collective-permute-done((f32[2,3,4,32,256]{4,3,2,1,0:T(8,128)}, f32[2,3,4,32,256]{4,3,2,1,0:T(8,128)}, u32[]{:S(2)}, u32[]{:S(2)}) %collective-permute-start.2) | collective-permute-done | bytes 786464 | tf_op jit(solution)/shard_map/ppermute | solution.py:212
  86.7 7.6 %shard_map.47 = f32[3,24,32,256]{3,2,1,0:T(8,128)} custom-call(s32[2]{0:T(128)} %add_convert_fusion.flag_ref, f32[3,24,32,256]{3,2,1,0:T(8,128)} %base_ref.3, f32[3,24,32,256]{3,2,1,0:T(8,128)} %adj_ref.3, f32[2,3,4,32,256]{4,3,2,1,0:T(8,128)} %collective-permute-done.tail_ref, ...), custom_call_target="tpu_custom_call", output_to_operand_aliasing={{}: (6, {})} | custom-call | tf_op jit(solution)/shard_map/pallas_call | solution.py:139
  94.3 0.0 all-to-all-done.1
  94.3 3.6 %fusion = f32[3,24,32,256]{3,2,1,0:T(8,128)} fusion(f32[3,24,32,256]{3,2,1,0:T(8,128)} %shard_map.47, pred[256]{0:T(512)(128)(4,1)S(1)} %compare_and_fusion, bf16[3,24,8,4,256]{4,2,1,0,3:T(8,128)(2,1)S(1)} %all-to-all-done.1), kind=kLoop, calls=%fused_computation.2 | loop fusion | flops 2359296 | bytes 5898496 | tf_op jit(solution)/shard_map/jit(_where)/select_n | solution.py:196
  (2 shorter events, 0.0 us)
Async XLA Ops:
  0.0 46.8 %copy-start = (bf16[1024,1024]{1,0:T(8,128)(2,1)S(1)}, bf16[1024,1024]{1,0:T(8,128)(2,1)}, u32[]{:S(2)}) copy-start(bf16[1024,1024]{1,0:T(8,128)(2,1)} %param.8) | copy-start | bytes 6291460
  0.0 3.1 %copy-start.1 = (f32[3,24,32,256]{3,2,1,0:T(8,128)S(1)}, f32[3,24,32,256]{3,2,1,0:T(8,128)}, u32[]{:S(2)}) copy-start(f32[3,24,32,256]{3,2,1,0:T(8,128)} %adj_ref.3) | copy-start | bytes 7077892
  6.0 35.3 %all-to-all-start = ((bf16[6,24,32,1,256]{4,1,0,3,2:T(8,128)(2,1)}), bf16[6,24,32,1,256]{4,1,0,3,2:T(8,128)(2,1)}, u32[]{:S(2)}, u32[]{:S(2)}) async-start(bf16[6,24,32,1,256]{4,1,0,3,2:T(8,128)(2,1)} %maximum_bitcast_fusion), calls=%async_computation | async-start | bytes 4718592 | tf_op jit(solution)/shard_map/all_to_all | solution.py:167
  15.2 15.0 %copy-start.2 = (f32[2,3,4,32,256]{4,3,2,1,0:T(8,128)}, f32[2,3,4,32,256]{4,3,2,1,0:T(8,128)S(1)}, u32[]{:S(2)}) copy-start(f32[2,3,4,32,256]{4,3,2,1,0:T(8,128)S(1)} %pad_maximum_fusion) | copy-start | bytes 2359300
  15.2 28.6 %collective-permute-start = (f32[2,3,4,32,256]{4,3,2,1,0:T(8,128)S(1)}, f32[2,3,4,32,256]{4,3,2,1,0:T(8,128)}, u32[]{:S(2)}, u32[]{:S(2)}) collective-permute-start(f32[2,3,4,32,256]{4,3,2,1,0:T(8,128)S(1)} %pad_maximum_fusion), channel_id=1, source_target_pairs={{0,4},{4,8},{8,12},{12,16},{16,20},{20,24},{24,28},{28,32},{32,36}... | collective-permute-start | bytes 2359304 | tf_op jit(solution)/shard_map/ppermute | solution.py:26
  18.9 24.9 %collective-permute-start.1 = (f32[2,3,4,32,256]{4,3,2,1,0:T(8,128)}, f32[2,3,4,32,256]{4,3,2,1,0:T(8,128)}, u32[]{:S(2)}, u32[]{:S(2)}) collective-permute-start(f32[2,3,4,32,256]{4,3,2,1,0:T(8,128)} %pad_maximum_fusion.1), channel_id=1, source_target_pairs={{4,0},{8,4},{12,8},{16,12},{20,16},{24,20},{28,24},{32,28},{36,32}... | collective-permute-start | bytes 2359304 | tf_op jit(solution)/shard_map/ppermute | solution.py:26
  43.8 1.6 %copy-start.3 = (bf16[1024,1024]{1,0:T(8,128)(2,1)S(1)}, bf16[1024,1024]{1,0:T(8,128)(2,1)}, u32[]{:S(2)}) copy-start(bf16[1024,1024]{1,0:T(8,128)(2,1)} %param.9) | copy-start | bytes 6291460
  51.3 43.0 %all-to-all-start.1 = ((bf16[3,24,8,4,256]{4,2,1,0,3:T(8,128)(2,1)}), bf16[3,24,8,4,256]{4,2,1,0,3:T(8,128)(2,1)S(1)}, u32[]{:S(2)}, u32[]{:S(2)}) async-start(bf16[3,24,8,4,256]{4,2,1,0,3:T(8,128)(2,1)} %copy.9), calls=%async_computation.1 | async-start | bytes 2359296 | tf_op jit(solution)/shard_map/all_to_all | solution.py:189
  58.0 28.8 %collective-permute-start.2 = (f32[2,3,4,32,256]{4,3,2,1,0:T(8,128)}, f32[2,3,4,32,256]{4,3,2,1,0:T(8,128)}, u32[]{:S(2)}, u32[]{:S(2)}) collective-permute-start(f32[2,3,4,32,256]{4,3,2,1,0:T(8,128)} %broadcast_select_fusion), channel_id=1, source_target_pairs={{124,128},{252,0},{128,124},{0,252},{125,129},{253,1},{129,125},{1... | collective-permute-start | bytes 2359304 | tf_op jit(solution)/shard_map/ppermute | solution.py:212

commit v10 on v7

--- a/solution.py
+++ b/solution.py
@@ -153,12 +153,14 @@
     head_cells = jnp.stack((base_flow[:, :HALO], adjoint[:, :HALO]), 0)
     tails = ring_shift(tail_cells, "gx", True, far, False)
     heads = ring_shift(head_cells, "gx", False, far, False)
+    far_pairs, sends_tail, gets_tail = far_plan(far)
+    far_send = jnp.where(sends_tail, tail_cells, head_cells)
     partial = interior_update(base_flow, adjoint)
-    lines, partial, tails, heads, tail_cells, head_cells = lax.optimization_barrier(
-        (lines, partial, tails, heads, tail_cells, head_cells)
-    )
-    far_tails = ring_shift(tail_cells, "gx", True, far, True)
-    far_heads = ring_shift(head_cells, "gx", False, far, True)
+    lines, partial, tails, heads, far_send = lax.optimization_barrier((lines, partial, tails, heads, far_send))
+    received = lax.ppermute(far_send, "gx", far_pairs)
+    zero = jnp.zeros_like(received)
+    far_tails = jnp.where(gets_tail, received, zero)
+    far_heads = jnp.where(sends_tail, received, zero)
     lines = lines.reshape(2 * comps, cells, part, total_rows)
     base_lines = lines[:comps]
     adj_lines = lines[comps:]
@@ -181,6 +183,22 @@
     return jnp.where(interior, updated, jnp.float32(0.0))
 
 
+def far_plan(far):
+    count = lax.axis_size("gx")
+    links = [i for i in range(count) if far[i]]
+    tail_senders = {i for i in links}
+    head_senders = {(i + 1) % count for i in links}
+    assert links and not (tail_senders & head_senders)
+    pairs = [(i, (i + 1) % count) for i in links] + [((i + 1) % count, i) for i in links]
+    position = lax.axis_index("gx")
+    sends_tail = jnp.zeros((), jnp.bool_)
+    gets_tail = jnp.zeros((), jnp.bool_)
+    for i in links:
+        sends_tail = sends_tail | (position == i)
+        gets_tail = gets_tail | (position == (i + 1) % count)
+    return pairs, sends_tail, gets_tail
+
+
 def far_links(mesh):
     devices = mesh.devices
     count = devices.shape[0]

time: 97.9 us -> 88 us (0.90)
  waiting for transfers between devices: 27.3 us -> 19 us
  starting transfers between devices: 28.9 us -> 26.2 us
  other arithmetic: 7.65 us -> 9.75 us
    ppermute x4 -> x2, waiting for transfers between devices: 16.3 us -> 0.01 us  [ring_shift(): return lax.ppermute(value, axis, pairs)]
    ppermute x4 -> x2, starting transfers between devices: 16.8 us -> 3.16 us  [ring_shift(): return lax.ppermute(value, axis, pairs)]
    ppermute x0 -> x1, starting transfers between devices: none -> 10.6 us  [body(): received = lax.ppermute(far_send, 'gx', far_pairs)]
    ppermute x0 -> x1, waiting for transfers between devices: none -> 6.56 us  [body(): received = lax.ppermute(far_send, 'gx', far_pairs)]
    select_n x0 -> x2, other arithmetic: none -> 4.02 us  [the longest x1 2.49 us: body(): far_heads = jnp.where(sends_tail, received, zero)]
    another operation x2 -> x0, other arithmetic: 1.92 us -> none  [the longest x1 0.97 us: body(): jnp.stack((base_flow[:, cells - HALO:], adjoint[:, cells - HALO:]), 0)]
  transfers between devices with their start and end apart: 6 -> 5, of which waited for: 3 -> 3; matrix products, arithmetic and copies ran while one was open for 6% -> 16% of each run, Pallas kernels for 18% -> 20%
where the time goes in v10:
time: 88 us; the launch traced here: 87.5 us
  starting transfers between devices  26.2 us (30%)
  waiting for transfers between devices  19 us (22%)
  Pallas kernels  17.8 us (20%)
  local copies, waits for them, and re-layouts  10.4 us (12%)
  other arithmetic  9.75 us (11%)
  matrix products  4.32 us (5%)
    all_to_all x1, waiting for transfers between devices, body(): lines = lax.all_to_all(low, 'gy', split_axis=2, concat_axis=3, tiled=True)  11.5 us
    ppermute x1, starting transfers between devices, body(): received = lax.ppermute(far_send, 'gx', far_pairs)  10.6 us
    pallas_call x1, Pallas kernels, interior_update(): pl.pallas_call(interior_kernel, grid=(rows // LANES, cells // HALO - 2),...  10 us
    pallas_call x1, Pallas kernels, boundary_update(): pl.pallas_call(boundary_kernel, grid=(2,), in_specs=[full_spec, full_spec...  7.76 us
    all_to_all x1, starting transfers between devices, body(): lines = lax.all_to_all(low, 'gy', split_axis=2, concat_axis=3, tiled=True)  7.66 us
    ppermute x1, waiting for transfers between devices, body(): received = lax.ppermute(far_send, 'gx', far_pairs)  6.56 us
    unnamed x10, local copies, waits for them, and re-layouts  5 us
    all_to_all x1, starting transfers between devices, body(): lax.all_to_all(wall_part, 'gy', split_axis=3, concat_axis=2, tiled=True)  4.74 us
  transfers between devices with their start and end apart: 5, of which 3 were waited for; matrix products, arithmetic and copies ran while one was open for 16% of the time, Pallas kernels for 20%

profile of v10, /device:TPU:1, one launch (start us, length us, event | category | flops | bytes accessed | tf_op | source)
XLA Modules:
  0.0 87.5 jit_solution(16417314236603208427)
XLA Ops:
  0.0 0.0 copy-start
  0.0 0.0 copy-start.1
  0.0 3.1 %copy.18 = bf16[3,24,32,256]{3,1,0,2:T(8,128)(2,1)S(1)} copy(f32[3,24,32,256]{3,2,1,0:T(8,128)} %base_ref.3) | data formatting | bytes 3538944 | tf_op args[0]
  3.1 0.0 copy-done.1
  3.1 1.3 %copy.17 = bf16[3,24,32,256]{3,1,0,2:T(8,128)(2,1)S(1)} copy(f32[3,24,32,256]{3,2,1,0:T(8,128)S(1)} %copy-done.1) | data formatting | bytes 3538944 | tf_op args[1]
  4.4 1.6 %maximum_bitcast_fusion = bf16[6,24,32,1,256]{4,1,0,3,2:T(8,128)(2,1)} fusion(bf16[3,24,32,256]{3,1,0,2:T(8,128)(2,1)S(1)} %copy.17, bf16[3,24,32,256]{3,1,0,2:T(8,128)(2,1)S(1)} %copy.18), kind=kLoop, calls=%fused_computation | loop fusion | flops 1179648 | bytes 4718592 | tf_op jit(solution)/shard_map/reshape | solution.py:150
  6.0 7.7 %all-to-all-start = ((bf16[6,24,32,1,256]{4,1,0,3,2:T(8,128)(2,1)}), bf16[6,24,32,1,256]{4,1,0,3,2:T(8,128)(2,1)}, u32[]{:S(2)}, u32[]{:S(2)}) async-start(bf16[6,24,32,1,256]{4,1,0,3,2:T(8,128)(2,1)} %maximum_bitcast_fusion), calls=%async_computation | async-start | bytes 4718592 | tf_op jit(solution)/shard_map/all_to_all | solution.py:151
  13.6 1.5 %slice_bitcast_fusion = (f32[1,3,4,32,256]{4,3,2,1,0:T(8,128)S(1)}, f32[1,3,4,32,256]{4,3,2,1,0:T(8,128)S(1)}, f32[1,3,4,32,256]{4,3,2,1,0:T(8,128)S(1)}, f32[1,3,4,32,256]{4,3,2,1,0:T(8,128)S(1)}) fusion(f32[3,24,32,256]{3,2,1,0:T(8,128)} %adj_ref.3, f32[3,24,32,256]{3,2,1,0:T(8,128)} %base_ref.3), kind=kLoop, calls=%fused_computation.21 | loop fusion | bytes 3145728 | tf_op jit(solution)/shard_map/stack | solution.py:153
  15.1 1.5 %broadcast_select_fusion.2 = (f32[2,3,4,32,256]{4,3,2,1,0:T(8,128)}, f32[2,3,4,32,256]{4,3,2,1,0:T(8,128)}, f32[2,3,4,32,256]{4,3,2,1,0:T(8,128)}) fusion(pred[]{:T(512)S(6)} %or.6, f32[1,3,4,32,256]{4,3,2,1,0:T(8,128)S(1)} %get-tuple-element.35, f32[1,3,4,32,256]{4,3,2,1,0:T(8,128)S(1)} %get-tuple-element.43, ...), kind=kLoop, calls=%fused_computation.25 | loop fusion | flops 589824 | bytes 3932161 | tf_op jit(solution)/shard_map/jit(_where)/select_n | solution.py:157
  16.6 1.9 %collective-permute-start = (f32[2,3,4,32,256]{4,3,2,1,0:T(8,128)}, f32[2,3,4,32,256]{4,3,2,1,0:T(8,128)S(1)}, u32[]{:S(2)}, u32[]{:S(2)}) collective-permute-start(f32[2,3,4,32,256]{4,3,2,1,0:T(8,128)} %get-tuple-element.40), channel_id=1, source_target_pairs={{0,4},{4,8},{8,12},{12,16},{16,20},{20,24},{24,28},{28,32},{32,36}... | collective-permute-start | bytes 2359304 | tf_op jit(solution)/shard_map/ppermute | solution.py:26
  18.5 1.3 %collective-permute-start.1 = (f32[2,3,4,32,256]{4,3,2,1,0:T(8,128)}, f32[2,3,4,32,256]{4,3,2,1,0:T(8,128)}, u32[]{:S(2)}, u32[]{:S(2)}) collective-permute-start(f32[2,3,4,32,256]{4,3,2,1,0:T(8,128)} %get-tuple-element.41), channel_id=1, source_target_pairs={{4,0},{8,4},{12,8},{16,12},{20,16},{24,20},{28,24},{32,28},{36,32}... | collective-permute-start | bytes 2359304 | tf_op jit(solution)/shard_map/ppermute | solution.py:26
  19.8 10.0 %shard_map.46.prev_ref = f32[3,24,32,256]{3,2,1,0:T(8,128)} custom-call(f32[3,24,32,256]{3,2,1,0:T(8,128)} %base_ref.3, f32[3,24,32,256]{3,2,1,0:T(8,128)} %adj_ref.3), custom_call_target="tpu_custom_call" | custom-call | tf_op jit(solution)/shard_map/pallas_call | solution.py:89
  29.8 11.5 %all-to-all-done = bf16[6,24,32,1,256]{4,1,0,3,2:T(8,128)(2,1)} async-done(((bf16[6,24,32,1,256]{4,1,0,3,2:T(8,128)(2,1)}), bf16[6,24,32,1,256]{4,1,0,3,2:T(8,128)(2,1)}, u32[]{:S(2)}, u32[]{:S(2)}) %all-to-all-start) | async-done | bytes 2359328 | tf_op jit(solution)/shard_map/all_to_all | solution.py:151
  41.2 2.5 %copy.19 = bf16[6,24,4,8,1,256]{5,3,2,1,0,4:T(8,128)(2,1)S(1)} copy(bf16[6,24,4,8,1,256]{5,1,0,3,2,4:T(8,128)(2,1)} %bitcast.1) | data formatting | bytes 4718592 | tf_op jit(solution)/shard_map/all_to_all | solution.py:151
  43.8 0.0 collective-permute-done.tail_ref
  43.8 0.0 copy-start.2
  43.8 0.0 collective-permute-done.1.head_ref
  43.8 0.0 copy-start.3
  43.8 0.2 fusion.12
  44.0 0.6 copy-done.2
  44.7 0.1 convert.1
  44.8 10.6 %collective-permute-start.2 = (f32[2,3,4,32,256]{4,3,2,1,0:T(8,128)}, f32[2,3,4,32,256]{4,3,2,1,0:T(8,128)}, u32[]{:S(2)}, u32[]{:S(2)}) collective-permute-start(f32[2,3,4,32,256]{4,3,2,1,0:T(8,128)} %get-tuple-element.26), channel_id=1, source_target_pairs={{124,128},{252,0},{128,124},{0,252},{125,129},{253,1},{129,125},{1... | collective-permute-start | bytes 2359304 | tf_op jit(solution)/shard_map/ppermute | solution.py:160
  55.4 0.0 copy-done.3
  55.4 1.4 %fusion.1 = f32[3,24,8,1024]{3,2,1,0:T(8,128)S(1)} fusion(bf16[3,24,8,1024]{3,2,1,0:T(8,128)(2,1)S(1)} %bitcast.53, bf16[1024,1024]{1,0:T(8,128)(2,1)S(1)} %copy-done.3), kind=kOutput, calls=%fused_computation.9 | convolution fusion | flops 1207959552 | bytes 5636096 | tf_op jit(solution)/shard_map/fxzk,ik->fxzi/dot_general | solution.py:169
  56.8 0.0 copy-done
  56.8 1.5 %multiply_reduce_fusion = f32[24,8,1024]{2,1,0:T(8,128)S(1)} fusion(bf16[3,24,8,1024]{3,2,1,0:T(8,128)(2,1)S(1)} %bitcast.54, bf16[3,24,8,1024]{3,2,1,0:T(8,128)(2,1)S(1)} %bitcast.58, bf16[1024,1024]{1,0:T(8,128)(2,1)S(1)} %copy-done), kind=kOutput, calls=%fused_computation.7 | convolution fusion | flops 1209532416 | bytes 5242880 | tf_op jit(solution)/shard_map/fxzk,ik->fxzi/dot_general | solution.py:167
  58.3 1.5 %multiply_add_fusion = f32[3,24,8,1024]{3,2,1,0:T(8,128)S(1)} fusion(f32[3,24,8,1024]{3,2,1,0:T(8,128)S(1)} %fusion.1, bf16[3,24,8,1024]{3,2,1,0:T(8,128)(2,1)S(1)} %bitcast.55, bf16[1024,1024]{1,0:T(8,128)(2,1)S(1)} %copy-done, f32[24,8,1024]{2,1,0:T(8,128)S(1)} %convert.1), kind=kOutput, calls=%fused_computation.8 | convolution fusion | flops 1209729024 | bytes 8781824 | tf_op jit(solution)/shard_map/fxzk,ik->fxzi/dot_general | solution.py:168
  59.8 0.2 fusion.11
  60.0 0.2 convert_element_type.33
  60.2 1.1 %copy.9 = bf16[3,24,8,4,256]{4,2,1,0,3:T(8,128)(2,1)} copy(bf16[3,24,8,4,256]{4,2,3,1,0:T(8,128)(2,1)S(1)} %bitcast.56) | data formatting | bytes 2359296 | tf_op jit(solution)/shard_map/optimization_barrier | solution.py:175
  61.3 4.7 %all-to-all-start.1 = ((bf16[3,24,8,4,256]{4,2,1,0,3:T(8,128)(2,1)}), bf16[3,24,8,4,256]{4,2,1,0,3:T(8,128)(2,1)S(1)}, u32[]{:S(2)}, u32[]{:S(2)}) async-start(bf16[3,24,8,4,256]{4,2,1,0,3:T(8,128)(2,1)} %copy.9), calls=%async_computation.1 | async-start | bytes 2359296 | tf_op jit(solution)/shard_map/all_to_all | solution.py:176
  66.1 6.6 %collective-permute-done.2 = f32[2,3,4,32,256]{4,3,2,1,0:T(8,128)} collective-permute-done((f32[2,3,4,32,256]{4,3,2,1,0:T(8,128)}, f32[2,3,4,32,256]{4,3,2,1,0:T(8,128)}, u32[]{:S(2)}, u32[]{:S(2)}) %collective-permute-start.2) | collective-permute-done | bytes 786464 | tf_op jit(solution)/shard_map/ppermute | solution.py:160
  72.6 2.5 %broadcast_select_fusion = (f32[2,3,4,32,256]{4,3,2,1,0:T(8,128)}, f32[2,3,4,32,256]{4,3,2,1,0:T(8,128)}) fusion(f32[2,3,4,32,256]{4,3,2,1,0:T(8,128)} %collective-permute-done.2, pred[]{:T(512)S(6)} %or.6, pred[]{:T(512)S(6)} %or.7), kind=kLoop, calls=%fused_computation.19 | loop fusion | flops 393216 | bytes 2359298 | tf_op jit(solution)/shard_map/jit(_where)/select_n | solution.py:163
  75.1 7.8 %shard_map.47 = f32[3,24,32,256]{3,2,1,0:T(8,128)} custom-call(f32[3,24,32,256]{3,2,1,0:T(8,128)} %base_ref.3, f32[3,24,32,256]{3,2,1,0:T(8,128)} %adj_ref.3, f32[2,3,4,32,256]{4,3,2,1,0:T(8,128)} %copy-done.2, f32[2,3,4,32,256]{4,3,2,1,0:T(8,128)} %collective-permute-done.1.head_ref, ...), custom_call_target="tpu_custom_call", output_to_operand_aliasing={{}: (6, {})} | custom-call | tf_op jit(solution)/shard_map/pallas_call | solution.py:131
  82.9 0.9 %all-to-all-done.1 = bf16[3,24,8,4,256]{4,2,1,0,3:T(8,128)(2,1)S(1)} async-done(((bf16[3,24,8,4,256]{4,2,1,0,3:T(8,128)(2,1)}), bf16[3,24,8,4,256]{4,2,1,0,3:T(8,128)(2,1)S(1)}, u32[]{:S(2)}, u32[]{:S(2)}) %all-to-all-start.1) | async-done | bytes 1179680 | tf_op jit(solution)/shard_map/all_to_all | solution.py:176
  83.8 3.6 %fusion = f32[3,24,32,256]{3,2,1,0:T(8,128)} fusion(f32[3,24,32,256]{3,2,1,0:T(8,128)} %shard_map.47, pred[256]{0:T(512)(128)(4,1)S(1)} %compare_and_fusion, bf16[3,24,8,4,256]{4,2,1,0,3:T(8,128)(2,1)S(1)} %all-to-all-done.1), kind=kLoop, calls=%fused_computation.2 | loop fusion | flops 2359296 | bytes 5898496 | tf_op jit(solution)/shard_map/jit(_where)/select_n | solution.py:183
  (2 shorter events, 0.0 us)
Async XLA Ops:
  0.0 56.8 %copy-start = (bf16[1024,1024]{1,0:T(8,128)(2,1)S(1)}, bf16[1024,1024]{1,0:T(8,128)(2,1)}, u32[]{:S(2)}) copy-start(bf16[1024,1024]{1,0:T(8,128)(2,1)} %param.8) | copy-start | bytes 6291460
  0.0 3.1 %copy-start.1 = (f32[3,24,32,256]{3,2,1,0:T(8,128)S(1)}, f32[3,24,32,256]{3,2,1,0:T(8,128)}, u32[]{:S(2)}) copy-start(f32[3,24,32,256]{3,2,1,0:T(8,128)} %adj_ref.3) | copy-start | bytes 7077892
  6.0 35.3 %all-to-all-start = ((bf16[6,24,32,1,256]{4,1,0,3,2:T(8,128)(2,1)}), bf16[6,24,32,1,256]{4,1,0,3,2:T(8,128)(2,1)}, u32[]{:S(2)}, u32[]{:S(2)}) async-start(bf16[6,24,32,1,256]{4,1,0,3,2:T(8,128)(2,1)} %maximum_bitcast_fusion), calls=%async_computation | async-start | bytes 4718592 | tf_op jit(solution)/shard_map/all_to_all | solution.py:151
  16.6 27.2 %collective-permute-start = (f32[2,3,4,32,256]{4,3,2,1,0:T(8,128)}, f32[2,3,4,32,256]{4,3,2,1,0:T(8,128)S(1)}, u32[]{:S(2)}, u32[]{:S(2)}) collective-permute-start(f32[2,3,4,32,256]{4,3,2,1,0:T(8,128)} %get-tuple-element.40), channel_id=1, source_target_pairs={{0,4},{4,8},{8,12},{12,16},{16,20},{20,24},{24,28},{28,32},{32,36}... | collective-permute-start | bytes 2359304 | tf_op jit(solution)/shard_map/ppermute | solution.py:26
  18.5 25.3 %collective-permute-start.1 = (f32[2,3,4,32,256]{4,3,2,1,0:T(8,128)}, f32[2,3,4,32,256]{4,3,2,1,0:T(8,128)}, u32[]{:S(2)}, u32[]{:S(2)}) collective-permute-start(f32[2,3,4,32,256]{4,3,2,1,0:T(8,128)} %get-tuple-element.41), channel_id=1, source_target_pairs={{4,0},{8,4},{12,8},{16,12},{20,16},{24,20},{28,24},{32,28},{36,32}... | collective-permute-start | bytes 2359304 | tf_op jit(solution)/shard_map/ppermute | solution.py:26
  43.8 0.9 %copy-start.2 = (f32[2,3,4,32,256]{4,3,2,1,0:T(8,128)}, f32[2,3,4,32,256]{4,3,2,1,0:T(8,128)S(1)}, u32[]{:S(2)}) copy-start(f32[2,3,4,32,256]{4,3,2,1,0:T(8,128)S(1)} %collective-permute-done.tail_ref) | copy-start | bytes 2359300
  43.8 11.6 %copy-start.3 = (bf16[1024,1024]{1,0:T(8,128)(2,1)S(1)}, bf16[1024,1024]{1,0:T(8,128)(2,1)}, u32[]{:S(2)}) copy-start(bf16[1024,1024]{1,0:T(8,128)(2,1)} %param.9) | copy-start | bytes 6291460
  44.8 27.9 %collective-permute-start.2 = (f32[2,3,4,32,256]{4,3,2,1,0:T(8,128)}, f32[2,3,4,32,256]{4,3,2,1,0:T(8,128)}, u32[]{:S(2)}, u32[]{:S(2)}) collective-permute-start(f32[2,3,4,32,256]{4,3,2,1,0:T(8,128)} %get-tuple-element.26), channel_id=1, source_target_pairs={{124,128},{252,0},{128,124},{0,252},{125,129},{253,1},{129,125},{1... | collective-permute-start | bytes 2359304 | tf_op jit(solution)/shard_map/ppermute | solution.py:160
  61.3 22.5 %all-to-all-start.1 = ((bf16[3,24,8,4,256]{4,2,1,0,3:T(8,128)(2,1)}), bf16[3,24,8,4,256]{4,2,1,0,3:T(8,128)(2,1)S(1)}, u32[]{:S(2)}, u32[]{:S(2)}) async-start(bf16[3,24,8,4,256]{4,2,1,0,3:T(8,128)(2,1)} %copy.9), calls=%async_computation.1 | async-start | bytes 2359296 | tf_op jit(solution)/shard_map/all_to_all | solution.py:176

commit v11 on v10

--- a/solution.py
+++ b/solution.py
@@ -95,7 +95,7 @@
     )(base_flow, adjoint)
 
 
-def boundary_kernel(base_ref, adj_ref, tail_ref, head_ref, far_tail_ref, far_head_ref, prev_ref, out_ref, ext_ref):
+def boundary_kernel(base_ref, adj_ref, tail_ref, head_ref, prev_ref, out_ref, ext_ref):
     comps, cells, span, rows = base_ref.shape
     side = pl.program_id(0)
 
@@ -103,8 +103,8 @@
     def _():
         ext_ref[0, :, HALO : HALO + cells] = base_ref[...]
         ext_ref[1, :, HALO : HALO + cells] = adj_ref[...]
-        ext_ref[:, :, :HALO] = tail_ref[...] + far_tail_ref[...]
-        ext_ref[:, :, HALO + cells :] = head_ref[...] + far_head_ref[...]
+        ext_ref[:, :, :HALO] = tail_ref[...]
+        ext_ref[:, :, HALO + cells :] = head_ref[...]
 
     first = side * (cells - HALO)
     for lane in range(rows // LANES):
@@ -123,7 +123,7 @@
         lax.fori_loop(0, HALO, step, 0)
 
 
-def boundary_update(base_flow, adjoint, tails, heads, far_tails, far_heads, previous):
+def boundary_update(base_flow, adjoint, tails, heads, previous):
     comps, cells, span, rows = base_flow.shape
     full_spec = pl.BlockSpec((comps, cells, span, rows), lambda s: (0, 0, 0, 0))
     halo_spec = pl.BlockSpec((2, comps, HALO, span, rows), lambda s: (0, 0, 0, 0, 0))
@@ -131,12 +131,67 @@
     return pl.pallas_call(
         boundary_kernel,
         grid=(2,),
-        in_specs=[full_spec, full_spec, halo_spec, halo_spec, halo_spec, halo_spec, pl.BlockSpec(memory_space=pl.ANY)],
+        in_specs=[full_spec, full_spec, halo_spec, halo_spec, pl.BlockSpec(memory_space=pl.ANY)],
         out_specs=out_spec,
         out_shape=jax.ShapeDtypeStruct(base_flow.shape, jnp.float32),
         scratch_shapes=[pltpu.VMEM((2, comps, cells + 2 * HALO, span, rows), jnp.float32)],
-        input_output_aliases={6: 0},
-    )(base_flow, adjoint, tails, heads, far_tails, far_heads, previous)
+        input_output_aliases={4: 0},
+    )(base_flow, adjoint, tails, heads, previous)
+
+
+def side_kernel(side_ref, base_ref, adj_ref, halo_ref, prev_ref, out_ref, ext_ref):
+    comps, near, span, rows = base_ref.shape
+
+    @pl.when(side_ref[0] == 0)
+    def _():
+        ext_ref[:, :, :HALO] = halo_ref[...]
+        ext_ref[0, :, HALO:] = base_ref[...]
+        ext_ref[1, :, HALO:] = adj_ref[...]
+
+    @pl.when(side_ref[0] != 0)
+    def _():
+        ext_ref[0, :, :near] = base_ref[...]
+        ext_ref[1, :, :near] = adj_ref[...]
+        ext_ref[:, :, near:] = halo_ref[...]
+
+    for lane in range(rows // LANES):
+        lanes = pl.ds(lane * LANES, LANES)
+
+        def load(field, c, x, lanes=lanes):
+            return ext_ref[field, c, x, :, lanes]
+
+        def step(i, carry, lanes=lanes, load=load):
+            def write(c, value):
+                out_ref[c, i, :, lanes] = value
+
+            cell_update(load, HALO + i, write)
+            return carry
+
+        lax.fori_loop(0, HALO, step, 0)
+
+
+def side_update(base_flow, adjoint, halo, side, previous):
+    comps, cells, span, rows = base_flow.shape
+    near = 2 * HALO
+    last = cells // near - 1
+    body_spec = pl.BlockSpec((comps, near, span, rows), lambda i, side_ref: (0, side_ref[0] * last, 0, 0))
+    halo_spec = pl.BlockSpec((2, comps, HALO, span, rows), lambda i, side_ref: (0, 0, 0, 0, 0))
+    out_spec = pl.BlockSpec(
+        (comps, HALO, span, rows), lambda i, side_ref: (0, side_ref[0] * (cells // HALO - 1), 0, 0)
+    )
+    grid_spec = pltpu.PrefetchScalarGridSpec(
+        num_scalar_prefetch=1,
+        grid=(1,),
+        in_specs=[body_spec, body_spec, halo_spec, pl.BlockSpec(memory_space=pl.ANY)],
+        out_specs=out_spec,
+        scratch_shapes=[pltpu.VMEM((2, comps, near + HALO, span, rows), jnp.float32)],
+    )
+    return pl.pallas_call(
+        side_kernel,
+        grid_spec=grid_spec,
+        out_shape=jax.ShapeDtypeStruct(base_flow.shape, jnp.float32),
+        input_output_aliases={4: 0},
+    )(side, base_flow, adjoint, halo, previous)
 
 
 def body(base_flow, adjoint, first_op, second_op, far=()):
@@ -158,9 +213,8 @@
     partial = interior_update(base_flow, adjoint)
     lines, partial, tails, heads, far_send = lax.optimization_barrier((lines, partial, tails, heads, far_send))
     received = lax.ppermute(far_send, "gx", far_pairs)
-    zero = jnp.zeros_like(received)
-    far_tails = jnp.where(gets_tail, received, zero)
-    far_heads = jnp.where(sends_tail, received, zero)
+    far_side = jnp.where(sends_tail, 1, 0).astype(jnp.int32).reshape(1)
+    side_halo = jnp.where(gets_tail | sends_tail, received, tails)
     lines = lines.reshape(2 * comps, cells, part, total_rows)
     base_lines = lines[:comps]
     adj_lines = lines[comps:]
@@ -176,7 +230,8 @@
     wall_part = lax.all_to_all(wall_part, "gy", split_axis=3, concat_axis=2, tiled=True)
     wall_part = wall_part.reshape(comps, cells, spanwise, local_rows).astype(jnp.float32)
 
-    partial = boundary_update(base_flow, adjoint, tails, heads, far_tails, far_heads, partial)
+    partial = boundary_update(base_flow, adjoint, tails, heads, partial)
+    partial = side_update(base_flow, adjoint, side_halo, far_side, partial)
     updated = partial + STEP_WEIGHT * wall_part
     wall_index = lax.axis_index("gy") * local_rows + jnp.arange(local_rows, dtype=jnp.int32)
     interior = (wall_index > 0) & (wall_index < total_rows - 1)

time: 88 us -> 88 us (level)
  Pallas kernels: 17.8 us -> 21.4 us
  waiting for transfers between devices: 19 us -> 15.7 us
    ppermute x1, waiting for transfers between devices: 6.56 us -> 0.01 us  [body(): received = lax.ppermute(far_send, 'gx', far_pairs)]
    pallas_call x0 -> x1, Pallas kernels: none -> 4.15 us  [side_update(): pl.pallas_call(side_kernel, grid_spec=grid_spec, out_shape=jax.ShapeDtype...]
    all_to_all x1, waiting for transfers between devices: 0.94 us -> 4.17 us  [body(): lax.all_to_all(wall_part, 'gy', split_axis=3, concat_axis=2, tiled=True)]
  transfers between devices with their start and end apart: 5 -> 5, of which waited for: 3 -> 2; matrix products, arithmetic and copies ran while one was open for 16% -> 15% of each run, Pallas kernels for 20% -> 25%
where the time goes in v11:
time: 88 us; the launch traced here: 87.4 us
  starting transfers between devices  26.2 us (30%)
  Pallas kernels  21.4 us (24%)
  waiting for transfers between devices  15.7 us (18%)
  local copies, waits for them, and re-layouts  10.3 us (12%)
  other arithmetic  9.39 us (11%)
  matrix products  4.32 us (5%)
    all_to_all x1, waiting for transfers between devices, body(): lines = lax.all_to_all(low, 'gy', split_axis=2, concat_axis=3, tiled=True)  11.5 us
    ppermute x1, starting transfers between devices, body(): received = lax.ppermute(far_send, 'gx', far_pairs)  10.6 us
    pallas_call x1, Pallas kernels, interior_update(): pl.pallas_call(interior_kernel, grid=(rows // LANES, cells // HALO - 2),...  10 us
    all_to_all x1, starting transfers between devices, body(): lines = lax.all_to_all(low, 'gy', split_axis=2, concat_axis=3, tiled=True)  7.64 us
    pallas_call x1, Pallas kernels, boundary_update(): pl.pallas_call(boundary_kernel, grid=(2,), in_specs=[full_spec, full_spec...  7.28 us
    unnamed x10, local copies, waits for them, and re-layouts  4.98 us
    all_to_all x1, starting transfers between devices, body(): lax.all_to_all(wall_part, 'gy', split_axis=3, concat_axis=2, tiled=True)  4.76 us
    all_to_all x1, waiting for transfers between devices, body(): lax.all_to_all(wall_part, 'gy', split_axis=3, concat_axis=2, tiled=True)  4.17 us
  transfers between devices with their start and end apart: 5, of which 2 were waited for; matrix products, arithmetic and copies ran while one was open for 15% of the time, Pallas kernels for 25%

profile of v11, /device:TPU:1, one launch (start us, length us, event | category | flops | bytes accessed | tf_op | source)
XLA Modules:
  0.0 87.4 jit_solution(2743758756316864273)
XLA Ops:
  0.0 0.0 copy-start
  0.0 0.0 copy-start.1
  0.0 3.1 %copy.19 = bf16[3,24,32,256]{3,1,0,2:T(8,128)(2,1)S(1)} copy(f32[3,24,32,256]{3,2,1,0:T(8,128)} %base_ref.5) | data formatting | bytes 3538944 | tf_op args[0]
  3.1 0.0 copy-done.1
  3.1 1.3 %copy.18 = bf16[3,24,32,256]{3,1,0,2:T(8,128)(2,1)S(1)} copy(f32[3,24,32,256]{3,2,1,0:T(8,128)S(1)} %copy-done.1) | data formatting | bytes 3538944 | tf_op args[1]
  4.4 1.6 %maximum_bitcast_fusion = bf16[6,24,32,1,256]{4,1,0,3,2:T(8,128)(2,1)} fusion(bf16[3,24,32,256]{3,1,0,2:T(8,128)(2,1)S(1)} %copy.18, bf16[3,24,32,256]{3,1,0,2:T(8,128)(2,1)S(1)} %copy.19), kind=kLoop, calls=%fused_computation | loop fusion | flops 1179648 | bytes 4718592 | tf_op jit(solution)/shard_map/reshape | solution.py:205
  6.0 7.6 %all-to-all-start = ((bf16[6,24,32,1,256]{4,1,0,3,2:T(8,128)(2,1)}), bf16[6,24,32,1,256]{4,1,0,3,2:T(8,128)(2,1)}, u32[]{:S(2)}, u32[]{:S(2)}) async-start(bf16[6,24,32,1,256]{4,1,0,3,2:T(8,128)(2,1)} %maximum_bitcast_fusion), calls=%async_computation | async-start | bytes 4718592 | tf_op jit(solution)/shard_map/all_to_all | solution.py:206
  13.6 1.5 %slice_bitcast_fusion = (f32[1,3,4,32,256]{4,3,2,1,0:T(8,128)S(1)}, f32[1,3,4,32,256]{4,3,2,1,0:T(8,128)S(1)}, f32[1,3,4,32,256]{4,3,2,1,0:T(8,128)S(1)}, f32[1,3,4,32,256]{4,3,2,1,0:T(8,128)S(1)}) fusion(f32[3,24,32,256]{3,2,1,0:T(8,128)} %adj_ref.5, f32[3,24,32,256]{3,2,1,0:T(8,128)} %base_ref.5), kind=kLoop, calls=%fused_computation.19 | loop fusion | bytes 3145728 | tf_op jit(solution)/shard_map/stack | solution.py:208
  15.1 1.5 %broadcast_select_fusion = (f32[2,3,4,32,256]{4,3,2,1,0:T(8,128)}, f32[2,3,4,32,256]{4,3,2,1,0:T(8,128)}, f32[2,3,4,32,256]{4,3,2,1,0:T(8,128)}) fusion(pred[]{:T(512)S(6)} %or.9, f32[1,3,4,32,256]{4,3,2,1,0:T(8,128)S(1)} %get-tuple-element.35, f32[1,3,4,32,256]{4,3,2,1,0:T(8,128)S(1)} %get-tuple-element.41, f32[1,3,4,32,256]{4,3,2,1,0:T(8,128)S(1)} %get-tuple-element.36, ...), kind=kLoop, calls=%fused_computation.23 | loop fusion | flops 589824 | bytes 3932161 | tf_op jit(solution)/shard_map/jit(_where)/select_n | solution.py:212
  16.6 1.9 %collective-permute-start = (f32[2,3,4,32,256]{4,3,2,1,0:T(8,128)}, f32[2,3,4,32,256]{4,3,2,1,0:T(8,128)S(1)}, u32[]{:S(2)}, u32[]{:S(2)}) collective-permute-start(f32[2,3,4,32,256]{4,3,2,1,0:T(8,128)} %get-tuple-element.38), channel_id=1, source_target_pairs={{0,4},{4,8},{8,12},{12,16},{16,20},{20,24},{24,28},{28,32},{32,36}... | collective-permute-start | bytes 2359304 | tf_op jit(solution)/shard_map/ppermute | solution.py:26
  18.4 1.3 %collective-permute-start.1 = (f32[2,3,4,32,256]{4,3,2,1,0:T(8,128)}, f32[2,3,4,32,256]{4,3,2,1,0:T(8,128)}, u32[]{:S(2)}, u32[]{:S(2)}) collective-permute-start(f32[2,3,4,32,256]{4,3,2,1,0:T(8,128)} %get-tuple-element.39), channel_id=1, source_target_pairs={{4,0},{8,4},{12,8},{16,12},{20,16},{24,20},{28,24},{32,28},{36,32}... | collective-permute-start | bytes 2359304 | tf_op jit(solution)/shard_map/ppermute | solution.py:26
  19.7 10.0 %shard_map.46.prev_ref = f32[3,24,32,256]{3,2,1,0:T(8,128)} custom-call(f32[3,24,32,256]{3,2,1,0:T(8,128)} %base_ref.5, f32[3,24,32,256]{3,2,1,0:T(8,128)} %adj_ref.5), custom_call_target="tpu_custom_call" | custom-call | tf_op jit(solution)/shard_map/pallas_call | solution.py:89
  29.7 11.5 %all-to-all-done = bf16[6,24,32,1,256]{4,1,0,3,2:T(8,128)(2,1)} async-done(((bf16[6,24,32,1,256]{4,1,0,3,2:T(8,128)(2,1)}), bf16[6,24,32,1,256]{4,1,0,3,2:T(8,128)(2,1)}, u32[]{:S(2)}, u32[]{:S(2)}) %all-to-all-start) | async-done | bytes 2359328 | tf_op jit(solution)/shard_map/all_to_all | solution.py:206
  41.2 2.5 %copy.20 = bf16[6,24,4,8,1,256]{5,3,2,1,0,4:T(8,128)(2,1)S(1)} copy(bf16[6,24,4,8,1,256]{5,1,0,3,2,4:T(8,128)(2,1)} %bitcast.2) | data formatting | bytes 4718592 | tf_op jit(solution)/shard_map/all_to_all | solution.py:206
  43.8 0.0 collective-permute-done.tail_ref
  43.8 0.0 copy-start.2
  43.8 0.0 collective-permute-done.1.head_ref
  43.8 0.0 copy-start.3
  43.8 0.2 fusion.12
  44.0 0.6 copy-done.2
  44.7 0.1 convert.1
  44.8 10.6 %collective-permute-start.2 = (f32[2,3,4,32,256]{4,3,2,1,0:T(8,128)}, f32[2,3,4,32,256]{4,3,2,1,0:T(8,128)}, u32[]{:S(2)}, u32[]{:S(2)}) collective-permute-start(f32[2,3,4,32,256]{4,3,2,1,0:T(8,128)} %get-tuple-element.24), channel_id=1, source_target_pairs={{124,128},{252,0},{128,124},{0,252},{125,129},{253,1},{129,125},{1... | collective-permute-start | bytes 2359304 | tf_op jit(solution)/shard_map/ppermute | solution.py:215
  55.4 0.0 copy-done.3
  55.4 1.4 %fusion.1 = f32[3,24,8,1024]{3,2,1,0:T(8,128)S(1)} fusion(bf16[3,24,8,1024]{3,2,1,0:T(8,128)(2,1)S(1)} %bitcast.54, bf16[1024,1024]{1,0:T(8,128)(2,1)S(1)} %copy-done.3), kind=kOutput, calls=%fused_computation.9 | convolution fusion | flops 1207959552 | bytes 5636096 | tf_op jit(solution)/shard_map/fxzk,ik->fxzi/dot_general | solution.py:223
  56.8 0.0 copy-done
  56.8 1.4 %multiply_reduce_fusion = f32[24,8,1024]{2,1,0:T(8,128)S(1)} fusion(bf16[3,24,8,1024]{3,2,1,0:T(8,128)(2,1)S(1)} %bitcast.55, bf16[3,24,8,1024]{3,2,1,0:T(8,128)(2,1)S(1)} %bitcast.59, bf16[1024,1024]{1,0:T(8,128)(2,1)S(1)} %copy-done), kind=kOutput, calls=%fused_computation.7 | convolution fusion | flops 1209532416 | bytes 5242880 | tf_op jit(solution)/shard_map/fxzk,ik->fxzi/dot_general | solution.py:221
  58.3 1.5 %multiply_add_fusion = f32[3,24,8,1024]{3,2,1,0:T(8,128)S(1)} fusion(f32[3,24,8,1024]{3,2,1,0:T(8,128)S(1)} %fusion.1, bf16[3,24,8,1024]{3,2,1,0:T(8,128)(2,1)S(1)} %bitcast.56, bf16[1024,1024]{1,0:T(8,128)(2,1)S(1)} %copy-done, f32[24,8,1024]{2,1,0:T(8,128)S(1)} %convert.1), kind=kOutput, calls=%fused_computation.8 | convolution fusion | flops 1209729024 | bytes 8781824 | tf_op jit(solution)/shard_map/fxzk,ik->fxzi/dot_general | solution.py:222
  59.7 0.2 fusion.11
  60.0 0.2 convert_element_type.33
  60.2 1.1 %copy.10 = bf16[3,24,8,4,256]{4,2,1,0,3:T(8,128)(2,1)} copy(bf16[3,24,8,4,256]{4,2,3,1,0:T(8,128)(2,1)S(1)} %bitcast.57) | data formatting | bytes 2359296 | tf_op jit(solution)/shard_map/optimization_barrier | solution.py:229
  61.3 4.8 %all-to-all-start.1 = ((bf16[3,24,8,4,256]{4,2,1,0,3:T(8,128)(2,1)}), bf16[3,24,8,4,256]{4,2,1,0,3:T(8,128)(2,1)S(1)}, u32[]{:S(2)}, u32[]{:S(2)}) async-start(bf16[3,24,8,4,256]{4,2,1,0,3:T(8,128)(2,1)} %copy.10), calls=%async_computation.1 | async-start | bytes 2359296 | tf_op jit(solution)/shard_map/all_to_all | solution.py:230
  66.1 7.3 %shard_map.47.prev_ref = f32[3,24,32,256]{3,2,1,0:T(8,128)} custom-call(f32[3,24,32,256]{3,2,1,0:T(8,128)} %base_ref.5, f32[3,24,32,256]{3,2,1,0:T(8,128)} %adj_ref.5, f32[2,3,4,32,256]{4,3,2,1,0:T(8,128)} %copy-done.2, f32[2,3,4,32,256]{4,3,2,1,0:T(8,128)} %collective-permute-done.1.head_ref, ...), custom_call_target="tpu_custom_call", output_to_operand_aliasing={{}: (4, {})} | custom-call | tf_op jit(solution)/shard_map/pallas_call | solution.py:131
  73.3 0.0 collective-permute-done.2
  73.3 2.2 %broadcast_select_fusion.1.halo_ref = f32[2,3,4,32,256]{4,3,2,1,0:T(8,128)} fusion(f32[2,3,4,32,256]{4,3,2,1,0:T(8,128)} %collective-permute-done.2, f32[2,3,4,32,256]{4,3,2,1,0:T(8,128)} %copy-done.2, pred[]{:T(512)S(6)} %or.11), kind=kLoop, calls=%fused_computation.24 | loop fusion | flops 196608 | bytes 2359297 | tf_op jit(solution)/shard_map/jit(_where)/select_n | solution.py:217
  75.5 4.1 %shard_map.48 = f32[3,24,32,256]{3,2,1,0:T(8,128)} custom-call(s32[1]{0:T(128)} %bitcast.side_ref, f32[3,24,32,256]{3,2,1,0:T(8,128)} %base_ref.5, f32[3,24,32,256]{3,2,1,0:T(8,128)} %adj_ref.5, f32[2,3,4,32,256]{4,3,2,1,0:T(8,128)} %broadcast_select_fusion.1.halo_ref, f32[3,24,32,256]{3,2,1,0:T(8,128)} %shard_map.47.prev_ref), custom_call_target="tpu_custom_call", output_to_operand_aliasing={{}: (4, {})} | custom-call | tf_op jit(solution)/shard_map/pallas_call | solution.py:189
  79.6 4.2 %all-to-all-done.1 = bf16[3,24,8,4,256]{4,2,1,0,3:T(8,128)(2,1)S(1)} async-done(((bf16[3,24,8,4,256]{4,2,1,0,3:T(8,128)(2,1)}), bf16[3,24,8,4,256]{4,2,1,0,3:T(8,128)(2,1)S(1)}, u32[]{:S(2)}, u32[]{:S(2)}) %all-to-all-start.1) | async-done | bytes 1179680 | tf_op jit(solution)/shard_map/all_to_all | solution.py:230
  83.8 3.6 %fusion = f32[3,24,32,256]{3,2,1,0:T(8,128)} fusion(f32[3,24,32,256]{3,2,1,0:T(8,128)} %shard_map.48, pred[256]{0:T(512)(128)(4,1)S(1)} %compare_and_fusion, bf16[3,24,8,4,256]{4,2,1,0,3:T(8,128)(2,1)S(1)} %all-to-all-done.1), kind=kLoop, calls=%fused_computation.2 | loop fusion | flops 2359296 | bytes 5898496 | tf_op jit(solution)/shard_map/jit(_where)/select_n | solution.py:238
  (2 shorter events, 0.0 us)
Async XLA Ops:
  0.0 56.8 %copy-start = (bf16[1024,1024]{1,0:T(8,128)(2,1)S(1)}, bf16[1024,1024]{1,0:T(8,128)(2,1)}, u32[]{:S(2)}) copy-start(bf16[1024,1024]{1,0:T(8,128)(2,1)} %param.8) | copy-start | bytes 6291460
  0.0 3.1 %copy-start.1 = (f32[3,24,32,256]{3,2,1,0:T(8,128)S(1)}, f32[3,24,32,256]{3,2,1,0:T(8,128)}, u32[]{:S(2)}) copy-start(f32[3,24,32,256]{3,2,1,0:T(8,128)} %adj_ref.5) | copy-start | bytes 7077892
  6.0 35.3 %all-to-all-start = ((bf16[6,24,32,1,256]{4,1,0,3,2:T(8,128)(2,1)}), bf16[6,24,32,1,256]{4,1,0,3,2:T(8,128)(2,1)}, u32[]{:S(2)}, u32[]{:S(2)}) async-start(bf16[6,24,32,1,256]{4,1,0,3,2:T(8,128)(2,1)} %maximum_bitcast_fusion), calls=%async_computation | async-start | bytes 4718592 | tf_op jit(solution)/shard_map/all_to_all | solution.py:206
  16.6 27.2 %collective-permute-start = (f32[2,3,4,32,256]{4,3,2,1,0:T(8,128)}, f32[2,3,4,32,256]{4,3,2,1,0:T(8,128)S(1)}, u32[]{:S(2)}, u32[]{:S(2)}) collective-permute-start(f32[2,3,4,32,256]{4,3,2,1,0:T(8,128)} %get-tuple-element.38), channel_id=1, source_target_pairs={{0,4},{4,8},{8,12},{12,16},{16,20},{20,24},{24,28},{28,32},{32,36}... | collective-permute-start | bytes 2359304 | tf_op jit(solution)/shard_map/ppermute | solution.py:26
  18.4 25.3 %collective-permute-start.1 = (f32[2,3,4,32,256]{4,3,2,1,0:T(8,128)}, f32[2,3,4,32,256]{4,3,2,1,0:T(8,128)}, u32[]{:S(2)}, u32[]{:S(2)}) collective-permute-start(f32[2,3,4,32,256]{4,3,2,1,0:T(8,128)} %get-tuple-element.39), channel_id=1, source_target_pairs={{4,0},{8,4},{12,8},{16,12},{20,16},{24,20},{28,24},{32,28},{36,32}... | collective-permute-start | bytes 2359304 | tf_op jit(solution)/shard_map/ppermute | solution.py:26
  43.8 0.9 %copy-start.2 = (f32[2,3,4,32,256]{4,3,2,1,0:T(8,128)}, f32[2,3,4,32,256]{4,3,2,1,0:T(8,128)S(1)}, u32[]{:S(2)}) copy-start(f32[2,3,4,32,256]{4,3,2,1,0:T(8,128)S(1)} %collective-permute-done.tail_ref) | copy-start | bytes 2359300
  43.8 11.6 %copy-start.3 = (bf16[1024,1024]{1,0:T(8,128)(2,1)S(1)}, bf16[1024,1024]{1,0:T(8,128)(2,1)}, u32[]{:S(2)}) copy-start(bf16[1024,1024]{1,0:T(8,128)(2,1)} %param.9) | copy-start | bytes 6291460
  44.8 28.6 %collective-permute-start.2 = (f32[2,3,4,32,256]{4,3,2,1,0:T(8,128)}, f32[2,3,4,32,256]{4,3,2,1,0:T(8,128)}, u32[]{:S(2)}, u32[]{:S(2)}) collective-permute-start(f32[2,3,4,32,256]{4,3,2,1,0:T(8,128)} %get-tuple-element.24), channel_id=1, source_target_pairs={{124,128},{252,0},{128,124},{0,252},{125,129},{253,1},{129,125},{1... | collective-permute-start | bytes 2359304 | tf_op jit(solution)/shard_map/ppermute | solution.py:215
  61.3 22.5 %all-to-all-start.1 = ((bf16[3,24,8,4,256]{4,2,1,0,3:T(8,128)(2,1)}), bf16[3,24,8,4,256]{4,2,1,0,3:T(8,128)(2,1)S(1)}, u32[]{:S(2)}, u32[]{:S(2)}) async-start(bf16[3,24,8,4,256]{4,2,1,0,3:T(8,128)(2,1)} %copy.10), calls=%async_computation.1 | async-start | bytes 2359296 | tf_op jit(solution)/shard_map/all_to_all | solution.py:230

commit v12 on v11

--- a/solution.py
+++ b/solution.py
@@ -211,8 +211,9 @@
     far_pairs, sends_tail, gets_tail = far_plan(far)
     far_send = jnp.where(sends_tail, tail_cells, head_cells)
     partial = interior_update(base_flow, adjoint)
-    lines, partial, tails, heads, far_send = lax.optimization_barrier((lines, partial, tails, heads, far_send))
+    partial, far_send = lax.optimization_barrier((partial, far_send))
     received = lax.ppermute(far_send, "gx", far_pairs)
+    lines, partial, tails, heads = lax.optimization_barrier((lines, partial, tails, heads))
     far_side = jnp.where(sends_tail, 1, 0).astype(jnp.int32).reshape(1)
     side_halo = jnp.where(gets_tail | sends_tail, received, tails)
     lines = lines.reshape(2 * comps, cells, part, total_rows)

time: 88 us -> 89.8 us (1.020)
  the two profiles are of different devices: /device:TPU:1 before, /device:TPU:246 now
where the time goes in v12:
time: 89.8 us; the launch traced here: 89.2 us
  waiting for transfers between devices  27.5 us (31%)
  Pallas kernels  21.4 us (24%)
  starting transfers between devices  15 us (17%)
  local copies, waits for them, and re-layouts  11.2 us (12%)
  other arithmetic  9.43 us (11%)
  matrix products  4.32 us (5%)
    all_to_all x1, waiting for transfers between devices, body(): lines = lax.all_to_all(low, 'gy', split_axis=2, concat_axis=3, tiled=True)  25.4 us
    pallas_call x1, Pallas kernels, interior_update(): pl.pallas_call(interior_kernel, grid=(rows // LANES, cells // HALO - 2),...  10 us
    pallas_call x1, Pallas kernels, boundary_update(): pl.pallas_call(boundary_kernel, grid=(2,), in_specs=[full_spec, full_spec...  7.29 us
    unnamed x10, local copies, waits for them, and re-layouts  5.89 us
    ppermute x2, starting transfers between devices, ring_shift(): return lax.ppermute(value, axis, pairs)  5.1 us
    all_to_all x1, starting transfers between devices, body(): lines = lax.all_to_all(low, 'gy', split_axis=2, concat_axis=3, tiled=True)  4.48 us
    pallas_call x1, Pallas kernels, side_update(): pl.pallas_call(side_kernel, grid_spec=grid_spec, out_shape=jax.ShapeDtype...  4.14 us
    select_n x1, other arithmetic, body(): return jnp.where(interior, updated, jnp.float32(0.0))  3.63 us
  transfers between devices with their start and end apart: 5, of which 2 were waited for; matrix products, arithmetic and copies ran while one was open for 16% of the time, Pallas kernels for 24%

profile of v12, /device:TPU:246, one launch (start us, length us, event | category | flops | bytes accessed | tf_op | source)
XLA Modules:
  0.0 89.2 jit_solution(9409254599986225288)
XLA Ops:
  0.0 0.0 copy-start
  0.0 0.0 copy-start.1
  0.0 3.1 %copy.19 = bf16[3,24,32,256]{3,1,0,2:T(8,128)(2,1)S(1)} copy(f32[3,24,32,256]{3,2,1,0:T(8,128)} %base_ref.5) | data formatting | bytes 3538944 | tf_op args[0]
  3.1 0.0 copy-done.1
  3.1 1.3 %copy.18 = bf16[3,24,32,256]{3,1,0,2:T(8,128)(2,1)S(1)} copy(f32[3,24,32,256]{3,2,1,0:T(8,128)S(1)} %copy-done.1) | data formatting | bytes 3538944 | tf_op args[1]
  4.4 1.6 %maximum_bitcast_fusion = bf16[6,24,32,1,256]{4,1,0,3,2:T(8,128)(2,1)} fusion(bf16[3,24,32,256]{3,1,0,2:T(8,128)(2,1)S(1)} %copy.18, bf16[3,24,32,256]{3,1,0,2:T(8,128)(2,1)S(1)} %copy.19), kind=kLoop, calls=%fused_computation | loop fusion | flops 1179648 | bytes 4718592 | tf_op jit(solution)/shard_map/reshape | solution.py:205
  6.0 4.5 %all-to-all-start = ((bf16[6,24,32,1,256]{4,1,0,3,2:T(8,128)(2,1)}), bf16[6,24,32,1,256]{4,1,0,3,2:T(8,128)(2,1)}, u32[]{:S(2)}, u32[]{:S(2)}) async-start(bf16[6,24,32,1,256]{4,1,0,3,2:T(8,128)(2,1)} %maximum_bitcast_fusion), calls=%async_computation | async-start | bytes 4718592 | tf_op jit(solution)/shard_map/all_to_all | solution.py:206
  10.5 1.5 %slice_bitcast_fusion.2 = (f32[1,3,4,32,256]{4,3,2,1,0:T(8,128)S(1)}, f32[1,3,4,32,256]{4,3,2,1,0:T(8,128)S(1)}, f32[1,3,4,32,256]{4,3,2,1,0:T(8,128)S(1)}, f32[1,3,4,32,256]{4,3,2,1,0:T(8,128)S(1)}) fusion(f32[3,24,32,256]{3,2,1,0:T(8,128)} %adj_ref.5, f32[3,24,32,256]{3,2,1,0:T(8,128)} %base_ref.5), kind=kLoop, calls=%fused_computation.21 | loop fusion | bytes 3145728 | tf_op jit(solution)/shard_map/stack | solution.py:207
  11.9 1.5 %pad_maximum_fusion.1 = (f32[2,3,4,32,256]{4,3,2,1,0:T(8,128)}, f32[2,3,4,32,256]{4,3,2,1,0:T(8,128)}, f32[2,3,4,32,256]{4,3,2,1,0:T(8,128)}) fusion(f32[1,3,4,32,256]{4,3,2,1,0:T(8,128)S(1)} %get-tuple-element.38, f32[1,3,4,32,256]{4,3,2,1,0:T(8,128)S(1)} %get-tuple-element.42, f32[1,3,4,32,256]{4,3,2,1,0:T(8,128)S(1)} %get-tuple-element.37, ...), kind=kLoop, calls=%fused_computation.18 | loop fusion | flops 589824 | bytes 3932161 | tf_op jit(solution)/shard_map/stack | solution.py:208
  13.5 3.8 %collective-permute-start.2 = (f32[2,3,4,32,256]{4,3,2,1,0:T(8,128)}, f32[2,3,4,32,256]{4,3,2,1,0:T(8,128)}, u32[]{:S(2)}, u32[]{:S(2)}) collective-permute-start(f32[2,3,4,32,256]{4,3,2,1,0:T(8,128)} %get-tuple-element.39), channel_id=1, source_target_pairs={{4,0},{8,4},{12,8},{16,12},{20,16},{24,20},{28,24},{32,28},{36,32}... | collective-permute-start | bytes 2359304 | tf_op jit(solution)/shard_map/ppermute | solution.py:26
  17.3 1.3 %collective-permute-start.1 = (f32[2,3,4,32,256]{4,3,2,1,0:T(8,128)}, f32[2,3,4,32,256]{4,3,2,1,0:T(8,128)S(1)}, u32[]{:S(2)}, u32[]{:S(2)}) collective-permute-start(f32[2,3,4,32,256]{4,3,2,1,0:T(8,128)} %get-tuple-element.41), channel_id=1, source_target_pairs={{0,4},{4,8},{8,12},{12,16},{16,20},{20,24},{24,28},{28,32},{32,36}... | collective-permute-start | bytes 2359304 | tf_op jit(solution)/shard_map/ppermute | solution.py:26
  18.6 10.0 %shard_map.46.prev_ref = f32[3,24,32,256]{3,2,1,0:T(8,128)} custom-call(f32[3,24,32,256]{3,2,1,0:T(8,128)} %base_ref.5, f32[3,24,32,256]{3,2,1,0:T(8,128)} %adj_ref.5), custom_call_target="tpu_custom_call" | custom-call | tf_op jit(solution)/shard_map/pallas_call | solution.py:89
  28.6 1.9 %collective-permute-start = (f32[2,3,4,32,256]{4,3,2,1,0:T(8,128)}, f32[2,3,4,32,256]{4,3,2,1,0:T(8,128)}, u32[]{:S(2)}, u32[]{:S(2)}) collective-permute-start(f32[2,3,4,32,256]{4,3,2,1,0:T(8,128)} %get-tuple-element.25), channel_id=1, source_target_pairs={{124,128},{252,0},{128,124},{0,252},{125,129},{253,1},{129,125},{1... | collective-permute-start | bytes 2359304 | tf_op jit(solution)/shard_map/ppermute | solution.py:215
  30.5 25.4 %all-to-all-done = bf16[6,24,32,1,256]{4,1,0,3,2:T(8,128)(2,1)} async-done(((bf16[6,24,32,1,256]{4,1,0,3,2:T(8,128)(2,1)}), bf16[6,24,32,1,256]{4,1,0,3,2:T(8,128)(2,1)}, u32[]{:S(2)}, u32[]{:S(2)}) %all-to-all-start) | async-done | bytes 2359328 | tf_op jit(solution)/shard_map/all_to_all | solution.py:206
  55.8 2.5 %copy.20 = bf16[6,24,4,8,1,256]{5,3,2,1,0,4:T(8,128)(2,1)S(1)} copy(bf16[6,24,4,8,1,256]{5,1,0,3,2,4:T(8,128)(2,1)} %bitcast.6) | data formatting | bytes 4718592 | tf_op jit(solution)/shard_map/all_to_all | solution.py:206
  58.4 0.0 collective-permute-done.2.head_ref
  58.4 0.0 collective-permute-done.1.tail_ref
  58.4 0.0 copy-start.2
  58.4 0.0 copy-start.3
  58.5 0.2 fusion.12
  58.7 0.6 copy-done.2
  59.3 0.1 convert.1
  59.4 0.9 %copy-done.3 = bf16[1024,1024]{1,0:T(8,128)(2,1)S(1)} copy-done((bf16[1024,1024]{1,0:T(8,128)(2,1)S(1)}, bf16[1024,1024]{1,0:T(8,128)(2,1)}, u32[]{:S(2)}) %copy-start.3) | copy-done | bytes 2097176
  60.3 1.4 %fusion.1 = f32[3,24,8,1024]{3,2,1,0:T(8,128)S(1)} fusion(bf16[3,24,8,1024]{3,2,1,0:T(8,128)(2,1)S(1)} %bitcast.54, bf16[1024,1024]{1,0:T(8,128)(2,1)S(1)} %copy-done.3), kind=kOutput, calls=%fused_computation.9 | convolution fusion | flops 1207959552 | bytes 5636096 | tf_op jit(solution)/shard_map/fxzk,ik->fxzi/dot_general | solution.py:224
  61.7 0.0 copy-done
  61.7 1.4 %multiply_reduce_fusion = f32[24,8,1024]{2,1,0:T(8,128)S(1)} fusion(bf16[3,24,8,1024]{3,2,1,0:T(8,128)(2,1)S(1)} %bitcast.55, bf16[3,24,8,1024]{3,2,1,0:T(8,128)(2,1)S(1)} %bitcast.59, bf16[1024,1024]{1,0:T(8,128)(2,1)S(1)} %copy-done), kind=kOutput, calls=%fused_computation.7 | convolution fusion | flops 1209532416 | bytes 5242880 | tf_op jit(solution)/shard_map/fxzk,ik->fxzi/dot_general | solution.py:222
  63.2 1.5 %multiply_add_fusion = f32[3,24,8,1024]{3,2,1,0:T(8,128)S(1)} fusion(f32[3,24,8,1024]{3,2,1,0:T(8,128)S(1)} %fusion.1, bf16[3,24,8,1024]{3,2,1,0:T(8,128)(2,1)S(1)} %bitcast.56, bf16[1024,1024]{1,0:T(8,128)(2,1)S(1)} %copy-done, f32[24,8,1024]{2,1,0:T(8,128)S(1)} %convert.1), kind=kOutput, calls=%fused_computation.8 | convolution fusion | flops 1209729024 | bytes 8781824 | tf_op jit(solution)/shard_map/fxzk,ik->fxzi/dot_general | solution.py:223
  64.6 0.2 fusion.11
  64.9 0.2 convert_element_type.33
  65.1 1.1 %copy.10 = bf16[3,24,8,4,256]{4,2,1,0,3:T(8,128)(2,1)} copy(bf16[3,24,8,4,256]{4,2,3,1,0:T(8,128)(2,1)S(1)} %bitcast.57) | data formatting | bytes 2359296 | tf_op jit(solution)/shard_map/optimization_barrier | solution.py:230
  66.2 3.5 %all-to-all-start.1 = ((bf16[3,24,8,4,256]{4,2,1,0,3:T(8,128)(2,1)}), bf16[3,24,8,4,256]{4,2,1,0,3:T(8,128)(2,1)S(1)}, u32[]{:S(2)}, u32[]{:S(2)}) async-start(bf16[3,24,8,4,256]{4,2,1,0,3:T(8,128)(2,1)} %copy.10), calls=%async_computation.1 | async-start | bytes 2359296 | tf_op jit(solution)/shard_map/all_to_all | solution.py:231
  69.8 7.3 %shard_map.47.prev_ref = f32[3,24,32,256]{3,2,1,0:T(8,128)} custom-call(f32[3,24,32,256]{3,2,1,0:T(8,128)} %base_ref.5, f32[3,24,32,256]{3,2,1,0:T(8,128)} %adj_ref.5, f32[2,3,4,32,256]{4,3,2,1,0:T(8,128)} %copy-done.2, f32[2,3,4,32,256]{4,3,2,1,0:T(8,128)} %collective-permute-done.2.head_ref, ...), custom_call_target="tpu_custom_call", output_to_operand_aliasing={{}: (4, {})} | custom-call | tf_op jit(solution)/shard_map/pallas_call | solution.py:131
  77.1 0.0 collective-permute-done
  77.1 2.2 %broadcast_select_fusion.1.halo_ref = f32[2,3,4,32,256]{4,3,2,1,0:T(8,128)} fusion(f32[2,3,4,32,256]{4,3,2,1,0:T(8,128)} %collective-permute-done, f32[2,3,4,32,256]{4,3,2,1,0:T(8,128)} %copy-done.2, pred[]{:T(512)S(6)} %or.11), kind=kLoop, calls=%fused_computation.24 | loop fusion | flops 196608 | bytes 2359297 | tf_op jit(solution)/shard_map/jit(_where)/select_n | solution.py:218
  79.2 4.1 %shard_map.48 = f32[3,24,32,256]{3,2,1,0:T(8,128)} custom-call(s32[1]{0:T(128)} %bitcast.side_ref, f32[3,24,32,256]{3,2,1,0:T(8,128)} %base_ref.5, f32[3,24,32,256]{3,2,1,0:T(8,128)} %adj_ref.5, f32[2,3,4,32,256]{4,3,2,1,0:T(8,128)} %broadcast_select_fusion.1.halo_ref, f32[3,24,32,256]{3,2,1,0:T(8,128)} %shard_map.47.prev_ref), custom_call_target="tpu_custom_call", output_to_operand_aliasing={{}: (4, {})} | custom-call | tf_op jit(solution)/shard_map/pallas_call | solution.py:189
  83.4 2.2 %all-to-all-done.1 = bf16[3,24,8,4,256]{4,2,1,0,3:T(8,128)(2,1)S(1)} async-done(((bf16[3,24,8,4,256]{4,2,1,0,3:T(8,128)(2,1)}), bf16[3,24,8,4,256]{4,2,1,0,3:T(8,128)(2,1)S(1)}, u32[]{:S(2)}, u32[]{:S(2)}) %all-to-all-start.1) | async-done | bytes 1179680 | tf_op jit(solution)/shard_map/all_to_all | solution.py:231
  85.5 3.6 %fusion = f32[3,24,32,256]{3,2,1,0:T(8,128)} fusion(f32[3,24,32,256]{3,2,1,0:T(8,128)} %shard_map.48, pred[256]{0:T(512)(128)(4,1)S(1)} %compare_and_fusion, bf16[3,24,8,4,256]{4,2,1,0,3:T(8,128)(2,1)S(1)} %all-to-all-done.1), kind=kLoop, calls=%fused_computation.2 | loop fusion | flops 2359296 | bytes 5898496 | tf_op jit(solution)/shard_map/jit(_where)/select_n | solution.py:239
  (2 shorter events, 0.0 us)
Async XLA Ops:
  0.0 61.7 %copy-start = (bf16[1024,1024]{1,0:T(8,128)(2,1)S(1)}, bf16[1024,1024]{1,0:T(8,128)(2,1)}, u32[]{:S(2)}) copy-start(bf16[1024,1024]{1,0:T(8,128)(2,1)} %param.8) | copy-start | bytes 6291460
  0.0 3.1 %copy-start.1 = (f32[3,24,32,256]{3,2,1,0:T(8,128)S(1)}, f32[3,24,32,256]{3,2,1,0:T(8,128)}, u32[]{:S(2)}) copy-start(f32[3,24,32,256]{3,2,1,0:T(8,128)} %adj_ref.5) | copy-start | bytes 7077892
  6.0 49.9 %all-to-all-start = ((bf16[6,24,32,1,256]{4,1,0,3,2:T(8,128)(2,1)}), bf16[6,24,32,1,256]{4,1,0,3,2:T(8,128)(2,1)}, u32[]{:S(2)}, u32[]{:S(2)}) async-start(bf16[6,24,32,1,256]{4,1,0,3,2:T(8,128)(2,1)} %maximum_bitcast_fusion), calls=%async_computation | async-start | bytes 4718592 | tf_op jit(solution)/shard_map/all_to_all | solution.py:206
  13.5 44.9 %collective-permute-start.2 = (f32[2,3,4,32,256]{4,3,2,1,0:T(8,128)}, f32[2,3,4,32,256]{4,3,2,1,0:T(8,128)}, u32[]{:S(2)}, u32[]{:S(2)}) collective-permute-start(f32[2,3,4,32,256]{4,3,2,1,0:T(8,128)} %get-tuple-element.39), channel_id=1, source_target_pairs={{4,0},{8,4},{12,8},{16,12},{20,16},{24,20},{28,24},{32,28},{36,32}... | collective-permute-start | bytes 2359304 | tf_op jit(solution)/shard_map/ppermute | solution.py:26
  17.3 41.1 %collective-permute-start.1 = (f32[2,3,4,32,256]{4,3,2,1,0:T(8,128)}, f32[2,3,4,32,256]{4,3,2,1,0:T(8,128)S(1)}, u32[]{:S(2)}, u32[]{:S(2)}) collective-permute-start(f32[2,3,4,32,256]{4,3,2,1,0:T(8,128)} %get-tuple-element.41), channel_id=1, source_target_pairs={{0,4},{4,8},{8,12},{12,16},{16,20},{20,24},{24,28},{28,32},{32,36}... | collective-permute-start | bytes 2359304 | tf_op jit(solution)/shard_map/ppermute | solution.py:26
  28.6 48.5 %collective-permute-start = (f32[2,3,4,32,256]{4,3,2,1,0:T(8,128)}, f32[2,3,4,32,256]{4,3,2,1,0:T(8,128)}, u32[]{:S(2)}, u32[]{:S(2)}) collective-permute-start(f32[2,3,4,32,256]{4,3,2,1,0:T(8,128)} %get-tuple-element.25), channel_id=1, source_target_pairs={{124,128},{252,0},{128,124},{0,252},{125,129},{253,1},{129,125},{1... | collective-permute-start | bytes 2359304 | tf_op jit(solution)/shard_map/ppermute | solution.py:215
  58.4 0.9 %copy-start.2 = (f32[2,3,4,32,256]{4,3,2,1,0:T(8,128)}, f32[2,3,4,32,256]{4,3,2,1,0:T(8,128)S(1)}, u32[]{:S(2)}) copy-start(f32[2,3,4,32,256]{4,3,2,1,0:T(8,128)S(1)} %collective-permute-done.1.tail_ref) | copy-start | bytes 2359300
  58.4 1.8 %copy-start.3 = (bf16[1024,1024]{1,0:T(8,128)(2,1)S(1)}, bf16[1024,1024]{1,0:T(8,128)(2,1)}, u32[]{:S(2)}) copy-start(bf16[1024,1024]{1,0:T(8,128)(2,1)} %param.9) | copy-start | bytes 6291460
  66.2 19.3 %all-to-all-start.1 = ((bf16[3,24,8,4,256]{4,2,1,0,3:T(8,128)(2,1)}), bf16[3,24,8,4,256]{4,2,1,0,3:T(8,128)(2,1)S(1)}, u32[]{:S(2)}, u32[]{:S(2)}) async-start(bf16[3,24,8,4,256]{4,2,1,0,3:T(8,128)(2,1)} %copy.10), calls=%async_computation.1 | async-start | bytes 2359296 | tf_op jit(solution)/shard_map/all_to_all | solution.py:231

commit v13 on v11

--- a/solution.py
+++ b/solution.py
@@ -208,11 +208,21 @@
     head_cells = jnp.stack((base_flow[:, :HALO], adjoint[:, :HALO]), 0)
     tails = ring_shift(tail_cells, "gx", True, far, False)
     heads = ring_shift(head_cells, "gx", False, far, False)
-    far_pairs, sends_tail, gets_tail = far_plan(far)
+    count = lax.axis_size("gx")
+    far_all = [i for i in range(count) if far[i]]
+    assert far_all
+    early_links = [i for i in far_all if i != count - 1]
+    late_links = [i for i in far_all if i == count - 1]
+    _, sends_tail, gets_tail = far_plan(far_all)
     far_send = jnp.where(sends_tail, tail_cells, head_cells)
     partial = interior_update(base_flow, adjoint)
+    partial, far_send = lax.optimization_barrier((partial, far_send))
+    received = jnp.zeros_like(far_send)
+    if early_links:
+        received = lax.ppermute(far_send, "gx", far_plan(early_links)[0])
     lines, partial, tails, heads, far_send = lax.optimization_barrier((lines, partial, tails, heads, far_send))
-    received = lax.ppermute(far_send, "gx", far_pairs)
+    if late_links:
+        received = received + lax.ppermute(far_send, "gx", far_plan(late_links)[0])
     far_side = jnp.where(sends_tail, 1, 0).astype(jnp.int32).reshape(1)
     side_halo = jnp.where(gets_tail | sends_tail, received, tails)
     lines = lines.reshape(2 * comps, cells, part, total_rows)
@@ -238,12 +248,11 @@
     return jnp.where(interior, updated, jnp.float32(0.0))
 
 
-def far_plan(far):
+def far_plan(links):
     count = lax.axis_size("gx")
-    links = [i for i in range(count) if far[i]]
     tail_senders = {i for i in links}
     head_senders = {(i + 1) % count for i in links}
-    assert links and not (tail_senders & head_senders)
+    assert not (tail_senders & head_senders)
     pairs = [(i, (i + 1) % count) for i in links] + [((i + 1) % count, i) for i in links]
     position = lax.axis_index("gx")
     sends_tail = jnp.zeros((), jnp.bool_)

time: 88 us -> 102 us (1.16)
  starting transfers between devices: 26.2 us -> 46.7 us
  waiting for transfers between devices: 15.7 us -> 8.7 us
    ppermute x1 -> x2, starting transfers between devices: 10.6 us -> 29 us  [the longest x1 27.5 us: body(): received = received + lax.ppermute(far_send, 'gx', far_plan(late_links)[0])]
    all_to_all x1, waiting for transfers between devices: 11.5 us -> 7.73 us  [body(): lines = lax.all_to_all(low, 'gy', split_axis=2, concat_axis=3, tiled=True)]
    all_to_all x1, waiting for transfers between devices: 4.17 us -> 0.96 us  [body(): lax.all_to_all(wall_part, 'gy', split_axis=3, concat_axis=2, tiled=True)]
    ppermute x2, starting transfers between devices: 3.16 us -> 5.32 us  [ring_shift(): return lax.ppermute(value, axis, pairs)]
    another operation x0 -> x1, other arithmetic: none -> 1.56 us  [body(): head_cells = jnp.stack((base_flow[:, :HALO], adjoint[:, :HALO]), 0)]
    select_n x1 -> x0, other arithmetic: 1.5 us -> none  [body(): far_send = jnp.where(sends_tail, tail_cells, head_cells)]
  transfers between devices with their start and end apart: 5 -> 6, of which waited for: 2 -> 2; matrix products, arithmetic and copies ran while one was open for 15% -> 14% of each run, Pallas kernels for 25% -> 21%
where the time goes in v13:
time: 102 us; the launch traced here: 101 us
  starting transfers between devices  46.7 us (46%)
  Pallas kernels  21.4 us (21%)
  local copies, waits for them, and re-layouts  10.3 us (10%)
  other arithmetic  9.75 us (10%)
  waiting for transfers between devices  8.7 us (9%)
  matrix products  4.33 us (4%)
    ppermute x1, starting transfers between devices, body(): received = received + lax.ppermute(far_send, 'gx', far_plan(late_links)[0])  27.5 us
    pallas_call x1, Pallas kernels, interior_update(): pl.pallas_call(interior_kernel, grid=(rows // LANES, cells // HALO - 2),...  10 us
    all_to_all x1, waiting for transfers between devices, body(): lines = lax.all_to_all(low, 'gy', split_axis=2, concat_axis=3, tiled=True)  7.73 us
    all_to_all x1, starting transfers between devices, body(): lines = lax.all_to_all(low, 'gy', split_axis=2, concat_axis=3, tiled=True)  7.66 us
    pallas_call x1, Pallas kernels, boundary_update(): pl.pallas_call(boundary_kernel, grid=(2,), in_specs=[full_spec, full_spec...  7.28 us
    ppermute x2, starting transfers between devices, ring_shift(): return lax.ppermute(value, axis, pairs)  5.32 us
    unnamed x10, local copies, waits for them, and re-layouts  4.97 us
    all_to_all x1, starting transfers between devices, body(): lax.all_to_all(wall_part, 'gy', split_axis=3, concat_axis=2, tiled=True)  4.74 us
  transfers between devices with their start and end apart: 6, of which 2 were waited for; matrix products, arithmetic and copies ran while one was open for 14% of the time, Pallas kernels for 21%

profile of v13, /device:TPU:1, one launch (start us, length us, event | category | flops | bytes accessed | tf_op | source)
XLA Modules:
  0.0 101.4 jit_solution(9019406587691077318)
XLA Ops:
  0.0 0.0 copy-start
  0.0 0.0 copy-start.1
  0.0 3.1 %copy.19 = bf16[3,24,32,256]{3,1,0,2:T(8,128)(2,1)S(1)} copy(f32[3,24,32,256]{3,2,1,0:T(8,128)} %base_ref.5) | data formatting | bytes 3538944 | tf_op args[0]
  3.1 0.0 copy-done.1
  3.1 1.3 %copy.18 = bf16[3,24,32,256]{3,1,0,2:T(8,128)(2,1)S(1)} copy(f32[3,24,32,256]{3,2,1,0:T(8,128)S(1)} %copy-done.1) | data formatting | bytes 3538944 | tf_op args[1]
  4.4 1.6 %maximum_bitcast_fusion = bf16[6,24,32,1,256]{4,1,0,3,2:T(8,128)(2,1)} fusion(bf16[3,24,32,256]{3,1,0,2:T(8,128)(2,1)S(1)} %copy.18, bf16[3,24,32,256]{3,1,0,2:T(8,128)(2,1)S(1)} %copy.19), kind=kLoop, calls=%fused_computation | loop fusion | flops 1179648 | bytes 4718592 | tf_op jit(solution)/shard_map/reshape | solution.py:205
  6.0 7.7 %all-to-all-start = ((bf16[6,24,32,1,256]{4,1,0,3,2:T(8,128)(2,1)}), bf16[6,24,32,1,256]{4,1,0,3,2:T(8,128)(2,1)}, u32[]{:S(2)}, u32[]{:S(2)}) async-start(bf16[6,24,32,1,256]{4,1,0,3,2:T(8,128)(2,1)} %maximum_bitcast_fusion), calls=%async_computation | async-start | bytes 4718592 | tf_op jit(solution)/shard_map/all_to_all | solution.py:206
  13.6 1.5 %slice_bitcast_fusion.2 = (f32[1,3,4,32,256]{4,3,2,1,0:T(8,128)S(1)}, f32[1,3,4,32,256]{4,3,2,1,0:T(8,128)S(1)}, f32[1,3,4,32,256]{4,3,2,1,0:T(8,128)S(1)}, f32[1,3,4,32,256]{4,3,2,1,0:T(8,128)S(1)}) fusion(f32[3,24,32,256]{3,2,1,0:T(8,128)} %adj_ref.5, f32[3,24,32,256]{3,2,1,0:T(8,128)} %base_ref.5), kind=kLoop, calls=%fused_computation.22 | loop fusion | bytes 3145728 | tf_op jit(solution)/shard_map/stack | solution.py:207
  15.1 1.6 %pad_maximum_fusion.1 = (f32[2,3,4,32,256]{4,3,2,1,0:T(8,128)}, f32[2,3,4,32,256]{4,3,2,1,0:T(8,128)}, f32[2,3,4,32,256]{4,3,2,1,0:T(8,128)}) fusion(f32[1,3,4,32,256]{4,3,2,1,0:T(8,128)S(1)} %get-tuple-element.40, f32[1,3,4,32,256]{4,3,2,1,0:T(8,128)S(1)} %get-tuple-element.44, f32[1,3,4,32,256]{4,3,2,1,0:T(8,128)S(1)} %get-tuple-element.39, ...), kind=kLoop, calls=%fused_computation.18 | loop fusion | flops 589824 | bytes 3932161 | tf_op jit(solution)/shard_map/stack | solution.py:208
  16.6 1.3 %collective-permute-start.2 = (f32[2,3,4,32,256]{4,3,2,1,0:T(8,128)}, f32[2,3,4,32,256]{4,3,2,1,0:T(8,128)}, u32[]{:S(2)}, u32[]{:S(2)}) collective-permute-start(f32[2,3,4,32,256]{4,3,2,1,0:T(8,128)} %get-tuple-element.41), channel_id=1, source_target_pairs={{4,0},{8,4},{12,8},{16,12},{20,16},{24,20},{28,24},{32,28},{36,32}... | collective-permute-start | bytes 2359304 | tf_op jit(solution)/shard_map/ppermute | solution.py:26
  17.9 4.0 %collective-permute-start.1 = (f32[2,3,4,32,256]{4,3,2,1,0:T(8,128)}, f32[2,3,4,32,256]{4,3,2,1,0:T(8,128)S(1)}, u32[]{:S(2)}, u32[]{:S(2)}) collective-permute-start(f32[2,3,4,32,256]{4,3,2,1,0:T(8,128)} %get-tuple-element.43), channel_id=1, source_target_pairs={{0,4},{4,8},{8,12},{12,16},{16,20},{20,24},{24,28},{28,32},{32,36}... | collective-permute-start | bytes 2359304 | tf_op jit(solution)/shard_map/ppermute | solution.py:26
  22.0 10.0 %shard_map.46.prev_ref = f32[3,24,32,256]{3,2,1,0:T(8,128)} custom-call(f32[3,24,32,256]{3,2,1,0:T(8,128)} %base_ref.5, f32[3,24,32,256]{3,2,1,0:T(8,128)} %adj_ref.5), custom_call_target="tpu_custom_call" | custom-call | tf_op jit(solution)/shard_map/pallas_call | solution.py:89
  32.0 1.5 %collective-permute-start = (f32[2,3,4,32,256]{4,3,2,1,0:T(8,128)}, f32[2,3,4,32,256]{4,3,2,1,0:T(8,128)}, u32[]{:S(2)}, u32[]{:S(2)}) collective-permute-start(f32[2,3,4,32,256]{4,3,2,1,0:T(8,128)} %get-tuple-element.28), channel_id=1, source_target_pairs={{124,128},{128,124},{125,129},{129,125},{126,130},{130,126},{127,1... | collective-permute-start | bytes 2359304 | tf_op jit(solution)/shard_map/ppermute | solution.py:222
  33.5 7.7 %all-to-all-done = bf16[6,24,32,1,256]{4,1,0,3,2:T(8,128)(2,1)} async-done(((bf16[6,24,32,1,256]{4,1,0,3,2:T(8,128)(2,1)}), bf16[6,24,32,1,256]{4,1,0,3,2:T(8,128)(2,1)}, u32[]{:S(2)}, u32[]{:S(2)}) %all-to-all-start) | async-done | bytes 2359328 | tf_op jit(solution)/shard_map/all_to_all | solution.py:206
  41.2 2.5 %copy.20 = bf16[6,24,4,8,1,256]{5,3,2,1,0,4:T(8,128)(2,1)S(1)} copy(bf16[6,24,4,8,1,256]{5,1,0,3,2,4:T(8,128)(2,1)} %bitcast.6) | data formatting | bytes 4718592 | tf_op jit(solution)/shard_map/all_to_all | solution.py:206
  43.8 0.0 collective-permute-done.2.head_ref
  43.8 0.0 collective-permute-done.1.tail_ref
  43.8 0.0 copy-start.2
  43.8 0.0 copy-start.3
  43.8 0.2 fusion.12
  44.1 0.6 copy-done.2
  44.7 0.1 convert.1
  44.8 27.5 %collective-permute-start.3 = (f32[2,3,4,32,256]{4,3,2,1,0:T(8,128)}, f32[2,3,4,32,256]{4,3,2,1,0:T(8,128)}, u32[]{:S(2)}, u32[]{:S(2)}) collective-permute-start(f32[2,3,4,32,256]{4,3,2,1,0:T(8,128)} %get-tuple-element.28), channel_id=1, source_target_pairs={{252,0},{0,252},{253,1},{1,253},{254,2},{2,254},{255,3},{3,255}} | collective-permute-start | bytes 2359304 | tf_op jit(solution)/shard_map/ppermute | solution.py:225
  72.2 0.0 copy-done.3
  72.2 1.4 %fusion.1 = f32[3,24,8,1024]{3,2,1,0:T(8,128)S(1)} fusion(bf16[3,24,8,1024]{3,2,1,0:T(8,128)(2,1)S(1)} %bitcast.54, bf16[1024,1024]{1,0:T(8,128)(2,1)S(1)} %copy-done.3), kind=kOutput, calls=%fused_computation.9 | convolution fusion | flops 1207959552 | bytes 5636096 | tf_op jit(solution)/shard_map/fxzk,ik->fxzi/dot_general | solution.py:233
  73.7 0.0 copy-done
  73.7 1.4 %multiply_reduce_fusion = f32[24,8,1024]{2,1,0:T(8,128)S(1)} fusion(bf16[3,24,8,1024]{3,2,1,0:T(8,128)(2,1)S(1)} %bitcast.55, bf16[3,24,8,1024]{3,2,1,0:T(8,128)(2,1)S(1)} %bitcast.59, bf16[1024,1024]{1,0:T(8,128)(2,1)S(1)} %copy-done), kind=kOutput, calls=%fused_computation.7 | convolution fusion | flops 1209532416 | bytes 5242880 | tf_op jit(solution)/shard_map/fxzk,ik->fxzi/dot_general | solution.py:231
  75.1 1.5 %multiply_add_fusion = f32[3,24,8,1024]{3,2,1,0:T(8,128)S(1)} fusion(f32[3,24,8,1024]{3,2,1,0:T(8,128)S(1)} %fusion.1, bf16[3,24,8,1024]{3,2,1,0:T(8,128)(2,1)S(1)} %bitcast.56, bf16[1024,1024]{1,0:T(8,128)(2,1)S(1)} %copy-done, f32[24,8,1024]{2,1,0:T(8,128)S(1)} %convert.1), kind=kOutput, calls=%fused_computation.8 | convolution fusion | flops 1209729024 | bytes 8781824 | tf_op jit(solution)/shard_map/fxzk,ik->fxzi/dot_general | solution.py:232
  76.6 0.2 fusion.11
  76.8 0.2 convert_element_type.33
  77.0 1.1 %copy.10 = bf16[3,24,8,4,256]{4,2,1,0,3:T(8,128)(2,1)} copy(bf16[3,24,8,4,256]{4,2,3,1,0:T(8,128)(2,1)S(1)} %bitcast.57) | data formatting | bytes 2359296 | tf_op jit(solution)/shard_map/optimization_barrier | solution.py:239
  78.2 4.7 %all-to-all-start.1 = ((bf16[3,24,8,4,256]{4,2,1,0,3:T(8,128)(2,1)}), bf16[3,24,8,4,256]{4,2,1,0,3:T(8,128)(2,1)S(1)}, u32[]{:S(2)}, u32[]{:S(2)}) async-start(bf16[3,24,8,4,256]{4,2,1,0,3:T(8,128)(2,1)} %copy.10), calls=%async_computation.1 | async-start | bytes 2359296 | tf_op jit(solution)/shard_map/all_to_all | solution.py:240
  82.9 7.3 %shard_map.47.prev_ref = f32[3,24,32,256]{3,2,1,0:T(8,128)} custom-call(f32[3,24,32,256]{3,2,1,0:T(8,128)} %base_ref.5, f32[3,24,32,256]{3,2,1,0:T(8,128)} %adj_ref.5, f32[2,3,4,32,256]{4,3,2,1,0:T(8,128)} %copy-done.2, f32[2,3,4,32,256]{4,3,2,1,0:T(8,128)} %collective-permute-done.2.head_ref, ...), custom_call_target="tpu_custom_call", output_to_operand_aliasing={{}: (4, {})} | custom-call | tf_op jit(solution)/shard_map/pallas_call | solution.py:131
  90.2 0.0 collective-permute-done
  90.2 0.0 collective-permute-done.3
  90.2 2.5 %add_select_fusion.halo_ref = f32[2,3,4,32,256]{4,3,2,1,0:T(8,128)} fusion(f32[2,3,4,32,256]{4,3,2,1,0:T(8,128)} %copy-done.2, f32[2,3,4,32,256]{4,3,2,1,0:T(8,128)} %collective-permute-done, f32[2,3,4,32,256]{4,3,2,1,0:T(8,128)} %collective-permute-done.3, pred[]{:T(512)S(6)} %or.11), kind=kLoop, calls=%fused_computation.19 | loop fusion | flops 393216 | bytes 3145729 | tf_op jit(solution)/shard_map/jit(_where)/select_n | solution.py:227
  92.7 4.1 %shard_map.48 = f32[3,24,32,256]{3,2,1,0:T(8,128)} custom-call(s32[1]{0:T(128)} %bitcast.side_ref, f32[3,24,32,256]{3,2,1,0:T(8,128)} %base_ref.5, f32[3,24,32,256]{3,2,1,0:T(8,128)} %adj_ref.5, f32[2,3,4,32,256]{4,3,2,1,0:T(8,128)} %add_select_fusion.halo_ref, f32[3,24,32,256]{3,2,1,0:T(8,128)} %shard_map.47.prev_ref), custom_call_target="tpu_custom_call", output_to_operand_aliasing={{}: (4, {})} | custom-call | tf_op jit(solution)/shard_map/pallas_call | solution.py:189
  96.8 1.0 all-to-all-done.1
  97.8 3.6 %fusion = f32[3,24,32,256]{3,2,1,0:T(8,128)} fusion(f32[3,24,32,256]{3,2,1,0:T(8,128)} %shard_map.48, pred[256]{0:T(512)(128)(4,1)S(1)} %compare_and_fusion, bf16[3,24,8,4,256]{4,2,1,0,3:T(8,128)(2,1)S(1)} %all-to-all-done.1), kind=kLoop, calls=%fused_computation.2 | loop fusion | flops 2359296 | bytes 5898496 | tf_op jit(solution)/shard_map/jit(_where)/select_n | solution.py:248
  (2 shorter events, 0.0 us)
Async XLA Ops:
  0.0 73.7 %copy-start = (bf16[1024,1024]{1,0:T(8,128)(2,1)S(1)}, bf16[1024,1024]{1,0:T(8,128)(2,1)}, u32[]{:S(2)}) copy-start(bf16[1024,1024]{1,0:T(8,128)(2,1)} %param.8) | copy-start | bytes 6291460
  0.0 3.1 %copy-start.1 = (f32[3,24,32,256]{3,2,1,0:T(8,128)S(1)}, f32[3,24,32,256]{3,2,1,0:T(8,128)}, u32[]{:S(2)}) copy-start(f32[3,24,32,256]{3,2,1,0:T(8,128)} %adj_ref.5) | copy-start | bytes 7077892
  6.0 35.3 %all-to-all-start = ((bf16[6,24,32,1,256]{4,1,0,3,2:T(8,128)(2,1)}), bf16[6,24,32,1,256]{4,1,0,3,2:T(8,128)(2,1)}, u32[]{:S(2)}, u32[]{:S(2)}) async-start(bf16[6,24,32,1,256]{4,1,0,3,2:T(8,128)(2,1)} %maximum_bitcast_fusion), calls=%async_computation | async-start | bytes 4718592 | tf_op jit(solution)/shard_map/all_to_all | solution.py:206
  16.6 27.1 %collective-permute-start.2 = (f32[2,3,4,32,256]{4,3,2,1,0:T(8,128)}, f32[2,3,4,32,256]{4,3,2,1,0:T(8,128)}, u32[]{:S(2)}, u32[]{:S(2)}) collective-permute-start(f32[2,3,4,32,256]{4,3,2,1,0:T(8,128)} %get-tuple-element.41), channel_id=1, source_target_pairs={{4,0},{8,4},{12,8},{16,12},{20,16},{24,20},{28,24},{32,28},{36,32}... | collective-permute-start | bytes 2359304 | tf_op jit(solution)/shard_map/ppermute | solution.py:26
  17.9 25.9 %collective-permute-start.1 = (f32[2,3,4,32,256]{4,3,2,1,0:T(8,128)}, f32[2,3,4,32,256]{4,3,2,1,0:T(8,128)S(1)}, u32[]{:S(2)}, u32[]{:S(2)}) collective-permute-start(f32[2,3,4,32,256]{4,3,2,1,0:T(8,128)} %get-tuple-element.43), channel_id=1, source_target_pairs={{0,4},{4,8},{8,12},{12,16},{16,20},{20,24},{24,28},{28,32},{32,36}... | collective-permute-start | bytes 2359304 | tf_op jit(solution)/shard_map/ppermute | solution.py:26
  32.0 58.2 %collective-permute-start = (f32[2,3,4,32,256]{4,3,2,1,0:T(8,128)}, f32[2,3,4,32,256]{4,3,2,1,0:T(8,128)}, u32[]{:S(2)}, u32[]{:S(2)}) collective-permute-start(f32[2,3,4,32,256]{4,3,2,1,0:T(8,128)} %get-tuple-element.28), channel_id=1, source_target_pairs={{124,128},{128,124},{125,129},{129,125},{126,130},{130,126},{127,1... | collective-permute-start | bytes 2359304 | tf_op jit(solution)/shard_map/ppermute | solution.py:222
  43.8 0.9 copy-start.2
  43.8 28.4 %copy-start.3 = (bf16[1024,1024]{1,0:T(8,128)(2,1)S(1)}, bf16[1024,1024]{1,0:T(8,128)(2,1)}, u32[]{:S(2)}) copy-start(bf16[1024,1024]{1,0:T(8,128)(2,1)} %param.9) | copy-start | bytes 6291460
  44.8 45.4 %collective-permute-start.3 = (f32[2,3,4,32,256]{4,3,2,1,0:T(8,128)}, f32[2,3,4,32,256]{4,3,2,1,0:T(8,128)}, u32[]{:S(2)}, u32[]{:S(2)}) collective-permute-start(f32[2,3,4,32,256]{4,3,2,1,0:T(8,128)} %get-tuple-element.28), channel_id=1, source_target_pairs={{252,0},{0,252},{253,1},{1,253},{254,2},{2,254},{255,3},{3,255}} | collective-permute-start | bytes 2359304 | tf_op jit(solution)/shard_map/ppermute | solution.py:225
  78.2 19.6 %all-to-all-start.1 = ((bf16[3,24,8,4,256]{4,2,1,0,3:T(8,128)(2,1)}), bf16[3,24,8,4,256]{4,2,1,0,3:T(8,128)(2,1)S(1)}, u32[]{:S(2)}, u32[]{:S(2)}) async-start(bf16[3,24,8,4,256]{4,2,1,0,3:T(8,128)(2,1)} %copy.10), calls=%async_computation.1 | async-start | bytes 2359296 | tf_op jit(solution)/shard_map/all_to_all | solution.py:240

commit v14 on v11

--- a/solution.py
+++ b/solution.py
@@ -212,13 +212,14 @@
     far_send = jnp.where(sends_tail, tail_cells, head_cells)
     partial = interior_update(base_flow, adjoint)
     lines, partial, tails, heads, far_send = lax.optimization_barrier((lines, partial, tails, heads, far_send))
-    received = lax.ppermute(far_send, "gx", far_pairs)
-    far_side = jnp.where(sends_tail, 1, 0).astype(jnp.int32).reshape(1)
-    side_halo = jnp.where(gets_tail | sends_tail, received, tails)
     lines = lines.reshape(2 * comps, cells, part, total_rows)
     base_lines = lines[:comps]
     adj_lines = lines[comps:]
     slope_base = jnp.einsum("fxzk,ik->fxzi", base_lines, first_op, preferred_element_type=jnp.float32)
+    slope_base, far_send = lax.optimization_barrier((slope_base, far_send))
+    received = lax.ppermute(far_send, "gx", far_pairs)
+    far_side = jnp.where(sends_tail, 1, 0).astype(jnp.int32).reshape(1)
+    side_halo = jnp.where(gets_tail | sends_tail, received, tails)
     slope_adj = jnp.einsum("fxzk,ik->fxzi", adj_lines, first_op, preferred_element_type=jnp.float32)
     curves = jnp.einsum("fxzk,ik->fxzi", adj_lines, second_op, preferred_element_type=jnp.float32)
     normal_vel = base_lines[1].astype(jnp.float32)

time: 88 us -> 89.6 us (1.018)
  waiting for transfers between devices: 15.7 us -> 16.7 us
  transfers between devices with their start and end apart: 5 -> 5, of which waited for: 2 -> 3; matrix products, arithmetic and copies ran while one was open for 15% -> 14% of each run, Pallas kernels for 25% -> 24%
where the time goes in v14:
time: 89.6 us; the launch traced here: 89 us
  starting transfers between devices  26.3 us (29%)
  Pallas kernels  21.4 us (24%)
  waiting for transfers between devices  16.7 us (19%)
  local copies, waits for them, and re-layouts  10.3 us (11%)
  other arithmetic  9.75 us (11%)
  matrix products  4.3 us (5%)
    all_to_all x1, waiting for transfers between devices, body(): lines = lax.all_to_all(low, 'gy', split_axis=2, concat_axis=3, tiled=True)  11.5 us
    ppermute x1, starting transfers between devices, body(): received = lax.ppermute(far_send, 'gx', far_pairs)  10.7 us
    pallas_call x1, Pallas kernels, interior_update(): pl.pallas_call(interior_kernel, grid=(rows // LANES, cells // HALO - 2),...  10 us
    all_to_all x1, starting transfers between devices, body(): lines = lax.all_to_all(low, 'gy', split_axis=2, concat_axis=3, tiled=True)  7.64 us
    pallas_call x1, Pallas kernels, boundary_update(): pl.pallas_call(boundary_kernel, grid=(2,), in_specs=[full_spec, full_spec...  7.28 us
    unnamed x10, local copies, waits for them, and re-layouts  4.99 us
    all_to_all x1, waiting for transfers between devices, body(): lax.all_to_all(wall_part, 'gy', split_axis=3, concat_axis=2, tiled=True)  4.89 us
    all_to_all x1, starting transfers between devices, body(): lax.all_to_all(wall_part, 'gy', split_axis=3, concat_axis=2, tiled=True)  4.75 us
  transfers between devices with their start and end apart: 5, of which 3 were waited for; matrix products, arithmetic and copies ran while one was open for 14% of the time, Pallas kernels for 24%

profile of v14, /device:TPU:1, one launch (start us, length us, event | category | flops | bytes accessed | tf_op | source)
XLA Modules:
  0.0 89.0 jit_solution(2648096706587072256)
XLA Ops:
  0.0 0.0 copy-start
  0.0 0.0 copy-start.1
  0.0 3.1 %copy.19 = bf16[3,24,32,256]{3,1,0,2:T(8,128)(2,1)S(1)} copy(f32[3,24,32,256]{3,2,1,0:T(8,128)} %base_ref.5) | data formatting | bytes 3538944 | tf_op args[0]
  3.1 0.0 copy-done.1
  3.1 1.3 %copy.18 = bf16[3,24,32,256]{3,1,0,2:T(8,128)(2,1)S(1)} copy(f32[3,24,32,256]{3,2,1,0:T(8,128)S(1)} %copy-done.1) | data formatting | bytes 3538944 | tf_op args[1]
  4.4 1.6 %maximum_bitcast_fusion = bf16[6,24,32,1,256]{4,1,0,3,2:T(8,128)(2,1)} fusion(bf16[3,24,32,256]{3,1,0,2:T(8,128)(2,1)S(1)} %copy.18, bf16[3,24,32,256]{3,1,0,2:T(8,128)(2,1)S(1)} %copy.19), kind=kLoop, calls=%fused_computation | loop fusion | flops 1179648 | bytes 4718592 | tf_op jit(solution)/shard_map/reshape | solution.py:205
  6.0 7.6 %all-to-all-start = ((bf16[6,24,32,1,256]{4,1,0,3,2:T(8,128)(2,1)}), bf16[6,24,32,1,256]{4,1,0,3,2:T(8,128)(2,1)}, u32[]{:S(2)}, u32[]{:S(2)}) async-start(bf16[6,24,32,1,256]{4,1,0,3,2:T(8,128)(2,1)} %maximum_bitcast_fusion), calls=%async_computation | async-start | bytes 4718592 | tf_op jit(solution)/shard_map/all_to_all | solution.py:206
  13.6 1.5 %slice_bitcast_fusion = (f32[1,3,4,32,256]{4,3,2,1,0:T(8,128)S(1)}, f32[1,3,4,32,256]{4,3,2,1,0:T(8,128)S(1)}, f32[1,3,4,32,256]{4,3,2,1,0:T(8,128)S(1)}, f32[1,3,4,32,256]{4,3,2,1,0:T(8,128)S(1)}) fusion(f32[3,24,32,256]{3,2,1,0:T(8,128)} %adj_ref.5, f32[3,24,32,256]{3,2,1,0:T(8,128)} %base_ref.5), kind=kLoop, calls=%fused_computation.19 | loop fusion | bytes 3145728 | tf_op jit(solution)/shard_map/stack | solution.py:208
  15.1 1.5 %broadcast_select_fusion = (f32[2,3,4,32,256]{4,3,2,1,0:T(8,128)}, f32[2,3,4,32,256]{4,3,2,1,0:T(8,128)}, f32[2,3,4,32,256]{4,3,2,1,0:T(8,128)}) fusion(pred[]{:T(512)S(6)} %or.9, f32[1,3,4,32,256]{4,3,2,1,0:T(8,128)S(1)} %get-tuple-element.39, f32[1,3,4,32,256]{4,3,2,1,0:T(8,128)S(1)} %get-tuple-element.45, f32[1,3,4,32,256]{4,3,2,1,0:T(8,128)S(1)} %get-tuple-element.40, ...), kind=kLoop, calls=%fused_computation.23 | loop fusion | flops 589824 | bytes 3932161 | tf_op jit(solution)/shard_map/jit(_where)/select_n | solution.py:212
  16.6 1.9 %collective-permute-start = (f32[2,3,4,32,256]{4,3,2,1,0:T(8,128)}, f32[2,3,4,32,256]{4,3,2,1,0:T(8,128)S(1)}, u32[]{:S(2)}, u32[]{:S(2)}) collective-permute-start(f32[2,3,4,32,256]{4,3,2,1,0:T(8,128)} %get-tuple-element.42), channel_id=1, source_target_pairs={{0,4},{4,8},{8,12},{12,16},{16,20},{20,24},{24,28},{28,32},{32,36}... | collective-permute-start | bytes 2359304 | tf_op jit(solution)/shard_map/ppermute | solution.py:26
  18.4 1.3 %collective-permute-start.1 = (f32[2,3,4,32,256]{4,3,2,1,0:T(8,128)}, f32[2,3,4,32,256]{4,3,2,1,0:T(8,128)}, u32[]{:S(2)}, u32[]{:S(2)}) collective-permute-start(f32[2,3,4,32,256]{4,3,2,1,0:T(8,128)} %get-tuple-element.43), channel_id=1, source_target_pairs={{4,0},{8,4},{12,8},{16,12},{20,16},{24,20},{28,24},{32,28},{36,32}... | collective-permute-start | bytes 2359304 | tf_op jit(solution)/shard_map/ppermute | solution.py:26
  19.7 10.0 %shard_map.46.prev_ref = f32[3,24,32,256]{3,2,1,0:T(8,128)} custom-call(f32[3,24,32,256]{3,2,1,0:T(8,128)} %base_ref.5, f32[3,24,32,256]{3,2,1,0:T(8,128)} %adj_ref.5), custom_call_target="tpu_custom_call" | custom-call | tf_op jit(solution)/shard_map/pallas_call | solution.py:89
  29.7 11.5 %all-to-all-done = bf16[6,24,32,1,256]{4,1,0,3,2:T(8,128)(2,1)} async-done(((bf16[6,24,32,1,256]{4,1,0,3,2:T(8,128)(2,1)}), bf16[6,24,32,1,256]{4,1,0,3,2:T(8,128)(2,1)}, u32[]{:S(2)}, u32[]{:S(2)}) %all-to-all-start) | async-done | bytes 2359328 | tf_op jit(solution)/shard_map/all_to_all | solution.py:206
  41.2 2.5 %copy.20 = bf16[6,24,4,8,1,256]{5,3,2,1,0,4:T(8,128)(2,1)S(1)} copy(bf16[6,24,4,8,1,256]{5,1,0,3,2,4:T(8,128)(2,1)} %bitcast.2) | data formatting | bytes 4718592 | tf_op jit(solution)/shard_map/all_to_all | solution.py:206
  43.8 0.0 collective-permute-done.tail_ref
  43.8 0.0 copy-start.2
  43.8 0.0 collective-permute-done.1.head_ref
  43.8 0.2 fusion.10
  44.0 0.6 copy-done.2
  44.7 0.1 convert.1
  44.8 0.0 copy-done
  44.8 1.4 %fusion.5 = f32[3,24,8,1024]{3,2,1,0:T(8,128)S(1)} fusion(bf16[3,24,8,1024]{3,2,1,0:T(8,128)(2,1)S(1)} %bitcast.57, bf16[1024,1024]{1,0:T(8,128)(2,1)S(1)} %copy-done), kind=kOutput, calls=%fused_computation.13 | convolution fusion | flops 1207959552 | bytes 5636096 | tf_op jit(solution)/shard_map/fxzk,ik->fxzi/dot_general | solution.py:218
  46.2 0.0 copy-start.3
  46.2 10.7 %collective-permute-start.2 = (f32[2,3,4,32,256]{4,3,2,1,0:T(8,128)}, f32[2,3,4,32,256]{4,3,2,1,0:T(8,128)}, u32[]{:S(2)}, u32[]{:S(2)}) collective-permute-start(f32[2,3,4,32,256]{4,3,2,1,0:T(8,128)} %get-tuple-element.28), channel_id=1, source_target_pairs={{124,128},{252,0},{128,124},{0,252},{125,129},{253,1},{129,125},{1... | collective-permute-start | bytes 2359304 | tf_op jit(solution)/shard_map/ppermute | solution.py:220
  56.9 0.4 multiply_reduce_fusion
  57.3 0.0 copy-done.3
  57.3 1.4 %fusion.1 = f32[3,24,8,1024]{3,2,1,0:T(8,128)S(1)} fusion(bf16[3,24,8,1024]{3,2,1,0:T(8,128)(2,1)S(1)} %bitcast.53, bf16[1024,1024]{1,0:T(8,128)(2,1)S(1)} %copy-done.3), kind=kOutput, calls=%fused_computation.9 | convolution fusion | flops 1207959552 | bytes 5636096 | tf_op jit(solution)/shard_map/fxzk,ik->fxzi/dot_general | solution.py:224
  58.8 1.5 %multiply_add_fusion = f32[3,24,8,1024]{3,2,1,0:T(8,128)S(1)} fusion(f32[3,24,8,1024]{3,2,1,0:T(8,128)S(1)} %fusion.1, bf16[3,24,8,1024]{3,2,1,0:T(8,128)(2,1)S(1)} %bitcast.54, bf16[1024,1024]{1,0:T(8,128)(2,1)S(1)} %copy-done, f32[24,8,1024]{2,1,0:T(8,128)S(1)} %convert.1), kind=kOutput, calls=%fused_computation.8 | convolution fusion | flops 1209729024 | bytes 8781824 | tf_op jit(solution)/shard_map/fxzk,ik->fxzi/dot_general | solution.py:223
  60.2 0.2 fusion.9
  60.5 0.2 convert_element_type.33
  60.7 1.1 %copy.10 = bf16[3,24,8,4,256]{4,2,1,0,3:T(8,128)(2,1)} copy(bf16[3,24,8,4,256]{4,2,3,1,0:T(8,128)(2,1)S(1)} %bitcast.55) | data formatting | bytes 2359296 | tf_op jit(solution)/shard_map/optimization_barrier | solution.py:230
  61.8 4.8 %all-to-all-start.1 = ((bf16[3,24,8,4,256]{4,2,1,0,3:T(8,128)(2,1)}), bf16[3,24,8,4,256]{4,2,1,0,3:T(8,128)(2,1)S(1)}, u32[]{:S(2)}, u32[]{:S(2)}) async-start(bf16[3,24,8,4,256]{4,2,1,0,3:T(8,128)(2,1)} %copy.10), calls=%async_computation.1 | async-start | bytes 2359296 | tf_op jit(solution)/shard_map/all_to_all | solution.py:231
  66.5 7.3 %shard_map.47.prev_ref = f32[3,24,32,256]{3,2,1,0:T(8,128)} custom-call(f32[3,24,32,256]{3,2,1,0:T(8,128)} %base_ref.5, f32[3,24,32,256]{3,2,1,0:T(8,128)} %adj_ref.5, f32[2,3,4,32,256]{4,3,2,1,0:T(8,128)} %copy-done.2, f32[2,3,4,32,256]{4,3,2,1,0:T(8,128)} %collective-permute-done.1.head_ref, ...), custom_call_target="tpu_custom_call", output_to_operand_aliasing={{}: (4, {})} | custom-call | tf_op jit(solution)/shard_map/pallas_call | solution.py:131
  73.8 0.4 collective-permute-done.2
  74.2 2.2 %broadcast_select_fusion.1.halo_ref = f32[2,3,4,32,256]{4,3,2,1,0:T(8,128)} fusion(f32[2,3,4,32,256]{4,3,2,1,0:T(8,128)} %collective-permute-done.2, f32[2,3,4,32,256]{4,3,2,1,0:T(8,128)} %copy-done.2, pred[]{:T(512)S(6)} %or.11), kind=kLoop, calls=%fused_computation.24 | loop fusion | flops 196608 | bytes 2359297 | tf_op jit(solution)/shard_map/jit(_where)/select_n | solution.py:222
  76.4 4.1 %shard_map.48 = f32[3,24,32,256]{3,2,1,0:T(8,128)} custom-call(s32[1]{0:T(128)} %bitcast.side_ref, f32[3,24,32,256]{3,2,1,0:T(8,128)} %base_ref.5, f32[3,24,32,256]{3,2,1,0:T(8,128)} %adj_ref.5, f32[2,3,4,32,256]{4,3,2,1,0:T(8,128)} %broadcast_select_fusion.1.halo_ref, f32[3,24,32,256]{3,2,1,0:T(8,128)} %shard_map.47.prev_ref), custom_call_target="tpu_custom_call", output_to_operand_aliasing={{}: (4, {})} | custom-call | tf_op jit(solution)/shard_map/pallas_call | solution.py:189
  80.5 4.9 %all-to-all-done.1 = bf16[3,24,8,4,256]{4,2,1,0,3:T(8,128)(2,1)S(1)} async-done(((bf16[3,24,8,4,256]{4,2,1,0,3:T(8,128)(2,1)}), bf16[3,24,8,4,256]{4,2,1,0,3:T(8,128)(2,1)S(1)}, u32[]{:S(2)}, u32[]{:S(2)}) %all-to-all-start.1) | async-done | bytes 1179680 | tf_op jit(solution)/shard_map/all_to_all | solution.py:231
  85.4 3.6 %fusion = f32[3,24,32,256]{3,2,1,0:T(8,128)} fusion(f32[3,24,32,256]{3,2,1,0:T(8,128)} %shard_map.48, pred[256]{0:T(512)(128)(4,1)S(1)} %compare_and_fusion, bf16[3,24,8,4,256]{4,2,1,0,3:T(8,128)(2,1)S(1)} %all-to-all-done.1), kind=kLoop, calls=%fused_computation.2 | loop fusion | flops 2359296 | bytes 5898496 | tf_op jit(solution)/shard_map/jit(_where)/select_n | solution.py:239
  (2 shorter events, 0.0 us)
Async XLA Ops:
  0.0 44.8 %copy-start = (bf16[1024,1024]{1,0:T(8,128)(2,1)S(1)}, bf16[1024,1024]{1,0:T(8,128)(2,1)}, u32[]{:S(2)}) copy-start(bf16[1024,1024]{1,0:T(8,128)(2,1)} %param.8) | copy-start | bytes 6291460
  0.0 3.1 %copy-start.1 = (f32[3,24,32,256]{3,2,1,0:T(8,128)S(1)}, f32[3,24,32,256]{3,2,1,0:T(8,128)}, u32[]{:S(2)}) copy-start(f32[3,24,32,256]{3,2,1,0:T(8,128)} %adj_ref.5) | copy-start | bytes 7077892
  6.0 35.3 %all-to-all-start = ((bf16[6,24,32,1,256]{4,1,0,3,2:T(8,128)(2,1)}), bf16[6,24,32,1,256]{4,1,0,3,2:T(8,128)(2,1)}, u32[]{:S(2)}, u32[]{:S(2)}) async-start(bf16[6,24,32,1,256]{4,1,0,3,2:T(8,128)(2,1)} %maximum_bitcast_fusion), calls=%async_computation | async-start | bytes 4718592 | tf_op jit(solution)/shard_map/all_to_all | solution.py:206
  16.6 27.2 %collective-permute-start = (f32[2,3,4,32,256]{4,3,2,1,0:T(8,128)}, f32[2,3,4,32,256]{4,3,2,1,0:T(8,128)S(1)}, u32[]{:S(2)}, u32[]{:S(2)}) collective-permute-start(f32[2,3,4,32,256]{4,3,2,1,0:T(8,128)} %get-tuple-element.42), channel_id=1, source_target_pairs={{0,4},{4,8},{8,12},{12,16},{16,20},{20,24},{24,28},{28,32},{32,36}... | collective-permute-start | bytes 2359304 | tf_op jit(solution)/shard_map/ppermute | solution.py:26
  18.4 25.3 %collective-permute-start.1 = (f32[2,3,4,32,256]{4,3,2,1,0:T(8,128)}, f32[2,3,4,32,256]{4,3,2,1,0:T(8,128)}, u32[]{:S(2)}, u32[]{:S(2)}) collective-permute-start(f32[2,3,4,32,256]{4,3,2,1,0:T(8,128)} %get-tuple-element.43), channel_id=1, source_target_pairs={{4,0},{8,4},{12,8},{16,12},{20,16},{24,20},{28,24},{32,28},{36,32}... | collective-permute-start | bytes 2359304 | tf_op jit(solution)/shard_map/ppermute | solution.py:26
  43.8 0.9 %copy-start.2 = (f32[2,3,4,32,256]{4,3,2,1,0:T(8,128)}, f32[2,3,4,32,256]{4,3,2,1,0:T(8,128)S(1)}, u32[]{:S(2)}) copy-start(f32[2,3,4,32,256]{4,3,2,1,0:T(8,128)S(1)} %collective-permute-done.tail_ref) | copy-start | bytes 2359300
  46.2 11.1 %copy-start.3 = (bf16[1024,1024]{1,0:T(8,128)(2,1)S(1)}, bf16[1024,1024]{1,0:T(8,128)(2,1)}, u32[]{:S(2)}) copy-start(bf16[1024,1024]{1,0:T(8,128)(2,1)} %param.9) | copy-start | bytes 6291460
  46.2 28.0 %collective-permute-start.2 = (f32[2,3,4,32,256]{4,3,2,1,0:T(8,128)}, f32[2,3,4,32,256]{4,3,2,1,0:T(8,128)}, u32[]{:S(2)}, u32[]{:S(2)}) collective-permute-start(f32[2,3,4,32,256]{4,3,2,1,0:T(8,128)} %get-tuple-element.28), channel_id=1, source_target_pairs={{124,128},{252,0},{128,124},{0,252},{125,129},{253,1},{129,125},{1... | collective-permute-start | bytes 2359304 | tf_op jit(solution)/shard_map/ppermute | solution.py:220
  61.8 23.6 %all-to-all-start.1 = ((bf16[3,24,8,4,256]{4,2,1,0,3:T(8,128)(2,1)}), bf16[3,24,8,4,256]{4,2,1,0,3:T(8,128)(2,1)S(1)}, u32[]{:S(2)}, u32[]{:S(2)}) async-start(bf16[3,24,8,4,256]{4,2,1,0,3:T(8,128)(2,1)} %copy.10), calls=%async_computation.1 | async-start | bytes 2359296 | tf_op jit(solution)/shard_map/all_to_all | solution.py:231

commit v15 on v13

--- a/solution.py
+++ b/solution.py
@@ -211,8 +211,8 @@
     count = lax.axis_size("gx")
     far_all = [i for i in range(count) if far[i]]
     assert far_all
-    early_links = [i for i in far_all if i != count - 1]
-    late_links = [i for i in far_all if i == count - 1]
+    early_links = [i for i in far_all if i == count - 1]
+    late_links = [i for i in far_all if i != count - 1]
     _, sends_tail, gets_tail = far_plan(far_all)
     far_send = jnp.where(sends_tail, tail_cells, head_cells)
     partial = interior_update(base_flow, adjoint)

time: 102 us -> 88 us (0.86)
  starting transfers between devices: 46.7 us -> 28.7 us
  waiting for transfers between devices: 8.7 us -> 12.7 us
    ppermute x1, starting transfers between devices: 27.5 us -> 1.56 us  [body(): received = received + lax.ppermute(far_send, 'gx', far_plan(late_links)[0])]
    all_to_all x1, waiting for transfers between devices: 0.96 us -> 12.7 us  [body(): lax.all_to_all(wall_part, 'gy', split_axis=3, concat_axis=2, tiled=True)]
    ppermute x1, starting transfers between devices: 1.54 us -> 10.1 us  [body(): received = lax.ppermute(far_send, 'gx', far_plan(early_links)[0])]
    all_to_all x1, waiting for transfers between devices: 7.73 us -> 0.01 us  [body(): lines = lax.all_to_all(low, 'gy', split_axis=2, concat_axis=3, tiled=True)]
  transfers between devices with their start and end apart: 6 -> 6, of which waited for: 2 -> 1; matrix products, arithmetic and copies ran while one was open for 14% -> 16% of each run, Pallas kernels for 21% -> 25%
where the time goes in v15:
time: 88 us; the launch traced here: 87.4 us
  starting transfers between devices  28.7 us (33%)
  Pallas kernels  21.4 us (24%)
  waiting for transfers between devices  12.7 us (14%)
  local copies, waits for them, and re-layouts  10.3 us (12%)
  other arithmetic  9.75 us (11%)
  matrix products  4.32 us (5%)
    all_to_all x1, waiting for transfers between devices, body(): lax.all_to_all(wall_part, 'gy', split_axis=3, concat_axis=2, tiled=True)  12.7 us
    ppermute x1, starting transfers between devices, body(): received = lax.ppermute(far_send, 'gx', far_plan(early_links)[0])  10.1 us
    pallas_call x1, Pallas kernels, interior_update(): pl.pallas_call(interior_kernel, grid=(rows // LANES, cells // HALO - 2),...  10 us
    all_to_all x1, starting transfers between devices, body(): lines = lax.all_to_all(low, 'gy', split_axis=2, concat_axis=3, tiled=True)  7.66 us
    pallas_call x1, Pallas kernels, boundary_update(): pl.pallas_call(boundary_kernel, grid=(2,), in_specs=[full_spec, full_spec...  7.28 us
    ppermute x2, starting transfers between devices, ring_shift(): return lax.ppermute(value, axis, pairs)  5.32 us
    unnamed x10, local copies, waits for them, and re-layouts  4.97 us
    pallas_call x1, Pallas kernels, side_update(): pl.pallas_call(side_kernel, grid_spec=grid_spec, out_shape=jax.ShapeDtype...  4.15 us
  transfers between devices with their start and end apart: 6, of which 1 were waited for; matrix products, arithmetic and copies ran while one was open for 16% of the time, Pallas kernels for 25%

profile of v15, /device:TPU:1, one launch (start us, length us, event | category | flops | bytes accessed | tf_op | source)
XLA Modules:
  0.0 87.4 jit_solution(10989771779390803199)
XLA Ops:
  0.0 0.0 copy-start
  0.0 0.0 copy-start.1
  0.0 3.1 %copy.19 = bf16[3,24,32,256]{3,1,0,2:T(8,128)(2,1)S(1)} copy(f32[3,24,32,256]{3,2,1,0:T(8,128)} %base_ref.5) | data formatting | bytes 3538944 | tf_op args[0]
  3.1 0.0 copy-done.1
  3.1 1.3 %copy.18 = bf16[3,24,32,256]{3,1,0,2:T(8,128)(2,1)S(1)} copy(f32[3,24,32,256]{3,2,1,0:T(8,128)S(1)} %copy-done.1) | data formatting | bytes 3538944 | tf_op args[1]
  4.4 1.6 %maximum_bitcast_fusion = bf16[6,24,32,1,256]{4,1,0,3,2:T(8,128)(2,1)} fusion(bf16[3,24,32,256]{3,1,0,2:T(8,128)(2,1)S(1)} %copy.18, bf16[3,24,32,256]{3,1,0,2:T(8,128)(2,1)S(1)} %copy.19), kind=kLoop, calls=%fused_computation | loop fusion | flops 1179648 | bytes 4718592 | tf_op jit(solution)/shard_map/reshape | solution.py:205
  6.0 7.7 %all-to-all-start = ((bf16[6,24,32,1,256]{4,1,0,3,2:T(8,128)(2,1)}), bf16[6,24,32,1,256]{4,1,0,3,2:T(8,128)(2,1)}, u32[]{:S(2)}, u32[]{:S(2)}) async-start(bf16[6,24,32,1,256]{4,1,0,3,2:T(8,128)(2,1)} %maximum_bitcast_fusion), calls=%async_computation | async-start | bytes 4718592 | tf_op jit(solution)/shard_map/all_to_all | solution.py:206
  13.6 1.5 %slice_bitcast_fusion.2 = (f32[1,3,4,32,256]{4,3,2,1,0:T(8,128)S(1)}, f32[1,3,4,32,256]{4,3,2,1,0:T(8,128)S(1)}, f32[1,3,4,32,256]{4,3,2,1,0:T(8,128)S(1)}, f32[1,3,4,32,256]{4,3,2,1,0:T(8,128)S(1)}) fusion(f32[3,24,32,256]{3,2,1,0:T(8,128)} %adj_ref.5, f32[3,24,32,256]{3,2,1,0:T(8,128)} %base_ref.5), kind=kLoop, calls=%fused_computation.22 | loop fusion | bytes 3145728 | tf_op jit(solution)/shard_map/stack | solution.py:207
  15.1 1.6 %pad_maximum_fusion.1 = (f32[2,3,4,32,256]{4,3,2,1,0:T(8,128)}, f32[2,3,4,32,256]{4,3,2,1,0:T(8,128)}, f32[2,3,4,32,256]{4,3,2,1,0:T(8,128)}) fusion(f32[1,3,4,32,256]{4,3,2,1,0:T(8,128)S(1)} %get-tuple-element.40, f32[1,3,4,32,256]{4,3,2,1,0:T(8,128)S(1)} %get-tuple-element.44, f32[1,3,4,32,256]{4,3,2,1,0:T(8,128)S(1)} %get-tuple-element.39, ...), kind=kLoop, calls=%fused_computation.18 | loop fusion | flops 589824 | bytes 3932161 | tf_op jit(solution)/shard_map/stack | solution.py:208
  16.6 1.3 %collective-permute-start.2 = (f32[2,3,4,32,256]{4,3,2,1,0:T(8,128)}, f32[2,3,4,32,256]{4,3,2,1,0:T(8,128)}, u32[]{:S(2)}, u32[]{:S(2)}) collective-permute-start(f32[2,3,4,32,256]{4,3,2,1,0:T(8,128)} %get-tuple-element.41), channel_id=1, source_target_pairs={{4,0},{8,4},{12,8},{16,12},{20,16},{24,20},{28,24},{32,28},{36,32}... | collective-permute-start | bytes 2359304 | tf_op jit(solution)/shard_map/ppermute | solution.py:26
  17.9 4.0 %collective-permute-start.1 = (f32[2,3,4,32,256]{4,3,2,1,0:T(8,128)}, f32[2,3,4,32,256]{4,3,2,1,0:T(8,128)S(1)}, u32[]{:S(2)}, u32[]{:S(2)}) collective-permute-start(f32[2,3,4,32,256]{4,3,2,1,0:T(8,128)} %get-tuple-element.43), channel_id=1, source_target_pairs={{0,4},{4,8},{8,12},{12,16},{16,20},{20,24},{24,28},{28,32},{32,36}... | collective-permute-start | bytes 2359304 | tf_op jit(solution)/shard_map/ppermute | solution.py:26
  22.0 10.0 %shard_map.46.prev_ref = f32[3,24,32,256]{3,2,1,0:T(8,128)} custom-call(f32[3,24,32,256]{3,2,1,0:T(8,128)} %base_ref.5, f32[3,24,32,256]{3,2,1,0:T(8,128)} %adj_ref.5), custom_call_target="tpu_custom_call" | custom-call | tf_op jit(solution)/shard_map/pallas_call | solution.py:89
  32.0 10.1 %collective-permute-start = (f32[2,3,4,32,256]{4,3,2,1,0:T(8,128)}, f32[2,3,4,32,256]{4,3,2,1,0:T(8,128)}, u32[]{:S(2)}, u32[]{:S(2)}) collective-permute-start(f32[2,3,4,32,256]{4,3,2,1,0:T(8,128)} %get-tuple-element.28), channel_id=1, source_target_pairs={{252,0},{0,252},{253,1},{1,253},{254,2},{2,254},{255,3},{3,255}} | collective-permute-start | bytes 2359304 | tf_op jit(solution)/shard_map/ppermute | solution.py:222
  42.0 0.0 all-to-all-done
  42.1 2.5 %copy.20 = bf16[6,24,4,8,1,256]{5,3,2,1,0,4:T(8,128)(2,1)S(1)} copy(bf16[6,24,4,8,1,256]{5,1,0,3,2,4:T(8,128)(2,1)} %bitcast.6) | data formatting | bytes 4718592 | tf_op jit(solution)/shard_map/all_to_all | solution.py:206
  44.6 0.0 collective-permute-done.2.head_ref
  44.6 0.0 collective-permute-done.1.tail_ref
  44.6 0.0 copy-start.2
  44.7 0.0 copy-start.3
  44.7 0.2 fusion.12
  44.9 0.6 copy-done.2
  45.5 0.1 convert.1
  45.6 1.6 %collective-permute-start.3 = (f32[2,3,4,32,256]{4,3,2,1,0:T(8,128)}, f32[2,3,4,32,256]{4,3,2,1,0:T(8,128)}, u32[]{:S(2)}, u32[]{:S(2)}) collective-permute-start(f32[2,3,4,32,256]{4,3,2,1,0:T(8,128)} %get-tuple-element.28), channel_id=1, source_target_pairs={{124,128},{128,124},{125,129},{129,125},{126,130},{130,126},{127,1... | collective-permute-start | bytes 2359304 | tf_op jit(solution)/shard_map/ppermute | solution.py:225
  47.1 0.0 copy-done.3
  47.2 1.4 %fusion.1 = f32[3,24,8,1024]{3,2,1,0:T(8,128)S(1)} fusion(bf16[3,24,8,1024]{3,2,1,0:T(8,128)(2,1)S(1)} %bitcast.54, bf16[1024,1024]{1,0:T(8,128)(2,1)S(1)} %copy-done.3), kind=kOutput, calls=%fused_computation.9 | convolution fusion | flops 1207959552 | bytes 5636096 | tf_op jit(solution)/shard_map/fxzk,ik->fxzi/dot_general | solution.py:233
  48.6 0.0 copy-done
  48.6 1.5 %multiply_reduce_fusion = f32[24,8,1024]{2,1,0:T(8,128)S(1)} fusion(bf16[3,24,8,1024]{3,2,1,0:T(8,128)(2,1)S(1)} %bitcast.55, bf16[3,24,8,1024]{3,2,1,0:T(8,128)(2,1)S(1)} %bitcast.59, bf16[1024,1024]{1,0:T(8,128)(2,1)S(1)} %copy-done), kind=kOutput, calls=%fused_computation.7 | convolution fusion | flops 1209532416 | bytes 5242880 | tf_op jit(solution)/shard_map/fxzk,ik->fxzi/dot_general | solution.py:231
  50.0 1.5 %multiply_add_fusion = f32[3,24,8,1024]{3,2,1,0:T(8,128)S(1)} fusion(f32[3,24,8,1024]{3,2,1,0:T(8,128)S(1)} %fusion.1, bf16[3,24,8,1024]{3,2,1,0:T(8,128)(2,1)S(1)} %bitcast.56, bf16[1024,1024]{1,0:T(8,128)(2,1)S(1)} %copy-done, f32[24,8,1024]{2,1,0:T(8,128)S(1)} %convert.1), kind=kOutput, calls=%fused_computation.8 | convolution fusion | flops 1209729024 | bytes 8781824 | tf_op jit(solution)/shard_map/fxzk,ik->fxzi/dot_general | solution.py:232
  51.5 0.2 fusion.11
  51.8 0.2 convert_element_type.33
  51.9 1.1 %copy.10 = bf16[3,24,8,4,256]{4,2,1,0,3:T(8,128)(2,1)} copy(bf16[3,24,8,4,256]{4,2,3,1,0:T(8,128)(2,1)S(1)} %bitcast.57) | data formatting | bytes 2359296 | tf_op jit(solution)/shard_map/optimization_barrier | solution.py:239
  53.1 4.1 %all-to-all-start.1 = ((bf16[3,24,8,4,256]{4,2,1,0,3:T(8,128)(2,1)}), bf16[3,24,8,4,256]{4,2,1,0,3:T(8,128)(2,1)S(1)}, u32[]{:S(2)}, u32[]{:S(2)}) async-start(bf16[3,24,8,4,256]{4,2,1,0,3:T(8,128)(2,1)} %copy.10), calls=%async_computation.1 | async-start | bytes 2359296 | tf_op jit(solution)/shard_map/all_to_all | solution.py:240
  57.2 7.3 %shard_map.47.prev_ref = f32[3,24,32,256]{3,2,1,0:T(8,128)} custom-call(f32[3,24,32,256]{3,2,1,0:T(8,128)} %base_ref.5, f32[3,24,32,256]{3,2,1,0:T(8,128)} %adj_ref.5, f32[2,3,4,32,256]{4,3,2,1,0:T(8,128)} %copy-done.2, f32[2,3,4,32,256]{4,3,2,1,0:T(8,128)} %collective-permute-done.2.head_ref, ...), custom_call_target="tpu_custom_call", output_to_operand_aliasing={{}: (4, {})} | custom-call | tf_op jit(solution)/shard_map/pallas_call | solution.py:131
  64.5 0.0 collective-permute-done
  64.5 0.0 collective-permute-done.3
  64.5 2.5 %add_select_fusion.halo_ref = f32[2,3,4,32,256]{4,3,2,1,0:T(8,128)} fusion(f32[2,3,4,32,256]{4,3,2,1,0:T(8,128)} %copy-done.2, f32[2,3,4,32,256]{4,3,2,1,0:T(8,128)} %collective-permute-done, f32[2,3,4,32,256]{4,3,2,1,0:T(8,128)} %collective-permute-done.3, pred[]{:T(512)S(6)} %or.11), kind=kLoop, calls=%fused_computation.19 | loop fusion | flops 393216 | bytes 3145729 | tf_op jit(solution)/shard_map/jit(_where)/select_n | solution.py:227
  67.0 4.1 %shard_map.48 = f32[3,24,32,256]{3,2,1,0:T(8,128)} custom-call(s32[1]{0:T(128)} %bitcast.side_ref, f32[3,24,32,256]{3,2,1,0:T(8,128)} %base_ref.5, f32[3,24,32,256]{3,2,1,0:T(8,128)} %adj_ref.5, f32[2,3,4,32,256]{4,3,2,1,0:T(8,128)} %add_select_fusion.halo_ref, f32[3,24,32,256]{3,2,1,0:T(8,128)} %shard_map.47.prev_ref), custom_call_target="tpu_custom_call", output_to_operand_aliasing={{}: (4, {})} | custom-call | tf_op jit(solution)/shard_map/pallas_call | solution.py:189
  71.1 12.7 %all-to-all-done.1 = bf16[3,24,8,4,256]{4,2,1,0,3:T(8,128)(2,1)S(1)} async-done(((bf16[3,24,8,4,256]{4,2,1,0,3:T(8,128)(2,1)}), bf16[3,24,8,4,256]{4,2,1,0,3:T(8,128)(2,1)S(1)}, u32[]{:S(2)}, u32[]{:S(2)}) %all-to-all-start.1) | async-done | bytes 1179680 | tf_op jit(solution)/shard_map/all_to_all | solution.py:240
  83.8 3.6 %fusion = f32[3,24,32,256]{3,2,1,0:T(8,128)} fusion(f32[3,24,32,256]{3,2,1,0:T(8,128)} %shard_map.48, pred[256]{0:T(512)(128)(4,1)S(1)} %compare_and_fusion, bf16[3,24,8,4,256]{4,2,1,0,3:T(8,128)(2,1)S(1)} %all-to-all-done.1), kind=kLoop, calls=%fused_computation.2 | loop fusion | flops 2359296 | bytes 5898496 | tf_op jit(solution)/shard_map/jit(_where)/select_n | solution.py:248
  (2 shorter events, 0.0 us)
Async XLA Ops:
  0.0 48.6 %copy-start = (bf16[1024,1024]{1,0:T(8,128)(2,1)S(1)}, bf16[1024,1024]{1,0:T(8,128)(2,1)}, u32[]{:S(2)}) copy-start(bf16[1024,1024]{1,0:T(8,128)(2,1)} %param.8) | copy-start | bytes 6291460
  0.0 3.1 %copy-start.1 = (f32[3,24,32,256]{3,2,1,0:T(8,128)S(1)}, f32[3,24,32,256]{3,2,1,0:T(8,128)}, u32[]{:S(2)}) copy-start(f32[3,24,32,256]{3,2,1,0:T(8,128)} %adj_ref.5) | copy-start | bytes 7077892
  6.0 36.1 %all-to-all-start = ((bf16[6,24,32,1,256]{4,1,0,3,2:T(8,128)(2,1)}), bf16[6,24,32,1,256]{4,1,0,3,2:T(8,128)(2,1)}, u32[]{:S(2)}, u32[]{:S(2)}) async-start(bf16[6,24,32,1,256]{4,1,0,3,2:T(8,128)(2,1)} %maximum_bitcast_fusion), calls=%async_computation | async-start | bytes 4718592 | tf_op jit(solution)/shard_map/all_to_all | solution.py:206
  16.6 28.0 %collective-permute-start.2 = (f32[2,3,4,32,256]{4,3,2,1,0:T(8,128)}, f32[2,3,4,32,256]{4,3,2,1,0:T(8,128)}, u32[]{:S(2)}, u32[]{:S(2)}) collective-permute-start(f32[2,3,4,32,256]{4,3,2,1,0:T(8,128)} %get-tuple-element.41), channel_id=1, source_target_pairs={{4,0},{8,4},{12,8},{16,12},{20,16},{24,20},{28,24},{32,28},{36,32}... | collective-permute-start | bytes 2359304 | tf_op jit(solution)/shard_map/ppermute | solution.py:26
  17.9 26.7 %collective-permute-start.1 = (f32[2,3,4,32,256]{4,3,2,1,0:T(8,128)}, f32[2,3,4,32,256]{4,3,2,1,0:T(8,128)S(1)}, u32[]{:S(2)}, u32[]{:S(2)}) collective-permute-start(f32[2,3,4,32,256]{4,3,2,1,0:T(8,128)} %get-tuple-element.43), channel_id=1, source_target_pairs={{0,4},{4,8},{8,12},{12,16},{16,20},{20,24},{24,28},{28,32},{32,36}... | collective-permute-start | bytes 2359304 | tf_op jit(solution)/shard_map/ppermute | solution.py:26
  32.0 32.5 %collective-permute-start = (f32[2,3,4,32,256]{4,3,2,1,0:T(8,128)}, f32[2,3,4,32,256]{4,3,2,1,0:T(8,128)}, u32[]{:S(2)}, u32[]{:S(2)}) collective-permute-start(f32[2,3,4,32,256]{4,3,2,1,0:T(8,128)} %get-tuple-element.28), channel_id=1, source_target_pairs={{252,0},{0,252},{253,1},{1,253},{254,2},{2,254},{255,3},{3,255}} | collective-permute-start | bytes 2359304 | tf_op jit(solution)/shard_map/ppermute | solution.py:222
  44.6 0.9 %copy-start.2 = (f32[2,3,4,32,256]{4,3,2,1,0:T(8,128)}, f32[2,3,4,32,256]{4,3,2,1,0:T(8,128)S(1)}, u32[]{:S(2)}) copy-start(f32[2,3,4,32,256]{4,3,2,1,0:T(8,128)S(1)} %collective-permute-done.1.tail_ref) | copy-start | bytes 2359300
  44.7 2.5 %copy-start.3 = (bf16[1024,1024]{1,0:T(8,128)(2,1)S(1)}, bf16[1024,1024]{1,0:T(8,128)(2,1)}, u32[]{:S(2)}) copy-start(bf16[1024,1024]{1,0:T(8,128)(2,1)} %param.9) | copy-start | bytes 6291460
  45.6 18.9 %collective-permute-start.3 = (f32[2,3,4,32,256]{4,3,2,1,0:T(8,128)}, f32[2,3,4,32,256]{4,3,2,1,0:T(8,128)}, u32[]{:S(2)}, u32[]{:S(2)}) collective-permute-start(f32[2,3,4,32,256]{4,3,2,1,0:T(8,128)} %get-tuple-element.28), channel_id=1, source_target_pairs={{124,128},{128,124},{125,129},{129,125},{126,130},{130,126},{127,1... | collective-permute-start | bytes 2359304 | tf_op jit(solution)/shard_map/ppermute | solution.py:225
  53.1 30.7 %all-to-all-start.1 = ((bf16[3,24,8,4,256]{4,2,1,0,3:T(8,128)(2,1)}), bf16[3,24,8,4,256]{4,2,1,0,3:T(8,128)(2,1)S(1)}, u32[]{:S(2)}, u32[]{:S(2)}) async-start(bf16[3,24,8,4,256]{4,2,1,0,3:T(8,128)(2,1)} %copy.10), calls=%async_computation.1 | async-start | bytes 2359296 | tf_op jit(solution)/shard_map/all_to_all | solution.py:240

commit v16 on v11

--- a/solution.py
+++ b/solution.py
@@ -200,9 +200,8 @@
     total_rows = local_rows * groups
     part = spanwise // groups
 
-    base_low = lax.optimization_barrier(base_flow.astype(jnp.bfloat16))
-    adjoint_low = lax.optimization_barrier(adjoint.astype(jnp.bfloat16))
-    low = jnp.concatenate((base_low, adjoint_low), 0).reshape(2 * comps, cells, spanwise, 1, local_rows)
+    low = jnp.concatenate((base_flow, adjoint), 0).astype(jnp.bfloat16)
+    low = low.reshape(2 * comps, cells, spanwise, 1, local_rows)
     lines = lax.all_to_all(low, "gy", split_axis=2, concat_axis=3, tiled=True)
     tail_cells = jnp.stack((base_flow[:, cells - HALO :], adjoint[:, cells - HALO :]), 0)
     head_cells = jnp.stack((base_flow[:, :HALO], adjoint[:, :HALO]), 0)

time: 88 us -> 88.7 us (level)
    concatenate x0 -> x1, local copies, waits for them, and re-layouts: none -> 5.03 us  [body(): low = jnp.concatenate((base_flow, adjoint), 0).astype(jnp.bfloat16)]
    unnamed x10 -> x6, local copies, waits for them, and re-layouts: 4.98 us -> 0.64 us
    concatenate x0 -> x1, other arithmetic: none -> 1.61 us  [body(): low = jnp.concatenate((base_flow, adjoint), 0).astype(jnp.bfloat16)]
    reshape x1 -> x0, other arithmetic: 1.61 us -> none  [body(): jnp.concatenate((base_low, adjoint_low), 0)]
  transfers between devices with their start and end apart: 5 -> 5, of which waited for: 2 -> 2; matrix products, arithmetic and copies ran while one was open for 15% -> 15% of each run, Pallas kernels for 25% -> 24%
where the time goes in v16:
time: 88.7 us; the launch traced here: 88.1 us
  starting transfers between devices  26.1 us (29%)
  Pallas kernels  21.4 us (24%)
  waiting for transfers between devices  15.7 us (18%)
  local copies, waits for them, and re-layouts  11 us (12%)
  other arithmetic  9.39 us (11%)
  matrix products  4.33 us (5%)
    all_to_all x1, waiting for transfers between devices, body(): lines = lax.all_to_all(low, 'gy', split_axis=2, concat_axis=3, tiled=True)  11.5 us
    ppermute x1, starting transfers between devices, body(): received = lax.ppermute(far_send, 'gx', far_pairs)  10.6 us
    pallas_call x1, Pallas kernels, interior_update(): pl.pallas_call(interior_kernel, grid=(rows // LANES, cells // HALO - 2),...  10 us
    all_to_all x1, starting transfers between devices, body(): lines = lax.all_to_all(low, 'gy', split_axis=2, concat_axis=3, tiled=True)  7.64 us
    pallas_call x1, Pallas kernels, boundary_update(): pl.pallas_call(boundary_kernel, grid=(2,), in_specs=[full_spec, full_spec...  7.28 us
    concatenate x1, local copies, waits for them, and re-layouts, body(): low = jnp.concatenate((base_flow, adjoint), 0).astype(jnp.bfloat16)  5.03 us
    all_to_all x1, starting transfers between devices, body(): lax.all_to_all(wall_part, 'gy', split_axis=3, concat_axis=2, tiled=True)  4.74 us
    all_to_all x1, waiting for transfers between devices, body(): lax.all_to_all(wall_part, 'gy', split_axis=3, concat_axis=2, tiled=True)  4.18 us
  transfers between devices with their start and end apart: 5, of which 2 were waited for; matrix products, arithmetic and copies ran while one was open for 15% of the time, Pallas kernels for 24%

profile of v16, /device:TPU:1, one launch (start us, length us, event | category | flops | bytes accessed | tf_op | source)
XLA Modules:
  0.0 88.1 jit_solution(3609820173297190328)
XLA Ops:
  0.0 0.0 copy-start
  0.0 5.0 %fusion.9 = (bf16[3,24,32,1,256]{4,1,0,3,2:T(8,128)(2,1)S(1)}, bf16[3,24,32,1,256]{4,1,0,3,2:T(8,128)(2,1)S(1)}) fusion(f32[3,24,32,256]{3,2,1,0:T(8,128)} %base_ref.5, f32[3,24,32,256]{3,2,1,0:T(8,128)} %adj_ref.5), kind=kLoop, calls=%fused_computation.15 | loop fusion | bytes 7077888 | tf_op jit(solution)/shard_map/concatenate | solution.py:203
  5.0 1.6 %pad_maximum_fusion = bf16[6,24,32,1,256]{4,1,0,3,2:T(8,128)(2,1)} fusion(bf16[3,24,32,1,256]{4,1,0,3,2:T(8,128)(2,1)S(1)} %get-tuple-element.41, bf16[3,24,32,1,256]{4,1,0,3,2:T(8,128)(2,1)S(1)} %get-tuple-element.40), kind=kLoop, calls=%fused_computation | loop fusion | flops 1179648 | bytes 4718592 | tf_op jit(solution)/shard_map/concatenate | solution.py:203
  6.6 7.6 %all-to-all-start = ((bf16[6,24,32,1,256]{4,1,0,3,2:T(8,128)(2,1)}), bf16[6,24,32,1,256]{4,1,0,3,2:T(8,128)(2,1)}, u32[]{:S(2)}, u32[]{:S(2)}) async-start(bf16[6,24,32,1,256]{4,1,0,3,2:T(8,128)(2,1)} %pad_maximum_fusion), calls=%async_computation | async-start | bytes 4718592 | tf_op jit(solution)/shard_map/all_to_all | solution.py:205
  14.3 1.5 %slice_bitcast_fusion = (f32[1,3,4,32,256]{4,3,2,1,0:T(8,128)S(1)}, f32[1,3,4,32,256]{4,3,2,1,0:T(8,128)S(1)}, f32[1,3,4,32,256]{4,3,2,1,0:T(8,128)S(1)}, f32[1,3,4,32,256]{4,3,2,1,0:T(8,128)S(1)}) fusion(f32[3,24,32,256]{3,2,1,0:T(8,128)} %adj_ref.5, f32[3,24,32,256]{3,2,1,0:T(8,128)} %base_ref.5), kind=kLoop, calls=%fused_computation.21 | loop fusion | bytes 3145728 | tf_op jit(solution)/shard_map/stack | solution.py:207
  15.7 1.5 %broadcast_select_fusion = (f32[2,3,4,32,256]{4,3,2,1,0:T(8,128)}, f32[2,3,4,32,256]{4,3,2,1,0:T(8,128)}, f32[2,3,4,32,256]{4,3,2,1,0:T(8,128)}) fusion(pred[]{:T(512)S(6)} %or.9, f32[1,3,4,32,256]{4,3,2,1,0:T(8,128)S(1)} %get-tuple-element.35, f32[1,3,4,32,256]{4,3,2,1,0:T(8,128)S(1)} %get-tuple-element.43, f32[1,3,4,32,256]{4,3,2,1,0:T(8,128)S(1)} %get-tuple-element.36, ...), kind=kLoop, calls=%fused_computation.25 | loop fusion | flops 589824 | bytes 3932161 | tf_op jit(solution)/shard_map/jit(_where)/select_n | solution.py:211
  17.2 1.9 %collective-permute-start = (f32[2,3,4,32,256]{4,3,2,1,0:T(8,128)}, f32[2,3,4,32,256]{4,3,2,1,0:T(8,128)S(1)}, u32[]{:S(2)}, u32[]{:S(2)}) collective-permute-start(f32[2,3,4,32,256]{4,3,2,1,0:T(8,128)} %get-tuple-element.38), channel_id=1, source_target_pairs={{0,4},{4,8},{8,12},{12,16},{16,20},{20,24},{24,28},{28,32},{32,36}... | collective-permute-start | bytes 2359304 | tf_op jit(solution)/shard_map/ppermute | solution.py:26
  19.1 1.3 %collective-permute-start.1 = (f32[2,3,4,32,256]{4,3,2,1,0:T(8,128)}, f32[2,3,4,32,256]{4,3,2,1,0:T(8,128)}, u32[]{:S(2)}, u32[]{:S(2)}) collective-permute-start(f32[2,3,4,32,256]{4,3,2,1,0:T(8,128)} %get-tuple-element.39), channel_id=1, source_target_pairs={{4,0},{8,4},{12,8},{16,12},{20,16},{24,20},{28,24},{32,28},{36,32}... | collective-permute-start | bytes 2359304 | tf_op jit(solution)/shard_map/ppermute | solution.py:26
  20.4 10.0 %shard_map.46.prev_ref = f32[3,24,32,256]{3,2,1,0:T(8,128)} custom-call(f32[3,24,32,256]{3,2,1,0:T(8,128)} %base_ref.5, f32[3,24,32,256]{3,2,1,0:T(8,128)} %adj_ref.5), custom_call_target="tpu_custom_call" | custom-call | tf_op jit(solution)/shard_map/pallas_call | solution.py:89
  30.4 11.5 %all-to-all-done = bf16[6,24,32,1,256]{4,1,0,3,2:T(8,128)(2,1)} async-done(((bf16[6,24,32,1,256]{4,1,0,3,2:T(8,128)(2,1)}), bf16[6,24,32,1,256]{4,1,0,3,2:T(8,128)(2,1)}, u32[]{:S(2)}, u32[]{:S(2)}) %all-to-all-start) | async-done | bytes 2359328 | tf_op jit(solution)/shard_map/all_to_all | solution.py:205
  41.9 2.5 %copy.22 = bf16[6,24,4,8,1,256]{5,3,2,1,0,4:T(8,128)(2,1)S(1)} copy(bf16[6,24,4,8,1,256]{5,1,0,3,2,4:T(8,128)(2,1)} %bitcast.3) | data formatting | bytes 4718592 | tf_op jit(solution)/shard_map/all_to_all | solution.py:205
  44.4 0.0 collective-permute-done.tail_ref
  44.4 0.0 copy-start.1
  44.5 0.0 collective-permute-done.1.head_ref
  44.5 0.0 copy-start.2
  44.5 0.2 fusion.14
  44.7 0.6 copy-done.1
  45.4 0.1 convert.11
  45.4 10.6 %collective-permute-start.2 = (f32[2,3,4,32,256]{4,3,2,1,0:T(8,128)}, f32[2,3,4,32,256]{4,3,2,1,0:T(8,128)}, u32[]{:S(2)}, u32[]{:S(2)}) collective-permute-start(f32[2,3,4,32,256]{4,3,2,1,0:T(8,128)} %get-tuple-element.24), channel_id=1, source_target_pairs={{124,128},{252,0},{128,124},{0,252},{125,129},{253,1},{129,125},{1... | collective-permute-start | bytes 2359304 | tf_op jit(solution)/shard_map/ppermute | solution.py:214
  56.0 0.0 copy-done.2
  56.1 1.4 %fusion.1 = f32[3,24,8,1024]{3,2,1,0:T(8,128)S(1)} fusion(bf16[3,24,8,1024]{3,2,1,0:T(8,128)(2,1)S(1)} %bitcast.56, bf16[1024,1024]{1,0:T(8,128)(2,1)S(1)} %copy-done.2), kind=kOutput, calls=%fused_computation.9 | convolution fusion | flops 1207959552 | bytes 5636096 | tf_op jit(solution)/shard_map/fxzk,ik->fxzi/dot_general | solution.py:222
  57.5 0.0 copy-done
  57.5 1.4 %multiply_reduce_fusion = f32[24,8,1024]{2,1,0:T(8,128)S(1)} fusion(bf16[3,24,8,1024]{3,2,1,0:T(8,128)(2,1)S(1)} %bitcast.57, bf16[3,24,8,1024]{3,2,1,0:T(8,128)(2,1)S(1)} %bitcast.61, bf16[1024,1024]{1,0:T(8,128)(2,1)S(1)} %copy-done), kind=kOutput, calls=%fused_computation.7 | convolution fusion | flops 1209532416 | bytes 5242880 | tf_op jit(solution)/shard_map/fxzk,ik->fxzi/dot_general | solution.py:220
  59.0 1.5 %multiply_add_fusion = f32[3,24,8,1024]{3,2,1,0:T(8,128)S(1)} fusion(f32[3,24,8,1024]{3,2,1,0:T(8,128)S(1)} %fusion.1, bf16[3,24,8,1024]{3,2,1,0:T(8,128)(2,1)S(1)} %bitcast.58, bf16[1024,1024]{1,0:T(8,128)(2,1)S(1)} %copy-done, f32[24,8,1024]{2,1,0:T(8,128)S(1)} %convert.11), kind=kOutput, calls=%fused_computation.8 | convolution fusion | flops 1209729024 | bytes 8781824 | tf_op jit(solution)/shard_map/fxzk,ik->fxzi/dot_general | solution.py:221
  60.4 0.2 fusion.13
  60.7 0.2 convert_element_type.33
  60.8 1.1 %copy.10 = bf16[3,24,8,4,256]{4,2,1,0,3:T(8,128)(2,1)} copy(bf16[3,24,8,4,256]{4,2,3,1,0:T(8,128)(2,1)S(1)} %bitcast.59) | data formatting | bytes 2359296 | tf_op jit(solution)/shard_map/optimization_barrier | solution.py:228
  62.0 4.7 %all-to-all-start.1 = ((bf16[3,24,8,4,256]{4,2,1,0,3:T(8,128)(2,1)}), bf16[3,24,8,4,256]{4,2,1,0,3:T(8,128)(2,1)S(1)}, u32[]{:S(2)}, u32[]{:S(2)}) async-start(bf16[3,24,8,4,256]{4,2,1,0,3:T(8,128)(2,1)} %copy.10), calls=%async_computation.1 | async-start | bytes 2359296 | tf_op jit(solution)/shard_map/all_to_all | solution.py:229
  66.7 7.3 %shard_map.47.prev_ref = f32[3,24,32,256]{3,2,1,0:T(8,128)} custom-call(f32[3,24,32,256]{3,2,1,0:T(8,128)} %base_ref.5, f32[3,24,32,256]{3,2,1,0:T(8,128)} %adj_ref.5, f32[2,3,4,32,256]{4,3,2,1,0:T(8,128)} %copy-done.1, f32[2,3,4,32,256]{4,3,2,1,0:T(8,128)} %collective-permute-done.1.head_ref, ...), custom_call_target="tpu_custom_call", output_to_operand_aliasing={{}: (4, {})} | custom-call | tf_op jit(solution)/shard_map/pallas_call | solution.py:131
  74.0 0.0 collective-permute-done.2
  74.0 2.2 %broadcast_select_fusion.1.halo_ref = f32[2,3,4,32,256]{4,3,2,1,0:T(8,128)} fusion(f32[2,3,4,32,256]{4,3,2,1,0:T(8,128)} %collective-permute-done.2, f32[2,3,4,32,256]{4,3,2,1,0:T(8,128)} %copy-done.1, pred[]{:T(512)S(6)} %or.11), kind=kLoop, calls=%fused_computation.26 | loop fusion | flops 196608 | bytes 2359297 | tf_op jit(solution)/shard_map/jit(_where)/select_n | solution.py:216
  76.2 4.1 %shard_map.48 = f32[3,24,32,256]{3,2,1,0:T(8,128)} custom-call(s32[1]{0:T(128)} %bitcast.side_ref, f32[3,24,32,256]{3,2,1,0:T(8,128)} %base_ref.5, f32[3,24,32,256]{3,2,1,0:T(8,128)} %adj_ref.5, f32[2,3,4,32,256]{4,3,2,1,0:T(8,128)} %broadcast_select_fusion.1.halo_ref, f32[3,24,32,256]{3,2,1,0:T(8,128)} %shard_map.47.prev_ref), custom_call_target="tpu_custom_call", output_to_operand_aliasing={{}: (4, {})} | custom-call | tf_op jit(solution)/shard_map/pallas_call | solution.py:189
  80.3 4.2 %all-to-all-done.1 = bf16[3,24,8,4,256]{4,2,1,0,3:T(8,128)(2,1)S(1)} async-done(((bf16[3,24,8,4,256]{4,2,1,0,3:T(8,128)(2,1)}), bf16[3,24,8,4,256]{4,2,1,0,3:T(8,128)(2,1)S(1)}, u32[]{:S(2)}, u32[]{:S(2)}) %all-to-all-start.1) | async-done | bytes 1179680 | tf_op jit(solution)/shard_map/all_to_all | solution.py:229
  84.5 3.6 %fusion = f32[3,24,32,256]{3,2,1,0:T(8,128)} fusion(f32[3,24,32,256]{3,2,1,0:T(8,128)} %shard_map.48, pred[256]{0:T(512)(128)(4,1)S(1)} %compare_and_fusion, bf16[3,24,8,4,256]{4,2,1,0,3:T(8,128)(2,1)S(1)} %all-to-all-done.1), kind=kLoop, calls=%fused_computation.2 | loop fusion | flops 2359296 | bytes 5898496 | tf_op jit(solution)/shard_map/jit(_where)/select_n | solution.py:237
  (2 shorter events, 0.0 us)
Async XLA Ops:
  0.0 57.5 %copy-start = (bf16[1024,1024]{1,0:T(8,128)(2,1)S(1)}, bf16[1024,1024]{1,0:T(8,128)(2,1)}, u32[]{:S(2)}) copy-start(bf16[1024,1024]{1,0:T(8,128)(2,1)} %param.8) | copy-start | bytes 6291460
  6.6 35.3 %all-to-all-start = ((bf16[6,24,32,1,256]{4,1,0,3,2:T(8,128)(2,1)}), bf16[6,24,32,1,256]{4,1,0,3,2:T(8,128)(2,1)}, u32[]{:S(2)}, u32[]{:S(2)}) async-start(bf16[6,24,32,1,256]{4,1,0,3,2:T(8,128)(2,1)} %pad_maximum_fusion), calls=%async_computation | async-start | bytes 4718592 | tf_op jit(solution)/shard_map/all_to_all | solution.py:205
  17.2 27.2 %collective-permute-start = (f32[2,3,4,32,256]{4,3,2,1,0:T(8,128)}, f32[2,3,4,32,256]{4,3,2,1,0:T(8,128)S(1)}, u32[]{:S(2)}, u32[]{:S(2)}) collective-permute-start(f32[2,3,4,32,256]{4,3,2,1,0:T(8,128)} %get-tuple-element.38), channel_id=1, source_target_pairs={{0,4},{4,8},{8,12},{12,16},{16,20},{20,24},{24,28},{28,32},{32,36}... | collective-permute-start | bytes 2359304 | tf_op jit(solution)/shard_map/ppermute | solution.py:26
  19.1 25.3 %collective-permute-start.1 = (f32[2,3,4,32,256]{4,3,2,1,0:T(8,128)}, f32[2,3,4,32,256]{4,3,2,1,0:T(8,128)}, u32[]{:S(2)}, u32[]{:S(2)}) collective-permute-start(f32[2,3,4,32,256]{4,3,2,1,0:T(8,128)} %get-tuple-element.39), channel_id=1, source_target_pairs={{4,0},{8,4},{12,8},{16,12},{20,16},{24,20},{28,24},{32,28},{36,32}... | collective-permute-start | bytes 2359304 | tf_op jit(solution)/shard_map/ppermute | solution.py:26
  44.4 0.9 %copy-start.1 = (f32[2,3,4,32,256]{4,3,2,1,0:T(8,128)}, f32[2,3,4,32,256]{4,3,2,1,0:T(8,128)S(1)}, u32[]{:S(2)}) copy-start(f32[2,3,4,32,256]{4,3,2,1,0:T(8,128)S(1)} %collective-permute-done.tail_ref) | copy-start | bytes 2359300
  44.5 11.6 %copy-start.2 = (bf16[1024,1024]{1,0:T(8,128)(2,1)S(1)}, bf16[1024,1024]{1,0:T(8,128)(2,1)}, u32[]{:S(2)}) copy-start(bf16[1024,1024]{1,0:T(8,128)(2,1)} %param.9) | copy-start | bytes 6291460
  45.4 28.6 %collective-permute-start.2 = (f32[2,3,4,32,256]{4,3,2,1,0:T(8,128)}, f32[2,3,4,32,256]{4,3,2,1,0:T(8,128)}, u32[]{:S(2)}, u32[]{:S(2)}) collective-permute-start(f32[2,3,4,32,256]{4,3,2,1,0:T(8,128)} %get-tuple-element.24), channel_id=1, source_target_pairs={{124,128},{252,0},{128,124},{0,252},{125,129},{253,1},{129,125},{1... | collective-permute-start | bytes 2359304 | tf_op jit(solution)/shard_map/ppermute | solution.py:214
  62.0 22.5 %all-to-all-start.1 = ((bf16[3,24,8,4,256]{4,2,1,0,3:T(8,128)(2,1)}), bf16[3,24,8,4,256]{4,2,1,0,3:T(8,128)(2,1)S(1)}, u32[]{:S(2)}, u32[]{:S(2)}) async-start(bf16[3,24,8,4,256]{4,2,1,0,3:T(8,128)(2,1)} %copy.10), calls=%async_computation.1 | async-start | bytes 2359296 | tf_op jit(solution)/shard_map/all_to_all | solution.py:229
